TPU v7x, 256 devices: a whole 4x4x8 slice. The times are simulated.
256 devices in a mesh: rep: 32 (over x, y, core), tp: 8 (over z).
Axes of the slice: x: 4, y: 4, z: 8, core: 2. Of those that a mesh axis runs over, the one named last changes fastest.
Arguments:
- prompt_rows: bfloat16 [20480, 2048], P(('rep', 'tp')), may hold values from -6 to 6
- prompt_pieces: int32 [32, 640], P('rep'), may hold values from 0 to 9, never falling along the last dimension, each value on 1 to 320 neighbouring positions
- decode_rows: bfloat16 [1280, 2048], P('rep'), may hold values from -6 to 6
- request_ages: int32 [1280], P('rep'), may hold values from 2 to 127
- migrate_to: int32 [512, 1], P('rep'), may hold values from 0 to 31, as said below
- past_cache: bfloat16 [1280, 2, 128, 2048], P('rep', None, None, 'tp'), may hold values from -8 to 8
- norm_gain: float32 [2048], replicated, may hold values from 0.5 to 1.5
- norm_bias: float32 [2048], replicated, may hold values from -2 to 2
- qkv_weight: bfloat16 [3, 2048, 2048], P(None, None, 'tp'), may hold values from -0.125 to 0.125
- qkv_bias: float32 [3, 2048], P(None, 'tp'), may hold values from -4 to 4
- out_weight: bfloat16 [2048, 2048], P('tp'), may hold values from -0.125 to 0.125
- out_bias: float32 [2048], replicated, may hold values from -3 to 3
Outputs:
- prompt_out: bfloat16 [20480, 2048], P(('rep', 'tp'))
- prompt_cache: bfloat16 [2, 20480, 2048], P(None, 'rep', 'tp')
- kept_out: bfloat16 [768, 2048], P('rep')
- kept_cache: bfloat16 [768, 2, 128, 2048], P('rep', None, None, 'tp')
- moved_out: bfloat16 [1024, 2048], P('rep')
- moved_cache: bfloat16 [1024, 2, 128, 2048], P('rep', None, None, 'tp')
Inputs may be any that keep to these rules, and one draw needn't show every extreme that they name: `migrate_to`: the 16 requests that leave one replica name 16 different target replicas, and one target replica is named by every replica. `prompt_pieces`: piece numbers never fall along a replica's prompt tokens; a piece has at most 320 tokens, and some piece exactly that many.
All inputs are finite; a program needn't handle non-finite values.
Results may differ from a plain program's by a relative error of at most 0.014.
Values may be sent and summed in bfloat16 or wider, within the bound.
No kernel may reach another device: no remote copies, remote signals or barrier semaphores. Data moves between devices by JAX's collectives and lax.ppermute only.
A program may use at most 128 MiB of HBM per device.

v0:
```python
import jax
import jax.numpy as jnp
from jax import lax
from jax.sharding import PartitionSpec as P

HEAD_DIM = 128
CAP = 1


EPSILON = 1e-05


def layer_norm(values, norm_gain, norm_bias):
    wide = values.astype(jnp.float32)
    center = jnp.mean(wide, axis=-1, keepdims=True)
    spread = jnp.mean(jnp.square(wide - center), axis=-1, keepdims=True)
    scaled = (wide - center) * lax.rsqrt(spread + EPSILON)
    return (scaled * norm_gain + norm_bias).astype(jnp.bfloat16)


def decode_partial(
    rows, cache, live, position, norm_gain, norm_bias, qkv_weight, qkv_bias, out_weight
):
    count = rows.shape[0]
    width = qkv_weight.shape[2]
    heads_here = width // HEAD_DIM
    length = cache.shape[2]
    normed = layer_norm(rows, norm_gain, norm_bias)
    projected = jnp.einsum("rd,cde->cre", normed, qkv_weight, preferred_element_type=jnp.float32)
    queries = (projected[0] + qkv_bias[0]).astype(jnp.bfloat16).reshape(count, heads_here, HEAD_DIM)
    key_new = (projected[1] + qkv_bias[1]).astype(jnp.bfloat16)
    value_new = (projected[2] + qkv_bias[2]).astype(jnp.bfloat16)
    old_keys = cache[:, 0].reshape(count, length, heads_here, HEAD_DIM)
    old_values = cache[:, 1].reshape(count, length, heads_here, HEAD_DIM)
    scale = HEAD_DIM ** (-0.5)
    scores = (
        jnp.einsum("rhe,rlhe->rhl", queries, old_keys, preferred_element_type=jnp.float32) * scale
    )
    own = (
        jnp.sum(
            queries.astype(jnp.float32)
            * key_new.astype(jnp.float32).reshape(count, heads_here, HEAD_DIM),
            axis=-1,
        )
        * scale
    )
    scores = jnp.where(live[:, None, :], scores, -1e30)
    highest = jnp.maximum(jnp.max(scores, axis=-1), own)
    weights = jnp.exp(scores - highest[..., None])
    own_weight = jnp.exp(own - highest)
    total = jnp.sum(weights, axis=-1) + own_weight
    probs = (weights / total[..., None]).astype(jnp.bfloat16)
    own_prob = (own_weight / total).astype(jnp.bfloat16)
    context = jnp.einsum("rhl,rlhe->rhe", probs, old_values, preferred_element_type=jnp.float32)
    context = context + own_prob.astype(jnp.float32)[..., None] * value_new.astype(
        jnp.float32
    ).reshape(count, heads_here, HEAD_DIM)
    context = context.reshape(count, width).astype(jnp.bfloat16)
    partial_value = jnp.dot(context, out_weight, preferred_element_type=jnp.float32)
    written = (jnp.arange(length)[None, :] == position[:, None])[:, :, None]
    new_keys = jnp.where(written, key_new[:, None, :], cache[:, 0])
    new_values = jnp.where(written, value_new[:, None, :], cache[:, 1])
    return (partial_value, jnp.stack([new_keys, new_values], axis=1))


def on_device(
    prompt_rows,
    prompt_pieces,
    decode_rows,
    request_ages,
    migrate_to,
    past_cache,
    norm_gain,
    norm_bias,
    qkv_weight,
    qkv_bias,
    out_weight,
    out_bias,
):
    rep_count = lax.axis_size("rep")
    width = qkv_weight.shape[2]
    heads_here = width // HEAD_DIM
    length = past_cache.shape[2]
    leaving = migrate_to.shape[0]
    staying = decode_rows.shape[0] - leaving
    slot_count = rep_count * CAP
    normed = layer_norm(lax.all_gather(prompt_rows, "tp", axis=0, tiled=True), norm_gain, norm_bias)
    projected = jnp.einsum("rd,cde->cre", normed, qkv_weight, preferred_element_type=jnp.float32)
    total_rows = projected.shape[1]
    queries = (projected[0] + qkv_bias[0]).astype(jnp.bfloat16)
    key_rows = (projected[1] + qkv_bias[1]).astype(jnp.bfloat16)
    value_rows = (projected[2] + qkv_bias[2]).astype(jnp.bfloat16)
    head_q = queries.reshape(total_rows, heads_here, HEAD_DIM)
    head_k = key_rows.reshape(total_rows, heads_here, HEAD_DIM)
    head_v = value_rows.reshape(total_rows, heads_here, HEAD_DIM)
    scores = jnp.einsum(
        "qhe,khe->hqk", head_q, head_k, preferred_element_type=jnp.float32
    ) * HEAD_DIM ** (-0.5)
    pieces = prompt_pieces[0]
    position = jnp.arange(total_rows)
    allowed = (pieces[:, None] == pieces[None, :]) & (position[None, :] <= position[:, None])
    scores = jnp.where(allowed[None], scores, -1e30)
    highest = jnp.max(scores, axis=-1, keepdims=True)
    weights = jnp.exp(scores - highest)
    probs = (weights / jnp.sum(weights, axis=-1, keepdims=True)).astype(jnp.bfloat16)
    context = jnp.einsum("hqk,khe->qhe", probs, head_v, preferred_element_type=jnp.float32)
    context = context.reshape(total_rows, width).astype(jnp.bfloat16)
    attended = lax.psum_scatter(
        jnp.dot(context, out_weight, preferred_element_type=jnp.float32).astype(jnp.bfloat16),
        "tp",
        scatter_dimension=0,
        tiled=True,
    ).astype(jnp.float32)
    prompt_out = (prompt_rows.astype(jnp.float32) + attended + out_bias).astype(jnp.bfloat16)
    prompt_cache = jnp.stack([key_rows, value_rows])
    targets = migrate_to[:, 0]
    onehot = (targets[:, None] == jnp.arange(rep_count)[None, :]).astype(jnp.float32)
    lower = (jnp.arange(leaving)[:, None] > jnp.arange(leaving)[None, :]).astype(jnp.float32)
    earlier = jnp.dot(lower, onehot)
    rank = jnp.sum(earlier * onehot, axis=1).astype(jnp.int32)
    slot = targets * CAP + rank
    placing = (jnp.arange(slot_count)[:, None] == slot[None, :]).astype(jnp.bfloat16)
    cells = jnp.arange(length)
    live = cells[None, :] < request_ages[:, None]
    partial_value, updated = decode_partial(
        decode_rows,
        past_cache,
        live,
        request_ages,
        norm_gain,
        norm_bias,
        qkv_weight,
        qkv_bias,
        out_weight,
    )
    summed = lax.psum(partial_value.astype(jnp.bfloat16), "tp").astype(jnp.float32)
    decode_out = (decode_rows.astype(jnp.float32) + summed + out_bias).astype(jnp.bfloat16)
    kept_out = decode_out[:staying]
    kept_cache = updated[:staying]
    send_cache = jnp.einsum(
        "so,oklh->sklh", placing, updated[staying:], preferred_element_type=jnp.float32
    ).astype(jnp.bfloat16)
    send_rows = jnp.dot(placing, decode_out[staying:], preferred_element_type=jnp.float32).astype(
        jnp.bfloat16
    )
    moved_cache, moved_out = (
        lax.all_to_all(send_cache, "rep", split_axis=0, concat_axis=0, tiled=True),
        lax.all_to_all(send_rows, "rep", split_axis=0, concat_axis=0, tiled=True),
    )
    return (prompt_out, prompt_cache, kept_out, kept_cache, moved_out, moved_cache)


def solution(mesh):
    placed = (
        P(("rep", "tp"), None),
        P("rep", None),
        P("rep", None),
        P("rep"),
        P("rep", None),
        P("rep", None, None, "tp"),
        P(),
        P(),
        P(None, None, "tp"),
        P(None, "tp"),
        P("tp", None),
        P(),
    )
    return jax.shard_map(
        on_device,
        mesh=mesh,
        in_specs=placed,
        out_specs=(
            P(("rep", "tp"), None),
            P(None, "rep", "tp"),
            P("rep", None),
            P("rep", None, None, "tp"),
            P("rep", None),
            P("rep", None, None, "tp"),
        ),
        check_vma=False,
    )
```

profile of v0, /device:TPU:8, one launch (start us, length us, event | category | flops | bytes accessed | tf_op | source)
XLA Modules:
  0.0 225.0 jit_solution(8399299144730349695)
XLA Ops:
  7.2 0.0 copy-start
  7.2 0.0 all-gather.2.cloned.1.call-start
  7.2 0.7 all-gather.2.cloned.1.call-update
  7.9 0.0 all-reduce.2.cloned.1.call-start
  8.0 0.8 iota_compare_fusion.1
  8.8 0.1 copy.66
  8.9 1.0 convert_reduce_fusion.1
  10.0 1.1 fusion.32
  11.1 1.6 convolution_bitcast_fusion
  12.9 0.1 multiply_reduce_fusion
  13.0 0.1 copy.68
  13.1 5.5 %fusion.71 = (bf16[40,1,128,256]{3,2,1,0:T(8,128)(2,1)}, bf16[40,1,128,256]{3,2,1,0:T(8,128)(2,1)}) fusion(bf16[40,2,128,256]{3,2,1,0:T(8,128)(2,1)} %param.17), kind=kLoop, calls=%fused_computation.117 | loop fusion | bytes 10485760 | tf_op jit(solution)/shard_map/slice | solution.py:33
  18.6 4.4 %copy.84 = bf16[40,1,128,256]{2,3,0,1:T(8,128)(2,1)} copy(bf16[40,1,128,256]{3,2,1,0:T(8,128)(2,1)} %get-tuple-element.36) | data formatting | bytes 5242880 | tf_op jit(solution)/shard_map/reshape;squeeze | solution.py:33
  23.0 2.6 %fusion.53 = f32[40,2,1,128]{3,2,1,0:T(1,128)S(1)} fusion(bf16[40,128,2,128]{1,3,2,0:T(8,128)(2,1)} %bitcast.75, bf16[40,2,128,1]{2,1,0,3:T(2,128)(2,1)S(1)} %get-tuple-element.49), kind=kOutput, calls=%fused_computation.82 | convolution fusion | flops 2621440 | bytes 2682880 | tf_op jit(solution)/shard_map/rhe,rlhe->rhl/dot_general | solution.py:37
  25.7 0.1 fusion.56
  25.8 0.2 fusion.55
  26.0 0.1 copy.70
  26.1 4.9 %reshape.266 = bf16[40,128,2,128]{3,2,1,0:T(2,128)(2,1)} reshape(bf16[40,1,128,256]{3,2,1,0:T(8,128)(2,1)} %get-tuple-element.37) | data formatting | bytes 5242880 | tf_op jit(solution)/shard_map/reshape;squeeze | solution.py:34
  31.0 0.1 fusion.59
  31.1 0.0 copy-start.4
  31.1 4.4 %fusion.11 = f32[40,2,1,128]{3,2,1,0:T(1,128)S(1)} fusion(bf16[40,2,128,1]{2,0,1,3:T(8,128)(2,1)S(1)} %fusion.59, bf16[40,128,2,128]{3,2,1,0:T(2,128)(2,1)} %reshape.266), kind=kOutput, calls=%fused_computation.20 | convolution fusion | flops 2621440 | bytes 2682880 | tf_op jit(solution)/shard_map/rhl,rlhe->rhe/dot_general | solution.py:54
  35.5 0.1 add_convert_fusion.9
  35.7 1.0 convolution_convert_fusion.2
  36.6 0.0 all-reduce.2.cloned.1.call-update
  36.6 0.2 reduce-scatter.2.cloned.1.call-start
  36.9 0.3 fusion.29
  37.2 1.0 fusion.23
  38.3 8.5 %broadcast_select_fusion = (bf16[40,1,128,256]{3,0,2,1:T(8,128)(2,1)}, bf16[40,1,128,256]{3,0,2,1:T(8,128)(2,1)}) fusion(pred[40,128]{0,1:T(8,128)(4,1)S(1)} %get-tuple-element.57, bf16[40,256]{1,0:T(8,128)(2,1)S(1)} %get-tuple-element.43, bf16[40,1,128,256]{3,2,1,0:T(8,128)(2,1)} %get-tuple-element.37, bf16[40,1,128,256]{3,2,1,0:T(8,128)(2,1)} %get-tuple-element.36, ...), kind=kLoop, calls=%fused_computation.26 | loop fusion | flops 2621440 | bytes 10531840 | tf_op jit(solution)/shard_map/jit(_where)/select_n | solution.py:62
  46.8 8.3 %all-gather.2.cloned.1.call-done = bf16[640,2048]{1,0:T(8,128)(2,1)} async-done(((bf16[80,2048]{1,0:T(8,128)(2,1)}), bf16[640,2048]{1,0:T(8,128)(2,1)}) %all-gather.2.cloned.1.call-update) | async-done | bytes 2621456 | tf_op jit(solution)/shard_map/all_gather | solution.py:87
  55.1 2.3 %convert_reduce_fusion = f32[640]{0:T(1024)S(1)} fusion(bf16[640,2048]{1,0:T(8,128)(2,1)} %all-gather.2.cloned.1.call-done), kind=kLoop, calls=%fused_computation.2 | loop fusion | flops 2620800 | bytes 2624000 | tf_op jit(solution)/shard_map/reduce_sum | solution.py:15
  57.4 0.2 copy-done.3
  57.6 0.8 fusion.3
  58.4 3.1 %fusion.25 = f32[3,640,256]{1,2,0:T(8,128)S(1)} fusion(bf16[3,2048,256]{2,1,0:T(8,128)(2,1)S(1)} %copy-done, bf16[640,2048]{1,0:T(8,128)(2,1)S(1)} %copy-done.3, f32[2048]{0:T(1024)S(1)} %copy-done.12, f32[2048]{0:T(1024)S(1)} %copy-done.13, f32[640]{0:T(1024)S(1)} %add_rsqrt_fusion, f32[640]{0:T(1024)S(1)} %broadcast_multiply_fusion), kind=kOutput, calls=%fused_computation.39 | convolution fusion | flops 2021130240 | bytes 7754752 | tf_op jit(solution)/shard_map/rd,cde->cre/dot_general | solution.py:88
  61.5 0.2 add_convert_fusion.1
  61.7 0.2 copy.64
  62.0 0.2 copy.63
  62.2 0.6 fusion.38
  62.8 0.4 copy-done.10
  63.2 2.0 fusion.74
  65.2 0.5 fusion.28
  65.7 0.7 copy-done.5
  66.4 2.4 %convolution_convert_fusion = bf16[640,2048]{1,0:T(8,128)(2,1)} fusion(bf16[640,256]{0,1:T(8,128)(2,1)S(1)} %bitcast.78, bf16[256,2048]{1,0:T(8,128)(2,1)S(1)} %copy-done.5), kind=kOutput, calls=%fused_computation.14 | convolution fusion | flops 672399360 | bytes 3997696 | tf_op jit(solution)/shard_map/dot_general | solution.py:109
  68.8 0.0 reduce-scatter.2.cloned.1.call-update
  68.9 60.0 %all-reduce.2.cloned.1.call-done = bf16[40,2048]{1,0:T(8,128)(2,1)} async-done(((bf16[40,2048]{1,0:T(8,128)(2,1)}), bf16[40,2048]{1,0:T(8,128)(2,1)}) %all-reduce.2.cloned.1.call-update) | async-done | bytes 163856 | tf_op jit(solution)/shard_map/psum | solution.py:136
  128.8 1.0 fusion.37
  129.8 0.7 copy-done.8
  130.5 0.3 fusion.18
  130.8 0.5 broadcast.160
  131.3 1.3 reduce.1
  132.6 1.6 reshape.267
  134.3 7.4 %all-to-all-start = ((bf16[32,2,1024]{2,1,0:T(2,128)(2,1)}), bf16[32,2,1024]{2,1,0:T(2,128)(2,1)S(1)}, u32[]{:S(2)}, u32[]{:S(2)}) async-start(bf16[32,2,1024]{2,1,0:T(2,128)(2,1)} %reshape.267), calls=%async_computation.1 | async-start | bytes 262144 | tf_op jit(solution)/shard_map/all_to_all | solution.py:148
  141.7 2.6 %convolution_convert_fusion.1 = bf16[32,2,128,256]{3,0,2,1:T(8,128)(2,1)S(1)} fusion(bf16[40,1,128,256]{3,0,2,1:T(8,128)(2,1)S(1)} %copy-done.2, bf16[40,1,128,256]{3,0,2,1:T(8,128)(2,1)} %get-tuple-element.51, s32[16]{0:T(128)S(1)} %convert_add_fusion.1), kind=kOutput, calls=%fused_computation.16 | convolution fusion | flops 73400832 | bytes 9437248 | tf_op jit(solution)/shard_map/so,oklh->sklh/dot_general | solution.py:140
  144.3 4.4 %copy.72 = bf16[32,2,128,256]{3,2,1,0:T(8,128)(2,1)} copy(bf16[32,2,128,256]{3,0,2,1:T(8,128)(2,1)S(1)} %convolution_convert_fusion.1) | data formatting | bytes 8388608 | tf_op jit(solution)/shard_map/convert_element_type | solution.py:142
  148.7 7.4 %all-to-all-start.1 = ((bf16[32,2,128,256]{3,2,1,0:T(8,128)(2,1)}), bf16[32,2,128,256]{3,2,1,0:T(8,128)(2,1)}, u32[]{:S(2)}, u32[]{:S(2)}) async-start(bf16[32,2,128,256]{3,2,1,0:T(8,128)(2,1)} %copy.72), calls=%async_computation.2 | async-start | bytes 8388608 | tf_op jit(solution)/shard_map/all_to_all | solution.py:147
  156.2 1.6 fusion.7
  157.8 2.4 %copy.74 = bf16[24,2,128,256]{3,2,1,0:T(8,128)(2,1)} copy(bf16[24,2,128,256]{3,0,2,1:T(8,128)(2,1)S(1)} %fusion.7) | data formatting | bytes 6291456
  160.1 0.6 slice.71
  160.8 0.1 reshape.268
  160.9 0.7 copy.116
  161.6 49.1 %all-to-all-done.1 = bf16[32,2,128,256]{3,2,1,0:T(8,128)(2,1)} async-done(((bf16[32,2,128,256]{3,2,1,0:T(8,128)(2,1)}), bf16[32,2,128,256]{3,2,1,0:T(8,128)(2,1)}, u32[]{:S(2)}, u32[]{:S(2)}) %all-to-all-start.1) | async-done | bytes 4194336 | tf_op jit(solution)/shard_map/all_to_all | solution.py:147
  210.7 0.1 pad_maximum_fusion.2
  210.8 1.1 copy.73
  211.9 1.8 add_convert_fusion.2
  213.7 4.8 %copy.120 = bf16[32,2,128,256]{3,2,1,0:T(8,128)(2,1)} copy(bf16[32,2,128,256]{3,2,1,0:T(8,128)(2,1)} %all-to-all-done.1) | data formatting | bytes 8388608
  (44 shorter events, 0.2 us)
Async XLA Ops:
  7.2 4.0 %copy-start = (bf16[3,2048,256]{2,1,0:T(8,128)(2,1)S(1)}, bf16[3,2048,256]{2,1,0:T(8,128)(2,1)}, u32[]{:S(2)}) copy-start(bf16[3,2048,256]{2,1,0:T(8,128)(2,1)} %param.20) | copy-start | bytes 9437188
  7.2 5.7 %copy-start.15 = (f32[3,256]{1,0:T(4,128)S(1)}, f32[3,256]{1,0:T(4,128)}, u32[]{:S(2)}) copy-start(f32[3,256]{1,0:T(4,128)} %param.21) | copy-start | bytes 9220
  7.2 47.9 %all-gather.2.cloned.1.call-start = ((), (), s32[]{:S(2)}) async-start(), calls=%async_computation.3 | async-start | bytes 2949120 | tf_op jit(solution)/shard_map/all_gather | solution.py:87
  7.9 120.9 %all-reduce.2.cloned.1.call-start = ((), (), s32[]{:S(2)}) async-start(), calls=%async_computation.5 | async-start | bytes 327680 | tf_op jit(solution)/shard_map/psum | solution.py:136
  31.1 4.6 %copy-start.4 = (bf16[256,2048]{1,0:T(8,128)(2,1)S(1)}, bf16[256,2048]{1,0:T(8,128)(2,1)}, u32[]{:S(2)}) copy-start(bf16[256,2048]{1,0:T(8,128)(2,1)} %param.22) | copy-start | bytes 3145732
  31.1 5.8 %copy-start.16 = (s32[16,1]{0,1:T(1,128)S(1)}, s32[16,1]{0,1:T(1,128)}, u32[]{:S(2)}) copy-start(s32[16,1]{0,1:T(1,128)} %param.16) | copy-start | bytes 196
  31.1 6.1 %copy-start.14 = (s32[1,640]{1,0:T(1,128)S(1)}, s32[1,640]{1,0:T(1,128)}, u32[]{:S(2)}) copy-start(s32[1,640]{1,0:T(1,128)} %param.13) | copy-start | bytes 7684
  36.6 175.2 %reduce-scatter.2.cloned.1.call-start = ((), (), s32[]{:S(2)}) async-start(), calls=%async_computation.4 | async-start | bytes 2949120 | tf_op jit(solution)/shard_map/reduce_scatter | solution.py:108
  46.8 11.7 %copy-start.12 = (f32[2048]{0:T(1024)S(1)}, f32[2048]{0:T(1024)}, u32[]{:S(2)}) copy-start(f32[2048]{0:T(1024)} %param.19) | copy-start | bytes 24580
  55.1 2.5 %copy-start.3 = (bf16[640,2048]{1,0:T(8,128)(2,1)S(1)}, bf16[640,2048]{1,0:T(8,128)(2,1)}, u32[]{:S(2)}) copy-start(bf16[640,2048]{1,0:T(8,128)(2,1)} %all-gather.2.cloned.1.call-done) | copy-start | bytes 7864324
  55.1 3.4 %copy-start.13 = (f32[2048]{0:T(1024)S(1)}, f32[2048]{0:T(1024)}, u32[]{:S(2)}) copy-start(f32[2048]{0:T(1024)} %param.18) | copy-start | bytes 24580
  62.2 1.0 copy-start.10
  65.2 1.2 copy-start.5
  66.4 62.4 %copy-start.6 = (bf16[40,2048]{1,0:T(8,128)(2,1)S(1)}, bf16[40,2048]{1,0:T(8,128)(2,1)}, u32[]{:S(2)}) copy-start(bf16[40,2048]{1,0:T(8,128)(2,1)} %param.14) | copy-start | bytes 491524
  66.4 62.4 %copy-start.11 = (f32[2048]{0:T(1024)S(1)}, f32[2048]{0:T(1024)}, u32[]{:S(2)}) copy-start(f32[2048]{0:T(1024)} %param.23) | copy-start | bytes 24580
  68.8 72.9 %copy-start.2 = (bf16[40,1,128,256]{3,0,2,1:T(8,128)(2,1)S(1)}, bf16[40,1,128,256]{3,0,2,1:T(8,128)(2,1)}, u32[]{:S(2)}) copy-start(bf16[40,1,128,256]{3,0,2,1:T(8,128)(2,1)} %get-tuple-element.50) | copy-start | bytes 7864324
  129.8 0.7 copy-start.8
  134.3 14.5 %all-to-all-start = ((bf16[32,2,1024]{2,1,0:T(2,128)(2,1)}), bf16[32,2,1024]{2,1,0:T(2,128)(2,1)S(1)}, u32[]{:S(2)}, u32[]{:S(2)}) async-start(bf16[32,2,1024]{2,1,0:T(2,128)(2,1)} %reshape.267), calls=%async_computation.1 | async-start | bytes 262144 | tf_op jit(solution)/shard_map/all_to_all | solution.py:148
  148.7 62.0 %all-to-all-start.1 = ((bf16[32,2,128,256]{3,2,1,0:T(8,128)(2,1)}), bf16[32,2,128,256]{3,2,1,0:T(8,128)(2,1)}, u32[]{:S(2)}, u32[]{:S(2)}) async-start(bf16[32,2,128,256]{3,2,1,0:T(8,128)(2,1)} %copy.72), calls=%async_computation.2 | async-start | bytes 8388608 | tf_op jit(solution)/shard_map/all_to_all | solution.py:147
  157.8 2.4 %copy-start.9 = (bf16[40,2048]{1,0:T(8,128)(2,1)S(1)}, bf16[40,2048]{1,0:T(8,128)(2,1)}, u32[]{:S(2)}) copy-start(bf16[40,2048]{1,0:T(8,128)(2,1)} %copy-done.8) | copy-start | bytes 491524
  160.1 51.7 %copy-start.7 = (bf16[80,2048]{1,0:T(8,128)(2,1)S(1)}, bf16[80,2048]{1,0:T(8,128)(2,1)}, u32[]{:S(2)}) copy-start(bf16[80,2048]{1,0:T(8,128)(2,1)} %param.12) | copy-start | bytes 983044
  213.7 4.9 %copy-start.1 = (bf16[3,2048,256]{2,1,0:T(8,128)(2,1)S(1)}, bf16[3,2048,256]{2,1,0:T(8,128)(2,1)}, u32[]{:S(2)}) copy-start(bf16[3,2048,256]{2,1,0:T(8,128)(2,1)} %param.20) | copy-start | bytes 9437188
Sparse Core Ops, SparseCore 0:
  9.8 45.1 all-gather.1
  58.0 70.8 all-reduce.1
  131.6 42.1 reduce-scatter.1
where the time goes:
time: 226 us; the launch traced here: 225 us
  waiting for transfers between devices  118 us (52%)
  local copies, waits for them, and re-layouts  34.1 us (15%)
  other arithmetic  24.3 us (11%)
  matrix products  19.4 us (9%)
  starting transfers between devices  15.1 us (7%)
  between operations  14.1 us (6%)
    psum x1, waiting for transfers between devices, on_device(): lax.psum(partial_value.astype(jnp.bfloat16), 'tp').astype(jnp.float32)  60 us
    all_to_all x1, waiting for transfers between devices, on_device(): lax.all_to_all(send_cache, 'rep', split_axis=0, concat_axis=0, tiled=True)  49.1 us
    unnamed x40, local copies, waits for them, and re-layouts  12.8 us
    select_n x1, other arithmetic, decode_partial(): new_values = jnp.where(written, value_new[:, None, :], cache[:, 1])  8.49 us
    all_gather x1, waiting for transfers between devices, on_device(): lax.all_gather(prompt_rows, 'tp', axis=0, tiled=True)  8.31 us
    all_to_all x1, starting transfers between devices, on_device(): lax.all_to_all(send_cache, 'rep', split_axis=0, concat_axis=0, tiled=True)  7.44 us
    all_to_all x1, starting transfers between devices, on_device(): lax.all_to_all(send_rows, 'rep', split_axis=0, concat_axis=0, tiled=True)  7.41 us
    slice x1, local copies, waits for them, and re-layouts, decode_partial(): old_keys = cache[:, 0].reshape(count, length, heads_here, HEAD_DIM)  5.54 us
  transfers between devices with their start and end apart: 5, of which 3 were waited for; matrix products, arithmetic and copies ran while one was open for 31% of the time, Pallas kernels for 0%

commit v1 on v0

--- a/solution.py
+++ b/solution.py
@@ -61,6 +61,27 @@
     new_keys = jnp.where(written, key_new[:, None, :], cache[:, 0])
     new_values = jnp.where(written, value_new[:, None, :], cache[:, 1])
     return (partial_value, jnp.stack([new_keys, new_values], axis=1))
+
+
+def reduce_over_tp(partial_value, rows, out_bias):
+    n = lax.axis_size("tp")
+    me = lax.axis_index("tp")
+    count, model = rows.shape
+    share = count // n
+    pieces = partial_value.astype(jnp.bfloat16).reshape(n, share, model)
+    rolled = jnp.take(pieces, (me + jnp.arange(n)) % n, axis=0)
+    total = rolled[0].astype(jnp.float32)
+    for shift in range(1, n):
+        incoming = lax.ppermute(rolled[shift], "tp", [(i, (i + shift) % n) for i in range(n)])
+        total = total + incoming.astype(jnp.float32)
+    own_rows = lax.dynamic_slice_in_dim(rows, me * share, share, 0)
+    own_out = (own_rows.astype(jnp.float32) + total + out_bias).astype(jnp.bfloat16)
+    held = [own_out]
+    for shift in range(1, n):
+        held.append(lax.ppermute(own_out, "tp", [(i, (i + shift) % n) for i in range(n)]))
+    stacked = jnp.stack(held)
+    order = (me - jnp.arange(n)) % n
+    return jnp.take(stacked, order, axis=0).reshape(count, model)
 
 
 def on_device(
@@ -84,6 +105,30 @@
     leaving = migrate_to.shape[0]
     staying = decode_rows.shape[0] - leaving
     slot_count = rep_count * CAP
+    targets = migrate_to[:, 0]
+    onehot = (targets[:, None] == jnp.arange(rep_count)[None, :]).astype(jnp.float32)
+    lower = (jnp.arange(leaving)[:, None] > jnp.arange(leaving)[None, :]).astype(jnp.float32)
+    earlier = jnp.dot(lower, onehot)
+    rank = jnp.sum(earlier * onehot, axis=1).astype(jnp.int32)
+    slot = targets * CAP + rank
+    placing = (jnp.arange(slot_count)[:, None] == slot[None, :]).astype(jnp.bfloat16)
+    cells = jnp.arange(length)
+    live = cells[None, :] < request_ages[:, None]
+    partial_value, updated = decode_partial(
+        decode_rows,
+        past_cache,
+        live,
+        request_ages,
+        norm_gain,
+        norm_bias,
+        qkv_weight,
+        qkv_bias,
+        out_weight,
+    )
+    send_cache = jnp.einsum(
+        "so,oklh->sklh", placing, updated[staying:], preferred_element_type=jnp.float32
+    ).astype(jnp.bfloat16)
+    moved_cache = lax.all_to_all(send_cache, "rep", split_axis=0, concat_axis=0, tiled=True)
     normed = layer_norm(lax.all_gather(prompt_rows, "tp", axis=0, tiled=True), norm_gain, norm_bias)
     projected = jnp.einsum("rd,cde->cre", normed, qkv_weight, preferred_element_type=jnp.float32)
     total_rows = projected.shape[1]
@@ -105,6 +150,8 @@
     probs = (weights / jnp.sum(weights, axis=-1, keepdims=True)).astype(jnp.bfloat16)
     context = jnp.einsum("hqk,khe->qhe", probs, head_v, preferred_element_type=jnp.float32)
     context = context.reshape(total_rows, width).astype(jnp.bfloat16)
+    decode_out = reduce_over_tp(partial_value, decode_rows, out_bias)
+    context, moved_cache, decode_out = lax.optimization_barrier((context, moved_cache, decode_out))
     attended = lax.psum_scatter(
         jnp.dot(context, out_weight, preferred_element_type=jnp.float32).astype(jnp.bfloat16),
         "tp",
@@ -113,40 +160,12 @@
     ).astype(jnp.float32)
     prompt_out = (prompt_rows.astype(jnp.float32) + attended + out_bias).astype(jnp.bfloat16)
     prompt_cache = jnp.stack([key_rows, value_rows])
-    targets = migrate_to[:, 0]
-    onehot = (targets[:, None] == jnp.arange(rep_count)[None, :]).astype(jnp.float32)
-    lower = (jnp.arange(leaving)[:, None] > jnp.arange(leaving)[None, :]).astype(jnp.float32)
-    earlier = jnp.dot(lower, onehot)
-    rank = jnp.sum(earlier * onehot, axis=1).astype(jnp.int32)
-    slot = targets * CAP + rank
-    placing = (jnp.arange(slot_count)[:, None] == slot[None, :]).astype(jnp.bfloat16)
-    cells = jnp.arange(length)
-    live = cells[None, :] < request_ages[:, None]
-    partial_value, updated = decode_partial(
-        decode_rows,
-        past_cache,
-        live,
-        request_ages,
-        norm_gain,
-        norm_bias,
-        qkv_weight,
-        qkv_bias,
-        out_weight,
-    )
-    summed = lax.psum(partial_value.astype(jnp.bfloat16), "tp").astype(jnp.float32)
-    decode_out = (decode_rows.astype(jnp.float32) + summed + out_bias).astype(jnp.bfloat16)
     kept_out = decode_out[:staying]
     kept_cache = updated[:staying]
-    send_cache = jnp.einsum(
-        "so,oklh->sklh", placing, updated[staying:], preferred_element_type=jnp.float32
-    ).astype(jnp.bfloat16)
     send_rows = jnp.dot(placing, decode_out[staying:], preferred_element_type=jnp.float32).astype(
         jnp.bfloat16
     )
-    moved_cache, moved_out = (
-        lax.all_to_all(send_cache, "rep", split_axis=0, concat_axis=0, tiled=True),
-        lax.all_to_all(send_rows, "rep", split_axis=0, concat_axis=0, tiled=True),
-    )
+    moved_out = lax.all_to_all(send_rows, "rep", split_axis=0, concat_axis=0, tiled=True)
     return (prompt_out, prompt_cache, kept_out, kept_cache, moved_out, moved_cache)
 
 

time: 226 us -> 194 us (0.86)
  the two profiles are of different devices: /device:TPU:8 before, /device:TPU:2 now
where the time goes in v1:
time: 194 us; the launch traced here: 193 us
  starting transfers between devices  50.5 us (26%)
  local copies, waits for them, and re-layouts  45.7 us (24%)
  waiting for transfers between devices  34.5 us (18%)
  other arithmetic  26.6 us (14%)
  matrix products  20.9 us (11%)
  between operations  14.5 us (7%)
    reduce_scatter x1, waiting for transfers between devices, on_device(): lax.psum_scatter(jnp.dot(context, out_weight, preferred_element_type=jnp....  21 us
    ppermute x7, starting transfers between devices, reduce_over_tp(): lax.ppermute(rolled[shift], 'tp', [(i, (i + shift) % n) for i in range(n)])  18.5 us
    unnamed x52, local copies, waits for them, and re-layouts  16.6 us
    ppermute x7, starting transfers between devices, reduce_over_tp(): lax.ppermute(own_out, 'tp', [(i, (i + shift) % n) for i in range(n)])  15 us
    all_to_all x1, starting transfers between devices, on_device(): lax.all_to_all(send_rows, 'rep', split_axis=0, concat_axis=0, tiled=True)  9.08 us
    all_to_all x1, starting transfers between devices, on_device(): lax.all_to_all(send_cache, 'rep', split_axis=0, concat_axis=0, tiled=True)  7.8 us
    select_n x1, other arithmetic, decode_partial(): new_keys = jnp.where(written, key_new[:, None, :], cache[:, 0])  6.64 us
    slice x1, local copies, waits for them, and re-layouts, decode_partial(): new_keys = jnp.where(written, key_new[:, None, :], cache[:, 0])  5.54 us
  transfers between devices with their start and end apart: 18, of which 5 were waited for; matrix products, arithmetic and copies ran while one was open for 41% of the time, Pallas kernels for 0%

profile of v1, /device:TPU:2, one launch (start us, length us, event | category | flops | bytes accessed | tf_op | source)
XLA Modules:
  0.0 192.6 jit_solution(18306466765346924837)
XLA Ops:
  7.2 0.7 all-gather.2.cloned.1.call-update
  8.5 1.0 convert_reduce_fusion.1
  9.5 1.1 fusion.33
  10.7 0.8 fusion.84
  12.1 0.7 iota_compare_fusion.1
  12.9 1.6 convolution_bitcast_fusion
  14.8 5.5 %fusion.82 = (bf16[40,1,128,256]{3,2,1,0:T(8,128)(2,1)}, bf16[40,1,128,256]{3,2,1,0:T(8,128)(2,1)}) fusion(bf16[40,2,128,256]{3,2,1,0:T(8,128)(2,1)} %param.19), kind=kLoop, calls=%fused_computation.157 | loop fusion | bytes 10485760 | tf_op jit(solution)/shard_map/slice | solution.py:61
  20.3 4.4 %copy.94 = bf16[40,1,128,256]{2,3,0,1:T(8,128)(2,1)} copy(bf16[40,1,128,256]{3,2,1,0:T(8,128)(2,1)} %get-tuple-element.51) | data formatting | bytes 5242880 | tf_op jit(solution)/shard_map/reshape;squeeze | solution.py:33
  24.7 2.5 %fusion.61 = f32[40,2,1,128]{3,2,1,0:T(1,128)S(1)} fusion(bf16[40,128,2,128]{1,3,2,0:T(8,128)(2,1)} %bitcast.111, bf16[40,2,128,1]{2,1,0,3:T(2,128)(2,1)S(1)} %get-tuple-element.71), kind=kOutput, calls=%fused_computation.92 | convolution fusion | flops 2621440 | bytes 2682880 | tf_op jit(solution)/shard_map/rhe,rlhe->rhl/dot_general | solution.py:37
  27.8 4.9 %reshape.304 = bf16[40,128,2,128]{3,2,1,0:T(2,128)(2,1)} reshape(bf16[40,1,128,256]{3,2,1,0:T(8,128)(2,1)} %get-tuple-element.52) | data formatting | bytes 5242880 | tf_op jit(solution)/shard_map/reshape;squeeze | solution.py:34
  32.7 4.4 %fusion.10 = f32[40,2,1,128]{3,2,1,0:T(1,128)S(1)} fusion(bf16[40,2,128,1]{2,0,1,3:T(8,128)(2,1)S(1)} %fusion.67, bf16[40,128,2,128]{3,2,1,0:T(2,128)(2,1)} %reshape.304), kind=kOutput, calls=%fused_computation.20 | convolution fusion | flops 2621440 | bytes 2682880 | tf_op jit(solution)/shard_map/rhl,rlhe->rhe/dot_general | solution.py:54
  37.2 1.0 convolution_convert_fusion.2
  38.2 1.0 reshape.271
  39.2 1.4 gather_fusion
  40.6 1.0 broadcast_select_fusion.2
  41.6 0.7 slice_bitcast_fusion.6
  42.3 1.9 collective-permute-start
  44.2 4.0 %collective-permute-start.6 = (bf16[5,2048]{1,0:T(8,128)(2,1)}, bf16[5,2048]{1,0:T(8,128)(2,1)}, u32[]{:S(2)}, u32[]{:S(2)}) collective-permute-start(bf16[5,2048]{1,0:T(8,128)(2,1)} %get-tuple-element.59), channel_id=1, source_target_pairs={{0,7},{1,0},{2,1},{3,2},{4,3},{5,4},{6,5},{7,6},{8,15},{9,8},{10,9... | collective-permute-start | bytes 61448 | tf_op jit(solution)/shard_map/ppermute | solution.py:75
  48.3 2.4 %collective-permute-start.5 = (bf16[5,2048]{1,0:T(8,128)(2,1)}, bf16[5,2048]{1,0:T(8,128)(2,1)}, u32[]{:S(2)}, u32[]{:S(2)}) collective-permute-start(bf16[5,2048]{1,0:T(8,128)(2,1)} %get-tuple-element.60), channel_id=1, source_target_pairs={{0,6},{1,7},{2,0},{3,1},{4,2},{5,3},{6,4},{7,5},{8,14},{9,15},{10,... | collective-permute-start | bytes 61448 | tf_op jit(solution)/shard_map/ppermute | solution.py:75
  50.7 2.1 %collective-permute-start.4 = (bf16[5,2048]{1,0:T(8,128)(2,1)}, bf16[5,2048]{1,0:T(8,128)(2,1)}, u32[]{:S(2)}, u32[]{:S(2)}) collective-permute-start(bf16[5,2048]{1,0:T(8,128)(2,1)} %get-tuple-element.61), channel_id=1, source_target_pairs={{0,5},{1,6},{2,7},{3,0},{4,1},{5,2},{6,3},{7,4},{8,13},{9,14},{10,... | collective-permute-start | bytes 61448 | tf_op jit(solution)/shard_map/ppermute | solution.py:75
  52.8 3.4 %collective-permute-start.3 = (bf16[5,2048]{1,0:T(8,128)(2,1)}, bf16[5,2048]{1,0:T(8,128)(2,1)}, u32[]{:S(2)}, u32[]{:S(2)}) collective-permute-start(bf16[5,2048]{1,0:T(8,128)(2,1)} %get-tuple-element.62), channel_id=1, source_target_pairs={{0,4},{1,5},{2,6},{3,7},{4,0},{5,1},{6,2},{7,3},{8,12},{9,13},{10,... | collective-permute-start | bytes 61448 | tf_op jit(solution)/shard_map/ppermute | solution.py:75
  56.2 1.0 fusion.30
  57.2 0.7 convert_add_fusion.1
  57.9 6.6 %copy_select_fusion = (bf16[40,1,128,256]{3,0,2,1:T(8,128)(2,1)S(1)}, bf16[40,1,128,256]{3,0,2,1:T(8,128)(2,1)S(1)}) fusion(bf16[40,1,128,256]{3,2,1,0:T(8,128)(2,1)} %get-tuple-element.51, pred[40,128]{0,1:T(8,128)(4,1)S(1)} %get-tuple-element.80, bf16[40,256]{1,0:T(8,128)(2,1)S(1)} %get-tuple-element.68, bf16[40,1,128,256]{3,2,1,0:T(8,128)(2,1)} %get-tuple-element.52, ...), kind=kLoop, calls=%fused_computation.19 | loop fusion | flops 2621440 | bytes 10531840 | tf_op jit(solution)/shard_map/jit(_where)/select_n | solution.py:61
  64.5 1.5 copy-done.2
  66.1 0.8 copy-done.4
  66.9 1.3 convolution_convert_fusion.1
  68.2 4.4 %copy.78 = bf16[32,2,128,256]{3,2,1,0:T(8,128)(2,1)} copy(bf16[32,2,128,256]{3,0,2,1:T(8,128)(2,1)S(1)} %convolution_convert_fusion.1) | data formatting | bytes 8388608 | tf_op jit(solution)/shard_map/convert_element_type | solution.py:130
  72.7 7.8 %all-to-all-start = ((bf16[32,2,128,256]{3,2,1,0:T(8,128)(2,1)}), bf16[32,2,128,256]{3,2,1,0:T(8,128)(2,1)}, u32[]{:S(2)}, u32[]{:S(2)}) async-start(bf16[32,2,128,256]{3,2,1,0:T(8,128)(2,1)} %copy.78), calls=%async_computation | async-start | bytes 8388608 | tf_op jit(solution)/shard_map/all_to_all | solution.py:131
  80.6 1.0 fusion.24
  82.2 4.1 %collective-permute-start.1 = (bf16[5,2048]{1,0:T(8,128)(2,1)S(1)}, bf16[5,2048]{1,0:T(8,128)(2,1)}, u32[]{:S(2)}, u32[]{:S(2)}) collective-permute-start(bf16[5,2048]{1,0:T(8,128)(2,1)S(1)} %copy-done.11), channel_id=1, source_target_pairs={{0,2},{1,3},{2,4},{3,5},{4,6},{5,7},{6,0},{7,1},{8,10},{9,11},{10,... | collective-permute-start | bytes 61448 | tf_op jit(solution)/shard_map/ppermute | solution.py:75
  86.9 3.3 %collective-permute-done.2 = bf16[5,2048]{1,0:T(8,128)(2,1)S(1)} collective-permute-done((bf16[5,2048]{1,0:T(8,128)(2,1)S(1)}, bf16[5,2048]{1,0:T(8,128)(2,1)S(1)}, u32[]{:S(2)}, u32[]{:S(2)}) %collective-permute-start.2) | collective-permute-done | bytes 20512 | tf_op jit(solution)/shard_map/ppermute | solution.py:75
  90.2 1.6 bitcast_dynamic-update-slice_fusion.7
  91.9 1.0 collective-permute-start.7
  92.9 1.5 collective-permute-start.12
  94.4 3.9 %collective-permute-start.11 = (bf16[5,2048]{1,0:T(8,128)(2,1)S(1)}, bf16[5,2048]{1,0:T(8,128)(2,1)S(1)}, u32[]{:S(2)}, u32[]{:S(2)}) collective-permute-start(bf16[5,2048]{1,0:T(8,128)(2,1)S(1)} %get-tuple-element.50), channel_id=1, source_target_pairs={{0,5},{1,6},{2,7},{3,0},{4,1},{5,2},{6,3},{7,4},{8,13},{9,14},{10,... | collective-permute-start | bytes 61448 | tf_op jit(solution)/shard_map/ppermute | solution.py:81
  98.3 2.8 %collective-permute-start.10 = (bf16[5,2048]{1,0:T(8,128)(2,1)S(1)}, bf16[5,2048]{1,0:T(8,128)(2,1)S(1)}, u32[]{:S(2)}, u32[]{:S(2)}) collective-permute-start(bf16[5,2048]{1,0:T(8,128)(2,1)S(1)} %get-tuple-element.50), channel_id=1, source_target_pairs={{0,4},{1,5},{2,6},{3,7},{4,0},{5,1},{6,2},{7,3},{8,12},{9,13},{10,... | collective-permute-start | bytes 61448 | tf_op jit(solution)/shard_map/ppermute | solution.py:81
  101.1 3.6 %collective-permute-start.8 = (bf16[5,2048]{1,0:T(8,128)(2,1)S(1)}, bf16[5,2048]{1,0:T(8,128)(2,1)S(1)}, u32[]{:S(2)}, u32[]{:S(2)}) collective-permute-start(bf16[5,2048]{1,0:T(8,128)(2,1)S(1)} %get-tuple-element.50), channel_id=1, source_target_pairs={{0,2},{1,3},{2,4},{3,5},{4,6},{5,7},{6,0},{7,1},{8,10},{9,11},{10,... | collective-permute-start | bytes 61448 | tf_op jit(solution)/shard_map/ppermute | solution.py:81
  105.4 2.1 %collective-permute-done.8 = bf16[5,2048]{1,0:T(8,128)(2,1)S(1)} collective-permute-done((bf16[5,2048]{1,0:T(8,128)(2,1)S(1)}, bf16[5,2048]{1,0:T(8,128)(2,1)S(1)}, u32[]{:S(2)}, u32[]{:S(2)}) %collective-permute-start.8) | collective-permute-done | bytes 20512 | tf_op jit(solution)/shard_map/ppermute | solution.py:81
  107.5 2.2 %collective-permute-start.13 = (bf16[5,2048]{1,0:T(8,128)(2,1)S(1)}, bf16[5,2048]{1,0:T(8,128)(2,1)S(1)}, u32[]{:S(2)}, u32[]{:S(2)}) collective-permute-start(bf16[5,2048]{1,0:T(8,128)(2,1)S(1)} %get-tuple-element.50), channel_id=1, source_target_pairs={{0,7},{1,0},{2,1},{3,2},{4,3},{5,4},{6,5},{7,6},{8,15},{9,8},{10,9... | collective-permute-start | bytes 61448 | tf_op jit(solution)/shard_map/ppermute | solution.py:81
  110.3 0.6 bitcast_dynamic-update-slice_fusion.4
  110.9 0.6 bitcast_dynamic-update-slice_fusion.3
  113.4 1.6 gather_fusion.1
  115.1 0.8 broadcast_select_fusion.1
  115.9 1.7 reshape.272
  117.6 2.3 %convert_reduce_fusion = f32[640]{0:T(1024)S(1)} fusion(bf16[640,2048]{1,0:T(8,128)(2,1)} %all-gather.2.cloned.1.call-done), kind=kLoop, calls=%fused_computation.4 | loop fusion | flops 2620800 | bytes 2624000 | tf_op jit(solution)/shard_map/reduce_sum | solution.py:15
  120.1 0.8 fusion.3
  120.9 3.1 %fusion.26 = f32[3,640,256]{1,2,0:T(8,128)S(1)} fusion(bf16[3,2048,256]{2,1,0:T(8,128)(2,1)S(1)} %copy-done, bf16[640,2048]{1,0:T(8,128)(2,1)S(1)} %copy-done.5, f32[2048]{0:T(1024)S(1)} %copy-done.15, f32[2048]{0:T(1024)S(1)} %copy-done.16, f32[640]{0:T(1024)S(1)} %add_rsqrt_fusion, f32[640]{0:T(1024)S(1)} %broadcast_multiply_fusion), kind=kOutput, calls=%fused_computation.40 | convolution fusion | flops 2021130240 | bytes 7754752 | tf_op jit(solution)/shard_map/rd,cde->cre/dot_general | solution.py:133
  125.7 2.0 %fusion.85 = (f32[2,640]{1,0:T(2,128)S(1)}, f32[2,640,640]{1,2,0:T(8,128)S(1)}) fusion(f32[2,640,640]{1,2,0:T(8,128)S(1)} %fusion.37, pred[640,640]{0,1:T(8,128)(4,1)S(1)} %copy-done.9), kind=kOutput, calls=%fused_computation.160 | output fusion | flops 4915839 | bytes 6968320 | tf_op jit(solution)/shard_map/sub | solution.py:149
  127.7 1.2 fusion.29
  128.9 1.8 all-to-all-done
  130.7 3.8 %convolution_convert_fusion = bf16[640,2048]{1,0:T(8,128)(2,1)} fusion(bf16[640,256]{0,1:T(8,128)(2,1)} %bitcast.114, bf16[256,2048]{1,0:T(8,128)(2,1)} %param.24), kind=kOutput, calls=%fused_computation.14 | convolution fusion | flops 672399360 | bytes 3997696 | tf_op jit(solution)/shard_map/dot_general | solution.py:156
  134.6 1.6 pad_maximum_fusion
  136.3 2.4 %copy.84 = bf16[24,2,128,256]{3,2,1,0:T(8,128)(2,1)} copy(bf16[24,2,128,256]{3,0,2,1:T(8,128)(2,1)S(1)} %pad_maximum_fusion) | data formatting | bytes 6291456
  138.6 0.6 slice.94
  140.1 0.7 reduce.1
  140.8 0.7 reshape.305
  141.5 9.1 %all-to-all-start.1 = ((bf16[32,2,1024]{2,1,0:T(2,128)(2,1)}), bf16[32,2,1024]{2,1,0:T(2,128)(2,1)S(1)}, u32[]{:S(2)}, u32[]{:S(2)}) async-start(bf16[32,2,1024]{2,1,0:T(2,128)(2,1)} %reshape.305), calls=%async_computation.2 | async-start | bytes 262144 | tf_op jit(solution)/shard_map/all_to_all | solution.py:168
  150.7 1.1 copy.83
  151.8 5.5 %all-to-all-done.1 = bf16[32,2,1024]{2,1,0:T(2,128)(2,1)S(1)} async-done(((bf16[32,2,1024]{2,1,0:T(2,128)(2,1)}), bf16[32,2,1024]{2,1,0:T(2,128)(2,1)S(1)}, u32[]{:S(2)}, u32[]{:S(2)}) %all-to-all-start.1) | async-done | bytes 131104 | tf_op jit(solution)/shard_map/all_to_all | solution.py:168
  157.3 0.7 copy.126
  158.1 21.0 %reduce-scatter.2.cloned.1.call-done = bf16[80,2048]{1,0:T(8,128)(2,1)} async-done(((bf16[640,2048]{1,0:T(8,128)(2,1)}), bf16[80,2048]{1,0:T(8,128)(2,1)}) %reduce-scatter.2.cloned.1.call-update) | async-done | bytes 327696 | tf_op jit(solution)/shard_map/reduce_scatter | solution.py:155
  179.1 1.8 add_convert_fusion.2
  180.9 4.8 %copy.136 = bf16[32,2,128,256]{3,2,1,0:T(8,128)(2,1)} copy(bf16[32,2,128,256]{3,2,1,0:T(8,128)(2,1)} %all-to-all-done) | data formatting | bytes 8388608
  (95 shorter events, 9.5 us)
Async XLA Ops:
  7.2 5.7 %copy-start = (bf16[3,2048,256]{2,1,0:T(8,128)(2,1)S(1)}, bf16[3,2048,256]{2,1,0:T(8,128)(2,1)}, u32[]{:S(2)}) copy-start(bf16[3,2048,256]{2,1,0:T(8,128)(2,1)} %param.22) | copy-start | bytes 9437188
  7.2 110.4 %all-gather.2.cloned.1.call-start = ((), (), s32[]{:S(2)}) async-start(), calls=%async_computation.3 | async-start | bytes 2949120 | tf_op jit(solution)/shard_map/all_gather | solution.py:132
  11.5 8.9 %copy-start.13 = (f32[1,256]{1,0:T(1,128)}, f32[1,256]{1,0:T(1,128)S(1)}, u32[]{:S(2)}) copy-start(f32[1,256]{1,0:T(1,128)S(1)} %get-tuple-element.76) | copy-start | bytes 3076
  32.7 4.5 %copy-start.6 = (bf16[256,2048]{1,0:T(8,128)(2,1)S(1)}, bf16[256,2048]{1,0:T(8,128)(2,1)}, u32[]{:S(2)}) copy-start(bf16[256,2048]{1,0:T(8,128)(2,1)} %param.24) | copy-start | bytes 3145732
  42.3 39.3 %collective-permute-start = (bf16[5,2048]{1,0:T(8,128)(2,1)}, bf16[5,2048]{1,0:T(8,128)(2,1)}, u32[]{:S(2)}, u32[]{:S(2)}) collective-permute-start(bf16[5,2048]{1,0:T(8,128)(2,1)} %get-tuple-element.58), channel_id=1, source_target_pairs={{0,1},{1,2},{2,3},{3,4},{4,5},{5,6},{6,7},{7,0},{8,9},{9,10},{10,1... | collective-permute-start | bytes 61448 | tf_op jit(solution)/shard_map/ppermute | solution.py:75
  44.2 37.9 %collective-permute-start.6 = (bf16[5,2048]{1,0:T(8,128)(2,1)}, bf16[5,2048]{1,0:T(8,128)(2,1)}, u32[]{:S(2)}, u32[]{:S(2)}) collective-permute-start(bf16[5,2048]{1,0:T(8,128)(2,1)} %get-tuple-element.59), channel_id=1, source_target_pairs={{0,7},{1,0},{2,1},{3,2},{4,3},{5,4},{6,5},{7,6},{8,15},{9,8},{10,9... | collective-permute-start | bytes 61448 | tf_op jit(solution)/shard_map/ppermute | solution.py:75
  48.3 38.6 %collective-permute-start.5 = (bf16[5,2048]{1,0:T(8,128)(2,1)}, bf16[5,2048]{1,0:T(8,128)(2,1)}, u32[]{:S(2)}, u32[]{:S(2)}) collective-permute-start(bf16[5,2048]{1,0:T(8,128)(2,1)} %get-tuple-element.60), channel_id=1, source_target_pairs={{0,6},{1,7},{2,0},{3,1},{4,2},{5,3},{6,4},{7,5},{8,14},{9,15},{10,... | collective-permute-start | bytes 61448 | tf_op jit(solution)/shard_map/ppermute | solution.py:75
  50.7 36.2 %collective-permute-start.4 = (bf16[5,2048]{1,0:T(8,128)(2,1)}, bf16[5,2048]{1,0:T(8,128)(2,1)}, u32[]{:S(2)}, u32[]{:S(2)}) collective-permute-start(bf16[5,2048]{1,0:T(8,128)(2,1)} %get-tuple-element.61), channel_id=1, source_target_pairs={{0,5},{1,6},{2,7},{3,0},{4,1},{5,2},{6,3},{7,4},{8,13},{9,14},{10,... | collective-permute-start | bytes 61448 | tf_op jit(solution)/shard_map/ppermute | solution.py:75
  52.8 34.1 %collective-permute-start.3 = (bf16[5,2048]{1,0:T(8,128)(2,1)}, bf16[5,2048]{1,0:T(8,128)(2,1)}, u32[]{:S(2)}, u32[]{:S(2)}) collective-permute-start(bf16[5,2048]{1,0:T(8,128)(2,1)} %get-tuple-element.62), channel_id=1, source_target_pairs={{0,4},{1,5},{2,6},{3,7},{4,0},{5,1},{6,2},{7,3},{8,12},{9,13},{10,... | collective-permute-start | bytes 61448 | tf_op jit(solution)/shard_map/ppermute | solution.py:75
  57.9 6.7 %copy-start.18 = (s32[16]{0:T(128)}, s32[16]{0:T(128)S(1)}, u32[]{:S(2)}) copy-start(s32[16]{0:T(128)S(1)} %convert_add_fusion.1) | copy-start | bytes 196
  64.5 1.5 copy-start.2
  64.5 2.3 %copy-start.4 = (bf16[40,1,128,256]{3,0,2,1:T(8,128)(2,1)}, bf16[40,1,128,256]{3,0,2,1:T(8,128)(2,1)S(1)}, u32[]{:S(2)}) copy-start(bf16[40,1,128,256]{3,0,2,1:T(8,128)(2,1)S(1)} %get-tuple-element.73) | copy-start | bytes 7864324
  72.7 7.9 %copy-start.17 = (s32[1,640]{1,0:T(1,128)S(1)}, s32[1,640]{1,0:T(1,128)}, u32[]{:S(2)}) copy-start(s32[1,640]{1,0:T(1,128)} %param.15) | copy-start | bytes 7684
  72.7 9.0 %copy-start.12 = (bf16[5,2048]{1,0:T(8,128)(2,1)S(1)}, bf16[5,2048]{1,0:T(8,128)(2,1)}, u32[]{:S(2)}) copy-start(bf16[5,2048]{1,0:T(8,128)(2,1)} %get-tuple-element.63) | copy-start | bytes 61444
  72.7 9.5 %copy-start.11 = (bf16[5,2048]{1,0:T(8,128)(2,1)S(1)}, bf16[5,2048]{1,0:T(8,128)(2,1)}, u32[]{:S(2)}) copy-start(bf16[5,2048]{1,0:T(8,128)(2,1)} %get-tuple-element.64) | copy-start | bytes 61444
  72.7 17.6 %copy-start.10 = (f32[2048]{0:T(1024)S(1)}, f32[2048]{0:T(1024)}, u32[]{:S(2)}) copy-start(f32[2048]{0:T(1024)} %param.25) | copy-start | bytes 24580
  72.7 58.1 %all-to-all-start = ((bf16[32,2,128,256]{3,2,1,0:T(8,128)(2,1)}), bf16[32,2,128,256]{3,2,1,0:T(8,128)(2,1)}, u32[]{:S(2)}, u32[]{:S(2)}) async-start(bf16[32,2,128,256]{3,2,1,0:T(8,128)(2,1)} %copy.78), calls=%async_computation | async-start | bytes 8388608 | tf_op jit(solution)/shard_map/all_to_all | solution.py:131
  80.5 98.6 %reduce-scatter.2.cloned.1.call-start = ((), (), s32[]{:S(2)}) async-start(), calls=%async_computation.4 | async-start | bytes 2949120 | tf_op jit(solution)/shard_map/reduce_scatter | solution.py:155
  81.6 8.6 %collective-permute-start.2 = (bf16[5,2048]{1,0:T(8,128)(2,1)S(1)}, bf16[5,2048]{1,0:T(8,128)(2,1)S(1)}, u32[]{:S(2)}, u32[]{:S(2)}) collective-permute-start(bf16[5,2048]{1,0:T(8,128)(2,1)S(1)} %copy-done.12), channel_id=1, source_target_pairs={{0,3},{1,4},{2,5},{3,6},{4,7},{5,0},{6,1},{7,2},{8,11},{9,12},{10,... | collective-permute-start | bytes 61448 | tf_op jit(solution)/shard_map/ppermute | solution.py:75
  82.2 8.1 %collective-permute-start.1 = (bf16[5,2048]{1,0:T(8,128)(2,1)S(1)}, bf16[5,2048]{1,0:T(8,128)(2,1)}, u32[]{:S(2)}, u32[]{:S(2)}) collective-permute-start(bf16[5,2048]{1,0:T(8,128)(2,1)S(1)} %copy-done.11), channel_id=1, source_target_pairs={{0,2},{1,3},{2,4},{3,5},{4,6},{5,7},{6,0},{7,1},{8,10},{9,11},{10,... | collective-permute-start | bytes 61448 | tf_op jit(solution)/shard_map/ppermute | solution.py:75
  91.9 9.3 %collective-permute-start.7 = (bf16[5,2048]{1,0:T(8,128)(2,1)S(1)}, bf16[5,2048]{1,0:T(8,128)(2,1)S(1)}, u32[]{:S(2)}, u32[]{:S(2)}) collective-permute-start(bf16[5,2048]{1,0:T(8,128)(2,1)S(1)} %get-tuple-element.50), channel_id=1, source_target_pairs={{0,1},{1,2},{2,3},{3,4},{4,5},{5,6},{6,7},{7,0},{8,9},{9,10},{10,1... | collective-permute-start | bytes 61448 | tf_op jit(solution)/shard_map/ppermute | solution.py:81
  92.9 19.3 %collective-permute-start.12 = (bf16[5,2048]{1,0:T(8,128)(2,1)S(1)}, bf16[5,2048]{1,0:T(8,128)(2,1)S(1)}, u32[]{:S(2)}, u32[]{:S(2)}) collective-permute-start(bf16[5,2048]{1,0:T(8,128)(2,1)S(1)} %get-tuple-element.50), channel_id=1, source_target_pairs={{0,6},{1,7},{2,0},{3,1},{4,2},{5,3},{6,4},{7,5},{8,14},{9,15},{10,... | collective-permute-start | bytes 61448 | tf_op jit(solution)/shard_map/ppermute | solution.py:81
  94.4 17.2 %collective-permute-start.11 = (bf16[5,2048]{1,0:T(8,128)(2,1)S(1)}, bf16[5,2048]{1,0:T(8,128)(2,1)S(1)}, u32[]{:S(2)}, u32[]{:S(2)}) collective-permute-start(bf16[5,2048]{1,0:T(8,128)(2,1)S(1)} %get-tuple-element.50), channel_id=1, source_target_pairs={{0,5},{1,6},{2,7},{3,0},{4,1},{5,2},{6,3},{7,4},{8,13},{9,14},{10,... | collective-permute-start | bytes 61448 | tf_op jit(solution)/shard_map/ppermute | solution.py:81
  98.3 12.6 %collective-permute-start.10 = (bf16[5,2048]{1,0:T(8,128)(2,1)S(1)}, bf16[5,2048]{1,0:T(8,128)(2,1)S(1)}, u32[]{:S(2)}, u32[]{:S(2)}) collective-permute-start(bf16[5,2048]{1,0:T(8,128)(2,1)S(1)} %get-tuple-element.50), channel_id=1, source_target_pairs={{0,4},{1,5},{2,6},{3,7},{4,0},{5,1},{6,2},{7,3},{8,12},{9,13},{10,... | collective-permute-start | bytes 61448 | tf_op jit(solution)/shard_map/ppermute | solution.py:81
  101.1 9.2 %collective-permute-start.9 = (bf16[5,2048]{1,0:T(8,128)(2,1)S(1)}, bf16[5,2048]{1,0:T(8,128)(2,1)S(1)}, u32[]{:S(2)}, u32[]{:S(2)}) collective-permute-start(bf16[5,2048]{1,0:T(8,128)(2,1)S(1)} %get-tuple-element.50), channel_id=1, source_target_pairs={{0,3},{1,4},{2,5},{3,6},{4,7},{5,0},{6,1},{7,2},{8,11},{9,12},{10,... | collective-permute-start | bytes 61448 | tf_op jit(solution)/shard_map/ppermute | solution.py:81
  101.1 6.4 %collective-permute-start.8 = (bf16[5,2048]{1,0:T(8,128)(2,1)S(1)}, bf16[5,2048]{1,0:T(8,128)(2,1)S(1)}, u32[]{:S(2)}, u32[]{:S(2)}) collective-permute-start(bf16[5,2048]{1,0:T(8,128)(2,1)S(1)} %get-tuple-element.50), channel_id=1, source_target_pairs={{0,2},{1,3},{2,4},{3,5},{4,6},{5,7},{6,0},{7,1},{8,10},{9,11},{10,... | collective-permute-start | bytes 61448 | tf_op jit(solution)/shard_map/ppermute | solution.py:81
  107.5 5.3 %collective-permute-start.13 = (bf16[5,2048]{1,0:T(8,128)(2,1)S(1)}, bf16[5,2048]{1,0:T(8,128)(2,1)S(1)}, u32[]{:S(2)}, u32[]{:S(2)}) collective-permute-start(bf16[5,2048]{1,0:T(8,128)(2,1)S(1)} %get-tuple-element.50), channel_id=1, source_target_pairs={{0,7},{1,0},{2,1},{3,2},{4,3},{5,4},{6,5},{7,6},{8,15},{9,8},{10,9... | collective-permute-start | bytes 61448 | tf_op jit(solution)/shard_map/ppermute | solution.py:81
  115.0 5.9 %copy-start.15 = (f32[2048]{0:T(1024)S(1)}, f32[2048]{0:T(1024)}, u32[]{:S(2)}) copy-start(f32[2048]{0:T(1024)} %param.21) | copy-start | bytes 24580
  115.0 5.9 %copy-start.16 = (f32[2048]{0:T(1024)S(1)}, f32[2048]{0:T(1024)}, u32[]{:S(2)}) copy-start(f32[2048]{0:T(1024)} %param.20) | copy-start | bytes 24580
  117.6 2.5 %copy-start.5 = (bf16[640,2048]{1,0:T(8,128)(2,1)S(1)}, bf16[640,2048]{1,0:T(8,128)(2,1)}, u32[]{:S(2)}) copy-start(bf16[640,2048]{1,0:T(8,128)(2,1)} %all-gather.2.cloned.1.call-done) | copy-start | bytes 7864324
  124.0 0.7 copy-start.14
  124.7 1.0 copy-start.9
  130.7 3.9 %copy-start.3 = (bf16[40,1,128,256]{3,0,2,1:T(8,128)(2,1)S(1)}, bf16[40,1,128,256]{3,0,2,1:T(8,128)(2,1)}, u32[]{:S(2)}) copy-start(bf16[40,1,128,256]{3,0,2,1:T(8,128)(2,1)} %copy-done.2) | copy-start | bytes 7864324
  136.2 2.4 %copy-start.8 = (bf16[40,2048]{1,0:T(8,128)(2,1)S(1)}, bf16[40,2048]{1,0:T(8,128)(2,1)}, u32[]{:S(2)}) copy-start(bf16[40,2048]{1,0:T(8,128)(2,1)} %reshape.272) | copy-start | bytes 491524
  136.2 3.0 %copy-start.19 = (s32[16]{0:T(128)S(1)}, s32[16]{0:T(128)}, u32[]{:S(2)}) copy-start(s32[16]{0:T(128)} %copy-done.18) | copy-start | bytes 196
  138.6 40.5 %copy-start.7 = (bf16[80,2048]{1,0:T(8,128)(2,1)S(1)}, bf16[80,2048]{1,0:T(8,128)(2,1)}, u32[]{:S(2)}) copy-start(bf16[80,2048]{1,0:T(8,128)(2,1)} %param.14) | copy-start | bytes 983044
  141.5 15.7 %all-to-all-start.1 = ((bf16[32,2,1024]{2,1,0:T(2,128)(2,1)}), bf16[32,2,1024]{2,1,0:T(2,128)(2,1)S(1)}, u32[]{:S(2)}, u32[]{:S(2)}) async-start(bf16[32,2,1024]{2,1,0:T(2,128)(2,1)} %reshape.305), calls=%async_computation.2 | async-start | bytes 262144 | tf_op jit(solution)/shard_map/all_to_all | solution.py:168
  180.9 4.9 %copy-start.1 = (bf16[3,2048,256]{2,1,0:T(8,128)(2,1)S(1)}, bf16[3,2048,256]{2,1,0:T(8,128)(2,1)}, u32[]{:S(2)}) copy-start(bf16[3,2048,256]{2,1,0:T(8,128)(2,1)} %param.22) | copy-start | bytes 9437188
Sparse Core Ops, SparseCore 0:
  9.8 47.9 all-gather.1
  134.7 44.3 reduce-scatter.1

commit v2 on v1

v2 whole, which is shorter than its diff:
```python
import jax
import jax.numpy as jnp
from jax import lax
from jax.sharding import PartitionSpec as P

HEAD_DIM = 128
CAP = 1


EPSILON = 1e-05


def layer_norm(values, norm_gain, norm_bias):
    wide = values.astype(jnp.float32)
    center = jnp.mean(wide, axis=-1, keepdims=True)
    spread = jnp.mean(jnp.square(wide - center), axis=-1, keepdims=True)
    scaled = (wide - center) * lax.rsqrt(spread + EPSILON)
    return (scaled * norm_gain + norm_bias).astype(jnp.bfloat16)


def decode_partial(rows, cache, ages, norm_gain, norm_bias, qkv_weight, qkv_bias, out_weight):
    count = rows.shape[0]
    width = qkv_weight.shape[2]
    heads_here = width // HEAD_DIM
    length = cache.shape[2]
    normed = layer_norm(rows, norm_gain, norm_bias)
    projected = jnp.einsum("rd,cde->cre", normed, qkv_weight, preferred_element_type=jnp.float32)
    queries = (projected[0] + qkv_bias[0]).astype(jnp.bfloat16)
    key_new = (projected[1] + qkv_bias[1]).astype(jnp.bfloat16)
    value_new = (projected[2] + qkv_bias[2]).astype(jnp.bfloat16)
    head_of_col = jnp.arange(width) // HEAD_DIM
    diag = jnp.arange(heads_here)[:, None] == head_of_col[None, :]
    q_blocks = jnp.where(diag[None], queries[:, None, :], jnp.zeros((), jnp.bfloat16))
    scale = HEAD_DIM ** (-0.5)
    scores = (
        jnp.einsum("rhc,rlc->rhl", q_blocks, cache[:, 0], preferred_element_type=jnp.float32)
        * scale
    )
    own = (
        jnp.sum(
            (queries.astype(jnp.float32) * key_new.astype(jnp.float32)).reshape(
                count, heads_here, HEAD_DIM
            ),
            axis=-1,
        )
        * scale
    )
    live = jnp.arange(length)[None, :] < ages[:, None]
    scores = jnp.where(live[:, None, :], scores, -1e30)
    highest = jnp.maximum(jnp.max(scores, axis=-1), own)
    weights = jnp.exp(scores - highest[..., None])
    own_weight = jnp.exp(own - highest)
    total = jnp.sum(weights, axis=-1) + own_weight
    probs = (weights / total[..., None]).astype(jnp.bfloat16)
    own_prob = (own_weight / total).astype(jnp.bfloat16)
    mixed = jnp.einsum("rhl,rlc->rhc", probs, cache[:, 1], preferred_element_type=jnp.float32)
    context = jnp.sum(jnp.where(diag[None], mixed, 0.0), axis=1)
    context = context + own_prob.astype(jnp.float32)[:, head_of_col] * value_new.astype(jnp.float32)
    context = context.astype(jnp.bfloat16)
    partial_value = jnp.dot(context, out_weight, preferred_element_type=jnp.float32)
    return partial_value, key_new, value_new


def updated_rows(cache, key_new, value_new, ages, picks):
    length = cache.shape[2]
    fresh = jnp.stack([key_new, value_new], axis=1)[picks]
    written = jnp.arange(length)[None, :] == ages[picks][:, None]
    return jnp.where(written[:, None, :, None], fresh[:, :, None, :], cache[picks])


def reduce_over_tp(partial_value, rows, out_bias):
    n = lax.axis_size("tp")
    me = lax.axis_index("tp")
    count, model = rows.shape
    rounds = n.bit_length() - 1
    held = partial_value.astype(jnp.bfloat16).astype(jnp.float32)
    chunk = jnp.zeros((), jnp.int32)
    for k in range(rounds):
        mask = 1 << k
        bit = (me >> k) & 1
        halves = held.reshape(2, held.shape[0] // 2, model)
        keep = lax.dynamic_index_in_dim(halves, bit, 0, keepdims=False)
        give = lax.dynamic_index_in_dim(halves, 1 - bit, 0, keepdims=False)
        got = lax.ppermute(give, "tp", [(i, i ^ mask) for i in range(n)])
        held = keep + got
        chunk = chunk * 2 + bit
    share = count // n
    own_rows = lax.dynamic_slice_in_dim(rows, chunk * share, share, 0)
    out = (own_rows.astype(jnp.float32) + held + out_bias).astype(jnp.bfloat16)
    for k in reversed(range(rounds)):
        mask = 1 << k
        bit = (me >> k) & 1
        got = lax.ppermute(out, "tp", [(i, i ^ mask) for i in range(n)])
        out = jnp.where(bit == 0, jnp.concatenate([out, got]), jnp.concatenate([got, out]))
    return out


def on_device(
    prompt_rows,
    prompt_pieces,
    decode_rows,
    request_ages,
    migrate_to,
    past_cache,
    norm_gain,
    norm_bias,
    qkv_weight,
    qkv_bias,
    out_weight,
    out_bias,
):
    rep_count = lax.axis_size("rep")
    width = qkv_weight.shape[2]
    heads_here = width // HEAD_DIM
    leaving = migrate_to.shape[0]
    staying = decode_rows.shape[0] - leaving
    targets = migrate_to[:, 0]
    match = targets[None, :] == jnp.arange(rep_count * CAP)[:, None]
    has = jnp.any(match, axis=1)
    picks = staying + jnp.sum(jnp.where(match, jnp.arange(leaving)[None, :], 0), axis=1)
    partial_value, key_new, value_new = decode_partial(
        decode_rows, past_cache, request_ages, norm_gain, norm_bias, qkv_weight, qkv_bias, out_weight
    )
    kept_cache = updated_rows(past_cache, key_new, value_new, request_ages, jnp.arange(staying))
    send_cache = jnp.where(
        has[:, None, None, None],
        updated_rows(past_cache, key_new, value_new, request_ages, picks),
        jnp.zeros((), jnp.bfloat16),
    )
    moved_cache = lax.all_to_all(send_cache, "rep", split_axis=0, concat_axis=0, tiled=True)
    decode_out = reduce_over_tp(partial_value, decode_rows, out_bias)
    normed = layer_norm(lax.all_gather(prompt_rows, "tp", axis=0, tiled=True), norm_gain, norm_bias)
    projected = jnp.einsum("rd,cde->cre", normed, qkv_weight, preferred_element_type=jnp.float32)
    total_rows = projected.shape[1]
    queries = (projected[0] + qkv_bias[0]).astype(jnp.bfloat16)
    key_rows = (projected[1] + qkv_bias[1]).astype(jnp.bfloat16)
    value_rows = (projected[2] + qkv_bias[2]).astype(jnp.bfloat16)
    head_q = queries.reshape(total_rows, heads_here, HEAD_DIM)
    head_k = key_rows.reshape(total_rows, heads_here, HEAD_DIM)
    head_v = value_rows.reshape(total_rows, heads_here, HEAD_DIM)
    scores = jnp.einsum(
        "qhe,khe->hqk", head_q, head_k, preferred_element_type=jnp.float32
    ) * HEAD_DIM ** (-0.5)
    pieces = prompt_pieces[0]
    position = jnp.arange(total_rows)
    allowed = (pieces[:, None] == pieces[None, :]) & (position[None, :] <= position[:, None])
    scores = jnp.where(allowed[None], scores, -1e30)
    highest = jnp.max(scores, axis=-1, keepdims=True)
    weights = jnp.exp(scores - highest)
    probs = (weights / jnp.sum(weights, axis=-1, keepdims=True)).astype(jnp.bfloat16)
    context = jnp.einsum("hqk,khe->qhe", probs, head_v, preferred_element_type=jnp.float32)
    context = context.reshape(total_rows, width).astype(jnp.bfloat16)
    context, moved_cache, decode_out = lax.optimization_barrier((context, moved_cache, decode_out))
    attended = lax.psum_scatter(
        jnp.dot(context, out_weight, preferred_element_type=jnp.float32).astype(jnp.bfloat16),
        "tp",
        scatter_dimension=0,
        tiled=True,
    ).astype(jnp.float32)
    prompt_out = (prompt_rows.astype(jnp.float32) + attended + out_bias).astype(jnp.bfloat16)
    prompt_cache = jnp.stack([key_rows, value_rows])
    kept_out = decode_out[:staying]
    send_rows = jnp.where(has[:, None], decode_out[picks], jnp.zeros((), jnp.bfloat16))
    moved_out = lax.all_to_all(send_rows, "rep", split_axis=0, concat_axis=0, tiled=True)
    return (prompt_out, prompt_cache, kept_out, kept_cache, moved_out, moved_cache)


def solution(mesh):
    placed = (
        P(("rep", "tp"), None),
        P("rep", None),
        P("rep", None),
        P("rep"),
        P("rep", None),
        P("rep", None, None, "tp"),
        P(),
        P(),
        P(None, None, "tp"),
        P(None, "tp"),
        P("tp", None),
        P(),
    )
    return jax.shard_map(
        on_device,
        mesh=mesh,
        in_specs=placed,
        out_specs=(
            P(("rep", "tp"), None),
            P(None, "rep", "tp"),
            P("rep", None),
            P("rep", None, None, "tp"),
            P("rep", None),
            P("rep", None, None, "tp"),
        ),
        check_vma=False,
    )
```

time: 194 us -> 192 us (0.990)
  waiting for transfers between devices: 34.5 us -> 53.9 us
  starting transfers between devices: 50.5 us -> 32.2 us
  local copies, waits for them, and re-layouts: 45.7 us -> 37.1 us
  other arithmetic: 26.6 us -> 33.5 us
    all_to_all x1, waiting for transfers between devices: 1.79 us -> 20.7 us  [on_device(): lax.all_to_all(send_cache, 'rep', split_axis=0, concat_axis=0, tiled=True)]
    ppermute x14 -> x6, starting transfers between devices: 33.5 us -> 15.2 us  [the longest x3 12 us: reduce_over_tp(): got = lax.ppermute(give, 'tp', [(i, i ^ mask) for i in range(n)])]
    ppermute x14 -> x6, waiting for transfers between devices: 5.49 us -> 22.9 us  [the longest x3 13.4 us: reduce_over_tp(): got = lax.ppermute(give, 'tp', [(i, i ^ mask) for i in range(n)])]
    reduce_scatter x1, waiting for transfers between devices: 21 us -> 7.01 us  [on_device(): lax.psum_scatter(jnp.dot(context, out_weight, preferred_element_type=jnp....]
    gather x2 -> x9, local copies, waits for them, and re-layouts: 3.02 us -> 15.9 us  [the longest x2 10.4 us: updated_rows(): cache[picks]]
    another operation x3 -> x1, local copies, waits for them, and re-layouts: 9.96 us -> 0.03 us  [updated_rows(): fresh = jnp.stack([key_new, value_new], axis=1)[picks]]
    slice x2 -> x1, local copies, waits for them, and re-layouts: 5.55 us -> 0.01 us  [decode_partial(): key_new = (projected[1] + qkv_bias[1]).astype(jnp.bfloat16)]
    dot_general x5 -> x2, matrix products: 9.59 us -> 4.9 us  [the longest x1 2.61 us: decode_partial(): jnp.einsum('rhc,rlc->rhl', q_blocks, cache[:, 0], preferred_element_type=...]
  transfers between devices with their start and end apart: 18 -> 10, of which waited for: 5 -> 7; matrix products, arithmetic and copies ran while one was open for 41% -> 42% of each run, Pallas kernels for 0% -> 0%
where the time goes in v2:
time: 192 us; the launch traced here: 190 us
  waiting for transfers between devices  53.9 us (28%)
  local copies, waits for them, and re-layouts  37.1 us (19%)
  other arithmetic  33.5 us (17%)
  starting transfers between devices  32.2 us (17%)
  matrix products  19.2 us (10%)
  between operations  14.5 us (8%)
    all_to_all x1, waiting for transfers between devices, on_device(): lax.all_to_all(send_cache, 'rep', split_axis=0, concat_axis=0, tiled=True)  20.7 us
    ppermute x3, waiting for transfers between devices, reduce_over_tp(): got = lax.ppermute(give, 'tp', [(i, i ^ mask) for i in range(n)])  13.4 us
    unnamed x41, local copies, waits for them, and re-layouts  12.5 us
    ppermute x3, starting transfers between devices, reduce_over_tp(): got = lax.ppermute(give, 'tp', [(i, i ^ mask) for i in range(n)])  12 us
    gather x2, local copies, waits for them, and re-layouts, updated_rows(): cache[picks]  10.4 us
    ppermute x3, waiting for transfers between devices, reduce_over_tp(): got = lax.ppermute(out, 'tp', [(i, i ^ mask) for i in range(n)])  9.57 us
    all_to_all x1, starting transfers between devices, on_device(): lax.all_to_all(send_rows, 'rep', split_axis=0, concat_axis=0, tiled=True)  9.13 us
    all_to_all x1, starting transfers between devices, on_device(): lax.all_to_all(send_cache, 'rep', split_axis=0, concat_axis=0, tiled=True)  7.82 us
  transfers between devices with their start and end apart: 10, of which 7 were waited for; matrix products, arithmetic and copies ran while one was open for 42% of the time, Pallas kernels for 0%

profile of v2, /device:TPU:2, one launch (start us, length us, event | category | flops | bytes accessed | tf_op | source)
XLA Modules:
  0.0 190.4 jit_solution(10726945409189851949)
XLA Ops:
  7.2 0.7 all-gather.2.cloned.1.call-update
  8.0 1.2 convert_reduce_fusion.1
  9.2 1.1 fusion.45
  10.4 1.6 convolution_bitcast_fusion
  12.4 2.6 %fusion.86 = (f32[40,2]{1,0:T(8,128)S(1)}, f32[40,2,128]{2,1,0:T(2,128)S(1)}) fusion(bf16[40,2,128,256]{3,2,1,0:T(8,128)(2,1)} %param.17, pred[2,256]{1,0:T(4,128)(4,1)S(1)} %iota_compare_fusion.5, bf16[40,256]{1,0:T(8,128)(2,1)S(1)} %fusion.65, pred[40,128]{1,0:T(8,128)(4,1)S(1)} %iota_compare_fusion.1), kind=kOutput, calls=%fused_computation.149 | convolution fusion | flops 5294000 | bytes 2688832 | tf_op jit(solution)/shard_map/rhc,rlc->rhl/dot_general | solution.py:36
  15.2 0.2 fusion.68
  15.6 2.3 %fusion.34 = f32[40,256]{1,0:T(8,128)S(1)} fusion(bf16[40,2,128,256]{3,2,1,0:T(8,128)(2,1)} %param.17, pred[2,256]{1,0:T(4,128)(4,1)S(1)} %iota_compare_fusion.5, f32[40,2,128]{2,1,0:T(2,128)S(1)} %get-tuple-element.59, f32[40,2]{1,0:T(8,128)S(1)} %copy.82, f32[40,2]{1,0:T(8,128)S(1)} %copy.80), kind=kOutput, calls=%fused_computation.48 | convolution fusion | flops 5304320 | bytes 2704512 | tf_op jit(solution)/shard_map/rhl,rlc->rhc/dot_general | solution.py:56
  17.9 0.7 gather_fusion.3
  18.7 2.2 %fusion.21 = f32[40,2048]{1,0:T(8,128)} fusion(bf16[256,2048]{1,0:T(8,128)(2,1)} %param.22, f32[40,256]{1,0:T(8,128)S(1)} %fusion.34, f32[256,40]{0,1:T(8,128)S(1)} %copy.84, f32[3,40,256]{2,1,0:T(8,128)S(1)} %convolution_bitcast_fusion, f32[256]{0:T(256)S(1)} %bitcast.115), kind=kOutput, calls=%fused_computation.37 | convolution fusion | flops 42168320 | bytes 1500160 | tf_op jit(solution)/shard_map/dot_general | solution.py:60
  21.0 1.0 reshape.450
  22.0 0.7 dynamic-slice_bitcast_fusion
  22.7 1.9 %collective-permute-start = (f32[20,2048]{1,0:T(8,128)}, f32[20,2048]{1,0:T(8,128)}, u32[]{:S(2)}, u32[]{:S(2)}) collective-permute-start(f32[20,2048]{1,0:T(8,128)} %dynamic-slice_bitcast_fusion), channel_id=1, source_target_pairs={{0,1},{1,0},{2,3},{3,2},{4,5},{5,4},{6,7},{7,6},{8,9},{9,8},{10,11... | collective-permute-start | bytes 491528 | tf_op jit(solution)/shard_map/ppermute | solution.py:84
  24.6 0.7 select_reduce_fusion
  25.4 1.2 gather_fusion
  26.6 1.4 fusion.67
  28.0 0.7 iota_compare_fusion.2
  28.7 5.4 %collective-permute-done = f32[20,2048]{1,0:T(8,128)} collective-permute-done((f32[20,2048]{1,0:T(8,128)}, f32[20,2048]{1,0:T(8,128)}, u32[]{:S(2)}, u32[]{:S(2)}) %collective-permute-start) | collective-permute-done | bytes 163872 | tf_op jit(solution)/shard_map/ppermute | solution.py:84
  34.1 1.6 bitcast_add_fusion
  35.7 1.0 reshape.447
  36.7 3.6 %collective-permute-start.1 = (f32[10,2048]{1,0:T(8,128)S(1)}, f32[10,2048]{1,0:T(8,128)S(1)}, u32[]{:S(2)}, u32[]{:S(2)}) collective-permute-start(f32[10,2048]{1,0:T(8,128)S(1)} %dynamic-slice_bitcast_fusion.1), channel_id=1, source_target_pairs={{0,2},{1,3},{2,0},{3,1},{4,6},{5,7},{6,4},{7,5},{8,10},{9,11},{10,... | collective-permute-start | bytes 245768 | tf_op jit(solution)/shard_map/ppermute | solution.py:84
  40.4 1.3 fusion.76
  41.6 8.0 %collective-permute-done.1 = f32[10,2048]{1,0:T(8,128)S(1)} collective-permute-done((f32[10,2048]{1,0:T(8,128)S(1)}, f32[10,2048]{1,0:T(8,128)S(1)}, u32[]{:S(2)}, u32[]{:S(2)}) %collective-permute-start.1) | collective-permute-done | bytes 81952 | tf_op jit(solution)/shard_map/ppermute | solution.py:84
  49.7 6.5 %collective-permute-start.2 = (f32[5,2048]{1,0:T(8,128)S(1)}, f32[5,2048]{1,0:T(8,128)S(1)}, u32[]{:S(2)}, u32[]{:S(2)}) collective-permute-start(f32[5,2048]{1,0:T(8,128)S(1)} %dynamic-slice_bitcast_fusion.2), channel_id=1, source_target_pairs={{0,4},{1,5},{2,6},{3,7},{4,0},{5,1},{6,2},{7,3},{8,12},{9,13},{10,... | collective-permute-start | bytes 122888 | tf_op jit(solution)/shard_map/ppermute | solution.py:84
  56.2 0.8 pad_maximum_fusion.1
  56.9 5.4 %gather_fusion.2 = bf16[32,2,128,256]{3,2,1,0:T(8,128)(2,1)} fusion(bf16[40,2,128,256]{3,2,1,0:T(8,128)(2,1)} %param.17, s32[1024]{0:T(1024)S(1)} %pad_clamp_fusion.2), kind=kCustom, calls=%fused_computation.2 | custom fusion | bytes 8388736 | tf_op jit(solution)/shard_map/gather | solution.py:68
  62.3 0.6 gather_fusion.1
  63.0 0.9 fusion.61
  63.9 2.8 %collective-permute-start.3 = (bf16[5,2048]{1,0:T(8,128)(2,1)S(1)}, bf16[5,2048]{1,0:T(8,128)(2,1)S(1)}, u32[]{:S(2)}, u32[]{:S(2)}) collective-permute-start(bf16[5,2048]{1,0:T(8,128)(2,1)S(1)} %fusion.61), channel_id=1, source_target_pairs={{0,4},{1,5},{2,6},{3,7},{4,0},{5,1},{6,2},{7,3},{8,12},{9,13},{10,... | collective-permute-start | bytes 61448 | tf_op jit(solution)/shard_map/ppermute | solution.py:93
  66.7 4.0 %select_select_fusion = bf16[32,2,128,256]{3,2,1,0:T(8,128)(2,1)} fusion(bf16[32,2,128,256]{3,2,1,0:T(8,128)(2,1)} %gather_fusion.2, pred[32]{0:T(512)(128)(4,1)S(1)} %copy-done.16, pred[32,128]{1,0:T(8,128)(4,1)S(1)} %iota_compare_fusion.2, bf16[32,2,256]{2,1,0:T(2,128)(2,1)S(1)} %gather_fusion.1), kind=kLoop, calls=%fused_computation.17 | loop fusion | flops 4194304 | bytes 8425504 | tf_op jit(solution)/shard_map/jit(_where)/select_n | solution.py:125
  70.6 7.8 %all-to-all-start = ((bf16[32,2,128,256]{3,2,1,0:T(8,128)(2,1)}), bf16[32,2,128,256]{3,2,1,0:T(8,128)(2,1)}, u32[]{:S(2)}, u32[]{:S(2)}) async-start(bf16[32,2,128,256]{3,2,1,0:T(8,128)(2,1)} %select_select_fusion), calls=%async_computation | async-start | bytes 8388608 | tf_op jit(solution)/shard_map/all_to_all | solution.py:130
  78.7 5.8 %collective-permute-done.4 = bf16[10,2048]{1,0:T(8,128)(2,1)S(1)} collective-permute-done((bf16[10,2048]{1,0:T(8,128)(2,1)S(1)}, bf16[10,2048]{1,0:T(8,128)(2,1)S(1)}, u32[]{:S(2)}, u32[]{:S(2)}) %collective-permute-start.4) | collective-permute-done | bytes 40992 | tf_op jit(solution)/shard_map/ppermute | solution.py:93
  84.6 0.3 collective-permute-start.5
  84.9 1.1 fusion.25
  86.0 3.7 %collective-permute-done.5 = bf16[20,2048]{1,0:T(8,128)(2,1)S(1)} collective-permute-done((bf16[20,2048]{1,0:T(8,128)(2,1)S(1)}, bf16[20,2048]{1,0:T(8,128)(2,1)S(1)}, u32[]{:S(2)}, u32[]{:S(2)}) %collective-permute-start.5) | collective-permute-done | bytes 81952 | tf_op jit(solution)/shard_map/ppermute | solution.py:93
  89.8 2.3 %convert_reduce_fusion = f32[640]{0:T(1024)S(1)} fusion(bf16[640,2048]{1,0:T(8,128)(2,1)} %all-gather.2.cloned.1.call-done), kind=kLoop, calls=%fused_computation.10 | loop fusion | flops 2620800 | bytes 2624000 | tf_op jit(solution)/shard_map/reduce_sum | solution.py:15
  92.3 0.8 fusion.3
  93.2 3.6 %fusion.27 = f32[3,640,256]{1,2,0:T(8,128)S(1)} fusion(bf16[3,2048,256]{2,1,0:T(8,128)(2,1)S(1)} %copy-done, bf16[640,2048]{1,0:T(8,128)(2,1)S(1)} %copy-done.2, f32[2048]{0:T(1024)} %param.19, f32[2048]{0:T(1024)} %param.18, f32[640]{0:T(1024)S(1)} %add_rsqrt_fusion, f32[640]{0:T(1024)S(1)} %broadcast_multiply_fusion), kind=kOutput, calls=%fused_computation.44 | convolution fusion | flops 2021130240 | bytes 7754752 | tf_op jit(solution)/shard_map/rd,cde->cre/dot_general | solution.py:133
  96.8 1.7 add_convert_fusion.1
  98.4 2.2 %copy.73 = f32[640,2,128]{2,0,1:T(8,128)} copy(f32[640,2,128]{0,2,1:T(8,128)} %bitcast.107) | data formatting | bytes 1310720 | tf_op jit(solution)/shard_map/squeeze | solution.py:135
  100.6 2.2 %copy.74 = f32[640,2,128]{2,0,1:T(8,128)} copy(f32[640,2,128]{0,2,1:T(8,128)} %bitcast.106) | data formatting | bytes 1310720 | tf_op jit(solution)/shard_map/squeeze | solution.py:136
  102.8 1.9 %fusion.49 = f32[2,640,640]{1,2,0:T(8,128)S(1)} fusion(f32[640,2,128]{2,0,1:T(8,128)} %copy.73, f32[640,2,128]{2,0,1:T(8,128)} %copy.74, f32[2,128]{1,0:T(2,128)S(1)} %bitcast.114, f32[2,128]{1,0:T(2,128)S(1)} %bitcast.121), kind=kOutput, calls=%fused_computation.66 | convolution fusion | flops 210370560 | bytes 4589568 | tf_op jit(solution)/shard_map/qhe,khe->hqk/dot_general | solution.py:141
  104.7 2.0 %fusion.85 = (f32[2,640]{1,0:T(2,128)S(1)}, f32[2,640,640]{1,2,0:T(8,128)S(1)}) fusion(f32[2,640,640]{1,2,0:T(8,128)S(1)} %fusion.49, pred[640,640]{0,1:T(8,128)(4,1)S(1)} %copy-done.6), kind=kOutput, calls=%fused_computation.148 | output fusion | flops 4915839 | bytes 6968320 | tf_op jit(solution)/shard_map/sub | solution.py:149
  106.7 1.3 fusion.30
  108.0 20.7 %all-to-all-done = bf16[32,2,128,256]{3,2,1,0:T(8,128)(2,1)} async-done(((bf16[32,2,128,256]{3,2,1,0:T(8,128)(2,1)}), bf16[32,2,128,256]{3,2,1,0:T(8,128)(2,1)}, u32[]{:S(2)}, u32[]{:S(2)}) %all-to-all-start) | async-done | bytes 4194336 | tf_op jit(solution)/shard_map/all_to_all | solution.py:130
  128.7 3.7 %convolution_convert_fusion = bf16[640,2048]{1,0:T(8,128)(2,1)} fusion(bf16[640,256]{0,1:T(8,128)(2,1)} %bitcast.108, bf16[256,2048]{1,0:T(8,128)(2,1)} %param.22), kind=kOutput, calls=%fused_computation.21 | convolution fusion | flops 672399360 | bytes 3997696 | tf_op jit(solution)/shard_map/dot_general | solution.py:155
  132.5 0.6 gather_fusion.5
  133.1 5.0 %gather_fusion.6 = bf16[24,2,128,256]{3,2,1,0:T(8,128)(2,1)} fusion(bf16[40,2,128,256]{3,2,1,0:T(8,128)(2,1)} %param.17, s32[1024]{0:T(1024)S(1)} %pad_clamp_fusion), kind=kCustom, calls=%fused_computation.6 | custom fusion | bytes 6291552 | tf_op jit(solution)/shard_map/gather | solution.py:68
  138.1 0.7 gather_fusion.4
  138.9 3.4 %broadcast_select_fusion = bf16[24,2,128,256]{3,2,1,0:T(8,128)(2,1)} fusion(bf16[24,2,128,256]{3,2,1,0:T(8,128)(2,1)} %gather_fusion.6, pred[24,128]{1,0:T(8,128)(4,1)S(1)} %iota_compare_fusion.3, bf16[24,2,256]{2,1,0:T(2,128)(2,1)S(1)} %gather_fusion.5), kind=kLoop, calls=%fused_computation.22 | loop fusion | flops 1572864 | bytes 6319104 | tf_op jit(solution)/shard_map/jit(_where)/select_n | solution.py:68
  142.2 1.6 gather_fusion.7
  143.8 0.6 slice.56
  144.4 1.7 bitcast_select_fusion
  146.1 0.5 broadcast.374
  146.7 2.2 %reduce.1 = bf16[32,2048]{1,0:T(8,128)(2,1)} reduce(bf16[32,1,2048]{2,0,1:T(8,128)(2,1)} %bitcast_select_fusion, bf16[]{:T(256)} %broadcast.374), dimensions={1}, to_apply=%copy.86.reduce_sub_computation | reduce | bytes 262146 | tf_op jit(solution)/shard_map/jit(_where)/select_n | solution.py:163
  148.9 1.6 reshape.519
  150.5 9.1 %all-to-all-start.1 = ((bf16[32,2,1024]{2,1,0:T(2,128)(2,1)}), bf16[32,2,1024]{2,1,0:T(2,128)(2,1)}, u32[]{:S(2)}, u32[]{:S(2)}) async-start(bf16[32,2,1024]{2,1,0:T(2,128)(2,1)} %reshape.519), calls=%async_computation.2 | async-start | bytes 262144 | tf_op jit(solution)/shard_map/all_to_all | solution.py:164
  159.7 2.0 %pad_maximum_fusion = bf16[2,640,256]{1,2,0:T(8,128)(2,1)} fusion(bf16[1,640,256]{1,2,0:T(8,128)(2,1)} %get-tuple-element.43, bf16[1,640,256]{1,2,0:T(8,128)(2,1)} %get-tuple-element.42), kind=kLoop, calls=%fused_computation.51 | loop fusion | flops 327680 | bytes 1310720 | tf_op jit(solution)/shard_map/stack | solution.py:161
  161.7 2.2 %copy.87 = bf16[2,640,256]{2,1,0:T(8,128)(2,1)} copy(bf16[2,640,256]{1,2,0:T(8,128)(2,1)} %pad_maximum_fusion) | data formatting | bytes 1310720
  163.8 2.5 %all-to-all-done.1 = bf16[32,2,1024]{2,1,0:T(2,128)(2,1)} async-done(((bf16[32,2,1024]{2,1,0:T(2,128)(2,1)}), bf16[32,2,1024]{2,1,0:T(2,128)(2,1)}, u32[]{:S(2)}, u32[]{:S(2)}) %all-to-all-start.1) | async-done | bytes 131104 | tf_op jit(solution)/shard_map/all_to_all | solution.py:164
  166.4 2.0 %reshape.520 = bf16[32,1,2048]{2,1,0:T(2,128)(2,1)} reshape(bf16[32,2,1024]{2,1,0:T(2,128)(2,1)} %all-to-all-done.1) | data formatting | bytes 262144
  168.4 1.7 copy.94
  170.0 7.0 %reduce-scatter.2.cloned.1.call-done = bf16[80,2048]{1,0:T(8,128)(2,1)} async-done(((bf16[640,2048]{1,0:T(8,128)(2,1)}), bf16[80,2048]{1,0:T(8,128)(2,1)}) %reduce-scatter.2.cloned.1.call-update) | async-done | bytes 327696 | tf_op jit(solution)/shard_map/reduce_scatter | solution.py:154
  177.1 1.8 add_convert_fusion.2
  178.9 4.7 %copy.97 = bf16[32,2,128,256]{3,2,1,0:T(8,128)(2,1)} copy(bf16[32,2,128,256]{3,2,1,0:T(8,128)(2,1)} %all-to-all-done) | data formatting | bytes 8388608
  (80 shorter events, 1.7 us)
Async XLA Ops:
  7.2 3.2 %copy-start = (bf16[3,2048,256]{2,1,0:T(8,128)(2,1)S(1)}, bf16[3,2048,256]{2,1,0:T(8,128)(2,1)}, u32[]{:S(2)}) copy-start(bf16[3,2048,256]{2,1,0:T(8,128)(2,1)} %param.20) | copy-start | bytes 9437188
  7.2 4.9 %copy-start.15 = (f32[3,256]{1,0:T(4,128)S(1)}, f32[3,256]{1,0:T(4,128)}, u32[]{:S(2)}) copy-start(f32[3,256]{1,0:T(4,128)} %param.21) | copy-start | bytes 9220
  7.2 5.2 %copy-start.1 = (s32[40]{0:T(128)S(1)}, s32[40]{0:T(128)}, u32[]{:S(2)}) copy-start(s32[40]{0:T(128)} %param.15) | copy-start | bytes 484
  7.2 82.6 %all-gather.2.cloned.1.call-start = ((), (), s32[]{:S(2)}) async-start(), calls=%async_computation.3 | async-start | bytes 2949120 | tf_op jit(solution)/shard_map/all_gather | solution.py:132
  12.0 6.8 %copy-start.4 = (f32[3,40,256]{2,1,0:T(8,128)}, f32[3,40,256]{2,1,0:T(8,128)S(1)}, u32[]{:S(2)}) copy-start(f32[3,40,256]{2,1,0:T(8,128)S(1)} %convolution_bitcast_fusion) | copy-start | bytes 368644
  12.1 3.3 %copy-start.11 = (f32[1,256]{1,0:T(1,128)}, f32[1,256]{1,0:T(1,128)S(1)}, u32[]{:S(2)}) copy-start(f32[1,256]{1,0:T(1,128)S(1)} %get-tuple-element.53) | copy-start | bytes 3076
  12.1 14.5 %copy-start.9 = (f32[1,256]{1,0:T(1,128)}, f32[1,256]{1,0:T(1,128)S(1)}, u32[]{:S(2)}) copy-start(f32[1,256]{1,0:T(1,128)S(1)} %get-tuple-element.51) | copy-start | bytes 3076
  22.7 11.4 %collective-permute-start = (f32[20,2048]{1,0:T(8,128)}, f32[20,2048]{1,0:T(8,128)}, u32[]{:S(2)}, u32[]{:S(2)}) collective-permute-start(f32[20,2048]{1,0:T(8,128)} %dynamic-slice_bitcast_fusion), channel_id=1, source_target_pairs={{0,1},{1,0},{2,3},{3,2},{4,5},{5,4},{6,7},{7,6},{8,9},{9,8},{10,11... | collective-permute-start | bytes 491528 | tf_op jit(solution)/shard_map/ppermute | solution.py:84
  25.4 36.9 %copy-start.13 = (s32[1024]{0:T(1024)}, s32[1024]{0:T(1024)S(1)}, u32[]{:S(2)}) copy-start(s32[1024]{0:T(1024)S(1)} %pad_clamp_fusion.2) | copy-start | bytes 12292
  36.7 12.9 %collective-permute-start.1 = (f32[10,2048]{1,0:T(8,128)S(1)}, f32[10,2048]{1,0:T(8,128)S(1)}, u32[]{:S(2)}, u32[]{:S(2)}) collective-permute-start(f32[10,2048]{1,0:T(8,128)S(1)} %dynamic-slice_bitcast_fusion.1), channel_id=1, source_target_pairs={{0,2},{1,3},{2,0},{3,1},{4,6},{5,7},{6,4},{7,5},{8,10},{9,11},{10,... | collective-permute-start | bytes 245768 | tf_op jit(solution)/shard_map/ppermute | solution.py:84
  49.7 13.3 %collective-permute-start.2 = (f32[5,2048]{1,0:T(8,128)S(1)}, f32[5,2048]{1,0:T(8,128)S(1)}, u32[]{:S(2)}, u32[]{:S(2)}) collective-permute-start(f32[5,2048]{1,0:T(8,128)S(1)} %dynamic-slice_bitcast_fusion.2), channel_id=1, source_target_pairs={{0,4},{1,5},{2,6},{3,7},{4,0},{5,1},{6,2},{7,3},{8,12},{9,13},{10,... | collective-permute-start | bytes 122888 | tf_op jit(solution)/shard_map/ppermute | solution.py:84
  56.9 6.1 %copy-start.7 = (f32[2048]{0:T(1024)S(1)}, f32[2048]{0:T(1024)}, u32[]{:S(2)}) copy-start(f32[2048]{0:T(1024)} %param.23) | copy-start | bytes 24580
  56.9 9.8 %copy-start.16 = (pred[32]{0:T(512)(128)(4,1)S(1)}, pred[32]{0:T(512)(128)(4,1)}, u32[]{:S(2)}) copy-start(pred[32]{0:T(512)(128)(4,1)} %fusion.76) | copy-start | bytes 100
  63.9 14.7 %collective-permute-start.3 = (bf16[5,2048]{1,0:T(8,128)(2,1)S(1)}, bf16[5,2048]{1,0:T(8,128)(2,1)S(1)}, u32[]{:S(2)}, u32[]{:S(2)}) collective-permute-start(bf16[5,2048]{1,0:T(8,128)(2,1)S(1)} %fusion.61), channel_id=1, source_target_pairs={{0,4},{1,5},{2,6},{3,7},{4,0},{5,1},{6,2},{7,3},{8,12},{9,13},{10,... | collective-permute-start | bytes 61448 | tf_op jit(solution)/shard_map/ppermute | solution.py:93
  70.6 8.1 %copy-start.14 = (s32[1,640]{1,0:T(1,128)S(1)}, s32[1,640]{1,0:T(1,128)}, u32[]{:S(2)}) copy-start(s32[1,640]{1,0:T(1,128)} %param.13) | copy-start | bytes 7684
  70.6 58.1 %all-to-all-start = ((bf16[32,2,128,256]{3,2,1,0:T(8,128)(2,1)}), bf16[32,2,128,256]{3,2,1,0:T(8,128)(2,1)}, u32[]{:S(2)}, u32[]{:S(2)}) async-start(bf16[32,2,128,256]{3,2,1,0:T(8,128)(2,1)} %select_select_fusion), calls=%async_computation | async-start | bytes 8388608 | tf_op jit(solution)/shard_map/all_to_all | solution.py:130
  78.5 98.6 %reduce-scatter.2.cloned.1.call-start = ((), (), s32[]{:S(2)}) async-start(), calls=%async_computation.4 | async-start | bytes 2949120 | tf_op jit(solution)/shard_map/reduce_scatter | solution.py:154
  78.6 6.0 %collective-permute-start.4 = (bf16[10,2048]{1,0:T(8,128)(2,1)S(1)}, bf16[10,2048]{1,0:T(8,128)(2,1)S(1)}, u32[]{:S(2)}, u32[]{:S(2)}) collective-permute-start(bf16[10,2048]{1,0:T(8,128)(2,1)S(1)} %maximum_select_fusion.2), channel_id=1, source_target_pairs={{0,2},{1,3},{2,0},{3,1},{4,6},{5,7},{6,4},{7,5},{8,10},{9,11},{10,... | collective-permute-start | bytes 122888 | tf_op jit(solution)/shard_map/ppermute | solution.py:93
  84.6 5.1 %collective-permute-start.5 = (bf16[20,2048]{1,0:T(8,128)(2,1)S(1)}, bf16[20,2048]{1,0:T(8,128)(2,1)S(1)}, u32[]{:S(2)}, u32[]{:S(2)}) collective-permute-start(bf16[20,2048]{1,0:T(8,128)(2,1)S(1)} %maximum_select_fusion.1), channel_id=1, source_target_pairs={{0,1},{1,0},{2,3},{3,2},{4,5},{5,4},{6,7},{7,6},{8,9},{9,8},{10,11... | collective-permute-start | bytes 245768 | tf_op jit(solution)/shard_map/ppermute | solution.py:93
  89.8 2.5 %copy-start.2 = (bf16[640,2048]{1,0:T(8,128)(2,1)S(1)}, bf16[640,2048]{1,0:T(8,128)(2,1)}, u32[]{:S(2)}) copy-start(bf16[640,2048]{1,0:T(8,128)(2,1)} %all-gather.2.cloned.1.call-done) | copy-start | bytes 7864324
  93.1 3.6 %copy-start.10 = (f32[1,256]{1,0:T(1,128)S(1)}, f32[1,256]{1,0:T(1,128)}, u32[]{:S(2)}) copy-start(f32[1,256]{1,0:T(1,128)} %copy-done.9) | copy-start | bytes 3076
  96.8 6.0 %copy-start.12 = (f32[1,256]{1,0:T(1,128)S(1)}, f32[1,256]{1,0:T(1,128)}, u32[]{:S(2)}) copy-start(f32[1,256]{1,0:T(1,128)} %copy-done.11) | copy-start | bytes 3076
  102.8 1.9 %copy-start.6 = (pred[640,640]{0,1:T(8,128)(4,1)S(1)}, pred[640,640]{0,1:T(8,128)(4,1)}, u32[]{:S(2)}) copy-start(pred[640,640]{0,1:T(8,128)(4,1)} %fusion.25) | copy-start | bytes 1228804
  104.7 2.0 %copy-start.5 = (f32[1,640,256]{1,2,0:T(8,128)S(1)}, f32[1,640,256]{1,2,0:T(8,128)}, u32[]{:S(2)}) copy-start(f32[1,640,256]{1,2,0:T(8,128)} %get-tuple-element.46) | copy-start | bytes 1966084
  138.9 5.6 %copy-start.17 = (pred[32]{0:T(512)(128)(4,1)S(1)}, pred[32]{0:T(512)(128)(4,1)}, u32[]{:S(2)}) copy-start(pred[32]{0:T(512)(128)(4,1)} %fusion.76) | copy-start | bytes 100
  142.2 34.8 %copy-start.8 = (f32[2048]{0:T(1024)S(1)}, f32[2048]{0:T(1024)}, u32[]{:S(2)}) copy-start(f32[2048]{0:T(1024)} %param.23) | copy-start | bytes 24580
  144.4 32.6 %copy-start.3 = (bf16[80,2048]{1,0:T(8,128)(2,1)S(1)}, bf16[80,2048]{1,0:T(8,128)(2,1)}, u32[]{:S(2)}) copy-start(bf16[80,2048]{1,0:T(8,128)(2,1)} %param.12) | copy-start | bytes 983044
  150.5 15.8 %all-to-all-start.1 = ((bf16[32,2,1024]{2,1,0:T(2,128)(2,1)}), bf16[32,2,1024]{2,1,0:T(2,128)(2,1)}, u32[]{:S(2)}, u32[]{:S(2)}) async-start(bf16[32,2,1024]{2,1,0:T(2,128)(2,1)} %reshape.519), calls=%async_computation.2 | async-start | bytes 262144 | tf_op jit(solution)/shard_map/all_to_all | solution.py:164
Sparse Core Ops, SparseCore 0:
  9.8 55.5 all-gather.1
  132.6 44.4 reduce-scatter.1

commit v3 on v2

--- a/solution.py
+++ b/solution.py
@@ -68,31 +68,16 @@
     return jnp.where(written[:, None, :, None], fresh[:, :, None, :], cache[picks])
 
 
-def reduce_over_tp(partial_value, rows, out_bias):
+def reduce_over_tp(pieces, rows, out_bias):
     n = lax.axis_size("tp")
-    me = lax.axis_index("tp")
     count, model = rows.shape
-    rounds = n.bit_length() - 1
-    held = partial_value.astype(jnp.bfloat16).astype(jnp.float32)
-    chunk = jnp.zeros((), jnp.int32)
-    for k in range(rounds):
-        mask = 1 << k
-        bit = (me >> k) & 1
-        halves = held.reshape(2, held.shape[0] // 2, model)
-        keep = lax.dynamic_index_in_dim(halves, bit, 0, keepdims=False)
-        give = lax.dynamic_index_in_dim(halves, 1 - bit, 0, keepdims=False)
-        got = lax.ppermute(give, "tp", [(i, i ^ mask) for i in range(n)])
-        held = keep + got
-        chunk = chunk * 2 + bit
     share = count // n
-    own_rows = lax.dynamic_slice_in_dim(rows, chunk * share, share, 0)
-    out = (own_rows.astype(jnp.float32) + held + out_bias).astype(jnp.bfloat16)
-    for k in reversed(range(rounds)):
-        mask = 1 << k
-        bit = (me >> k) & 1
-        got = lax.ppermute(out, "tp", [(i, i ^ mask) for i in range(n)])
-        out = jnp.where(bit == 0, jnp.concatenate([out, got]), jnp.concatenate([got, out]))
-    return out
+    arrived = lax.all_to_all(pieces, "tp", 0, 0, tiled=True)
+    summed = jnp.sum(arrived.astype(jnp.float32), axis=0)
+    own_rows = lax.dynamic_slice_in_dim(rows, lax.axis_index("tp") * share, share, 0)
+    own_out = (own_rows.astype(jnp.float32) + summed + out_bias).astype(jnp.bfloat16)
+    spread = jnp.broadcast_to(own_out[None], (n, share, model))
+    return lax.all_to_all(spread, "tp", 0, 0, tiled=True).reshape(count, model)
 
 
 def on_device(
@@ -128,7 +113,10 @@
         jnp.zeros((), jnp.bfloat16),
     )
     moved_cache = lax.all_to_all(send_cache, "rep", split_axis=0, concat_axis=0, tiled=True)
-    decode_out = reduce_over_tp(partial_value, decode_rows, out_bias)
+    tp_count = lax.axis_size("tp")
+    decode_pieces = partial_value.astype(jnp.bfloat16).reshape(
+        tp_count, decode_rows.shape[0] // tp_count, decode_rows.shape[1]
+    )
     normed = layer_norm(lax.all_gather(prompt_rows, "tp", axis=0, tiled=True), norm_gain, norm_bias)
     projected = jnp.einsum("rd,cde->cre", normed, qkv_weight, preferred_element_type=jnp.float32)
     total_rows = projected.shape[1]
@@ -150,13 +138,15 @@
     probs = (weights / jnp.sum(weights, axis=-1, keepdims=True)).astype(jnp.bfloat16)
     context = jnp.einsum("hqk,khe->qhe", probs, head_v, preferred_element_type=jnp.float32)
     context = context.reshape(total_rows, width).astype(jnp.bfloat16)
-    context, moved_cache, decode_out = lax.optimization_barrier((context, moved_cache, decode_out))
-    attended = lax.psum_scatter(
-        jnp.dot(context, out_weight, preferred_element_type=jnp.float32).astype(jnp.bfloat16),
-        "tp",
-        scatter_dimension=0,
-        tiled=True,
-    ).astype(jnp.float32)
+    prompt_partial = jnp.dot(context, out_weight, preferred_element_type=jnp.float32).astype(
+        jnp.bfloat16
+    )
+    prompt_partial, decode_pieces = lax.optimization_barrier((prompt_partial, decode_pieces))
+    attended = lax.psum_scatter(prompt_partial, "tp", scatter_dimension=0, tiled=True).astype(
+        jnp.float32
+    )
+    decode_pieces, moved_cache = lax.optimization_barrier((decode_pieces, moved_cache))
+    decode_out = reduce_over_tp(decode_pieces, decode_rows, out_bias)
     prompt_out = (prompt_rows.astype(jnp.float32) + attended + out_bias).astype(jnp.bfloat16)
     prompt_cache = jnp.stack([key_rows, value_rows])
     kept_out = decode_out[:staying]

time: 192 us -> 163 us (0.85)
  waiting for transfers between devices: 53.9 us -> 43.4 us
  other arithmetic: 33.5 us -> 26.2 us
  matrix products: 19.2 us -> 14.7 us
  starting transfers between devices: 32.2 us -> 28.3 us
  local copies, waits for them, and re-layouts: 37.1 us -> 33.3 us
    ppermute x6 -> x0, waiting for transfers between devices: 22.9 us -> none  [the longest x3 13.4 us: reduce_over_tp(): got = lax.ppermute(give, 'tp', [(i, i ^ mask) for i in range(n)])]
    all_to_all x0 -> x2, waiting for transfers between devices: none -> 20.3 us  [the longest x1 11.6 us: reduce_over_tp(): return lax.all_to_all(spread, 'tp', 0, 0, tiled=True).reshape(count, model)]
    ppermute x6 -> x0, starting transfers between devices: 15.2 us -> none  [the longest x3 12 us: reduce_over_tp(): got = lax.ppermute(give, 'tp', [(i, i ^ mask) for i in range(n)])]
    all_to_all x1, waiting for transfers between devices: 20.7 us -> 6.76 us  [on_device(): lax.all_to_all(send_cache, 'rep', split_axis=0, concat_axis=0, tiled=True)]
    all_gather x1, waiting for transfers between devices: 0.02 us -> 13.9 us  [on_device(): lax.all_gather(prompt_rows, 'tp', axis=0, tiled=True)]
    all_to_all x0 -> x2, starting transfers between devices: none -> 12.5 us  [the longest x1 8.47 us: reduce_over_tp(): arrived = lax.all_to_all(pieces, 'tp', 0, 0, tiled=True)]
    reduce_scatter x1, waiting for transfers between devices: 7.01 us -> 0.01 us  [on_device(): lax.psum_scatter(prompt_partial, 'tp', scatter_dimension=0, tiled=True)]
    unnamed x41 -> x37, local copies, waits for them, and re-layouts: 12.5 us -> 9.43 us
  transfers between devices with their start and end apart: 10 -> 6, of which waited for: 7 -> 5; matrix products, arithmetic and copies ran while one was open for 42% -> 42% of each run, Pallas kernels for 0% -> 0%
where the time goes in v3:
time: 163 us; the launch traced here: 160 us
  waiting for transfers between devices  43.4 us (27%)
  local copies, waits for them, and re-layouts  33.3 us (20%)
  starting transfers between devices  28.3 us (17%)
  other arithmetic  26.2 us (16%)
  matrix products  14.7 us (9%)
  between operations  14.4 us (9%)
    all_gather x1, waiting for transfers between devices, on_device(): lax.all_gather(prompt_rows, 'tp', axis=0, tiled=True)  13.9 us
    all_to_all x1, waiting for transfers between devices, reduce_over_tp(): return lax.all_to_all(spread, 'tp', 0, 0, tiled=True).reshape(count, model)  11.6 us
    gather x2, local copies, waits for them, and re-layouts, updated_rows(): cache[picks]  10.4 us
    unnamed x37, local copies, waits for them, and re-layouts  9.43 us
    all_to_all x1, waiting for transfers between devices, reduce_over_tp(): arrived = lax.all_to_all(pieces, 'tp', 0, 0, tiled=True)  8.64 us
    all_to_all x1, starting transfers between devices, reduce_over_tp(): arrived = lax.all_to_all(pieces, 'tp', 0, 0, tiled=True)  8.47 us
    all_to_all x1, starting transfers between devices, on_device(): lax.all_to_all(send_rows, 'rep', split_axis=0, concat_axis=0, tiled=True)  7.99 us
    all_to_all x1, starting transfers between devices, on_device(): lax.all_to_all(send_cache, 'rep', split_axis=0, concat_axis=0, tiled=True)  7.68 us
  transfers between devices with their start and end apart: 6, of which 5 were waited for; matrix products, arithmetic and copies ran while one was open for 42% of the time, Pallas kernels for 0%

profile of v3, /device:TPU:2, one launch (start us, length us, event | category | flops | bytes accessed | tf_op | source)
XLA Modules:
  0.0 160.4 jit_solution(1694001255088564538)
XLA Ops:
  7.2 0.7 all-gather.2.cloned.1.call-update
  7.9 1.2 convert_reduce_fusion.2
  9.2 1.1 fusion.44
  10.3 0.8 fusion.80
  11.1 1.6 %convolution_bitcast_fusion = f32[3,40,256]{2,1,0:T(8,128)S(1)} fusion(bf16[3,2048,256]{2,1,0:T(8,128)(2,1)S(1)} %copy-done, bf16[40,2048]{1,0:T(8,128)(2,1)} %param.14, f32[2048]{0:T(1024)} %param.19, f32[2048]{0:T(1024)} %param.18, f32[40]{0:T(128)S(1)} %add_rsqrt_fusion.1, f32[40]{0:T(128)S(1)} %broadcast_multiply_fusion.1), kind=kOutput, calls=%fused_computation.45 | convolution fusion | flops 126320640 | bytes 3449152 | tf_op jit(solution)/shard_map/rd,cde->cre/dot_general | solution.py:27
  12.9 0.1 select_reduce_fusion
  13.0 0.6 gather_fusion.2
  13.6 5.3 %gather_fusion.3 = bf16[32,2,128,256]{3,2,1,0:T(8,128)(2,1)} fusion(bf16[40,2,128,256]{3,2,1,0:T(8,128)(2,1)} %param.17, s32[1024]{0:T(1024)S(1)} %pad_clamp_fusion.1), kind=kCustom, calls=%fused_computation.3 | custom fusion | bytes 8388736 | tf_op jit(solution)/shard_map/gather | solution.py:68
  18.9 0.7 gather_fusion.1
  19.6 0.1 fusion.72
  19.8 4.0 %select_select_fusion = bf16[32,2,128,256]{3,2,1,0:T(8,128)(2,1)} fusion(bf16[32,2,128,256]{3,2,1,0:T(8,128)(2,1)} %gather_fusion.3, pred[32]{0:T(512)(128)(4,1)S(1)} %fusion.72, pred[32,128]{1,0:T(8,128)(4,1)S(1)} %iota_compare_fusion.2, bf16[32,2,256]{2,1,0:T(2,128)(2,1)S(1)} %gather_fusion.2), kind=kLoop, calls=%fused_computation.17 | loop fusion | flops 4194304 | bytes 8425504 | tf_op jit(solution)/shard_map/jit(_where)/select_n | solution.py:110
  23.8 7.7 %all-to-all-start = ((bf16[32,2,128,256]{3,2,1,0:T(8,128)(2,1)}), bf16[32,2,128,256]{3,2,1,0:T(8,128)(2,1)}, u32[]{:S(2)}, u32[]{:S(2)}) async-start(bf16[32,2,128,256]{3,2,1,0:T(8,128)(2,1)} %select_select_fusion), calls=%async_computation.1 | async-start | bytes 8388608 | tf_op jit(solution)/shard_map/all_to_all | solution.py:115
  31.6 0.1 multiply_reduce_fusion
  31.7 0.1 copy.77
  31.9 2.6 %fusion.82 = (f32[40,2]{1,0:T(8,128)S(1)}, f32[40,2,128]{2,1,0:T(2,128)S(1)}) fusion(bf16[40,2,128,256]{3,2,1,0:T(8,128)(2,1)} %param.17, pred[2,256]{1,0:T(4,128)(4,1)S(1)} %iota_compare_fusion.5, bf16[40,256]{1,0:T(8,128)(2,1)S(1)} %fusion.63, pred[40,128]{1,0:T(8,128)(4,1)S(1)} %iota_compare_fusion.1), kind=kOutput, calls=%fused_computation.138 | convolution fusion | flops 5294000 | bytes 2688832 | tf_op jit(solution)/shard_map/rhc,rlc->rhl/dot_general | solution.py:36
  34.6 0.1 copy.79
  34.7 0.2 fusion.64
  35.0 0.1 copy.81
  35.2 0.7 gather_fusion
  36.0 2.4 %fusion.33 = f32[40,256]{1,0:T(8,128)S(1)} fusion(bf16[40,2,128,256]{3,2,1,0:T(8,128)(2,1)} %param.17, pred[2,256]{1,0:T(4,128)(4,1)} %copy-done.14, f32[40,2,128]{2,1,0:T(2,128)} %copy-done.7, f32[40,2]{1,0:T(8,128)S(1)} %copy.81, f32[40,2]{1,0:T(8,128)S(1)} %copy.79), kind=kOutput, calls=%fused_computation.47 | convolution fusion | flops 5304320 | bytes 2705024 | tf_op jit(solution)/shard_map/rhl,rlc->rhc/dot_general | solution.py:56
  38.4 0.3 convolution_convert_fusion.1
  38.7 0.8 reshape.440
  39.5 0.7 reduce
  40.2 1.1 fusion.24
  41.2 13.9 %all-gather.2.cloned.1.call-done = bf16[640,2048]{1,0:T(8,128)(2,1)} async-done(((bf16[80,2048]{1,0:T(8,128)(2,1)}), bf16[640,2048]{1,0:T(8,128)(2,1)}) %all-gather.2.cloned.1.call-update) | async-done | bytes 2621456 | tf_op jit(solution)/shard_map/all_gather | solution.py:120
  55.1 2.3 %convert_reduce_fusion = f32[640]{0:T(1024)S(1)} fusion(bf16[640,2048]{1,0:T(8,128)(2,1)} %all-gather.2.cloned.1.call-done), kind=kLoop, calls=%fused_computation.10 | loop fusion | flops 2620800 | bytes 2624000 | tf_op jit(solution)/shard_map/reduce_sum | solution.py:15
  57.4 0.2 copy-done.2
  57.6 0.8 fusion.3
  58.5 2.9 %fusion.26 = f32[3,640,256]{1,2,0:T(8,128)S(1)} fusion(bf16[3,2048,256]{2,1,0:T(8,128)(2,1)S(1)} %copy-done, bf16[640,2048]{1,0:T(8,128)(2,1)S(1)} %copy-done.2, f32[2048]{0:T(1024)S(1)} %copy-done.10, f32[2048]{0:T(1024)S(1)} %copy-done.11, f32[640]{0:T(1024)S(1)} %add_rsqrt_fusion, f32[640]{0:T(1024)S(1)} %broadcast_multiply_fusion), kind=kOutput, calls=%fused_computation.43 | convolution fusion | flops 2021130240 | bytes 7754752 | tf_op jit(solution)/shard_map/rd,cde->cre/dot_general | solution.py:121
  61.4 1.7 %add_convert_fusion.1 = (bf16[1,640,256]{1,2,0:T(8,128)(2,1)}, bf16[1,640,256]{1,2,0:T(8,128)(2,1)}, f32[1,640,256]{1,2,0:T(8,128)}, f32[1,640,256]{1,2,0:T(8,128)}, f32[1,640,256]{1,2,0:T(8,128)}) fusion(f32[256]{0:T(256)S(1)} %bitcast.95, f32[3,640,256]{1,2,0:T(8,128)S(1)} %fusion.26, f32[256]{0:T(256)S(1)} %bitcast.99), kind=kLoop, calls=%fused_computation.52 | loop fusion | flops 655360 | bytes 4589568 | tf_op jit(solution)/shard_map/convert_element_type | solution.py:124
  63.0 2.2 %copy.73 = f32[640,2,128]{2,0,1:T(8,128)} copy(f32[640,2,128]{0,2,1:T(8,128)} %bitcast.89) | data formatting | bytes 1310720 | tf_op jit(solution)/shard_map/squeeze | solution.py:123
  65.2 2.2 %copy.74 = f32[640,2,128]{2,0,1:T(8,128)} copy(f32[640,2,128]{0,2,1:T(8,128)} %bitcast.88) | data formatting | bytes 1310720 | tf_op jit(solution)/shard_map/squeeze | solution.py:124
  67.4 1.9 %fusion.48 = f32[2,640,640]{1,2,0:T(8,128)S(1)} fusion(f32[640,2,128]{2,0,1:T(8,128)} %copy.73, f32[640,2,128]{2,0,1:T(8,128)} %copy.74, f32[2,128]{1,0:T(2,128)S(1)} %bitcast.96, f32[2,128]{1,0:T(2,128)S(1)} %bitcast.103), kind=kOutput, calls=%fused_computation.66 | convolution fusion | flops 210370560 | bytes 4589568 | tf_op jit(solution)/shard_map/qhe,khe->hqk/dot_general | solution.py:129
  69.3 2.0 %fusion.81 = (f32[2,640]{1,0:T(2,128)S(1)}, f32[2,640,640]{1,2,0:T(8,128)S(1)}) fusion(f32[2,640,640]{1,2,0:T(8,128)S(1)} %fusion.48, pred[640,640]{0,1:T(8,128)(4,1)S(1)} %copy-done.6), kind=kOutput, calls=%fused_computation.137 | output fusion | flops 4915839 | bytes 6968320 | tf_op jit(solution)/shard_map/sub | solution.py:137
  71.3 0.5 fusion.29
  71.9 0.7 copy-done.4
  72.5 2.4 %convolution_convert_fusion = bf16[640,2048]{1,0:T(8,128)(2,1)} fusion(bf16[640,256]{0,1:T(8,128)(2,1)S(1)} %bitcast.90, bf16[256,2048]{1,0:T(8,128)(2,1)S(1)} %copy-done.4), kind=kOutput, calls=%fused_computation.21 | convolution fusion | flops 672399360 | bytes 3997696 | tf_op jit(solution)/shard_map/dot_general | solution.py:141
  75.0 6.8 %all-to-all-done = bf16[32,2,128,256]{3,2,1,0:T(8,128)(2,1)} async-done(((bf16[32,2,128,256]{3,2,1,0:T(8,128)(2,1)}), bf16[32,2,128,256]{3,2,1,0:T(8,128)(2,1)}, u32[]{:S(2)}, u32[]{:S(2)}) %all-to-all-start) | async-done | bytes 4194336 | tf_op jit(solution)/shard_map/all_to_all | solution.py:115
  81.7 8.5 %all-to-all-start.1 = ((bf16[8,5,2048]{2,1,0:T(8,128)(2,1)}), bf16[8,5,2048]{2,1,0:T(8,128)(2,1)S(1)}, u32[]{:S(2)}, u32[]{:S(2)}) async-start(bf16[8,5,2048]{2,1,0:T(8,128)(2,1)} %reshape.440), calls=%async_computation.2 | async-start | bytes 524288 | tf_op jit(solution)/shard_map/all_to_all | solution.py:75
  90.2 0.6 gather_fusion.5
  90.9 5.1 %gather_fusion.6 = bf16[24,2,128,256]{3,2,1,0:T(8,128)(2,1)} fusion(bf16[40,2,128,256]{3,2,1,0:T(8,128)(2,1)} %param.17, s32[1024]{0:T(1024)S(1)} %pad_clamp_fusion), kind=kCustom, calls=%fused_computation.6 | custom fusion | bytes 6291552 | tf_op jit(solution)/shard_map/gather | solution.py:68
  95.9 0.7 gather_fusion.4
  96.6 0.1 iota_compare_fusion.3
  96.7 8.6 %all-to-all-done.1 = bf16[8,5,2048]{2,1,0:T(8,128)(2,1)S(1)} async-done(((bf16[8,5,2048]{2,1,0:T(8,128)(2,1)}), bf16[8,5,2048]{2,1,0:T(8,128)(2,1)S(1)}, u32[]{:S(2)}, u32[]{:S(2)}) %all-to-all-start.1) | async-done | bytes 163872 | tf_op jit(solution)/shard_map/all_to_all | solution.py:75
  105.4 0.9 add_convert_fusion.9
  106.3 0.7 broadcast_in_dim.189
  107.0 4.0 %all-to-all-start.2 = ((bf16[8,5,2048]{2,1,0:T(8,128)(2,1)}), bf16[8,5,2048]{2,1,0:T(8,128)(2,1)}, u32[]{:S(2)}, u32[]{:S(2)}) async-start(bf16[8,5,2048]{2,1,0:T(8,128)(2,1)} %broadcast_in_dim.189), calls=%async_computation.3 | async-start | bytes 524288 | tf_op jit(solution)/shard_map/all_to_all | solution.py:80
  111.0 3.4 %broadcast_select_fusion = bf16[24,2,128,256]{3,2,1,0:T(8,128)(2,1)} fusion(bf16[24,2,128,256]{3,2,1,0:T(8,128)(2,1)} %gather_fusion.6, pred[24,128]{1,0:T(8,128)(4,1)S(1)} %iota_compare_fusion.3, bf16[24,2,256]{2,1,0:T(2,128)(2,1)S(1)} %gather_fusion.5), kind=kLoop, calls=%fused_computation.22 | loop fusion | flops 1572864 | bytes 6319104 | tf_op jit(solution)/shard_map/jit(_where)/select_n | solution.py:68
  114.4 11.6 %all-to-all-done.2 = bf16[8,5,2048]{2,1,0:T(8,128)(2,1)} async-done(((bf16[8,5,2048]{2,1,0:T(8,128)(2,1)}), bf16[8,5,2048]{2,1,0:T(8,128)(2,1)}, u32[]{:S(2)}, u32[]{:S(2)}) %all-to-all-start.2) | async-done | bytes 163872 | tf_op jit(solution)/shard_map/all_to_all | solution.py:80
  126.0 1.0 reshape.441
  127.1 0.8 gather_fusion.7
  127.9 0.7 bitcast_select_fusion
  128.6 0.5 broadcast.367
  129.1 1.6 reduce.1
  130.7 0.7 reshape.509
  131.4 8.0 %all-to-all-start.3 = ((bf16[32,2,1024]{2,1,0:T(2,128)(2,1)}), bf16[32,2,1024]{2,1,0:T(2,128)(2,1)S(1)}, u32[]{:S(2)}, u32[]{:S(2)}) async-start(bf16[32,2,1024]{2,1,0:T(2,128)(2,1)} %reshape.509), calls=%async_computation.4 | async-start | bytes 262144 | tf_op jit(solution)/shard_map/all_to_all | solution.py:154
  139.4 2.0 %pad_maximum_fusion = bf16[2,640,256]{1,2,0:T(8,128)(2,1)} fusion(bf16[1,640,256]{1,2,0:T(8,128)(2,1)} %get-tuple-element.45, bf16[1,640,256]{1,2,0:T(8,128)(2,1)} %get-tuple-element.44), kind=kLoop, calls=%fused_computation.50 | loop fusion | flops 327680 | bytes 1310720 | tf_op jit(solution)/shard_map/stack | solution.py:151
  141.4 2.2 %copy.87 = bf16[2,640,256]{2,1,0:T(8,128)(2,1)} copy(bf16[2,640,256]{1,2,0:T(8,128)(2,1)} %pad_maximum_fusion) | data formatting | bytes 1310720
  143.6 0.6 slice.73
  144.2 1.9 %all-to-all-done.3 = bf16[32,2,1024]{2,1,0:T(2,128)(2,1)S(1)} async-done(((bf16[32,2,1024]{2,1,0:T(2,128)(2,1)}), bf16[32,2,1024]{2,1,0:T(2,128)(2,1)S(1)}, u32[]{:S(2)}, u32[]{:S(2)}) %all-to-all-start.3) | async-done | bytes 131104 | tf_op jit(solution)/shard_map/all_to_all | solution.py:154
  146.1 0.1 reshape.510
  146.2 0.7 copy.94
  146.9 1.9 %add_convert_fusion.2 = bf16[80,2048]{1,0:T(8,128)(2,1)} fusion(bf16[80,2048]{1,0:T(8,128)(2,1)} %reduce-scatter.2.cloned.1.call-done, bf16[80,2048]{1,0:T(8,128)(2,1)} %param.12, f32[2048]{0:T(1024)S(1)} %copy-done.8), kind=kLoop, calls=%fused_computation.53 | loop fusion | flops 819200 | bytes 991232 | tf_op jit(solution)/shard_map/convert_element_type | solution.py:150
  148.8 4.7 %copy.97 = bf16[32,2,128,256]{3,2,1,0:T(8,128)(2,1)} copy(bf16[32,2,128,256]{3,2,1,0:T(8,128)(2,1)} %all-to-all-done) | data formatting | bytes 8388608
  (61 shorter events, 0.8 us)
Async XLA Ops:
  7.2 4.0 %copy-start = (bf16[3,2048,256]{2,1,0:T(8,128)(2,1)S(1)}, bf16[3,2048,256]{2,1,0:T(8,128)(2,1)}, u32[]{:S(2)}) copy-start(bf16[3,2048,256]{2,1,0:T(8,128)(2,1)} %param.20) | copy-start | bytes 9437188
  7.2 5.7 %copy-start.15 = (s32[16,1]{0,1:T(1,128)S(1)}, s32[16,1]{0,1:T(1,128)}, u32[]{:S(2)}) copy-start(s32[16,1]{0,1:T(1,128)} %param.16) | copy-start | bytes 196
  7.2 47.9 %all-gather.2.cloned.1.call-start = ((), (), s32[]{:S(2)}) async-start(), calls=%async_computation.5 | async-start | bytes 2949120 | tf_op jit(solution)/shard_map/all_gather | solution.py:120
  13.0 6.0 %copy-start.9 = (s32[1024]{0:T(1024)}, s32[1024]{0:T(1024)S(1)}, u32[]{:S(2)}) copy-start(s32[1024]{0:T(1024)S(1)} %pad_clamp_fusion.1) | copy-start | bytes 12292
  13.6 5.3 %copy-start.1 = (s32[40]{0:T(128)S(1)}, s32[40]{0:T(128)}, u32[]{:S(2)}) copy-start(s32[40]{0:T(128)} %param.15) | copy-start | bytes 484
  19.7 4.1 %copy-start.12 = (pred[32]{0:T(512)(128)(4,1)}, pred[32]{0:T(512)(128)(4,1)S(1)}, u32[]{:S(2)}) copy-start(pred[32]{0:T(512)(128)(4,1)S(1)} %fusion.72) | copy-start | bytes 100
  23.8 57.9 %all-to-all-start = ((bf16[32,2,128,256]{3,2,1,0:T(8,128)(2,1)}), bf16[32,2,128,256]{3,2,1,0:T(8,128)(2,1)}, u32[]{:S(2)}, u32[]{:S(2)}) async-start(bf16[32,2,128,256]{3,2,1,0:T(8,128)(2,1)} %select_select_fusion), calls=%async_computation.1 | async-start | bytes 8388608 | tf_op jit(solution)/shard_map/all_to_all | solution.py:115
  31.5 115.4 %reduce-scatter.2.cloned.1.call-start = ((), (), s32[]{:S(2)}) async-start(), calls=%async_computation.6 | async-start | bytes 2949120 | tf_op jit(solution)/shard_map/reduce_scatter | solution.py:145
  31.8 3.4 %copy-start.14 = (pred[2,256]{1,0:T(4,128)(4,1)}, pred[2,256]{1,0:T(4,128)(4,1)S(1)}, u32[]{:S(2)}) copy-start(pred[2,256]{1,0:T(4,128)(4,1)S(1)} %iota_compare_fusion.5) | copy-start | bytes 1540
  34.6 0.6 copy-start.7
  36.0 2.4 %copy-start.3 = (bf16[256,2048]{1,0:T(8,128)(2,1)S(1)}, bf16[256,2048]{1,0:T(8,128)(2,1)}, u32[]{:S(2)}) copy-start(bf16[256,2048]{1,0:T(8,128)(2,1)} %param.22) | copy-start | bytes 3145732
  38.7 19.7 %copy-start.10 = (f32[2048]{0:T(1024)S(1)}, f32[2048]{0:T(1024)}, u32[]{:S(2)}) copy-start(f32[2048]{0:T(1024)} %param.19) | copy-start | bytes 24580
  38.7 19.7 %copy-start.11 = (f32[2048]{0:T(1024)S(1)}, f32[2048]{0:T(1024)}, u32[]{:S(2)}) copy-start(f32[2048]{0:T(1024)} %param.18) | copy-start | bytes 24580
  55.1 2.5 %copy-start.2 = (bf16[640,2048]{1,0:T(8,128)(2,1)S(1)}, bf16[640,2048]{1,0:T(8,128)(2,1)}, u32[]{:S(2)}) copy-start(bf16[640,2048]{1,0:T(8,128)(2,1)} %all-gather.2.cloned.1.call-done) | copy-start | bytes 7864324
  67.4 1.9 %copy-start.6 = (pred[640,640]{0,1:T(8,128)(4,1)S(1)}, pred[640,640]{0,1:T(8,128)(4,1)}, u32[]{:S(2)}) copy-start(pred[640,640]{0,1:T(8,128)(4,1)} %fusion.24) | copy-start | bytes 1228804
  69.3 2.0 %copy-start.5 = (f32[1,640,256]{1,2,0:T(8,128)S(1)}, f32[1,640,256]{1,2,0:T(8,128)}, u32[]{:S(2)}) copy-start(f32[1,640,256]{1,2,0:T(8,128)} %get-tuple-element.48) | copy-start | bytes 1966084
  71.3 1.2 copy-start.4
  81.7 23.6 %all-to-all-start.1 = ((bf16[8,5,2048]{2,1,0:T(8,128)(2,1)}), bf16[8,5,2048]{2,1,0:T(8,128)(2,1)S(1)}, u32[]{:S(2)}, u32[]{:S(2)}) async-start(bf16[8,5,2048]{2,1,0:T(8,128)(2,1)} %reshape.440), calls=%async_computation.2 | async-start | bytes 524288 | tf_op jit(solution)/shard_map/all_to_all | solution.py:75
  90.8 14.5 %copy-start.8 = (f32[2048]{0:T(1024)S(1)}, f32[2048]{0:T(1024)}, u32[]{:S(2)}) copy-start(f32[2048]{0:T(1024)} %param.23) | copy-start | bytes 24580
  107.0 19.1 %all-to-all-start.2 = ((bf16[8,5,2048]{2,1,0:T(8,128)(2,1)}), bf16[8,5,2048]{2,1,0:T(8,128)(2,1)}, u32[]{:S(2)}, u32[]{:S(2)}) async-start(bf16[8,5,2048]{2,1,0:T(8,128)(2,1)} %broadcast_in_dim.189), calls=%async_computation.3 | async-start | bytes 524288 | tf_op jit(solution)/shard_map/all_to_all | solution.py:80
  111.0 16.8 %copy-start.13 = (pred[32]{0:T(512)(128)(4,1)S(1)}, pred[32]{0:T(512)(128)(4,1)}, u32[]{:S(2)}) copy-start(pred[32]{0:T(512)(128)(4,1)} %copy-done.12) | copy-start | bytes 100
  131.4 14.6 %all-to-all-start.3 = ((bf16[32,2,1024]{2,1,0:T(2,128)(2,1)}), bf16[32,2,1024]{2,1,0:T(2,128)(2,1)S(1)}, u32[]{:S(2)}, u32[]{:S(2)}) async-start(bf16[32,2,1024]{2,1,0:T(2,128)(2,1)} %reshape.509), calls=%async_computation.4 | async-start | bytes 262144 | tf_op jit(solution)/shard_map/all_to_all | solution.py:154
Sparse Core Ops, SparseCore 0:
  9.8 45.2 all-gather.1
  75.1 51.9 reduce-scatter.1

commit v4 on v3

--- a/solution.py
+++ b/solution.py
@@ -68,16 +68,27 @@
     return jnp.where(written[:, None, :, None], fresh[:, :, None, :], cache[picks])
 
 
-def reduce_over_tp(pieces, rows, out_bias):
+def scatter_over_tp(pieces, rows, out_bias):
     n = lax.axis_size("tp")
-    count, model = rows.shape
-    share = count // n
-    arrived = lax.all_to_all(pieces, "tp", 0, 0, tiled=True)
-    summed = jnp.sum(arrived.astype(jnp.float32), axis=0)
-    own_rows = lax.dynamic_slice_in_dim(rows, lax.axis_index("tp") * share, share, 0)
-    own_out = (own_rows.astype(jnp.float32) + summed + out_bias).astype(jnp.bfloat16)
-    spread = jnp.broadcast_to(own_out[None], (n, share, model))
-    return lax.all_to_all(spread, "tp", 0, 0, tiled=True).reshape(count, model)
+    me = lax.axis_index("tp")
+    share = pieces.shape[1]
+    rolled = jnp.take(pieces, (me + jnp.arange(n)) % n, axis=0)
+    total = rolled[0].astype(jnp.float32)
+    for shift in range(1, n):
+        got = lax.ppermute(rolled[shift], "tp", [(i, (i + shift) % n) for i in range(n)])
+        total = total + got.astype(jnp.float32)
+    own_rows = lax.dynamic_slice_in_dim(rows, me * share, share, 0)
+    return (own_rows.astype(jnp.float32) + total + out_bias).astype(jnp.bfloat16)
+
+
+def gather_over_tp(own_out):
+    n = lax.axis_size("tp")
+    me = lax.axis_index("tp")
+    held = [own_out]
+    for shift in range(1, n):
+        held.append(lax.ppermute(own_out, "tp", [(i, (i + shift) % n) for i in range(n)]))
+    stacked = jnp.stack(held)
+    return jnp.take(stacked, (me - jnp.arange(n)) % n, axis=0).reshape(-1, own_out.shape[1])
 
 
 def on_device(
@@ -117,7 +128,8 @@
     decode_pieces = partial_value.astype(jnp.bfloat16).reshape(
         tp_count, decode_rows.shape[0] // tp_count, decode_rows.shape[1]
     )
-    normed = layer_norm(lax.all_gather(prompt_rows, "tp", axis=0, tiled=True), norm_gain, norm_bias)
+    own_out = scatter_over_tp(decode_pieces, decode_rows, out_bias)
+    normed = lax.all_gather(layer_norm(prompt_rows, norm_gain, norm_bias), "tp", axis=0, tiled=True)
     projected = jnp.einsum("rd,cde->cre", normed, qkv_weight, preferred_element_type=jnp.float32)
     total_rows = projected.shape[1]
     queries = (projected[0] + qkv_bias[0]).astype(jnp.bfloat16)
@@ -141,16 +153,18 @@
     prompt_partial = jnp.dot(context, out_weight, preferred_element_type=jnp.float32).astype(
         jnp.bfloat16
     )
-    prompt_partial, decode_pieces = lax.optimization_barrier((prompt_partial, decode_pieces))
+    prompt_partial, own_out, key_rows, value_rows = lax.optimization_barrier(
+        (prompt_partial, own_out, key_rows, value_rows)
+    )
     attended = lax.psum_scatter(prompt_partial, "tp", scatter_dimension=0, tiled=True).astype(
         jnp.float32
     )
-    decode_pieces, moved_cache = lax.optimization_barrier((decode_pieces, moved_cache))
-    decode_out = reduce_over_tp(decode_pieces, decode_rows, out_bias)
+    decode_out = gather_over_tp(own_out)
     prompt_out = (prompt_rows.astype(jnp.float32) + attended + out_bias).astype(jnp.bfloat16)
     prompt_cache = jnp.stack([key_rows, value_rows])
     kept_out = decode_out[:staying]
     send_rows = jnp.where(has[:, None], decode_out[picks], jnp.zeros((), jnp.bfloat16))
+    send_rows, moved_cache = lax.optimization_barrier((send_rows, moved_cache))
     moved_out = lax.all_to_all(send_rows, "rep", split_axis=0, concat_axis=0, tiled=True)
     return (prompt_out, prompt_cache, kept_out, kept_cache, moved_out, moved_cache)
 

time: 163 us -> 159 us (0.975)
  waiting for transfers between devices: 43.4 us -> 4.02 us
  starting transfers between devices: 28.3 us -> 46.4 us
  local copies, waits for them, and re-layouts: 33.3 us -> 43.1 us
  other arithmetic: 26.2 us -> 31.6 us
    ppermute x0 -> x14, starting transfers between devices: none -> 31.1 us  [the longest x7 18.5 us: scatter_over_tp(): lax.ppermute(rolled[shift], 'tp', [(i, (i + shift) % n) for i in range(n)])]
    all_to_all x2 -> x0, waiting for transfers between devices: 20.3 us -> none  [the longest x1 11.6 us: reduce_over_tp(): return lax.all_to_all(spread, 'tp', 0, 0, tiled=True).reshape(count, model)]
    all_gather x1, waiting for transfers between devices: 13.9 us -> 0.02 us  [on_device(): lax.all_gather(layer_norm(prompt_rows, norm_gain, norm_bias), 'tp', axis=...]
    all_to_all x2 -> x0, starting transfers between devices: 12.5 us -> none  [the longest x1 8.47 us: reduce_over_tp(): arrived = lax.all_to_all(pieces, 'tp', 0, 0, tiled=True)]
    all_to_all x1, waiting for transfers between devices: 6.76 us -> 0.01 us  [on_device(): lax.all_to_all(send_cache, 'rep', split_axis=0, concat_axis=0, tiled=True)]
    unnamed x37 -> x46, local copies, waits for them, and re-layouts: 9.43 us -> 14.2 us
    gather x0 -> x2, local copies, waits for them, and re-layouts: none -> 3.15 us  [the longest x1 1.64 us: gather_over_tp(): jnp.take(stacked, (me - jnp.arange(n)) % n, axis=0)]
    ppermute x0 -> x14, waiting for transfers between devices: none -> 2.11 us  [the longest x7 2.09 us: gather_over_tp(): lax.ppermute(own_out, 'tp', [(i, (i + shift) % n) for i in range(n)])]
  transfers between devices with their start and end apart: 6 -> 18, of which waited for: 5 -> 3; matrix products, arithmetic and copies ran while one was open for 42% -> 50% of each run, Pallas kernels for 0% -> 0%
where the time goes in v4:
time: 159 us; the launch traced here: 156 us
  starting transfers between devices  46.4 us (29%)
  local copies, waits for them, and re-layouts  43.1 us (27%)
  other arithmetic  31.6 us (20%)
  matrix products  16.1 us (10%)
  between operations  14.6 us (9%)
  waiting for transfers between devices  4.02 us (3%)
    ppermute x7, starting transfers between devices, scatter_over_tp(): lax.ppermute(rolled[shift], 'tp', [(i, (i + shift) % n) for i in range(n)])  18.5 us
    unnamed x46, local copies, waits for them, and re-layouts  14.2 us
    ppermute x7, starting transfers between devices, gather_over_tp(): lax.ppermute(own_out, 'tp', [(i, (i + shift) % n) for i in range(n)])  12.6 us
    gather x2, local copies, waits for them, and re-layouts, updated_rows(): cache[picks]  10.5 us
    all_to_all x1, starting transfers between devices, on_device(): lax.all_to_all(send_cache, 'rep', split_axis=0, concat_axis=0, tiled=True)  7.8 us
    all_to_all x1, starting transfers between devices, on_device(): lax.all_to_all(send_rows, 'rep', split_axis=0, concat_axis=0, tiled=True)  7.37 us
    dot_general x1, matrix products, on_device(): jnp.einsum('rd,cde->cre', normed, qkv_weight, preferred_element_type=jnp....  4.38 us
    sub x1, other arithmetic, on_device(): weights = jnp.exp(scores - highest)  4.07 us
  transfers between devices with their start and end apart: 18, of which 3 were waited for; matrix products, arithmetic and copies ran while one was open for 50% of the time, Pallas kernels for 0%

profile of v4, /device:TPU:2, one launch (start us, length us, event | category | flops | bytes accessed | tf_op | source)
XLA Modules:
  0.0 155.7 jit_solution(2795601017360615467)
XLA Ops:
  7.2 1.3 convert_reduce_fusion
  8.5 1.2 fusion.33
  9.8 2.0 %fusion.36 = bf16[80,2048]{1,0:T(8,128)(2,1)} fusion(bf16[80,2048]{1,0:T(8,128)(2,1)} %param.14, f32[2048]{0:T(1024)} %param.21, f32[2048]{0:T(1024)} %param.20, f32[80]{0:T(128)S(1)} %add_rsqrt_fusion.1, f32[80]{0:T(128)S(1)} %broadcast_multiply_fusion.1), kind=kLoop, calls=%fused_computation.48 | loop fusion | flops 983040 | bytes 672384 | tf_op jit(solution)/shard_map/convert_element_type | solution.py:18
  11.8 1.0 convert_reduce_fusion.1
  12.8 1.1 fusion.43
  14.0 1.6 %convolution_bitcast_fusion = f32[3,40,256]{2,1,0:T(8,128)S(1)} fusion(bf16[3,2048,256]{2,1,0:T(8,128)(2,1)S(1)} %copy-done, bf16[40,2048]{1,0:T(8,128)(2,1)} %param.16, f32[2048]{0:T(1024)} %param.21, f32[2048]{0:T(1024)} %param.20, f32[40]{0:T(128)S(1)} %add_rsqrt_fusion, f32[40]{0:T(128)S(1)} %broadcast_multiply_fusion), kind=kOutput, calls=%fused_computation.35 | convolution fusion | flops 126320640 | bytes 3449152 | tf_op jit(solution)/shard_map/rd,cde->cre/dot_general | solution.py:27
  16.0 2.6 %fusion.93 = (f32[40,2]{1,0:T(8,128)S(1)}, f32[40,2,128]{2,1,0:T(2,128)S(1)}) fusion(bf16[40,2,128,256]{3,2,1,0:T(8,128)(2,1)} %param.19, pred[2,256]{1,0:T(4,128)(4,1)S(1)} %iota_compare_fusion.5, bf16[40,256]{1,0:T(8,128)(2,1)S(1)} %fusion.71, pred[40,128]{1,0:T(8,128)(4,1)S(1)} %iota_compare_fusion.1), kind=kOutput, calls=%fused_computation.181 | convolution fusion | flops 5294000 | bytes 2688832 | tf_op jit(solution)/shard_map/rhc,rlc->rhl/dot_general | solution.py:36
  19.1 0.7 copy.81
  19.9 0.7 gather_fusion
  20.7 2.4 %fusion.22 = f32[40,256]{1,0:T(8,128)S(1)} fusion(bf16[40,2,128,256]{3,2,1,0:T(8,128)(2,1)} %param.19, pred[2,256]{1,0:T(4,128)(4,1)S(1)} %iota_compare_fusion.5, f32[40,2,128]{2,1,0:T(2,128)S(1)} %get-tuple-element.73, f32[40,2]{1,0:T(8,128)} %copy.81, f32[40,2]{1,0:T(8,128)S(1)} %copy.79), kind=kOutput, calls=%fused_computation.37 | convolution fusion | flops 5304320 | bytes 2724672 | tf_op jit(solution)/shard_map/rhl,rlc->rhc/dot_general | solution.py:56
  23.4 0.8 reshape.410
  24.2 1.5 gather_fusion.8
  25.8 0.7 copy-done.4
  26.5 2.0 %collective-permute-start = (bf16[5,2048]{1,0:T(8,128)(2,1)S(1)}, bf16[5,2048]{1,0:T(8,128)(2,1)S(1)}, u32[]{:S(2)}, u32[]{:S(2)}) collective-permute-start(bf16[5,2048]{1,0:T(8,128)(2,1)S(1)} %get-tuple-element.54), channel_id=1, source_target_pairs={{0,1},{1,2},{2,3},{3,4},{4,5},{5,6},{6,7},{7,0},{8,9},{9,10},{10,1... | collective-permute-start | bytes 61448 | tf_op jit(solution)/shard_map/ppermute | solution.py:78
  28.5 3.3 %collective-permute-start.1 = (bf16[5,2048]{1,0:T(8,128)(2,1)S(1)}, bf16[5,2048]{1,0:T(8,128)(2,1)}, u32[]{:S(2)}, u32[]{:S(2)}) collective-permute-start(bf16[5,2048]{1,0:T(8,128)(2,1)S(1)} %get-tuple-element.60), channel_id=1, source_target_pairs={{0,2},{1,3},{2,4},{3,5},{4,6},{5,7},{6,0},{7,1},{8,10},{9,11},{10,... | collective-permute-start | bytes 61448 | tf_op jit(solution)/shard_map/ppermute | solution.py:78
  31.8 4.0 %collective-permute-start.2 = (bf16[5,2048]{1,0:T(8,128)(2,1)S(1)}, bf16[5,2048]{1,0:T(8,128)(2,1)}, u32[]{:S(2)}, u32[]{:S(2)}) collective-permute-start(bf16[5,2048]{1,0:T(8,128)(2,1)S(1)} %get-tuple-element.59), channel_id=1, source_target_pairs={{0,3},{1,4},{2,5},{3,6},{4,7},{5,0},{6,1},{7,2},{8,11},{9,12},{10,... | collective-permute-start | bytes 61448 | tf_op jit(solution)/shard_map/ppermute | solution.py:78
  36.4 4.9 %collective-permute-start.4 = (bf16[5,2048]{1,0:T(8,128)(2,1)S(1)}, bf16[5,2048]{1,0:T(8,128)(2,1)}, u32[]{:S(2)}, u32[]{:S(2)}) collective-permute-start(bf16[5,2048]{1,0:T(8,128)(2,1)S(1)} %get-tuple-element.57), channel_id=1, source_target_pairs={{0,5},{1,6},{2,7},{3,0},{4,1},{5,2},{6,3},{7,4},{8,13},{9,14},{10,... | collective-permute-start | bytes 61448 | tf_op jit(solution)/shard_map/ppermute | solution.py:78
  41.5 5.3 %gather_fusion.7 = bf16[32,2,128,256]{3,2,1,0:T(8,128)(2,1)} fusion(bf16[40,2,128,256]{3,2,1,0:T(8,128)(2,1)} %param.19, s32[1024]{0:T(1024)S(1)} %get-tuple-element.74), kind=kCustom, calls=%fused_computation.9 | custom fusion | bytes 8388736 | tf_op jit(solution)/shard_map/gather | solution.py:68
  46.8 1.2 gather_fusion.5
  48.1 0.6 gather_fusion.6
  48.7 0.7 fusion.80
  49.5 0.7 iota_compare_fusion.2
  50.2 4.0 %select_select_fusion = bf16[32,2,128,256]{3,2,1,0:T(8,128)(2,1)} fusion(bf16[32,2,128,256]{3,2,1,0:T(8,128)(2,1)} %gather_fusion.7, pred[32]{0:T(512)(128)(4,1)S(1)} %fusion.80, pred[32,128]{1,0:T(8,128)(4,1)S(1)} %iota_compare_fusion.2, bf16[32,2,256]{2,1,0:T(2,128)(2,1)S(1)} %gather_fusion.6), kind=kLoop, calls=%fused_computation.11 | loop fusion | flops 4194304 | bytes 8425504 | tf_op jit(solution)/shard_map/jit(_where)/select_n | solution.py:121
  54.2 7.8 %all-to-all-start = ((bf16[32,2,128,256]{3,2,1,0:T(8,128)(2,1)}), bf16[32,2,128,256]{3,2,1,0:T(8,128)(2,1)}, u32[]{:S(2)}, u32[]{:S(2)}) async-start(bf16[32,2,128,256]{3,2,1,0:T(8,128)(2,1)} %select_select_fusion), calls=%async_computation.1 | async-start | bytes 8388608 | tf_op jit(solution)/shard_map/all_to_all | solution.py:126
  62.1 1.0 fusion.13
  63.8 2.7 %collective-permute-start.5 = (bf16[5,2048]{1,0:T(8,128)(2,1)S(1)}, bf16[5,2048]{1,0:T(8,128)(2,1)S(1)}, u32[]{:S(2)}, u32[]{:S(2)}) collective-permute-start(bf16[5,2048]{1,0:T(8,128)(2,1)S(1)} %get-tuple-element.56), channel_id=1, source_target_pairs={{0,6},{1,7},{2,0},{3,1},{4,2},{5,3},{6,4},{7,5},{8,14},{9,15},{10,... | collective-permute-start | bytes 61448 | tf_op jit(solution)/shard_map/ppermute | solution.py:78
  66.4 1.0 collective-permute-start.6
  68.7 5.1 %gather_fusion.3 = bf16[24,2,128,256]{3,2,1,0:T(8,128)(2,1)} fusion(bf16[40,2,128,256]{3,2,1,0:T(8,128)(2,1)} %param.19, s32[1024]{0:T(1024)} %copy-done.10), kind=kCustom, calls=%fused_computation.5 | custom fusion | bytes 6291552 | tf_op jit(solution)/shard_map/gather | solution.py:68
  73.8 0.8 gather_fusion.1
  74.7 1.0 fusion.65
  75.7 4.4 %fusion.15 = f32[3,640,256]{1,2,0:T(8,128)S(1)} fusion(bf16[3,2048,256]{2,1,0:T(8,128)(2,1)S(1)} %copy-done, bf16[640,2048]{1,0:T(8,128)(2,1)} %all-gather.2.cloned.1.call-done), kind=kOutput, calls=%fused_computation.33 | convolution fusion | flops 2013265920 | bytes 7733248 | tf_op jit(solution)/shard_map/rd,cde->cre/dot_general | solution.py:133
  80.1 1.3 fusion.89
  81.5 1.0 fusion.39
  82.4 2.2 %copy.73 = f32[640,2,128]{2,0,1:T(8,128)} copy(f32[640,2,128]{0,2,1:T(8,128)} %bitcast.133) | data formatting | bytes 1310720 | tf_op jit(solution)/shard_map/squeeze | solution.py:135
  84.6 2.2 %copy.74 = f32[640,2,128]{2,0,1:T(8,128)} copy(f32[640,2,128]{0,2,1:T(8,128)} %bitcast.132) | data formatting | bytes 1310720 | tf_op jit(solution)/shard_map/squeeze | solution.py:136
  86.8 1.9 %fusion.47 = f32[2,640,640]{1,2,0:T(8,128)S(1)} fusion(f32[640,2,128]{2,0,1:T(8,128)} %copy.73, f32[640,2,128]{2,0,1:T(8,128)} %copy.74, f32[2,128]{1,0:T(2,128)S(1)} %bitcast.143, f32[2,128]{1,0:T(2,128)S(1)} %bitcast.150), kind=kOutput, calls=%fused_computation.67 | convolution fusion | flops 210370560 | bytes 4589568 | tf_op jit(solution)/shard_map/qhe,khe->hqk/dot_general | solution.py:141
  88.7 4.1 %fusion.92 = (f32[2,640]{1,0:T(2,128)S(1)}, f32[2,640,640]{1,2,0:T(8,128)S(1)}) fusion(f32[2,640,640]{1,2,0:T(8,128)S(1)} %fusion.47, pred[640,640]{0,1:T(8,128)(4,1)} %fusion.13), kind=kOutput, calls=%fused_computation.180 | output fusion | flops 4915839 | bytes 6968320 | tf_op jit(solution)/shard_map/sub | solution.py:149
  93.3 0.7 copy-done.3
  94.0 2.4 %convolution_convert_fusion = bf16[640,2048]{1,0:T(8,128)(2,1)} fusion(bf16[640,256]{0,1:T(8,128)(2,1)S(1)} %bitcast.136, bf16[256,2048]{1,0:T(8,128)(2,1)S(1)} %copy-done.3), kind=kOutput, calls=%fused_computation.15 | convolution fusion | flops 672399360 | bytes 3997696 | tf_op jit(solution)/shard_map/dot_general | solution.py:153
  96.5 3.4 %broadcast_select_fusion = bf16[24,2,128,256]{3,2,1,0:T(8,128)(2,1)} fusion(bf16[24,2,128,256]{3,2,1,0:T(8,128)(2,1)} %gather_fusion.3, pred[24,128]{1,0:T(8,128)(4,1)S(1)} %iota_compare_fusion.3, bf16[24,2,256]{2,1,0:T(2,128)(2,1)S(1)} %gather_fusion.2), kind=kLoop, calls=%fused_computation.16 | loop fusion | flops 1572864 | bytes 6319104 | tf_op jit(solution)/shard_map/jit(_where)/select_n | solution.py:68
  99.9 1.0 collective-permute-start.7
  101.7 1.9 %collective-permute-start.9 = (bf16[5,2048]{1,0:T(8,128)(2,1)S(1)}, bf16[5,2048]{1,0:T(8,128)(2,1)S(1)}, u32[]{:S(2)}, u32[]{:S(2)}) collective-permute-start(bf16[5,2048]{1,0:T(8,128)(2,1)S(1)} %fusion.65), channel_id=1, source_target_pairs={{0,3},{1,4},{2,5},{3,6},{4,7},{5,0},{6,1},{7,2},{8,11},{9,12},{10,... | collective-permute-start | bytes 61448 | tf_op jit(solution)/shard_map/ppermute | solution.py:89
  103.7 3.8 %collective-permute-start.10 = (bf16[5,2048]{1,0:T(8,128)(2,1)S(1)}, bf16[5,2048]{1,0:T(8,128)(2,1)S(1)}, u32[]{:S(2)}, u32[]{:S(2)}) collective-permute-start(bf16[5,2048]{1,0:T(8,128)(2,1)S(1)} %fusion.65), channel_id=1, source_target_pairs={{0,4},{1,5},{2,6},{3,7},{4,0},{5,1},{6,2},{7,3},{8,12},{9,13},{10,... | collective-permute-start | bytes 61448 | tf_op jit(solution)/shard_map/ppermute | solution.py:89
  107.4 1.8 %collective-permute-start.11 = (bf16[5,2048]{1,0:T(8,128)(2,1)S(1)}, bf16[5,2048]{1,0:T(8,128)(2,1)S(1)}, u32[]{:S(2)}, u32[]{:S(2)}) collective-permute-start(bf16[5,2048]{1,0:T(8,128)(2,1)S(1)} %fusion.65), channel_id=1, source_target_pairs={{0,5},{1,6},{2,7},{3,0},{4,1},{5,2},{6,3},{7,4},{8,13},{9,14},{10,... | collective-permute-start | bytes 61448 | tf_op jit(solution)/shard_map/ppermute | solution.py:89
  109.3 2.3 %collective-permute-start.12 = (bf16[5,2048]{1,0:T(8,128)(2,1)S(1)}, bf16[5,2048]{1,0:T(8,128)(2,1)S(1)}, u32[]{:S(2)}, u32[]{:S(2)}) collective-permute-start(bf16[5,2048]{1,0:T(8,128)(2,1)S(1)} %fusion.65), channel_id=1, source_target_pairs={{0,6},{1,7},{2,0},{3,1},{4,2},{5,3},{6,4},{7,5},{8,14},{9,15},{10,... | collective-permute-start | bytes 61448 | tf_op jit(solution)/shard_map/ppermute | solution.py:89
  112.2 1.5 collective-permute-start.13
  114.4 0.6 bitcast_dynamic-update-slice_fusion.4
  115.0 0.6 bitcast_dynamic-update-slice_fusion.3
  116.2 1.7 %collective-permute-done.12 = bf16[5,2048]{1,0:T(8,128)(2,1)S(1)} collective-permute-done((bf16[5,2048]{1,0:T(8,128)(2,1)S(1)}, bf16[5,2048]{1,0:T(8,128)(2,1)S(1)}, u32[]{:S(2)}, u32[]{:S(2)}) %collective-permute-start.12) | collective-permute-done | bytes 20512 | tf_op jit(solution)/shard_map/ppermute | solution.py:89
  119.6 1.6 %gather_fusion.9 = bf16[8,5,2048]{2,1,0:T(8,128)(2,1)S(1)} fusion(bf16[8,5,2048]{2,1,0:T(8,128)(2,1)} %bitcast_dynamic-update-slice_fusion, s32[1024]{0:T(1024)} %pad_clamp_fusion.2), kind=kCustom, calls=%fused_computation.1.clone | custom fusion | bytes 327712 | tf_op jit(solution)/shard_map/jit(_take)/gather | solution.py:91
  121.2 0.8 broadcast_select_fusion.1
  122.0 1.0 reshape.411
  123.0 0.8 gather_fusion.4
  123.8 0.7 broadcast_select_fusion.3
  125.1 1.6 %reduce.1 = bf16[32,2048]{1,0:T(8,128)(2,1)S(1)} reduce(bf16[32,1,2048]{2,0,1:T(8,128)(2,1)} %bitcast.138, bf16[]{:T(256)} %broadcast.385), dimensions={1}, to_apply=%copy.86.reduce_sub_computation | reduce | bytes 262146 | tf_op jit(solution)/shard_map/all_to_all | solution.py:168
  126.7 0.7 reshape.502
  127.4 7.4 %all-to-all-start.1 = ((bf16[32,2,1024]{2,1,0:T(2,128)(2,1)}), bf16[32,2,1024]{2,1,0:T(2,128)(2,1)S(1)}, u32[]{:S(2)}, u32[]{:S(2)}) async-start(bf16[32,2,1024]{2,1,0:T(2,128)(2,1)} %reshape.502), calls=%async_computation.2 | async-start | bytes 262144 | tf_op jit(solution)/shard_map/all_to_all | solution.py:168
  134.8 2.0 %pad_maximum_fusion = bf16[2,640,256]{1,2,0:T(8,128)(2,1)} fusion(bf16[1,640,256]{1,2,0:T(8,128)(2,1)} %bitcast.134, bf16[1,640,256]{1,2,0:T(8,128)(2,1)} %bitcast.135), kind=kLoop, calls=%fused_computation.51 | loop fusion | flops 327680 | bytes 1310720 | tf_op jit(solution)/shard_map/stack | solution.py:164
  136.8 2.2 %copy.87 = bf16[2,640,256]{2,1,0:T(8,128)(2,1)} copy(bf16[2,640,256]{1,2,0:T(8,128)(2,1)} %pad_maximum_fusion) | data formatting | bytes 1310720
  138.9 0.6 slice.117
  139.6 1.8 %all-to-all-done.1 = bf16[32,2,1024]{2,1,0:T(2,128)(2,1)S(1)} async-done(((bf16[32,2,1024]{2,1,0:T(2,128)(2,1)}), bf16[32,2,1024]{2,1,0:T(2,128)(2,1)S(1)}, u32[]{:S(2)}, u32[]{:S(2)}) %all-to-all-start.1) | async-done | bytes 131104 | tf_op jit(solution)/shard_map/all_to_all | solution.py:168
  141.5 0.7 copy.94
  142.3 1.9 %fusion.38 = bf16[80,2048]{1,0:T(8,128)(2,1)} fusion(bf16[80,2048]{1,0:T(8,128)(2,1)} %param.14, bf16[80,2048]{1,0:T(8,128)(2,1)} %reduce-scatter.2.cloned.1.call-done, f32[2048]{0:T(1024)S(1)} %copy-done.6), kind=kLoop, calls=%fused_computation.50 | loop fusion | flops 819200 | bytes 991232 | tf_op jit(solution)/shard_map/convert_element_type | solution.py:163
  144.2 4.7 %copy.104 = bf16[32,2,128,256]{3,2,1,0:T(8,128)(2,1)} copy(bf16[32,2,128,256]{3,2,1,0:T(8,128)(2,1)} %all-to-all-done) | data formatting | bytes 8388608
  (104 shorter events, 9.7 us)
Async XLA Ops:
  7.2 6.8 %copy-start = (bf16[3,2048,256]{2,1,0:T(8,128)(2,1)S(1)}, bf16[3,2048,256]{2,1,0:T(8,128)(2,1)}, u32[]{:S(2)}) copy-start(bf16[3,2048,256]{2,1,0:T(8,128)(2,1)} %param.22) | copy-start | bytes 9437188
  7.2 8.5 %copy-start.12 = (f32[3,256]{1,0:T(4,128)S(1)}, f32[3,256]{1,0:T(4,128)}, u32[]{:S(2)}) copy-start(f32[3,256]{1,0:T(4,128)} %param.23) | copy-start | bytes 9220
  7.2 8.8 %copy-start.1 = (s32[40]{0:T(128)S(1)}, s32[40]{0:T(128)}, u32[]{:S(2)}) copy-start(s32[40]{0:T(128)} %param.17) | copy-start | bytes 484
  7.2 68.5 %all-gather.2.cloned.1.call-start = ((), (), s32[]{:S(2)}) async-start(), calls=%async_computation.3 | async-start | bytes 2949120 | tf_op jit(solution)/shard_map/all_gather | solution.py:132
  15.7 3.3 %copy-start.7 = (f32[1,256]{1,0:T(1,128)}, f32[1,256]{1,0:T(1,128)S(1)}, u32[]{:S(2)}) copy-start(f32[1,256]{1,0:T(1,128)S(1)} %get-tuple-element.67) | copy-start | bytes 3076
  20.7 2.4 %copy-start.2 = (bf16[256,2048]{1,0:T(8,128)(2,1)S(1)}, bf16[256,2048]{1,0:T(8,128)(2,1)}, u32[]{:S(2)}) copy-start(bf16[256,2048]{1,0:T(8,128)(2,1)} %param.24) | copy-start | bytes 3145732
  20.7 20.6 %copy-start.16 = (s32[16,1]{0,1:T(1,128)S(1)}, s32[16,1]{0,1:T(1,128)}, u32[]{:S(2)}) copy-start(s32[16,1]{0,1:T(1,128)} %param.18) | copy-start | bytes 196
  25.8 0.7 copy-start.4
  26.5 37.2 %collective-permute-start = (bf16[5,2048]{1,0:T(8,128)(2,1)S(1)}, bf16[5,2048]{1,0:T(8,128)(2,1)S(1)}, u32[]{:S(2)}, u32[]{:S(2)}) collective-permute-start(bf16[5,2048]{1,0:T(8,128)(2,1)S(1)} %get-tuple-element.54), channel_id=1, source_target_pairs={{0,1},{1,2},{2,3},{3,4},{4,5},{5,6},{6,7},{7,0},{8,9},{9,10},{10,1... | collective-permute-start | bytes 61448 | tf_op jit(solution)/shard_map/ppermute | solution.py:78
  28.5 37.9 %collective-permute-start.1 = (bf16[5,2048]{1,0:T(8,128)(2,1)S(1)}, bf16[5,2048]{1,0:T(8,128)(2,1)}, u32[]{:S(2)}, u32[]{:S(2)}) collective-permute-start(bf16[5,2048]{1,0:T(8,128)(2,1)S(1)} %get-tuple-element.60), channel_id=1, source_target_pairs={{0,2},{1,3},{2,4},{3,5},{4,6},{5,7},{6,0},{7,1},{8,10},{9,11},{10,... | collective-permute-start | bytes 61448 | tf_op jit(solution)/shard_map/ppermute | solution.py:78
  31.8 42.8 %collective-permute-start.2 = (bf16[5,2048]{1,0:T(8,128)(2,1)S(1)}, bf16[5,2048]{1,0:T(8,128)(2,1)}, u32[]{:S(2)}, u32[]{:S(2)}) collective-permute-start(bf16[5,2048]{1,0:T(8,128)(2,1)S(1)} %get-tuple-element.59), channel_id=1, source_target_pairs={{0,3},{1,4},{2,5},{3,6},{4,7},{5,0},{6,1},{7,2},{8,11},{9,12},{10,... | collective-permute-start | bytes 61448 | tf_op jit(solution)/shard_map/ppermute | solution.py:78
  35.8 38.8 %collective-permute-start.3 = (bf16[5,2048]{1,0:T(8,128)(2,1)S(1)}, bf16[5,2048]{1,0:T(8,128)(2,1)}, u32[]{:S(2)}, u32[]{:S(2)}) collective-permute-start(bf16[5,2048]{1,0:T(8,128)(2,1)S(1)} %get-tuple-element.58), channel_id=1, source_target_pairs={{0,4},{1,5},{2,6},{3,7},{4,0},{5,1},{6,2},{7,3},{8,12},{9,13},{10,... | collective-permute-start | bytes 61448 | tf_op jit(solution)/shard_map/ppermute | solution.py:78
  36.4 38.3 %collective-permute-start.4 = (bf16[5,2048]{1,0:T(8,128)(2,1)S(1)}, bf16[5,2048]{1,0:T(8,128)(2,1)}, u32[]{:S(2)}, u32[]{:S(2)}) collective-permute-start(bf16[5,2048]{1,0:T(8,128)(2,1)S(1)} %get-tuple-element.57), channel_id=1, source_target_pairs={{0,5},{1,6},{2,7},{3,0},{4,1},{5,2},{6,3},{7,4},{8,13},{9,14},{10,... | collective-permute-start | bytes 61448 | tf_op jit(solution)/shard_map/ppermute | solution.py:78
  41.4 6.6 %copy-start.9 = (s32[1024]{0:T(1024)}, s32[1024]{0:T(1024)S(1)}, u32[]{:S(2)}) copy-start(s32[1024]{0:T(1024)S(1)} %get-tuple-element.74) | copy-start | bytes 12292
  41.5 26.6 %copy-start.10 = (s32[1024]{0:T(1024)}, s32[1024]{0:T(1024)S(1)}, u32[]{:S(2)}) copy-start(s32[1024]{0:T(1024)S(1)} %get-tuple-element.75) | copy-start | bytes 12292
  49.5 4.7 %copy-start.13 = (pred[32]{0:T(512)(128)(4,1)}, pred[32]{0:T(512)(128)(4,1)S(1)}, u32[]{:S(2)}) copy-start(pred[32]{0:T(512)(128)(4,1)S(1)} %fusion.80) | copy-start | bytes 100
  54.2 7.9 %copy-start.11 = (s32[1,640]{1,0:T(1,128)S(1)}, s32[1,640]{1,0:T(1,128)}, u32[]{:S(2)}) copy-start(s32[1,640]{1,0:T(1,128)} %param.15) | copy-start | bytes 7684
  54.2 70.4 %all-to-all-start = ((bf16[32,2,128,256]{3,2,1,0:T(8,128)(2,1)}), bf16[32,2,128,256]{3,2,1,0:T(8,128)(2,1)}, u32[]{:S(2)}, u32[]{:S(2)}) async-start(bf16[32,2,128,256]{3,2,1,0:T(8,128)(2,1)} %select_select_fusion), calls=%async_computation.1 | async-start | bytes 8388608 | tf_op jit(solution)/shard_map/all_to_all | solution.py:126
  62.0 80.3 %reduce-scatter.2.cloned.1.call-start = ((), (), s32[]{:S(2)}) async-start(), calls=%async_computation.4 | async-start | bytes 2949120 | tf_op jit(solution)/shard_map/reduce_scatter | solution.py:159
  63.8 10.9 %collective-permute-start.5 = (bf16[5,2048]{1,0:T(8,128)(2,1)S(1)}, bf16[5,2048]{1,0:T(8,128)(2,1)S(1)}, u32[]{:S(2)}, u32[]{:S(2)}) collective-permute-start(bf16[5,2048]{1,0:T(8,128)(2,1)S(1)} %get-tuple-element.56), channel_id=1, source_target_pairs={{0,6},{1,7},{2,0},{3,1},{4,2},{5,3},{6,4},{7,5},{8,14},{9,15},{10,... | collective-permute-start | bytes 61448 | tf_op jit(solution)/shard_map/ppermute | solution.py:78
  66.4 8.2 %collective-permute-start.6 = (bf16[5,2048]{1,0:T(8,128)(2,1)S(1)}, bf16[5,2048]{1,0:T(8,128)(2,1)S(1)}, u32[]{:S(2)}, u32[]{:S(2)}) collective-permute-start(bf16[5,2048]{1,0:T(8,128)(2,1)S(1)} %get-tuple-element.55), channel_id=1, source_target_pairs={{0,7},{1,0},{2,1},{3,2},{4,3},{5,4},{6,5},{7,6},{8,15},{9,8},{10,9... | collective-permute-start | bytes 61448 | tf_op jit(solution)/shard_map/ppermute | solution.py:78
  68.7 6.0 %copy-start.6 = (f32[2048]{0:T(1024)S(1)}, f32[2048]{0:T(1024)}, u32[]{:S(2)}) copy-start(f32[2048]{0:T(1024)} %param.25) | copy-start | bytes 24580
  81.5 5.3 %copy-start.8 = (f32[1,256]{1,0:T(1,128)S(1)}, f32[1,256]{1,0:T(1,128)}, u32[]{:S(2)}) copy-start(f32[1,256]{1,0:T(1,128)} %copy-done.7) | copy-start | bytes 3076
  88.7 4.1 %copy-start.5 = (f32[1,640,256]{1,2,0:T(8,128)S(1)}, f32[1,640,256]{1,2,0:T(8,128)}, u32[]{:S(2)}) copy-start(f32[1,640,256]{1,2,0:T(8,128)} %get-tuple-element.51) | copy-start | bytes 1966084
  92.8 1.2 copy-start.3
  96.5 24.7 %copy-start.15 = (pred[8]{0:T(512)(128)(4,1)S(1)}, pred[8]{0:T(512)(128)(4,1)}, u32[]{:S(2)}) copy-start(pred[8]{0:T(512)(128)(4,1)} %compare_and_fusion) | copy-start | bytes 28
  96.5 27.3 %copy-start.14 = (pred[32]{0:T(512)(128)(4,1)S(1)}, pred[32]{0:T(512)(128)(4,1)}, u32[]{:S(2)}) copy-start(pred[32]{0:T(512)(128)(4,1)} %copy-done.13) | copy-start | bytes 100
  99.9 9.4 %collective-permute-start.7 = (bf16[5,2048]{1,0:T(8,128)(2,1)S(1)}, bf16[5,2048]{1,0:T(8,128)(2,1)S(1)}, u32[]{:S(2)}, u32[]{:S(2)}) collective-permute-start(bf16[5,2048]{1,0:T(8,128)(2,1)S(1)} %fusion.65), channel_id=1, source_target_pairs={{0,1},{1,2},{2,3},{3,4},{4,5},{5,6},{6,7},{7,0},{8,9},{9,10},{10,1... | collective-permute-start | bytes 61448 | tf_op jit(solution)/shard_map/ppermute | solution.py:89
  101.5 10.7 %collective-permute-start.8 = (bf16[5,2048]{1,0:T(8,128)(2,1)S(1)}, bf16[5,2048]{1,0:T(8,128)(2,1)S(1)}, u32[]{:S(2)}, u32[]{:S(2)}) collective-permute-start(bf16[5,2048]{1,0:T(8,128)(2,1)S(1)} %fusion.65), channel_id=1, source_target_pairs={{0,2},{1,3},{2,4},{3,5},{4,6},{5,7},{6,0},{7,1},{8,10},{9,11},{10,... | collective-permute-start | bytes 61448 | tf_op jit(solution)/shard_map/ppermute | solution.py:89
  101.7 12.6 %collective-permute-start.9 = (bf16[5,2048]{1,0:T(8,128)(2,1)S(1)}, bf16[5,2048]{1,0:T(8,128)(2,1)S(1)}, u32[]{:S(2)}, u32[]{:S(2)}) collective-permute-start(bf16[5,2048]{1,0:T(8,128)(2,1)S(1)} %fusion.65), channel_id=1, source_target_pairs={{0,3},{1,4},{2,5},{3,6},{4,7},{5,0},{6,1},{7,2},{8,11},{9,12},{10,... | collective-permute-start | bytes 61448 | tf_op jit(solution)/shard_map/ppermute | solution.py:89
  103.7 11.3 %collective-permute-start.10 = (bf16[5,2048]{1,0:T(8,128)(2,1)S(1)}, bf16[5,2048]{1,0:T(8,128)(2,1)S(1)}, u32[]{:S(2)}, u32[]{:S(2)}) collective-permute-start(bf16[5,2048]{1,0:T(8,128)(2,1)S(1)} %fusion.65), channel_id=1, source_target_pairs={{0,4},{1,5},{2,6},{3,7},{4,0},{5,1},{6,2},{7,3},{8,12},{9,13},{10,... | collective-permute-start | bytes 61448 | tf_op jit(solution)/shard_map/ppermute | solution.py:89
  107.4 8.2 %collective-permute-start.11 = (bf16[5,2048]{1,0:T(8,128)(2,1)S(1)}, bf16[5,2048]{1,0:T(8,128)(2,1)S(1)}, u32[]{:S(2)}, u32[]{:S(2)}) collective-permute-start(bf16[5,2048]{1,0:T(8,128)(2,1)S(1)} %fusion.65), channel_id=1, source_target_pairs={{0,5},{1,6},{2,7},{3,0},{4,1},{5,2},{6,3},{7,4},{8,13},{9,14},{10,... | collective-permute-start | bytes 61448 | tf_op jit(solution)/shard_map/ppermute | solution.py:89
  109.3 8.7 %collective-permute-start.12 = (bf16[5,2048]{1,0:T(8,128)(2,1)S(1)}, bf16[5,2048]{1,0:T(8,128)(2,1)S(1)}, u32[]{:S(2)}, u32[]{:S(2)}) collective-permute-start(bf16[5,2048]{1,0:T(8,128)(2,1)S(1)} %fusion.65), channel_id=1, source_target_pairs={{0,6},{1,7},{2,0},{3,1},{4,2},{5,3},{6,4},{7,5},{8,14},{9,15},{10,... | collective-permute-start | bytes 61448 | tf_op jit(solution)/shard_map/ppermute | solution.py:89
  112.2 6.7 %collective-permute-start.13 = (bf16[5,2048]{1,0:T(8,128)(2,1)S(1)}, bf16[5,2048]{1,0:T(8,128)(2,1)S(1)}, u32[]{:S(2)}, u32[]{:S(2)}) collective-permute-start(bf16[5,2048]{1,0:T(8,128)(2,1)S(1)} %fusion.65), channel_id=1, source_target_pairs={{0,7},{1,0},{2,1},{3,2},{4,3},{5,4},{6,5},{7,6},{8,15},{9,8},{10,9... | collective-permute-start | bytes 61448 | tf_op jit(solution)/shard_map/ppermute | solution.py:89
  127.4 14.0 %all-to-all-start.1 = ((bf16[32,2,1024]{2,1,0:T(2,128)(2,1)}), bf16[32,2,1024]{2,1,0:T(2,128)(2,1)S(1)}, u32[]{:S(2)}, u32[]{:S(2)}) async-start(bf16[32,2,1024]{2,1,0:T(2,128)(2,1)} %reshape.502), calls=%async_computation.2 | async-start | bytes 262144 | tf_op jit(solution)/shard_map/all_to_all | solution.py:168
Sparse Core Ops, SparseCore 0:
  11.9 50.4 all-gather.1
  96.6 44.8 reduce-scatter.1

commit v5 on v4

--- a/solution.py
+++ b/solution.py
@@ -117,7 +117,6 @@
     partial_value, key_new, value_new = decode_partial(
         decode_rows, past_cache, request_ages, norm_gain, norm_bias, qkv_weight, qkv_bias, out_weight
     )
-    kept_cache = updated_rows(past_cache, key_new, value_new, request_ages, jnp.arange(staying))
     send_cache = jnp.where(
         has[:, None, None, None],
         updated_rows(past_cache, key_new, value_new, request_ages, picks),
@@ -153,9 +152,10 @@
     prompt_partial = jnp.dot(context, out_weight, preferred_element_type=jnp.float32).astype(
         jnp.bfloat16
     )
-    prompt_partial, own_out, key_rows, value_rows = lax.optimization_barrier(
-        (prompt_partial, own_out, key_rows, value_rows)
-    )
+    prompt_partial, own_out, key_rows, value_rows, key_new, value_new = lax.optimization_barrier(
+        (prompt_partial, own_out, key_rows, value_rows, key_new, value_new)
+    )
+    kept_cache = updated_rows(past_cache, key_new, value_new, request_ages, jnp.arange(staying))
     attended = lax.psum_scatter(prompt_partial, "tp", scatter_dimension=0, tiled=True).astype(
         jnp.float32
     )

time: 159 us -> 157 us (0.987)
  waiting for transfers between devices: 4.02 us -> 2.13 us
    sub x1, other arithmetic: 4.07 us -> 1.98 us  [on_device(): weights = jnp.exp(scores - highest)]
    ppermute x7, waiting for transfers between devices: 2.09 us -> 0.23 us  [gather_over_tp(): lax.ppermute(own_out, 'tp', [(i, (i + shift) % n) for i in range(n)])]
    unnamed x46 -> x60, local copies, waits for them, and re-layouts: 14.2 us -> 13.5 us
  transfers between devices with their start and end apart: 18 -> 18, of which waited for: 3 -> 2; matrix products, arithmetic and copies ran while one was open for 50% -> 51% of each run, Pallas kernels for 0% -> 0%
where the time goes in v5:
time: 157 us; the launch traced here: 153 us
  starting transfers between devices  46.5 us (30%)
  local copies, waits for them, and re-layouts  43.4 us (28%)
  other arithmetic  30.6 us (19%)
  matrix products  16.2 us (10%)
  between operations  14.6 us (9%)
  waiting for transfers between devices  2.13 us (1%)
    ppermute x7, starting transfers between devices, scatter_over_tp(): lax.ppermute(rolled[shift], 'tp', [(i, (i + shift) % n) for i in range(n)])  18.5 us
    unnamed x60, local copies, waits for them, and re-layouts  13.5 us
    ppermute x7, starting transfers between devices, gather_over_tp(): lax.ppermute(own_out, 'tp', [(i, (i + shift) % n) for i in range(n)])  12.7 us
    gather x2, local copies, waits for them, and re-layouts, updated_rows(): cache[picks]  10.5 us
    all_to_all x1, starting transfers between devices, on_device(): lax.all_to_all(send_cache, 'rep', split_axis=0, concat_axis=0, tiled=True)  7.76 us
    all_to_all x1, starting transfers between devices, on_device(): lax.all_to_all(send_rows, 'rep', split_axis=0, concat_axis=0, tiled=True)  7.38 us
    dot_general x1, matrix products, on_device(): jnp.einsum('rd,cde->cre', normed, qkv_weight, preferred_element_type=jnp....  4.47 us
    select_n x1, other arithmetic, on_device(): jnp.where(has[:, None, None, None], updated_rows(past_cache, key_new, val...  3.98 us
  transfers between devices with their start and end apart: 18, of which 2 were waited for; matrix products, arithmetic and copies ran while one was open for 51% of the time, Pallas kernels for 0%

profile of v5, /device:TPU:2, one launch (start us, length us, event | category | flops | bytes accessed | tf_op | source)
XLA Modules:
  0.0 153.4 jit_solution(634443267940049507)
XLA Ops:
  7.2 1.3 convert_reduce_fusion
  8.5 1.2 fusion.33
  9.8 2.0 %fusion.36 = bf16[80,2048]{1,0:T(8,128)(2,1)} fusion(bf16[80,2048]{1,0:T(8,128)(2,1)} %param.14, f32[2048]{0:T(1024)} %param.21, f32[2048]{0:T(1024)} %param.20, f32[80]{0:T(128)S(1)} %add_rsqrt_fusion.1, f32[80]{0:T(128)S(1)} %broadcast_multiply_fusion.1), kind=kLoop, calls=%fused_computation.48 | loop fusion | flops 983040 | bytes 672384 | tf_op jit(solution)/shard_map/convert_element_type | solution.py:18
  11.8 0.8 fusion.90
  12.6 1.0 convert_reduce_fusion.1
  13.6 1.1 fusion.43
  14.8 0.7 iota_compare_fusion.1
  15.5 1.6 %convolution_bitcast_fusion = f32[3,40,256]{2,1,0:T(8,128)S(1)} fusion(bf16[3,2048,256]{2,1,0:T(8,128)(2,1)S(1)} %copy-done, bf16[40,2048]{1,0:T(8,128)(2,1)} %param.16, f32[2048]{0:T(1024)} %param.21, f32[2048]{0:T(1024)} %param.20, f32[40]{0:T(128)S(1)} %add_rsqrt_fusion, f32[40]{0:T(128)S(1)} %broadcast_multiply_fusion), kind=kOutput, calls=%fused_computation.35 | convolution fusion | flops 126320640 | bytes 3449152 | tf_op jit(solution)/shard_map/rd,cde->cre/dot_general | solution.py:27
  17.8 2.6 %fusion.92 = (f32[40,2]{1,0:T(8,128)S(1)}, f32[40,2,128]{2,1,0:T(2,128)S(1)}) fusion(bf16[40,2,128,256]{3,2,1,0:T(8,128)(2,1)} %param.19, pred[2,256]{1,0:T(4,128)(4,1)S(1)} %iota_compare_fusion.5, bf16[40,256]{1,0:T(8,128)(2,1)S(1)} %get-tuple-element.68, pred[40,128]{1,0:T(8,128)(4,1)S(1)} %iota_compare_fusion.1), kind=kOutput, calls=%fused_computation.183 | convolution fusion | flops 5294000 | bytes 2688832 | tf_op jit(solution)/shard_map/rhc,rlc->rhl/dot_general | solution.py:36
  21.2 0.7 copy.81
  21.9 0.7 gather_fusion
  22.7 2.4 %fusion.22 = f32[40,256]{1,0:T(8,128)S(1)} fusion(bf16[40,2,128,256]{3,2,1,0:T(8,128)(2,1)} %param.19, pred[2,256]{1,0:T(4,128)(4,1)S(1)} %iota_compare_fusion.5, f32[40,2,128]{2,1,0:T(2,128)S(1)} %get-tuple-element.80, f32[40,2]{1,0:T(8,128)} %copy.81, f32[40,2]{1,0:T(8,128)S(1)} %copy.79), kind=kOutput, calls=%fused_computation.37 | convolution fusion | flops 5304320 | bytes 2724672 | tf_op jit(solution)/shard_map/rhl,rlc->rhc/dot_general | solution.py:56
  25.4 0.8 reshape.410
  26.2 1.5 gather_fusion.8
  27.8 0.7 slice_bitcast_fusion.6
  28.6 1.9 %collective-permute-start = (bf16[5,2048]{1,0:T(8,128)(2,1)}, bf16[5,2048]{1,0:T(8,128)(2,1)}, u32[]{:S(2)}, u32[]{:S(2)}) collective-permute-start(bf16[5,2048]{1,0:T(8,128)(2,1)} %get-tuple-element.58), channel_id=1, source_target_pairs={{0,1},{1,2},{2,3},{3,4},{4,5},{5,6},{6,7},{7,0},{8,9},{9,10},{10,1... | collective-permute-start | bytes 61448 | tf_op jit(solution)/shard_map/ppermute | solution.py:78
  30.5 3.3 %collective-permute-start.1 = (bf16[5,2048]{1,0:T(8,128)(2,1)}, bf16[5,2048]{1,0:T(8,128)(2,1)}, u32[]{:S(2)}, u32[]{:S(2)}) collective-permute-start(bf16[5,2048]{1,0:T(8,128)(2,1)} %get-tuple-element.64), channel_id=1, source_target_pairs={{0,2},{1,3},{2,4},{3,5},{4,6},{5,7},{6,0},{7,1},{8,10},{9,11},{10,... | collective-permute-start | bytes 61448 | tf_op jit(solution)/shard_map/ppermute | solution.py:78
  33.8 4.1 %collective-permute-start.2 = (bf16[5,2048]{1,0:T(8,128)(2,1)}, bf16[5,2048]{1,0:T(8,128)(2,1)}, u32[]{:S(2)}, u32[]{:S(2)}) collective-permute-start(bf16[5,2048]{1,0:T(8,128)(2,1)} %get-tuple-element.63), channel_id=1, source_target_pairs={{0,3},{1,4},{2,5},{3,6},{4,7},{5,0},{6,1},{7,2},{8,11},{9,12},{10,... | collective-permute-start | bytes 61448 | tf_op jit(solution)/shard_map/ppermute | solution.py:78
  38.4 5.0 %collective-permute-start.4 = (bf16[5,2048]{1,0:T(8,128)(2,1)}, bf16[5,2048]{1,0:T(8,128)(2,1)}, u32[]{:S(2)}, u32[]{:S(2)}) collective-permute-start(bf16[5,2048]{1,0:T(8,128)(2,1)} %get-tuple-element.61), channel_id=1, source_target_pairs={{0,5},{1,6},{2,7},{3,0},{4,1},{5,2},{6,3},{7,4},{8,13},{9,14},{10,... | collective-permute-start | bytes 61448 | tf_op jit(solution)/shard_map/ppermute | solution.py:78
  43.6 5.3 %gather_fusion.7 = bf16[32,2,128,256]{3,2,1,0:T(8,128)(2,1)} fusion(bf16[40,2,128,256]{3,2,1,0:T(8,128)(2,1)} %param.19, s32[1024]{0:T(1024)S(1)} %get-tuple-element.81), kind=kCustom, calls=%fused_computation.9 | custom fusion | bytes 8388736 | tf_op jit(solution)/shard_map/gather | solution.py:68
  48.9 0.7 gather_fusion.5
  49.7 0.6 gather_fusion.6
  50.5 4.0 %select_select_fusion = bf16[32,2,128,256]{3,2,1,0:T(8,128)(2,1)} fusion(bf16[32,2,128,256]{3,2,1,0:T(8,128)(2,1)} %gather_fusion.7, pred[32]{0:T(512)(128)(4,1)S(1)} %fusion.79, pred[32,128]{1,0:T(8,128)(4,1)S(1)} %iota_compare_fusion.2, bf16[32,2,256]{2,1,0:T(2,128)(2,1)S(1)} %gather_fusion.6), kind=kLoop, calls=%fused_computation.11 | loop fusion | flops 4194304 | bytes 8425504 | tf_op jit(solution)/shard_map/jit(_where)/select_n | solution.py:120
  54.5 7.8 %all-to-all-start = ((bf16[32,2,128,256]{3,2,1,0:T(8,128)(2,1)}), bf16[32,2,128,256]{3,2,1,0:T(8,128)(2,1)}, u32[]{:S(2)}, u32[]{:S(2)}) async-start(bf16[32,2,128,256]{3,2,1,0:T(8,128)(2,1)} %select_select_fusion), calls=%async_computation.1 | async-start | bytes 8388608 | tf_op jit(solution)/shard_map/all_to_all | solution.py:125
  62.3 0.7 gather_fusion.1
  63.6 0.7 iota_compare_fusion.3
  64.3 1.0 fusion.13
  65.4 2.8 %collective-permute-start.5 = (bf16[5,2048]{1,0:T(8,128)(2,1)}, bf16[5,2048]{1,0:T(8,128)(2,1)}, u32[]{:S(2)}, u32[]{:S(2)}) collective-permute-start(bf16[5,2048]{1,0:T(8,128)(2,1)} %get-tuple-element.60), channel_id=1, source_target_pairs={{0,6},{1,7},{2,0},{3,1},{4,2},{5,3},{6,4},{7,5},{8,14},{9,15},{10,... | collective-permute-start | bytes 61448 | tf_op jit(solution)/shard_map/ppermute | solution.py:78
  68.1 0.9 collective-permute-start.6
  69.7 5.1 %gather_fusion.3 = bf16[24,2,128,256]{3,2,1,0:T(8,128)(2,1)} fusion(bf16[40,2,128,256]{3,2,1,0:T(8,128)(2,1)} %param.19, s32[1024]{0:T(1024)} %copy-done.19), kind=kCustom, calls=%fused_computation.5 | custom fusion | bytes 6291552 | tf_op jit(solution)/shard_map/gather | solution.py:68
  74.8 1.7 %fusion.65 = bf16[5,2048]{1,0:T(8,128)(2,1)} fusion(bf16[5,2048]{1,0:T(8,128)(2,1)} %collective-permute-done.6, bf16[5,2048]{1,0:T(8,128)(2,1)} %collective-permute-done.5, bf16[5,2048]{1,0:T(8,128)(2,1)} %collective-permute-done.4, bf16[5,2048]{1,0:T(8,128)(2,1)} %collective-permute-done.3, bf16[5,2048]{1,0:T(8,128)(2,1)} %collective-permute-done.2, ...), kind=kLoop, calls=%fused_computation.90 | loop fusion | flops 194560 | bytes 212996 | tf_op jit(solution)/shard_map/convert_element_type | solution.py:81
  76.5 4.5 %fusion.15 = f32[3,640,256]{1,2,0:T(8,128)S(1)} fusion(bf16[3,2048,256]{2,1,0:T(8,128)(2,1)S(1)} %copy-done, bf16[640,2048]{1,0:T(8,128)(2,1)} %all-gather.2.cloned.1.call-done), kind=kOutput, calls=%fused_computation.33 | convolution fusion | flops 2013265920 | bytes 7733248 | tf_op jit(solution)/shard_map/rd,cde->cre/dot_general | solution.py:132
  81.0 1.3 fusion.88
  82.3 1.0 fusion.39
  83.3 2.2 %copy.73 = f32[640,2,128]{2,0,1:T(8,128)} copy(f32[640,2,128]{0,2,1:T(8,128)} %bitcast.136) | data formatting | bytes 1310720 | tf_op jit(solution)/shard_map/squeeze | solution.py:134
  85.4 2.2 %copy.74 = f32[640,2,128]{2,0,1:T(8,128)} copy(f32[640,2,128]{0,2,1:T(8,128)} %bitcast.135) | data formatting | bytes 1310720 | tf_op jit(solution)/shard_map/squeeze | solution.py:135
  87.6 1.9 %fusion.47 = f32[2,640,640]{1,2,0:T(8,128)S(1)} fusion(f32[640,2,128]{2,0,1:T(8,128)} %copy.73, f32[640,2,128]{2,0,1:T(8,128)} %copy.74, f32[2,128]{1,0:T(2,128)} %bitcast.148, f32[2,128]{1,0:T(2,128)} %bitcast.156), kind=kOutput, calls=%fused_computation.67 | convolution fusion | flops 210370560 | bytes 4589568 | tf_op jit(solution)/shard_map/qhe,khe->hqk/dot_general | solution.py:140
  89.5 2.0 %fusion.91 = (f32[2,640]{1,0:T(2,128)S(1)}, f32[2,640,640]{1,2,0:T(8,128)S(1)}) fusion(f32[2,640,640]{1,2,0:T(8,128)S(1)} %fusion.47, pred[640,640]{0,1:T(8,128)(4,1)S(1)} %fusion.13), kind=kOutput, calls=%fused_computation.182 | output fusion | flops 4915839 | bytes 6968320 | tf_op jit(solution)/shard_map/sub | solution.py:148
  92.1 0.7 copy-done.3
  92.8 2.4 %convolution_convert_fusion = bf16[640,2048]{1,0:T(8,128)(2,1)} fusion(bf16[640,256]{0,1:T(8,128)(2,1)S(1)} %bitcast.139, bf16[256,2048]{1,0:T(8,128)(2,1)S(1)} %copy-done.3), kind=kOutput, calls=%fused_computation.15 | convolution fusion | flops 672399360 | bytes 3997696 | tf_op jit(solution)/shard_map/dot_general | solution.py:152
  95.2 1.2 collective-permute-start.7
  96.6 1.9 %collective-permute-start.9 = (bf16[5,2048]{1,0:T(8,128)(2,1)S(1)}, bf16[5,2048]{1,0:T(8,128)(2,1)S(1)}, u32[]{:S(2)}, u32[]{:S(2)}) collective-permute-start(bf16[5,2048]{1,0:T(8,128)(2,1)S(1)} %copy-done.8), channel_id=1, source_target_pairs={{0,3},{1,4},{2,5},{3,6},{4,7},{5,0},{6,1},{7,2},{8,11},{9,12},{10,... | collective-permute-start | bytes 61448 | tf_op jit(solution)/shard_map/ppermute | solution.py:89
  98.5 3.9 %collective-permute-start.10 = (bf16[5,2048]{1,0:T(8,128)(2,1)S(1)}, bf16[5,2048]{1,0:T(8,128)(2,1)S(1)}, u32[]{:S(2)}, u32[]{:S(2)}) collective-permute-start(bf16[5,2048]{1,0:T(8,128)(2,1)S(1)} %copy-done.8), channel_id=1, source_target_pairs={{0,4},{1,5},{2,6},{3,7},{4,0},{5,1},{6,2},{7,3},{8,12},{9,13},{10,... | collective-permute-start | bytes 61448 | tf_op jit(solution)/shard_map/ppermute | solution.py:89
  102.4 1.6 %collective-permute-start.11 = (bf16[5,2048]{1,0:T(8,128)(2,1)S(1)}, bf16[5,2048]{1,0:T(8,128)(2,1)S(1)}, u32[]{:S(2)}, u32[]{:S(2)}) collective-permute-start(bf16[5,2048]{1,0:T(8,128)(2,1)S(1)} %copy-done.8), channel_id=1, source_target_pairs={{0,5},{1,6},{2,7},{3,0},{4,1},{5,2},{6,3},{7,4},{8,13},{9,14},{10,... | collective-permute-start | bytes 61448 | tf_op jit(solution)/shard_map/ppermute | solution.py:89
  104.1 0.7 gather_fusion.2
  105.5 3.3 %broadcast_select_fusion = bf16[24,2,128,256]{3,2,1,0:T(8,128)(2,1)} fusion(bf16[24,2,128,256]{3,2,1,0:T(8,128)(2,1)} %gather_fusion.3, pred[24,128]{1,0:T(8,128)(4,1)S(1)} %copy-done.17, bf16[24,2,256]{2,1,0:T(2,128)(2,1)S(1)} %gather_fusion.2), kind=kLoop, calls=%fused_computation.16 | loop fusion | flops 1572864 | bytes 6319104 | tf_op jit(solution)/shard_map/jit(_where)/select_n | solution.py:68
  108.8 2.4 %collective-permute-start.12 = (bf16[5,2048]{1,0:T(8,128)(2,1)S(1)}, bf16[5,2048]{1,0:T(8,128)(2,1)S(1)}, u32[]{:S(2)}, u32[]{:S(2)}) collective-permute-start(bf16[5,2048]{1,0:T(8,128)(2,1)S(1)} %copy-done.8), channel_id=1, source_target_pairs={{0,6},{1,7},{2,0},{3,1},{4,2},{5,3},{6,4},{7,5},{8,14},{9,15},{10,... | collective-permute-start | bytes 61448 | tf_op jit(solution)/shard_map/ppermute | solution.py:89
  111.9 1.5 collective-permute-start.13
  114.0 0.6 bitcast_dynamic-update-slice_fusion.4
  117.3 1.6 %gather_fusion.9 = bf16[8,5,2048]{2,1,0:T(8,128)(2,1)S(1)} fusion(bf16[8,5,2048]{2,1,0:T(8,128)(2,1)} %bitcast_dynamic-update-slice_fusion, s32[1024]{0:T(1024)} %pad_clamp_fusion.2), kind=kCustom, calls=%fused_computation.1.clone | custom fusion | bytes 327712 | tf_op jit(solution)/shard_map/jit(_take)/gather | solution.py:91
  118.9 0.8 broadcast_select_fusion.1
  119.7 1.0 reshape.411
  120.8 0.8 gather_fusion.4
  121.6 0.7 broadcast_select_fusion.3
  122.8 1.6 %reduce.1 = bf16[32,2048]{1,0:T(8,128)(2,1)S(1)} reduce(bf16[32,1,2048]{2,0,1:T(8,128)(2,1)} %bitcast.141, bf16[]{:T(256)} %broadcast.385), dimensions={1}, to_apply=%copy.86.reduce_sub_computation | reduce | bytes 262146 | tf_op jit(solution)/shard_map/all_to_all | solution.py:168
  124.4 0.7 reshape.502
  125.1 7.4 %all-to-all-start.1 = ((bf16[32,2,1024]{2,1,0:T(2,128)(2,1)}), bf16[32,2,1024]{2,1,0:T(2,128)(2,1)S(1)}, u32[]{:S(2)}, u32[]{:S(2)}) async-start(bf16[32,2,1024]{2,1,0:T(2,128)(2,1)} %reshape.502), calls=%async_computation.2 | async-start | bytes 262144 | tf_op jit(solution)/shard_map/all_to_all | solution.py:168
  132.5 2.0 %pad_maximum_fusion = bf16[2,640,256]{1,2,0:T(8,128)(2,1)} fusion(bf16[1,640,256]{1,2,0:T(8,128)(2,1)} %bitcast.137, bf16[1,640,256]{1,2,0:T(8,128)(2,1)} %bitcast.138), kind=kLoop, calls=%fused_computation.51 | loop fusion | flops 327680 | bytes 1310720 | tf_op jit(solution)/shard_map/stack | solution.py:164
  134.5 2.2 %copy.87 = bf16[2,640,256]{2,1,0:T(8,128)(2,1)} copy(bf16[2,640,256]{1,2,0:T(8,128)(2,1)} %pad_maximum_fusion) | data formatting | bytes 1310720
  136.7 0.6 slice.117
  137.3 1.8 %all-to-all-done.1 = bf16[32,2,1024]{2,1,0:T(2,128)(2,1)S(1)} async-done(((bf16[32,2,1024]{2,1,0:T(2,128)(2,1)}), bf16[32,2,1024]{2,1,0:T(2,128)(2,1)S(1)}, u32[]{:S(2)}, u32[]{:S(2)}) %all-to-all-start.1) | async-done | bytes 131104 | tf_op jit(solution)/shard_map/all_to_all | solution.py:168
  139.3 0.7 copy.94
  140.0 1.9 %fusion.38 = bf16[80,2048]{1,0:T(8,128)(2,1)} fusion(bf16[80,2048]{1,0:T(8,128)(2,1)} %param.14, bf16[80,2048]{1,0:T(8,128)(2,1)} %reduce-scatter.2.cloned.1.call-done, f32[2048]{0:T(1024)S(1)} %copy-done.12), kind=kLoop, calls=%fused_computation.50 | loop fusion | flops 819200 | bytes 991232 | tf_op jit(solution)/shard_map/convert_element_type | solution.py:163
  141.9 4.7 %copy.104 = bf16[32,2,128,256]{3,2,1,0:T(8,128)(2,1)} copy(bf16[32,2,128,256]{3,2,1,0:T(8,128)(2,1)} %all-to-all-done) | data formatting | bytes 8388608
  (120 shorter events, 10.1 us)
Async XLA Ops:
  7.2 8.4 %copy-start = (bf16[3,2048,256]{2,1,0:T(8,128)(2,1)S(1)}, bf16[3,2048,256]{2,1,0:T(8,128)(2,1)}, u32[]{:S(2)}) copy-start(bf16[3,2048,256]{2,1,0:T(8,128)(2,1)} %param.22) | copy-start | bytes 9437188
  7.2 69.3 %all-gather.2.cloned.1.call-start = ((), (), s32[]{:S(2)}) async-start(), calls=%async_computation.3 | async-start | bytes 2949120 | tf_op jit(solution)/shard_map/all_gather | solution.py:131
  12.6 8.0 %copy-start.16 = (f32[1,256]{1,0:T(1,128)}, f32[1,256]{1,0:T(1,128)S(1)}, u32[]{:S(2)}) copy-start(f32[1,256]{1,0:T(1,128)S(1)} %get-tuple-element.74) | copy-start | bytes 3076
  12.6 37.1 %copy-start.10 = (f32[1,256]{1,0:T(1,128)}, f32[1,256]{1,0:T(1,128)S(1)}, u32[]{:S(2)}) copy-start(f32[1,256]{1,0:T(1,128)S(1)} %get-tuple-element.73) | copy-start | bytes 3076
  12.6 37.1 %copy-start.13 = (f32[1,256]{1,0:T(1,128)}, f32[1,256]{1,0:T(1,128)S(1)}, u32[]{:S(2)}) copy-start(f32[1,256]{1,0:T(1,128)S(1)} %get-tuple-element.72) | copy-start | bytes 3076
  17.8 7.3 %copy-start.6 = (bf16[40,256]{1,0:T(8,128)(2,1)}, bf16[40,256]{1,0:T(8,128)(2,1)S(1)}, u32[]{:S(2)}) copy-start(bf16[40,256]{1,0:T(8,128)(2,1)S(1)} %get-tuple-element.20) | copy-start | bytes 61444
  22.7 2.4 %copy-start.2 = (bf16[256,2048]{1,0:T(8,128)(2,1)S(1)}, bf16[256,2048]{1,0:T(8,128)(2,1)}, u32[]{:S(2)}) copy-start(bf16[256,2048]{1,0:T(8,128)(2,1)} %param.24) | copy-start | bytes 3145732
  22.7 20.7 %copy-start.23 = (s32[16,1]{0,1:T(1,128)S(1)}, s32[16,1]{0,1:T(1,128)}, u32[]{:S(2)}) copy-start(s32[16,1]{0,1:T(1,128)} %param.18) | copy-start | bytes 196
  27.8 15.7 %copy-start.4 = (bf16[8,5,2048]{2,1,0:T(8,128)(2,1)}, bf16[8,5,2048]{2,1,0:T(8,128)(2,1)S(1)}, u32[]{:S(2)}) copy-start(bf16[8,5,2048]{2,1,0:T(8,128)(2,1)S(1)} %broadcast_select_fusion.2) | copy-start | bytes 491524
  28.6 36.8 %collective-permute-start = (bf16[5,2048]{1,0:T(8,128)(2,1)}, bf16[5,2048]{1,0:T(8,128)(2,1)}, u32[]{:S(2)}, u32[]{:S(2)}) collective-permute-start(bf16[5,2048]{1,0:T(8,128)(2,1)} %get-tuple-element.58), channel_id=1, source_target_pairs={{0,1},{1,2},{2,3},{3,4},{4,5},{5,6},{6,7},{7,0},{8,9},{9,10},{10,1... | collective-permute-start | bytes 61448 | tf_op jit(solution)/shard_map/ppermute | solution.py:78
  30.5 37.6 %collective-permute-start.1 = (bf16[5,2048]{1,0:T(8,128)(2,1)}, bf16[5,2048]{1,0:T(8,128)(2,1)}, u32[]{:S(2)}, u32[]{:S(2)}) collective-permute-start(bf16[5,2048]{1,0:T(8,128)(2,1)} %get-tuple-element.64), channel_id=1, source_target_pairs={{0,2},{1,3},{2,4},{3,5},{4,6},{5,7},{6,0},{7,1},{8,10},{9,11},{10,... | collective-permute-start | bytes 61448 | tf_op jit(solution)/shard_map/ppermute | solution.py:78
  33.8 41.0 %collective-permute-start.2 = (bf16[5,2048]{1,0:T(8,128)(2,1)}, bf16[5,2048]{1,0:T(8,128)(2,1)}, u32[]{:S(2)}, u32[]{:S(2)}) collective-permute-start(bf16[5,2048]{1,0:T(8,128)(2,1)} %get-tuple-element.63), channel_id=1, source_target_pairs={{0,3},{1,4},{2,5},{3,6},{4,7},{5,0},{6,1},{7,2},{8,11},{9,12},{10,... | collective-permute-start | bytes 61448 | tf_op jit(solution)/shard_map/ppermute | solution.py:78
  37.9 36.9 %collective-permute-start.3 = (bf16[5,2048]{1,0:T(8,128)(2,1)}, bf16[5,2048]{1,0:T(8,128)(2,1)}, u32[]{:S(2)}, u32[]{:S(2)}) collective-permute-start(bf16[5,2048]{1,0:T(8,128)(2,1)} %get-tuple-element.62), channel_id=1, source_target_pairs={{0,4},{1,5},{2,6},{3,7},{4,0},{5,1},{6,2},{7,3},{8,12},{9,13},{10,... | collective-permute-start | bytes 61448 | tf_op jit(solution)/shard_map/ppermute | solution.py:78
  38.4 36.4 %collective-permute-start.4 = (bf16[5,2048]{1,0:T(8,128)(2,1)}, bf16[5,2048]{1,0:T(8,128)(2,1)}, u32[]{:S(2)}, u32[]{:S(2)}) collective-permute-start(bf16[5,2048]{1,0:T(8,128)(2,1)} %get-tuple-element.61), channel_id=1, source_target_pairs={{0,5},{1,6},{2,7},{3,0},{4,1},{5,2},{6,3},{7,4},{8,13},{9,14},{10,... | collective-permute-start | bytes 61448 | tf_op jit(solution)/shard_map/ppermute | solution.py:78
  43.5 6.2 %copy-start.18 = (s32[1024]{0:T(1024)}, s32[1024]{0:T(1024)S(1)}, u32[]{:S(2)}) copy-start(s32[1024]{0:T(1024)S(1)} %get-tuple-element.81) | copy-start | bytes 12292
  43.6 18.8 %copy-start.19 = (s32[1024]{0:T(1024)}, s32[1024]{0:T(1024)S(1)}, u32[]{:S(2)}) copy-start(s32[1024]{0:T(1024)S(1)} %get-tuple-element.82) | copy-start | bytes 12292
  43.6 5.4 %copy-start.1 = (s32[40]{0:T(128)S(1)}, s32[40]{0:T(128)}, u32[]{:S(2)}) copy-start(s32[40]{0:T(128)} %param.17) | copy-start | bytes 484
  50.4 4.1 %copy-start.21 = (pred[32]{0:T(512)(128)(4,1)}, pred[32]{0:T(512)(128)(4,1)S(1)}, u32[]{:S(2)}) copy-start(pred[32]{0:T(512)(128)(4,1)S(1)} %fusion.79) | copy-start | bytes 100
  54.5 8.5 %copy-start.20 = (s32[1,640]{1,0:T(1,128)S(1)}, s32[1,640]{1,0:T(1,128)}, u32[]{:S(2)}) copy-start(s32[1,640]{1,0:T(1,128)} %param.15) | copy-start | bytes 7684
  54.5 67.8 %all-to-all-start = ((bf16[32,2,128,256]{3,2,1,0:T(8,128)(2,1)}), bf16[32,2,128,256]{3,2,1,0:T(8,128)(2,1)}, u32[]{:S(2)}, u32[]{:S(2)}) async-start(bf16[32,2,128,256]{3,2,1,0:T(8,128)(2,1)} %select_select_fusion), calls=%async_computation.1 | async-start | bytes 8388608 | tf_op jit(solution)/shard_map/all_to_all | solution.py:125
  62.3 77.7 %reduce-scatter.2.cloned.1.call-start = ((), (), s32[]{:S(2)}) async-start(), calls=%async_computation.4 | async-start | bytes 2949120 | tf_op jit(solution)/shard_map/reduce_scatter | solution.py:159
  65.4 9.4 %collective-permute-start.5 = (bf16[5,2048]{1,0:T(8,128)(2,1)}, bf16[5,2048]{1,0:T(8,128)(2,1)}, u32[]{:S(2)}, u32[]{:S(2)}) collective-permute-start(bf16[5,2048]{1,0:T(8,128)(2,1)} %get-tuple-element.60), channel_id=1, source_target_pairs={{0,6},{1,7},{2,0},{3,1},{4,2},{5,3},{6,4},{7,5},{8,14},{9,15},{10,... | collective-permute-start | bytes 61448 | tf_op jit(solution)/shard_map/ppermute | solution.py:78
  68.1 6.7 %collective-permute-start.6 = (bf16[5,2048]{1,0:T(8,128)(2,1)}, bf16[5,2048]{1,0:T(8,128)(2,1)}, u32[]{:S(2)}, u32[]{:S(2)}) collective-permute-start(bf16[5,2048]{1,0:T(8,128)(2,1)} %get-tuple-element.59), channel_id=1, source_target_pairs={{0,7},{1,0},{2,1},{3,2},{4,3},{5,4},{6,5},{7,6},{8,15},{9,8},{10,9... | collective-permute-start | bytes 61448 | tf_op jit(solution)/shard_map/ppermute | solution.py:78
  81.0 1.3 copy-start.11
  81.0 1.3 copy-start.14
  89.5 2.0 %copy-start.5 = (f32[1,640,256]{1,2,0:T(8,128)S(1)}, f32[1,640,256]{1,2,0:T(8,128)}, u32[]{:S(2)}) copy-start(f32[1,640,256]{1,2,0:T(8,128)} %get-tuple-element.55) | copy-start | bytes 1966084
  89.5 2.0 %copy-start.15 = (f32[1,256]{1,0:T(1,128)S(1)}, f32[1,256]{1,0:T(1,128)}, u32[]{:S(2)}) copy-start(f32[1,256]{1,0:T(1,128)} %copy-done.13) | copy-start | bytes 3076
  91.5 1.2 copy-start.3
  92.7 2.5 %copy-start.8 = (bf16[5,2048]{1,0:T(8,128)(2,1)S(1)}, bf16[5,2048]{1,0:T(8,128)(2,1)}, u32[]{:S(2)}) copy-start(bf16[5,2048]{1,0:T(8,128)(2,1)} %fusion.65) | copy-start | bytes 61444
  92.7 11.3 %copy-start.7 = (bf16[40,256]{1,0:T(8,128)(2,1)S(1)}, bf16[40,256]{1,0:T(8,128)(2,1)}, u32[]{:S(2)}) copy-start(bf16[40,256]{1,0:T(8,128)(2,1)} %copy-done.6) | copy-start | bytes 61444
  92.8 11.3 %copy-start.9 = (bf16[40,256]{1,0:T(8,128)(2,1)S(1)}, bf16[40,256]{1,0:T(8,128)(2,1)}, u32[]{:S(2)}) copy-start(bf16[40,256]{1,0:T(8,128)(2,1)} %get-tuple-element.19) | copy-start | bytes 61444
  92.8 12.7 %copy-start.17 = (pred[24,128]{1,0:T(8,128)(4,1)S(1)}, pred[24,128]{1,0:T(8,128)(4,1)}, u32[]{:S(2)}) copy-start(pred[24,128]{1,0:T(8,128)(4,1)} %iota_compare_fusion.3) | copy-start | bytes 9220
  95.2 13.6 %collective-permute-start.7 = (bf16[5,2048]{1,0:T(8,128)(2,1)S(1)}, bf16[5,2048]{1,0:T(8,128)(2,1)S(1)}, u32[]{:S(2)}, u32[]{:S(2)}) collective-permute-start(bf16[5,2048]{1,0:T(8,128)(2,1)S(1)} %copy-done.8), channel_id=1, source_target_pairs={{0,1},{1,2},{2,3},{3,4},{4,5},{5,6},{6,7},{7,0},{8,9},{9,10},{10,1... | collective-permute-start | bytes 61448 | tf_op jit(solution)/shard_map/ppermute | solution.py:89
  96.4 15.5 %collective-permute-start.8 = (bf16[5,2048]{1,0:T(8,128)(2,1)S(1)}, bf16[5,2048]{1,0:T(8,128)(2,1)S(1)}, u32[]{:S(2)}, u32[]{:S(2)}) collective-permute-start(bf16[5,2048]{1,0:T(8,128)(2,1)S(1)} %copy-done.8), channel_id=1, source_target_pairs={{0,2},{1,3},{2,4},{3,5},{4,6},{5,7},{6,0},{7,1},{8,10},{9,11},{10,... | collective-permute-start | bytes 61448 | tf_op jit(solution)/shard_map/ppermute | solution.py:89
  96.6 17.3 %collective-permute-start.9 = (bf16[5,2048]{1,0:T(8,128)(2,1)S(1)}, bf16[5,2048]{1,0:T(8,128)(2,1)S(1)}, u32[]{:S(2)}, u32[]{:S(2)}) collective-permute-start(bf16[5,2048]{1,0:T(8,128)(2,1)S(1)} %copy-done.8), channel_id=1, source_target_pairs={{0,3},{1,4},{2,5},{3,6},{4,7},{5,0},{6,1},{7,2},{8,11},{9,12},{10,... | collective-permute-start | bytes 61448 | tf_op jit(solution)/shard_map/ppermute | solution.py:89
  98.5 16.1 %collective-permute-start.10 = (bf16[5,2048]{1,0:T(8,128)(2,1)S(1)}, bf16[5,2048]{1,0:T(8,128)(2,1)S(1)}, u32[]{:S(2)}, u32[]{:S(2)}) collective-permute-start(bf16[5,2048]{1,0:T(8,128)(2,1)S(1)} %copy-done.8), channel_id=1, source_target_pairs={{0,4},{1,5},{2,6},{3,7},{4,0},{5,1},{6,2},{7,3},{8,12},{9,13},{10,... | collective-permute-start | bytes 61448 | tf_op jit(solution)/shard_map/ppermute | solution.py:89
  102.4 12.8 %collective-permute-start.11 = (bf16[5,2048]{1,0:T(8,128)(2,1)S(1)}, bf16[5,2048]{1,0:T(8,128)(2,1)S(1)}, u32[]{:S(2)}, u32[]{:S(2)}) collective-permute-start(bf16[5,2048]{1,0:T(8,128)(2,1)S(1)} %copy-done.8), channel_id=1, source_target_pairs={{0,5},{1,6},{2,7},{3,0},{4,1},{5,2},{6,3},{7,4},{8,13},{9,14},{10,... | collective-permute-start | bytes 61448 | tf_op jit(solution)/shard_map/ppermute | solution.py:89
  105.5 16.1 %copy-start.22 = (pred[32]{0:T(512)(128)(4,1)S(1)}, pred[32]{0:T(512)(128)(4,1)}, u32[]{:S(2)}) copy-start(pred[32]{0:T(512)(128)(4,1)} %copy-done.21) | copy-start | bytes 100
  108.8 7.0 %collective-permute-start.12 = (bf16[5,2048]{1,0:T(8,128)(2,1)S(1)}, bf16[5,2048]{1,0:T(8,128)(2,1)S(1)}, u32[]{:S(2)}, u32[]{:S(2)}) collective-permute-start(bf16[5,2048]{1,0:T(8,128)(2,1)S(1)} %copy-done.8), channel_id=1, source_target_pairs={{0,6},{1,7},{2,0},{3,1},{4,2},{5,3},{6,4},{7,5},{8,14},{9,15},{10,... | collective-permute-start | bytes 61448 | tf_op jit(solution)/shard_map/ppermute | solution.py:89
  111.9 4.8 %collective-permute-start.13 = (bf16[5,2048]{1,0:T(8,128)(2,1)S(1)}, bf16[5,2048]{1,0:T(8,128)(2,1)S(1)}, u32[]{:S(2)}, u32[]{:S(2)}) collective-permute-start(bf16[5,2048]{1,0:T(8,128)(2,1)S(1)} %copy-done.8), channel_id=1, source_target_pairs={{0,7},{1,0},{2,1},{3,2},{4,3},{5,4},{6,5},{7,6},{8,15},{9,8},{10,9... | collective-permute-start | bytes 61448 | tf_op jit(solution)/shard_map/ppermute | solution.py:89
  118.9 21.1 %copy-start.12 = (f32[2048]{0:T(1024)S(1)}, f32[2048]{0:T(1024)}, u32[]{:S(2)}) copy-start(f32[2048]{0:T(1024)} %param.25) | copy-start | bytes 24580
  125.1 14.0 %all-to-all-start.1 = ((bf16[32,2,1024]{2,1,0:T(2,128)(2,1)}), bf16[32,2,1024]{2,1,0:T(2,128)(2,1)S(1)}, u32[]{:S(2)}, u32[]{:S(2)}) async-start(bf16[32,2,1024]{2,1,0:T(2,128)(2,1)} %reshape.502), calls=%async_computation.2 | async-start | bytes 262144 | tf_op jit(solution)/shard_map/all_to_all | solution.py:168
Sparse Core Ops, SparseCore 0:
  11.9 50.8 all-gather.1
  95.3 42.6 reduce-scatter.1

commit v6 on v5

--- a/solution.py
+++ b/solution.py
@@ -129,16 +129,18 @@
     )
     own_out = scatter_over_tp(decode_pieces, decode_rows, out_bias)
     normed = lax.all_gather(layer_norm(prompt_rows, norm_gain, norm_bias), "tp", axis=0, tiled=True)
-    projected = jnp.einsum("rd,cde->cre", normed, qkv_weight, preferred_element_type=jnp.float32)
-    total_rows = projected.shape[1]
-    queries = (projected[0] + qkv_bias[0]).astype(jnp.bfloat16)
-    key_rows = (projected[1] + qkv_bias[1]).astype(jnp.bfloat16)
-    value_rows = (projected[2] + qkv_bias[2]).astype(jnp.bfloat16)
-    head_q = queries.reshape(total_rows, heads_here, HEAD_DIM)
-    head_k = key_rows.reshape(total_rows, heads_here, HEAD_DIM)
-    head_v = value_rows.reshape(total_rows, heads_here, HEAD_DIM)
+    model = qkv_weight.shape[1]
+    split_weight = qkv_weight.reshape(3, model, heads_here, HEAD_DIM)
+    split_bias = qkv_bias.reshape(3, heads_here, 1, HEAD_DIM)
+    projected = jnp.einsum(
+        "rd,cdhe->chre", normed, split_weight, preferred_element_type=jnp.float32
+    )
+    total_rows = projected.shape[2]
+    head_q = (projected[0] + split_bias[0]).astype(jnp.bfloat16)
+    head_k = (projected[1] + split_bias[1]).astype(jnp.bfloat16)
+    head_v = (projected[2] + split_bias[2]).astype(jnp.bfloat16)
     scores = jnp.einsum(
-        "qhe,khe->hqk", head_q, head_k, preferred_element_type=jnp.float32
+        "hqe,hke->hqk", head_q, head_k, preferred_element_type=jnp.float32
     ) * HEAD_DIM ** (-0.5)
     pieces = prompt_pieces[0]
     position = jnp.arange(total_rows)
@@ -147,15 +149,21 @@
     highest = jnp.max(scores, axis=-1, keepdims=True)
     weights = jnp.exp(scores - highest)
     probs = (weights / jnp.sum(weights, axis=-1, keepdims=True)).astype(jnp.bfloat16)
-    context = jnp.einsum("hqk,khe->qhe", probs, head_v, preferred_element_type=jnp.float32)
+    context = jnp.einsum("hqk,hke->qhe", probs, head_v, preferred_element_type=jnp.float32)
     context = context.reshape(total_rows, width).astype(jnp.bfloat16)
+    key_rows = jnp.transpose(head_k, (1, 0, 2)).reshape(total_rows, width)
+    value_rows = jnp.transpose(head_v, (1, 0, 2)).reshape(total_rows, width)
     prompt_partial = jnp.dot(context, out_weight, preferred_element_type=jnp.float32).astype(
         jnp.bfloat16
     )
     prompt_partial, own_out, key_rows, value_rows, key_new, value_new = lax.optimization_barrier(
         (prompt_partial, own_out, key_rows, value_rows, key_new, value_new)
     )
-    kept_cache = updated_rows(past_cache, key_new, value_new, request_ages, jnp.arange(staying))
+    written = (jnp.arange(past_cache.shape[2])[None, :] == request_ages[:staying, None])
+    fresh = jnp.stack([key_new[:staying], value_new[:staying]], axis=1)
+    kept_cache = jnp.where(
+        written[:, None, :, None], fresh[:, :, None, :], past_cache[:staying]
+    )
     attended = lax.psum_scatter(prompt_partial, "tp", scatter_dimension=0, tiled=True).astype(
         jnp.float32
     )

time: 157 us -> 147 us (0.936); the launches traced: 153 us -> 146 us
  local copies, waits for them, and re-layouts: 43.4 us -> 23.3 us
  waiting for transfers between devices: 2.13 us -> 20.9 us
  other arithmetic: 30.6 us -> 22.4 us
  starting transfers between devices: 46.5 us -> 48.4 us
    all_to_all x1, waiting for transfers between devices: 0.01 us -> 8.93 us  [on_device(): lax.all_to_all(send_cache, 'rep', split_axis=0, concat_axis=0, tiled=True)]
    unnamed x60 -> x23, local copies, waits for them, and re-layouts: 13.5 us -> 6.32 us
    dot_general x3 -> x2, matrix products: 6.9 us -> 1.15 us  [the longest x1 0.67 us: on_device(): jnp.einsum('hqe,hke->hqk', head_q, head_k, preferred_element_type=jnp.flo...]
    unnamed x0 -> x1, matrix products: none -> 5.32 us
    gather x2 -> x1, local copies, waits for them, and re-layouts: 10.5 us -> 5.35 us  [updated_rows(): cache[picks]]
    reshape x0 -> x1, local copies, waits for them, and re-layouts: none -> 4.64 us  [on_device(): split_weight = qkv_weight.reshape(3, model, heads_here, HEAD_DIM)]
    reduce_scatter x1, waiting for transfers between devices: 0.01 us -> 4.48 us  [on_device(): lax.psum_scatter(prompt_partial, 'tp', scatter_dimension=0, tiled=True)]
    squeeze x2 -> x0, local copies, waits for them, and re-layouts: 4.33 us -> none  [the longest x1 2.17 us: on_device(): queries = (projected[0] + qkv_bias[0]).astype(jnp.bfloat16)]
  transfers between devices with their start and end apart: 18 -> 18, of which waited for: 2 -> 5; matrix products, arithmetic and copies ran while one was open for 51% -> 35% of each run, Pallas kernels for 0% -> 0%
where the time goes in v6:
time: 147 us; the launch traced here: 146 us
  starting transfers between devices  48.4 us (33%)
  local copies, waits for them, and re-layouts  23.3 us (16%)
  other arithmetic  22.4 us (15%)
  waiting for transfers between devices  20.9 us (14%)
  matrix products  16.8 us (11%)
  between operations  14.5 us (10%)
    ppermute x7, starting transfers between devices, scatter_over_tp(): lax.ppermute(rolled[shift], 'tp', [(i, (i + shift) % n) for i in range(n)])  18.5 us
    ppermute x7, starting transfers between devices, gather_over_tp(): lax.ppermute(own_out, 'tp', [(i, (i + shift) % n) for i in range(n)])  12.9 us
    all_to_all x1, starting transfers between devices, on_device(): lax.all_to_all(send_rows, 'rep', split_axis=0, concat_axis=0, tiled=True)  9.08 us
    all_to_all x1, waiting for transfers between devices, on_device(): lax.all_to_all(send_cache, 'rep', split_axis=0, concat_axis=0, tiled=True)  8.93 us
    all_to_all x1, starting transfers between devices, on_device(): lax.all_to_all(send_cache, 'rep', split_axis=0, concat_axis=0, tiled=True)  7.8 us
    unnamed x23, local copies, waits for them, and re-layouts  6.32 us
    gather x1, local copies, waits for them, and re-layouts, updated_rows(): cache[picks]  5.35 us
    unnamed x1, matrix products  5.32 us
  transfers between devices with their start and end apart: 18, of which 5 were waited for; matrix products, arithmetic and copies ran while one was open for 35% of the time, Pallas kernels for 0%

profile of v6, /device:TPU:2, one launch (start us, length us, event | category | flops | bytes accessed | tf_op | source)
XLA Modules:
  0.0 146.2 jit_solution(6281104656729585556)
XLA Ops:
  7.2 1.2 convert_reduce_fusion
  8.4 1.2 fusion.28
  9.7 2.0 %fusion.31 = bf16[80,2048]{1,0:T(8,128)(2,1)} fusion(bf16[80,2048]{1,0:T(8,128)(2,1)} %param.14, f32[2048]{0:T(1024)} %param.21, f32[2048]{0:T(1024)} %param.20, f32[80]{0:T(128)S(1)} %add_rsqrt_fusion.1, f32[80]{0:T(128)S(1)} %broadcast_multiply_fusion.1), kind=kLoop, calls=%fused_computation.42 | loop fusion | flops 983040 | bytes 672384 | tf_op jit(solution)/shard_map/convert_element_type | solution.py:18
  11.7 1.0 convert_reduce_fusion.1
  12.7 1.1 fusion.42
  13.9 0.8 fusion.87
  14.7 0.7 iota_compare_fusion.1
  15.4 2.7 %convolution_bitcast_fusion = f32[3,40,256]{2,1,0:T(8,128)S(1)} fusion(bf16[3,2048,256]{2,1,0:T(8,128)(2,1)} %param.22, bf16[40,2048]{1,0:T(8,128)(2,1)} %param.16, f32[2048]{0:T(1024)} %param.21, f32[2048]{0:T(1024)} %param.20, f32[40]{0:T(128)S(1)} %add_rsqrt_fusion, f32[40]{0:T(128)S(1)} %broadcast_multiply_fusion), kind=kOutput, calls=%fused_computation.29 | convolution fusion | flops 126320640 | bytes 3449152 | tf_op jit(solution)/shard_map/rd,cde->cre/dot_general | solution.py:27
  18.2 2.6 %fusion.89 = (f32[40,2]{1,0:T(8,128)S(1)}, f32[40,2,128]{2,1,0:T(2,128)S(1)}) fusion(bf16[40,2,128,256]{3,2,1,0:T(8,128)(2,1)} %param.19, pred[2,256]{1,0:T(4,128)(4,1)S(1)} %iota_compare_fusion.5, bf16[40,256]{1,0:T(8,128)(2,1)S(1)} %get-tuple-element.35, pred[40,128]{1,0:T(8,128)(4,1)S(1)} %iota_compare_fusion.1), kind=kOutput, calls=%fused_computation.177 | convolution fusion | flops 5294000 | bytes 2688832 | tf_op jit(solution)/shard_map/rhc,rlc->rhl/dot_general | solution.py:36
  21.0 0.1 multiply_reduce_fusion
  21.3 0.2 fusion.71
  21.7 0.7 gather_fusion
  22.5 2.3 %fusion.17 = f32[40,256]{1,0:T(8,128)S(1)} fusion(bf16[40,2,128,256]{3,2,1,0:T(8,128)(2,1)} %param.19, pred[2,256]{1,0:T(4,128)(4,1)S(1)} %iota_compare_fusion.5, f32[40,2,128]{2,1,0:T(2,128)S(1)} %get-tuple-element.47, f32[40,2]{1,0:T(8,128)S(1)} %copy.85, f32[40,2]{1,0:T(8,128)S(1)} %copy.83), kind=kOutput, calls=%fused_computation.31 | convolution fusion | flops 5304320 | bytes 2704512 | tf_op jit(solution)/shard_map/rhl,rlc->rhc/dot_general | solution.py:56
  24.8 0.3 convolution_convert_fusion.1
  25.3 0.6 gather_fusion.5
  25.9 0.1 broadcast_select_fusion.1
  26.0 2.0 %collective-permute-start = (bf16[5,2048]{1,0:T(8,128)(2,1)S(1)}, bf16[5,2048]{1,0:T(8,128)(2,1)S(1)}, u32[]{:S(2)}, u32[]{:S(2)}) collective-permute-start(bf16[5,2048]{1,0:T(8,128)(2,1)S(1)} %get-tuple-element.25), channel_id=1, source_target_pairs={{0,1},{1,2},{2,3},{3,4},{4,5},{5,6},{6,7},{7,0},{8,9},{9,10},{10,1... | collective-permute-start | bytes 61448 | tf_op jit(solution)/shard_map/ppermute | solution.py:78
  28.0 3.3 %collective-permute-start.1 = (bf16[5,2048]{1,0:T(8,128)(2,1)S(1)}, bf16[5,2048]{1,0:T(8,128)(2,1)S(1)}, u32[]{:S(2)}, u32[]{:S(2)}) collective-permute-start(bf16[5,2048]{1,0:T(8,128)(2,1)S(1)} %get-tuple-element.31), channel_id=1, source_target_pairs={{0,2},{1,3},{2,4},{3,5},{4,6},{5,7},{6,0},{7,1},{8,10},{9,11},{10,... | collective-permute-start | bytes 61448 | tf_op jit(solution)/shard_map/ppermute | solution.py:78
  31.3 4.1 %collective-permute-start.2 = (bf16[5,2048]{1,0:T(8,128)(2,1)S(1)}, bf16[5,2048]{1,0:T(8,128)(2,1)S(1)}, u32[]{:S(2)}, u32[]{:S(2)}) collective-permute-start(bf16[5,2048]{1,0:T(8,128)(2,1)S(1)} %get-tuple-element.30), channel_id=1, source_target_pairs={{0,3},{1,4},{2,5},{3,6},{4,7},{5,0},{6,1},{7,2},{8,11},{9,12},{10,... | collective-permute-start | bytes 61448 | tf_op jit(solution)/shard_map/ppermute | solution.py:78
  35.4 0.5 collective-permute-start.3
  35.9 5.0 %collective-permute-start.4 = (bf16[5,2048]{1,0:T(8,128)(2,1)S(1)}, bf16[5,2048]{1,0:T(8,128)(2,1)S(1)}, u32[]{:S(2)}, u32[]{:S(2)}) collective-permute-start(bf16[5,2048]{1,0:T(8,128)(2,1)S(1)} %get-tuple-element.28), channel_id=1, source_target_pairs={{0,5},{1,6},{2,7},{3,0},{4,1},{5,2},{6,3},{7,4},{8,13},{9,14},{10,... | collective-permute-start | bytes 61448 | tf_op jit(solution)/shard_map/ppermute | solution.py:78
  40.9 5.4 %gather_fusion.4 = bf16[32,2,128,256]{3,2,1,0:T(8,128)(2,1)} fusion(bf16[40,2,128,256]{3,2,1,0:T(8,128)(2,1)} %param.19, s32[1024]{0:T(1024)S(1)} %get-tuple-element.48), kind=kCustom, calls=%fused_computation.6 | custom fusion | bytes 8388736 | tf_op jit(solution)/shard_map/gather | solution.py:68
  46.3 0.7 gather_fusion.2
  47.0 0.6 gather_fusion.3
  47.8 4.0 %select_select_fusion = bf16[32,2,128,256]{3,2,1,0:T(8,128)(2,1)} fusion(bf16[32,2,128,256]{3,2,1,0:T(8,128)(2,1)} %gather_fusion.4, pred[32]{0:T(512)(128)(4,1)S(1)} %fusion.77, pred[32,128]{1,0:T(8,128)(4,1)S(1)} %iota_compare_fusion.2, bf16[32,2,256]{2,1,0:T(2,128)(2,1)S(1)} %gather_fusion.3), kind=kLoop, calls=%fused_computation.8 | loop fusion | flops 4194304 | bytes 8425504 | tf_op jit(solution)/shard_map/jit(_where)/select_n | solution.py:120
  51.9 7.8 %all-to-all-start = ((bf16[32,2,128,256]{3,2,1,0:T(8,128)(2,1)}), bf16[32,2,128,256]{3,2,1,0:T(8,128)(2,1)}, u32[]{:S(2)}, u32[]{:S(2)}) async-start(bf16[32,2,128,256]{3,2,1,0:T(8,128)(2,1)} %select_select_fusion), calls=%async_computation.1 | async-start | bytes 8388608 | tf_op jit(solution)/shard_map/all_to_all | solution.py:125
  59.8 0.3 fusion.11
  60.1 2.6 %collective-permute-start.5 = (bf16[5,2048]{1,0:T(8,128)(2,1)S(1)}, bf16[5,2048]{1,0:T(8,128)(2,1)S(1)}, u32[]{:S(2)}, u32[]{:S(2)}) collective-permute-start(bf16[5,2048]{1,0:T(8,128)(2,1)S(1)} %get-tuple-element.27), channel_id=1, source_target_pairs={{0,6},{1,7},{2,0},{3,1},{4,2},{5,3},{6,4},{7,5},{8,14},{9,15},{10,... | collective-permute-start | bytes 61448 | tf_op jit(solution)/shard_map/ppermute | solution.py:78
  62.8 1.0 collective-permute-start.6
  63.8 4.6 %copy.96 = bf16[3,2048,256]{1,2,0:T(8,128)(2,1)} copy(bf16[3,2048,256]{2,1,0:T(8,128)(2,1)} %param.22) | data formatting | bytes 6291456 | tf_op jit(solution)/shard_map/reshape | solution.py:133
  68.5 0.9 fusion.63
  69.4 5.3 %fusion.90 = f32[640,768]{0,1:S(1)} fusion(bf16[640,2048]{1,0:T(8,128)(2,1)} %all-gather.2.cloned.1.call-done, bf16[2048,768]{0,1:T(8,128)(2,1)} %bitcast.157), kind=kOutput, calls=%fused_computation.178 | convolution fusion | flops 2013265920 | bytes 7733248
  74.7 0.1 fusion.35
  74.9 0.7 fusion.46
  75.6 2.0 %fusion.88 = (f32[2,640]{1,0:T(2,128)S(1)}, f32[2,640,640]{1,2,0:T(8,128)S(1)}) fusion(f32[2,640,640]{1,2,0:T(8,128)S(1)} %fusion.46, pred[640,640]{0,1:T(8,128)(4,1)S(1)} %fusion.11), kind=kOutput, calls=%fused_computation.176 | output fusion | flops 4915839 | bytes 6968320 | tf_op jit(solution)/shard_map/sub | solution.py:150
  77.6 0.5 fusion.13
  78.0 2.4 %convolution_convert_fusion = bf16[640,2048]{1,0:T(8,128)(2,1)} fusion(bf16[640,256]{0,1:T(8,128)(2,1)S(1)} %bitcast.164, bf16[256,2048]{1,0:T(8,128)(2,1)S(1)} %copy-done), kind=kOutput, calls=%fused_computation.12 | convolution fusion | flops 672399360 | bytes 3997696 | tf_op jit(solution)/shard_map/dot_general | solution.py:156
  80.4 1.0 collective-permute-start.7
  81.5 0.4 collective-permute-start.8
  81.8 2.1 %collective-permute-start.9 = (bf16[5,2048]{1,0:T(8,128)(2,1)S(1)}, bf16[5,2048]{1,0:T(8,128)(2,1)S(1)}, u32[]{:S(2)}, u32[]{:S(2)}) collective-permute-start(bf16[5,2048]{1,0:T(8,128)(2,1)S(1)} %fusion.63), channel_id=1, source_target_pairs={{0,3},{1,4},{2,5},{3,6},{4,7},{5,0},{6,1},{7,2},{8,11},{9,12},{10,... | collective-permute-start | bytes 61448 | tf_op jit(solution)/shard_map/ppermute | solution.py:89
  83.9 3.5 %collective-permute-start.10 = (bf16[5,2048]{1,0:T(8,128)(2,1)S(1)}, bf16[5,2048]{1,0:T(8,128)(2,1)S(1)}, u32[]{:S(2)}, u32[]{:S(2)}) collective-permute-start(bf16[5,2048]{1,0:T(8,128)(2,1)S(1)} %fusion.63), channel_id=1, source_target_pairs={{0,4},{1,5},{2,6},{3,7},{4,0},{5,1},{6,2},{7,3},{8,12},{9,13},{10,... | collective-permute-start | bytes 61448 | tf_op jit(solution)/shard_map/ppermute | solution.py:89
  87.4 2.2 %collective-permute-start.11 = (bf16[5,2048]{1,0:T(8,128)(2,1)S(1)}, bf16[5,2048]{1,0:T(8,128)(2,1)S(1)}, u32[]{:S(2)}, u32[]{:S(2)}) collective-permute-start(bf16[5,2048]{1,0:T(8,128)(2,1)S(1)} %fusion.63), channel_id=1, source_target_pairs={{0,5},{1,6},{2,7},{3,0},{4,1},{5,2},{6,3},{7,4},{8,13},{9,14},{10,... | collective-permute-start | bytes 61448 | tf_op jit(solution)/shard_map/ppermute | solution.py:89
  89.7 3.4 %slice_select_fusion = bf16[24,2,128,256]{3,2,1,0:T(8,128)(2,1)} fusion(bf16[40,2,128,256]{3,2,1,0:T(8,128)(2,1)} %param.19, pred[24,128]{1,0:T(8,128)(4,1)S(1)} %iota_compare_fusion.3, bf16[24,2,256]{2,1,0:T(2,128)(2,1)S(1)} %copy.90), kind=kLoop, calls=%fused_computation.13 | loop fusion | flops 1572864 | bytes 6319104 | tf_op jit(solution)/shard_map/jit(_where)/select_n | solution.py:164
  93.1 0.2 copy.88
  93.3 0.2 copy.89
  93.5 2.1 %collective-permute-start.12 = (bf16[5,2048]{1,0:T(8,128)(2,1)S(1)}, bf16[5,2048]{1,0:T(8,128)(2,1)S(1)}, u32[]{:S(2)}, u32[]{:S(2)}) collective-permute-start(bf16[5,2048]{1,0:T(8,128)(2,1)S(1)} %fusion.63), channel_id=1, source_target_pairs={{0,6},{1,7},{2,0},{3,1},{4,2},{5,3},{6,4},{7,5},{8,14},{9,15},{10,... | collective-permute-start | bytes 61448 | tf_op jit(solution)/shard_map/ppermute | solution.py:89
  95.6 1.6 %collective-permute-start.13 = (bf16[5,2048]{1,0:T(8,128)(2,1)S(1)}, bf16[5,2048]{1,0:T(8,128)(2,1)S(1)}, u32[]{:S(2)}, u32[]{:S(2)}) collective-permute-start(bf16[5,2048]{1,0:T(8,128)(2,1)S(1)} %fusion.63), channel_id=1, source_target_pairs={{0,7},{1,0},{2,1},{3,2},{4,3},{5,4},{6,5},{7,6},{8,15},{9,8},{10,9... | collective-permute-start | bytes 61448 | tf_op jit(solution)/shard_map/ppermute | solution.py:89
  97.2 1.6 %collective-permute-done.12 = bf16[5,2048]{1,0:T(8,128)(2,1)S(1)} collective-permute-done((bf16[5,2048]{1,0:T(8,128)(2,1)S(1)}, bf16[5,2048]{1,0:T(8,128)(2,1)S(1)}, u32[]{:S(2)}, u32[]{:S(2)}) %collective-permute-start.12) | collective-permute-done | bytes 20512 | tf_op jit(solution)/shard_map/ppermute | solution.py:89
  98.8 0.7 collective-permute-done.13
  99.5 0.6 gather_fusion.6
  100.2 0.7 gather_fusion.1
  101.0 8.9 %all-to-all-done = bf16[32,2,128,256]{3,2,1,0:T(8,128)(2,1)} async-done(((bf16[32,2,128,256]{3,2,1,0:T(8,128)(2,1)}), bf16[32,2,128,256]{3,2,1,0:T(8,128)(2,1)}, u32[]{:S(2)}, u32[]{:S(2)}) %all-to-all-start) | async-done | bytes 4194336 | tf_op jit(solution)/shard_map/all_to_all | solution.py:125
  109.9 0.5 broadcast.368
  110.4 0.7 reduce.1
  111.1 0.7 reshape.480
  111.8 9.1 %all-to-all-start.1 = ((bf16[32,2,1024]{2,1,0:T(2,128)(2,1)}), bf16[32,2,1024]{2,1,0:T(2,128)(2,1)S(1)}, u32[]{:S(2)}, u32[]{:S(2)}) async-start(bf16[32,2,1024]{2,1,0:T(2,128)(2,1)} %reshape.480), calls=%async_computation.2 | async-start | bytes 262144 | tf_op jit(solution)/shard_map/all_to_all | solution.py:176
  120.9 0.9 pad_maximum_fusion
  121.8 0.6 slice.130
  122.5 5.1 %all-to-all-done.1 = bf16[32,2,1024]{2,1,0:T(2,128)(2,1)S(1)} async-done(((bf16[32,2,1024]{2,1,0:T(2,128)(2,1)}), bf16[32,2,1024]{2,1,0:T(2,128)(2,1)S(1)}, u32[]{:S(2)}, u32[]{:S(2)}) %all-to-all-start.1) | async-done | bytes 131104 | tf_op jit(solution)/shard_map/all_to_all | solution.py:176
  127.6 0.1 reshape.481
  127.7 0.7 copy.101
  128.4 4.5 %reduce-scatter.2.cloned.1.call-done = bf16[80,2048]{1,0:T(8,128)(2,1)} async-done(((bf16[640,2048]{1,0:T(8,128)(2,1)}), bf16[80,2048]{1,0:T(8,128)(2,1)}) %reduce-scatter.2.cloned.1.call-update) | async-done | bytes 327696 | tf_op jit(solution)/shard_map/reduce_scatter | solution.py:167
  132.9 1.8 %fusion.33 = bf16[80,2048]{1,0:T(8,128)(2,1)} fusion(bf16[80,2048]{1,0:T(8,128)(2,1)S(1)} %copy-done.2, bf16[80,2048]{1,0:T(8,128)(2,1)} %reduce-scatter.2.cloned.1.call-done, f32[2048]{0:T(1024)S(1)} %copy-done.3), kind=kLoop, calls=%fused_computation.44 | loop fusion | flops 819200 | bytes 991232 | tf_op jit(solution)/shard_map/convert_element_type | solution.py:171
  134.7 4.7 %copy.111 = bf16[32,2,128,256]{3,2,1,0:T(8,128)(2,1)} copy(bf16[32,2,128,256]{3,2,1,0:T(8,128)(2,1)} %all-to-all-done) | data formatting | bytes 8388608
  (81 shorter events, 1.7 us)
Async XLA Ops:
  7.2 17.6 %copy-start = (bf16[256,2048]{1,0:T(8,128)(2,1)S(1)}, bf16[256,2048]{1,0:T(8,128)(2,1)}, u32[]{:S(2)}) copy-start(bf16[256,2048]{1,0:T(8,128)(2,1)} %param.24) | copy-start | bytes 3145732
  7.2 62.2 %all-gather.2.cloned.1.call-start = ((), (), s32[]{:S(2)}) async-start(), calls=%async_computation.3 | async-start | bytes 2949120 | tf_op jit(solution)/shard_map/all_gather | solution.py:131
  20.8 4.4 %copy-start.5 = (s32[16,1]{0,1:T(1,128)S(1)}, s32[16,1]{0,1:T(1,128)}, u32[]{:S(2)}) copy-start(s32[16,1]{0,1:T(1,128)} %param.18) | copy-start | bytes 196
  26.0 34.1 %collective-permute-start = (bf16[5,2048]{1,0:T(8,128)(2,1)S(1)}, bf16[5,2048]{1,0:T(8,128)(2,1)S(1)}, u32[]{:S(2)}, u32[]{:S(2)}) collective-permute-start(bf16[5,2048]{1,0:T(8,128)(2,1)S(1)} %get-tuple-element.25), channel_id=1, source_target_pairs={{0,1},{1,2},{2,3},{3,4},{4,5},{5,6},{6,7},{7,0},{8,9},{9,10},{10,1... | collective-permute-start | bytes 61448 | tf_op jit(solution)/shard_map/ppermute | solution.py:78
  28.0 34.8 %collective-permute-start.1 = (bf16[5,2048]{1,0:T(8,128)(2,1)S(1)}, bf16[5,2048]{1,0:T(8,128)(2,1)S(1)}, u32[]{:S(2)}, u32[]{:S(2)}) collective-permute-start(bf16[5,2048]{1,0:T(8,128)(2,1)S(1)} %get-tuple-element.31), channel_id=1, source_target_pairs={{0,2},{1,3},{2,4},{3,5},{4,6},{5,7},{6,0},{7,1},{8,10},{9,11},{10,... | collective-permute-start | bytes 61448 | tf_op jit(solution)/shard_map/ppermute | solution.py:78
  31.3 37.2 %collective-permute-start.2 = (bf16[5,2048]{1,0:T(8,128)(2,1)S(1)}, bf16[5,2048]{1,0:T(8,128)(2,1)S(1)}, u32[]{:S(2)}, u32[]{:S(2)}) collective-permute-start(bf16[5,2048]{1,0:T(8,128)(2,1)S(1)} %get-tuple-element.30), channel_id=1, source_target_pairs={{0,3},{1,4},{2,5},{3,6},{4,7},{5,0},{6,1},{7,2},{8,11},{9,12},{10,... | collective-permute-start | bytes 61448 | tf_op jit(solution)/shard_map/ppermute | solution.py:78
  35.4 33.1 %collective-permute-start.3 = (bf16[5,2048]{1,0:T(8,128)(2,1)S(1)}, bf16[5,2048]{1,0:T(8,128)(2,1)S(1)}, u32[]{:S(2)}, u32[]{:S(2)}) collective-permute-start(bf16[5,2048]{1,0:T(8,128)(2,1)S(1)} %get-tuple-element.29), channel_id=1, source_target_pairs={{0,4},{1,5},{2,6},{3,7},{4,0},{5,1},{6,2},{7,3},{8,12},{9,13},{10,... | collective-permute-start | bytes 61448 | tf_op jit(solution)/shard_map/ppermute | solution.py:78
  35.9 32.6 %collective-permute-start.4 = (bf16[5,2048]{1,0:T(8,128)(2,1)S(1)}, bf16[5,2048]{1,0:T(8,128)(2,1)S(1)}, u32[]{:S(2)}, u32[]{:S(2)}) collective-permute-start(bf16[5,2048]{1,0:T(8,128)(2,1)S(1)} %get-tuple-element.28), channel_id=1, source_target_pairs={{0,5},{1,6},{2,7},{3,0},{4,1},{5,2},{6,3},{7,4},{8,13},{9,14},{10,... | collective-permute-start | bytes 61448 | tf_op jit(solution)/shard_map/ppermute | solution.py:78
  40.9 5.4 %copy-start.1 = (s32[40]{0:T(128)S(1)}, s32[40]{0:T(128)}, u32[]{:S(2)}) copy-start(s32[40]{0:T(128)} %param.17) | copy-start | bytes 484
  51.9 7.9 %copy-start.4 = (s32[1,640]{1,0:T(1,128)S(1)}, s32[1,640]{1,0:T(1,128)}, u32[]{:S(2)}) copy-start(s32[1,640]{1,0:T(1,128)} %param.15) | copy-start | bytes 7684
  51.9 58.1 %all-to-all-start = ((bf16[32,2,128,256]{3,2,1,0:T(8,128)(2,1)}), bf16[32,2,128,256]{3,2,1,0:T(8,128)(2,1)}, u32[]{:S(2)}, u32[]{:S(2)}) async-start(bf16[32,2,128,256]{3,2,1,0:T(8,128)(2,1)} %select_select_fusion), calls=%async_computation.1 | async-start | bytes 8388608 | tf_op jit(solution)/shard_map/all_to_all | solution.py:125
  59.7 73.2 %reduce-scatter.2.cloned.1.call-start = ((), (), s32[]{:S(2)}) async-start(), calls=%async_computation.4 | async-start | bytes 2949120 | tf_op jit(solution)/shard_map/reduce_scatter | solution.py:167
  59.8 8.7 %copy-start.3 = (f32[2048]{0:T(1024)S(1)}, f32[2048]{0:T(1024)}, u32[]{:S(2)}) copy-start(f32[2048]{0:T(1024)} %param.25) | copy-start | bytes 24580
  60.1 8.3 %collective-permute-start.5 = (bf16[5,2048]{1,0:T(8,128)(2,1)S(1)}, bf16[5,2048]{1,0:T(8,128)(2,1)S(1)}, u32[]{:S(2)}, u32[]{:S(2)}) collective-permute-start(bf16[5,2048]{1,0:T(8,128)(2,1)S(1)} %get-tuple-element.27), channel_id=1, source_target_pairs={{0,6},{1,7},{2,0},{3,1},{4,2},{5,3},{6,4},{7,5},{8,14},{9,15},{10,... | collective-permute-start | bytes 61448 | tf_op jit(solution)/shard_map/ppermute | solution.py:78
  62.8 5.7 %collective-permute-start.6 = (bf16[5,2048]{1,0:T(8,128)(2,1)S(1)}, bf16[5,2048]{1,0:T(8,128)(2,1)S(1)}, u32[]{:S(2)}, u32[]{:S(2)}) collective-permute-start(bf16[5,2048]{1,0:T(8,128)(2,1)S(1)} %get-tuple-element.26), channel_id=1, source_target_pairs={{0,7},{1,0},{2,1},{3,2},{4,3},{5,4},{6,5},{7,6},{8,15},{9,8},{10,9... | collective-permute-start | bytes 61448 | tf_op jit(solution)/shard_map/ppermute | solution.py:78
  80.4 13.0 %collective-permute-start.7 = (bf16[5,2048]{1,0:T(8,128)(2,1)S(1)}, bf16[5,2048]{1,0:T(8,128)(2,1)S(1)}, u32[]{:S(2)}, u32[]{:S(2)}) collective-permute-start(bf16[5,2048]{1,0:T(8,128)(2,1)S(1)} %fusion.63), channel_id=1, source_target_pairs={{0,1},{1,2},{2,3},{3,4},{4,5},{5,6},{6,7},{7,0},{8,9},{9,10},{10,1... | collective-permute-start | bytes 61448 | tf_op jit(solution)/shard_map/ppermute | solution.py:89
  81.5 14.1 %collective-permute-start.8 = (bf16[5,2048]{1,0:T(8,128)(2,1)S(1)}, bf16[5,2048]{1,0:T(8,128)(2,1)S(1)}, u32[]{:S(2)}, u32[]{:S(2)}) collective-permute-start(bf16[5,2048]{1,0:T(8,128)(2,1)S(1)} %fusion.63), channel_id=1, source_target_pairs={{0,2},{1,3},{2,4},{3,5},{4,6},{5,7},{6,0},{7,1},{8,10},{9,11},{10,... | collective-permute-start | bytes 61448 | tf_op jit(solution)/shard_map/ppermute | solution.py:89
  81.8 15.3 %collective-permute-start.9 = (bf16[5,2048]{1,0:T(8,128)(2,1)S(1)}, bf16[5,2048]{1,0:T(8,128)(2,1)S(1)}, u32[]{:S(2)}, u32[]{:S(2)}) collective-permute-start(bf16[5,2048]{1,0:T(8,128)(2,1)S(1)} %fusion.63), channel_id=1, source_target_pairs={{0,3},{1,4},{2,5},{3,6},{4,7},{5,0},{6,1},{7,2},{8,11},{9,12},{10,... | collective-permute-start | bytes 61448 | tf_op jit(solution)/shard_map/ppermute | solution.py:89
  83.9 13.2 %collective-permute-start.10 = (bf16[5,2048]{1,0:T(8,128)(2,1)S(1)}, bf16[5,2048]{1,0:T(8,128)(2,1)S(1)}, u32[]{:S(2)}, u32[]{:S(2)}) collective-permute-start(bf16[5,2048]{1,0:T(8,128)(2,1)S(1)} %fusion.63), channel_id=1, source_target_pairs={{0,4},{1,5},{2,6},{3,7},{4,0},{5,1},{6,2},{7,3},{8,12},{9,13},{10,... | collective-permute-start | bytes 61448 | tf_op jit(solution)/shard_map/ppermute | solution.py:89
  87.4 9.8 %collective-permute-start.11 = (bf16[5,2048]{1,0:T(8,128)(2,1)S(1)}, bf16[5,2048]{1,0:T(8,128)(2,1)S(1)}, u32[]{:S(2)}, u32[]{:S(2)}) collective-permute-start(bf16[5,2048]{1,0:T(8,128)(2,1)S(1)} %fusion.63), channel_id=1, source_target_pairs={{0,5},{1,6},{2,7},{3,0},{4,1},{5,2},{6,3},{7,4},{8,13},{9,14},{10,... | collective-permute-start | bytes 61448 | tf_op jit(solution)/shard_map/ppermute | solution.py:89
  93.5 39.4 %copy-start.2 = (bf16[80,2048]{1,0:T(8,128)(2,1)S(1)}, bf16[80,2048]{1,0:T(8,128)(2,1)}, u32[]{:S(2)}) copy-start(bf16[80,2048]{1,0:T(8,128)(2,1)} %param.14) | copy-start | bytes 983044
  93.5 5.3 %collective-permute-start.12 = (bf16[5,2048]{1,0:T(8,128)(2,1)S(1)}, bf16[5,2048]{1,0:T(8,128)(2,1)S(1)}, u32[]{:S(2)}, u32[]{:S(2)}) collective-permute-start(bf16[5,2048]{1,0:T(8,128)(2,1)S(1)} %fusion.63), channel_id=1, source_target_pairs={{0,6},{1,7},{2,0},{3,1},{4,2},{5,3},{6,4},{7,5},{8,14},{9,15},{10,... | collective-permute-start | bytes 61448 | tf_op jit(solution)/shard_map/ppermute | solution.py:89
  95.6 3.9 %collective-permute-start.13 = (bf16[5,2048]{1,0:T(8,128)(2,1)S(1)}, bf16[5,2048]{1,0:T(8,128)(2,1)S(1)}, u32[]{:S(2)}, u32[]{:S(2)}) collective-permute-start(bf16[5,2048]{1,0:T(8,128)(2,1)S(1)} %fusion.63), channel_id=1, source_target_pairs={{0,7},{1,0},{2,1},{3,2},{4,3},{5,4},{6,5},{7,6},{8,15},{9,8},{10,9... | collective-permute-start | bytes 61448 | tf_op jit(solution)/shard_map/ppermute | solution.py:89
  111.8 15.7 %all-to-all-start.1 = ((bf16[32,2,1024]{2,1,0:T(2,128)(2,1)}), bf16[32,2,1024]{2,1,0:T(2,128)(2,1)S(1)}, u32[]{:S(2)}, u32[]{:S(2)}) async-start(bf16[32,2,1024]{2,1,0:T(2,128)(2,1)} %reshape.480), calls=%async_computation.2 | async-start | bytes 262144 | tf_op jit(solution)/shard_map/all_to_all | solution.py:176
Sparse Core Ops, SparseCore 0:
  11.8 50.3 all-gather.1
  89.8 43.0 reduce-scatter.1

commit v7 on v5

--- a/solution.py
+++ b/solution.py
@@ -122,6 +122,7 @@
         updated_rows(past_cache, key_new, value_new, request_ages, picks),
         jnp.zeros((), jnp.bfloat16),
     )
+    send_cache, partial_value = lax.optimization_barrier((send_cache, partial_value))
     moved_cache = lax.all_to_all(send_cache, "rep", split_axis=0, concat_axis=0, tiled=True)
     tp_count = lax.axis_size("tp")
     decode_pieces = partial_value.astype(jnp.bfloat16).reshape(
@@ -134,11 +135,10 @@
     queries = (projected[0] + qkv_bias[0]).astype(jnp.bfloat16)
     key_rows = (projected[1] + qkv_bias[1]).astype(jnp.bfloat16)
     value_rows = (projected[2] + qkv_bias[2]).astype(jnp.bfloat16)
-    head_q = queries.reshape(total_rows, heads_here, HEAD_DIM)
-    head_k = key_rows.reshape(total_rows, heads_here, HEAD_DIM)
-    head_v = value_rows.reshape(total_rows, heads_here, HEAD_DIM)
+    diag = jnp.arange(heads_here)[:, None] == (jnp.arange(width) // HEAD_DIM)[None, :]
+    q_blocks = jnp.where(diag[:, None, :], queries[None], jnp.zeros((), jnp.bfloat16))
     scores = jnp.einsum(
-        "qhe,khe->hqk", head_q, head_k, preferred_element_type=jnp.float32
+        "hqc,kc->hqk", q_blocks, key_rows, preferred_element_type=jnp.float32
     ) * HEAD_DIM ** (-0.5)
     pieces = prompt_pieces[0]
     position = jnp.arange(total_rows)
@@ -147,15 +147,19 @@
     highest = jnp.max(scores, axis=-1, keepdims=True)
     weights = jnp.exp(scores - highest)
     probs = (weights / jnp.sum(weights, axis=-1, keepdims=True)).astype(jnp.bfloat16)
-    context = jnp.einsum("hqk,khe->qhe", probs, head_v, preferred_element_type=jnp.float32)
-    context = context.reshape(total_rows, width).astype(jnp.bfloat16)
+    mixed = jnp.einsum("hqk,kc->hqc", probs, value_rows, preferred_element_type=jnp.float32)
+    context = jnp.sum(jnp.where(diag[:, None, :], mixed, 0.0), axis=0).astype(jnp.bfloat16)
     prompt_partial = jnp.dot(context, out_weight, preferred_element_type=jnp.float32).astype(
         jnp.bfloat16
     )
     prompt_partial, own_out, key_rows, value_rows, key_new, value_new = lax.optimization_barrier(
         (prompt_partial, own_out, key_rows, value_rows, key_new, value_new)
     )
-    kept_cache = updated_rows(past_cache, key_new, value_new, request_ages, jnp.arange(staying))
+    written = (jnp.arange(past_cache.shape[2])[None, :] == request_ages[:staying, None])
+    fresh = jnp.stack([key_new[:staying], value_new[:staying]], axis=1)
+    kept_cache = jnp.where(
+        written[:, None, :, None], fresh[:, :, None, :], past_cache[:staying]
+    )
     attended = lax.psum_scatter(prompt_partial, "tp", scatter_dimension=0, tiled=True).astype(
         jnp.float32
     )

time: 157 us -> 155 us (0.987); the launches traced: 153 us -> 154 us
  local copies, waits for them, and re-layouts: 43.4 us -> 30.2 us
  waiting for transfers between devices: 2.13 us -> 14.1 us
    reduce_scatter x1, waiting for transfers between devices: 0.01 us -> 5.53 us  [on_device(): lax.psum_scatter(prompt_partial, 'tp', scatter_dimension=0, tiled=True)]
    gather x2 -> x1, local copies, waits for them, and re-layouts: 10.5 us -> 5.32 us  [updated_rows(): cache[picks]]
    squeeze x2 -> x0, local copies, waits for them, and re-layouts: 4.33 us -> none  [the longest x1 2.17 us: on_device(): queries = (projected[0] + qkv_bias[0]).astype(jnp.bfloat16)]
    ppermute x7, waiting for transfers between devices: 0.02 us -> 2.64 us  [scatter_over_tp(): lax.ppermute(rolled[shift], 'tp', [(i, (i + shift) % n) for i in range(n)])]
    all_to_all x1, waiting for transfers between devices: 1.84 us -> 4.02 us  [on_device(): lax.all_to_all(send_rows, 'rep', split_axis=0, concat_axis=0, tiled=True)]
    all_to_all x1, starting transfers between devices: 7.38 us -> 9.08 us  [on_device(): lax.all_to_all(send_rows, 'rep', split_axis=0, concat_axis=0, tiled=True)]
    select_n x1, other arithmetic: 3.98 us -> 2.41 us  [on_device(): jnp.where(has[:, None, None, None], updated_rows(past_cache, key_new, val...]
    unnamed x60 -> x65, local copies, waits for them, and re-layouts: 13.5 us -> 12.5 us
  transfers between devices with their start and end apart: 18 -> 18, of which waited for: 2 -> 7; matrix products, arithmetic and copies ran while one was open for 51% -> 42% of each run, Pallas kernels for 0% -> 0%
where the time goes in v7:
time: 155 us; the launch traced here: 154 us
  starting transfers between devices  47.6 us (31%)
  other arithmetic  31.8 us (21%)
  local copies, waits for them, and re-layouts  30.2 us (19%)
  matrix products  15.8 us (10%)
  between operations  14.6 us (9%)
  waiting for transfers between devices  14.1 us (9%)
    ppermute x7, starting transfers between devices, scatter_over_tp(): lax.ppermute(rolled[shift], 'tp', [(i, (i + shift) % n) for i in range(n)])  18.3 us
    unnamed x65, local copies, waits for them, and re-layouts  12.5 us
    ppermute x7, starting transfers between devices, gather_over_tp(): lax.ppermute(own_out, 'tp', [(i, (i + shift) % n) for i in range(n)])  12.4 us
    all_to_all x1, starting transfers between devices, on_device(): lax.all_to_all(send_rows, 'rep', split_axis=0, concat_axis=0, tiled=True)  9.08 us
    all_to_all x1, starting transfers between devices, on_device(): lax.all_to_all(send_cache, 'rep', split_axis=0, concat_axis=0, tiled=True)  7.74 us
    reduce_scatter x1, waiting for transfers between devices, on_device(): lax.psum_scatter(prompt_partial, 'tp', scatter_dimension=0, tiled=True)  5.53 us
    gather x1, local copies, waits for them, and re-layouts, updated_rows(): cache[picks]  5.32 us
    all_to_all x1, waiting for transfers between devices, on_device(): lax.all_to_all(send_rows, 'rep', split_axis=0, concat_axis=0, tiled=True)  4.02 us
  transfers between devices with their start and end apart: 18, of which 7 were waited for; matrix products, arithmetic and copies ran while one was open for 42% of the time, Pallas kernels for 0%

profile of v7, /device:TPU:2, one launch (start us, length us, event | category | flops | bytes accessed | tf_op | source)
XLA Modules:
  0.0 154.0 jit_solution(5662188117032763120)
XLA Ops:
  7.2 1.3 convert_reduce_fusion
  8.5 1.2 fusion.32
  9.8 2.0 %fusion.35 = bf16[80,2048]{1,0:T(8,128)(2,1)} fusion(bf16[80,2048]{1,0:T(8,128)(2,1)} %param.14, f32[2048]{0:T(1024)} %param.21, f32[2048]{0:T(1024)} %param.20, f32[80]{0:T(128)S(1)} %add_rsqrt_fusion.1, f32[80]{0:T(128)S(1)} %broadcast_multiply_fusion.1), kind=kLoop, calls=%fused_computation.44 | loop fusion | flops 983040 | bytes 672384 | tf_op jit(solution)/shard_map/convert_element_type | solution.py:18
  11.8 0.8 fusion.98
  12.6 1.0 convert_reduce_fusion.1
  13.6 1.1 fusion.48
  14.8 0.7 iota_compare_fusion.1
  15.5 1.6 %convolution_bitcast_fusion = f32[3,40,256]{2,1,0:T(8,128)S(1)} fusion(bf16[3,2048,256]{2,1,0:T(8,128)(2,1)S(1)} %copy-done, bf16[40,2048]{1,0:T(8,128)(2,1)} %param.16, f32[2048]{0:T(1024)} %param.21, f32[2048]{0:T(1024)} %param.20, f32[40]{0:T(128)S(1)} %add_rsqrt_fusion, f32[40]{0:T(128)S(1)} %broadcast_multiply_fusion), kind=kOutput, calls=%fused_computation.31 | convolution fusion | flops 126320640 | bytes 3449152 | tf_op jit(solution)/shard_map/rd,cde->cre/dot_general | solution.py:27
  17.8 2.6 %fusion.100 = (f32[40,2]{1,0:T(8,128)S(1)}, f32[40,2,128]{2,1,0:T(2,128)S(1)}) fusion(bf16[40,2,128,256]{3,2,1,0:T(8,128)(2,1)} %param.19, pred[2,256]{1,0:T(4,128)(4,1)S(1)} %iota_compare_fusion.5, bf16[40,256]{1,0:T(8,128)(2,1)S(1)} %get-tuple-element.37, pred[40,128]{1,0:T(8,128)(4,1)S(1)} %iota_compare_fusion.1), kind=kOutput, calls=%fused_computation.187 | convolution fusion | flops 5294000 | bytes 2688832 | tf_op jit(solution)/shard_map/rhc,rlc->rhl/dot_general | solution.py:36
  21.2 5.3 %gather_fusion.2 = bf16[32,2,128,256]{3,2,1,0:T(8,128)(2,1)} fusion(bf16[40,2,128,256]{3,2,1,0:T(8,128)(2,1)} %param.19, s32[1024]{0:T(1024)S(1)} %pad_clamp_fusion.3), kind=kCustom, calls=%fused_computation.4 | custom fusion | bytes 8388736 | tf_op jit(solution)/shard_map/gather | solution.py:68
  26.6 1.2 gather_fusion
  28.6 0.7 gather_fusion.3
  29.4 0.6 fusion.79
  30.1 0.8 gather_fusion.1
  30.9 0.9 fusion.87
  31.8 1.0 iota_compare_fusion.2
  32.7 2.3 %fusion.21 = f32[40,256]{1,0:T(8,128)S(1)} fusion(bf16[40,2,128,256]{3,2,1,0:T(8,128)(2,1)} %param.19, pred[2,256]{1,0:T(4,128)(4,1)} %copy-done.20, f32[40,2,128]{2,1,0:T(2,128)S(1)} %get-tuple-element.51, f32[40,2]{1,0:T(8,128)S(1)} %copy.61, f32[40,2]{1,0:T(8,128)S(1)} %copy.59), kind=kOutput, calls=%fused_computation.33 | convolution fusion | flops 5304320 | bytes 2705024 | tf_op jit(solution)/shard_map/rhl,rlc->rhc/dot_general | solution.py:56
  35.1 1.5 fusion.81
  36.6 2.4 %select_select_fusion = bf16[32,2,128,256]{3,2,1,0:T(8,128)(2,1)} fusion(bf16[32,2,128,256]{3,2,1,0:T(8,128)(2,1)S(1)} %copy-done.2, pred[32]{0:T(512)(128)(4,1)S(1)} %fusion.87, pred[32,128]{1,0:T(8,128)(4,1)S(1)} %iota_compare_fusion.2, bf16[32,2,256]{2,1,0:T(2,128)(2,1)S(1)} %gather_fusion.1), kind=kLoop, calls=%fused_computation.8 | loop fusion | flops 4194304 | bytes 8425504 | tf_op jit(solution)/shard_map/jit(_where)/select_n | solution.py:120
  39.0 0.8 reshape.410
  39.8 1.6 %gather_fusion.5 = bf16[8,5,2048]{2,1,0:T(8,128)(2,1)S(1)} fusion(bf16[8,5,2048]{2,1,0:T(8,128)(2,1)} %reshape.410, s32[1024]{0:T(1024)} %get-tuple-element.52), kind=kCustom, calls=%fused_computation.clone | custom fusion | bytes 327712 | tf_op jit(solution)/shard_map/jit(_take)/gather | solution.py:75
  41.6 0.7 copy-done.6
  42.3 0.7 slice_bitcast_fusion.8
  42.9 1.9 %collective-permute-start = (bf16[5,2048]{1,0:T(8,128)(2,1)}, bf16[5,2048]{1,0:T(8,128)(2,1)}, u32[]{:S(2)}, u32[]{:S(2)}) collective-permute-start(bf16[5,2048]{1,0:T(8,128)(2,1)} %get-tuple-element.29), channel_id=1, source_target_pairs={{0,1},{1,2},{2,3},{3,4},{4,5},{5,6},{6,7},{7,0},{8,9},{9,10},{10,1... | collective-permute-start | bytes 61448 | tf_op jit(solution)/shard_map/ppermute | solution.py:78
  44.8 3.3 %collective-permute-start.1 = (bf16[5,2048]{1,0:T(8,128)(2,1)}, bf16[5,2048]{1,0:T(8,128)(2,1)}, u32[]{:S(2)}, u32[]{:S(2)}) collective-permute-start(bf16[5,2048]{1,0:T(8,128)(2,1)} %get-tuple-element.35), channel_id=1, source_target_pairs={{0,2},{1,3},{2,4},{3,5},{4,6},{5,7},{6,0},{7,1},{8,10},{9,11},{10,... | collective-permute-start | bytes 61448 | tf_op jit(solution)/shard_map/ppermute | solution.py:78
  48.1 4.0 %collective-permute-start.2 = (bf16[5,2048]{1,0:T(8,128)(2,1)}, bf16[5,2048]{1,0:T(8,128)(2,1)}, u32[]{:S(2)}, u32[]{:S(2)}) collective-permute-start(bf16[5,2048]{1,0:T(8,128)(2,1)} %get-tuple-element.34), channel_id=1, source_target_pairs={{0,3},{1,4},{2,5},{3,6},{4,7},{5,0},{6,1},{7,2},{8,11},{9,12},{10,... | collective-permute-start | bytes 61448 | tf_op jit(solution)/shard_map/ppermute | solution.py:78
  52.7 5.0 %collective-permute-start.4 = (bf16[5,2048]{1,0:T(8,128)(2,1)}, bf16[5,2048]{1,0:T(8,128)(2,1)}, u32[]{:S(2)}, u32[]{:S(2)}) collective-permute-start(bf16[5,2048]{1,0:T(8,128)(2,1)} %get-tuple-element.32), channel_id=1, source_target_pairs={{0,5},{1,6},{2,7},{3,0},{4,1},{5,2},{6,3},{7,4},{8,13},{9,14},{10,... | collective-permute-start | bytes 61448 | tf_op jit(solution)/shard_map/ppermute | solution.py:78
  57.7 7.7 %all-to-all-start = ((bf16[32,2,128,256]{3,2,1,0:T(8,128)(2,1)}), bf16[32,2,128,256]{3,2,1,0:T(8,128)(2,1)}, u32[]{:S(2)}, u32[]{:S(2)}) async-start(bf16[32,2,128,256]{3,2,1,0:T(8,128)(2,1)} %select_select_fusion), calls=%async_computation.1 | async-start | bytes 8388608 | tf_op jit(solution)/shard_map/all_to_all | solution.py:126
  66.1 0.7 iota_compare_fusion.3
  66.7 1.0 fusion.13
  68.4 2.6 %collective-permute-start.5 = (bf16[5,2048]{1,0:T(8,128)(2,1)}, bf16[5,2048]{1,0:T(8,128)(2,1)}, u32[]{:S(2)}, u32[]{:S(2)}) collective-permute-start(bf16[5,2048]{1,0:T(8,128)(2,1)} %get-tuple-element.31), channel_id=1, source_target_pairs={{0,6},{1,7},{2,0},{3,1},{4,2},{5,3},{6,4},{7,5},{8,14},{9,15},{10,... | collective-permute-start | bytes 61448 | tf_op jit(solution)/shard_map/ppermute | solution.py:78
  71.0 1.0 collective-permute-start.6
  72.6 1.1 collective-permute-done.5
  73.7 1.5 collective-permute-done.6
  75.2 1.7 %fusion.72 = bf16[5,2048]{1,0:T(8,128)(2,1)} fusion(bf16[5,2048]{1,0:T(8,128)(2,1)} %collective-permute-done.6, bf16[5,2048]{1,0:T(8,128)(2,1)} %collective-permute-done.5, bf16[5,2048]{1,0:T(8,128)(2,1)} %collective-permute-done.4, bf16[5,2048]{1,0:T(8,128)(2,1)} %collective-permute-done.3, bf16[5,2048]{1,0:T(8,128)(2,1)} %collective-permute-done.2, ...), kind=kLoop, calls=%fused_computation.92 | loop fusion | flops 194560 | bytes 212996 | tf_op jit(solution)/shard_map/convert_element_type | solution.py:81
  76.9 3.9 %fusion.15 = f32[3,640,256]{2,1,0:T(8,128)S(1)} fusion(bf16[3,2048,256]{2,1,0:T(8,128)(2,1)S(1)} %copy-done, bf16[640,2048]{1,0:T(8,128)(2,1)} %all-gather.2.cloned.1.call-done), kind=kOutput, calls=%fused_computation.29 | convolution fusion | flops 2013265920 | bytes 7733248 | tf_op jit(solution)/shard_map/rd,cde->cre/dot_general | solution.py:133
  81.1 0.7 copy-done.4
  81.8 0.6 fusion.43
  82.4 2.0 %fusion.99 = (f32[2,640]{1,0:T(2,128)S(1)}, f32[2,640,640]{1,2,0:T(8,128)S(1)}) fusion(f32[2,640,640]{1,2,0:T(8,128)S(1)} %fusion.43, pred[640,640]{0,1:T(8,128)(4,1)S(1)} %fusion.13), kind=kOutput, calls=%fused_computation.186 | output fusion | flops 4915839 | bytes 6968320 | tf_op jit(solution)/shard_map/sub | solution.py:148
  84.4 0.8 select_reduce_fusion
  85.6 2.4 %convolution_convert_fusion = bf16[640,2048]{1,0:T(8,128)(2,1)} fusion(bf16[256,2048]{1,0:T(8,128)(2,1)S(1)} %copy-done.3, bf16[640,256]{1,0:T(8,128)(2,1)S(1)} %select_reduce_fusion), kind=kOutput, calls=%fused_computation.12 | convolution fusion | flops 672399360 | bytes 3997696 | tf_op jit(solution)/shard_map/dot_general | solution.py:152
  88.0 1.7 %collective-permute-start.8 = (bf16[5,2048]{1,0:T(8,128)(2,1)S(1)}, bf16[5,2048]{1,0:T(8,128)(2,1)S(1)}, u32[]{:S(2)}, u32[]{:S(2)}) collective-permute-start(bf16[5,2048]{1,0:T(8,128)(2,1)S(1)} %copy-done.9), channel_id=1, source_target_pairs={{0,2},{1,3},{2,4},{3,5},{4,6},{5,7},{6,0},{7,1},{8,10},{9,11},{10,... | collective-permute-start | bytes 61448 | tf_op jit(solution)/shard_map/ppermute | solution.py:89
  89.7 3.6 %collective-permute-start.9 = (bf16[5,2048]{1,0:T(8,128)(2,1)S(1)}, bf16[5,2048]{1,0:T(8,128)(2,1)S(1)}, u32[]{:S(2)}, u32[]{:S(2)}) collective-permute-start(bf16[5,2048]{1,0:T(8,128)(2,1)S(1)} %copy-done.9), channel_id=1, source_target_pairs={{0,3},{1,4},{2,5},{3,6},{4,7},{5,0},{6,1},{7,2},{8,11},{9,12},{10,... | collective-permute-start | bytes 61448 | tf_op jit(solution)/shard_map/ppermute | solution.py:89
  93.3 1.5 collective-permute-start.10
  94.8 4.2 %collective-permute-start.11 = (bf16[5,2048]{1,0:T(8,128)(2,1)S(1)}, bf16[5,2048]{1,0:T(8,128)(2,1)S(1)}, u32[]{:S(2)}, u32[]{:S(2)}) collective-permute-start(bf16[5,2048]{1,0:T(8,128)(2,1)S(1)} %copy-done.9), channel_id=1, source_target_pairs={{0,5},{1,6},{2,7},{3,0},{4,1},{5,2},{6,3},{7,4},{8,13},{9,14},{10,... | collective-permute-start | bytes 61448 | tf_op jit(solution)/shard_map/ppermute | solution.py:89
  99.1 0.6 bitcast_dynamic-update-slice_fusion.7
  99.7 3.4 %slice_select_fusion = bf16[24,2,128,256]{3,2,1,0:T(8,128)(2,1)} fusion(bf16[40,2,128,256]{3,2,1,0:T(8,128)(2,1)} %param.19, pred[24,128]{1,0:T(8,128)(4,1)S(1)} %copy-done.18, bf16[24,2,256]{2,1,0:T(2,128)(2,1)S(1)} %copy.64), kind=kLoop, calls=%fused_computation.13 | loop fusion | flops 1572864 | bytes 6319104 | tf_op jit(solution)/shard_map/jit(_where)/select_n | solution.py:160
  103.1 1.0 collective-permute-start.12
  109.2 1.6 %gather_fusion.6 = bf16[8,5,2048]{2,1,0:T(8,128)(2,1)S(1)} fusion(bf16[8,5,2048]{2,1,0:T(8,128)(2,1)} %bitcast_dynamic-update-slice_fusion, s32[1024]{0:T(1024)} %pad_clamp_fusion), kind=kCustom, calls=%fused_computation.1.clone | custom fusion | bytes 327712 | tf_op jit(solution)/shard_map/jit(_take)/gather | solution.py:91
  110.9 0.8 broadcast_select_fusion
  111.7 1.0 reshape.411
  112.7 0.8 gather_fusion.4
  113.5 0.7 broadcast_select_fusion.2
  114.2 1.4 all-to-all-done
  116.2 1.6 %reduce.1 = bf16[32,2048]{1,0:T(8,128)(2,1)S(1)} reduce(bf16[32,1,2048]{2,0,1:T(8,128)(2,1)} %bitcast.146, bf16[]{:T(256)} %broadcast.382), dimensions={1}, to_apply=%copy.65.reduce_sub_computation | reduce | bytes 262146 | tf_op jit(solution)/shard_map/all_to_all | solution.py:172
  117.7 0.7 reshape.480
  118.5 9.1 %all-to-all-start.1 = ((bf16[32,2,1024]{2,1,0:T(2,128)(2,1)}), bf16[32,2,1024]{2,1,0:T(2,128)(2,1)S(1)}, u32[]{:S(2)}, u32[]{:S(2)}) async-start(bf16[32,2,1024]{2,1,0:T(2,128)(2,1)} %reshape.480), calls=%async_computation.2 | async-start | bytes 262144 | tf_op jit(solution)/shard_map/all_to_all | solution.py:172
  127.6 2.0 %pad_maximum_fusion = bf16[2,640,256]{2,1,0:T(8,128)(2,1)} fusion(bf16[1,640,256]{2,1,0:T(8,128)(2,1)} %bitcast.145, bf16[1,640,256]{2,1,0:T(8,128)(2,1)} %bitcast.144), kind=kLoop, calls=%fused_computation.55 | loop fusion | flops 327680 | bytes 1310720 | tf_op jit(solution)/shard_map/stack | solution.py:168
  129.5 0.6 slice.127
  130.2 4.0 %all-to-all-done.1 = bf16[32,2,1024]{2,1,0:T(2,128)(2,1)S(1)} async-done(((bf16[32,2,1024]{2,1,0:T(2,128)(2,1)}), bf16[32,2,1024]{2,1,0:T(2,128)(2,1)S(1)}, u32[]{:S(2)}, u32[]{:S(2)}) %all-to-all-start.1) | async-done | bytes 131104 | tf_op jit(solution)/shard_map/all_to_all | solution.py:172
  134.3 0.7 copy.71
  135.1 5.5 %reduce-scatter.2.cloned.1.call-done = bf16[80,2048]{1,0:T(8,128)(2,1)} async-done(((bf16[640,2048]{1,0:T(8,128)(2,1)}), bf16[80,2048]{1,0:T(8,128)(2,1)}) %reduce-scatter.2.cloned.1.call-update) | async-done | bytes 327696 | tf_op jit(solution)/shard_map/reduce_scatter | solution.py:163
  140.6 1.9 %fusion.37 = bf16[80,2048]{1,0:T(8,128)(2,1)} fusion(bf16[80,2048]{1,0:T(8,128)(2,1)} %param.14, bf16[80,2048]{1,0:T(8,128)(2,1)} %reduce-scatter.2.cloned.1.call-done, f32[2048]{0:T(1024)S(1)} %copy-done.11), kind=kLoop, calls=%fused_computation.46 | loop fusion | flops 819200 | bytes 991232 | tf_op jit(solution)/shard_map/convert_element_type | solution.py:167
  142.5 4.7 %copy.81 = bf16[32,2,128,256]{3,2,1,0:T(8,128)(2,1)} copy(bf16[32,2,128,256]{3,2,1,0:T(8,128)(2,1)} %all-to-all-done) | data formatting | bytes 8388608
  (121 shorter events, 11.4 us)
Async XLA Ops:
  7.2 8.4 %copy-start = (bf16[3,2048,256]{2,1,0:T(8,128)(2,1)S(1)}, bf16[3,2048,256]{2,1,0:T(8,128)(2,1)}, u32[]{:S(2)}) copy-start(bf16[3,2048,256]{2,1,0:T(8,128)(2,1)} %param.22) | copy-start | bytes 9437188
  7.2 69.7 %all-gather.2.cloned.1.call-start = ((), (), s32[]{:S(2)}) async-start(), calls=%async_computation.3 | async-start | bytes 2949120 | tf_op jit(solution)/shard_map/all_gather | solution.py:132
  12.6 7.9 %copy-start.16 = (f32[1,256]{1,0:T(1,128)}, f32[1,256]{1,0:T(1,128)S(1)}, u32[]{:S(2)}) copy-start(f32[1,256]{1,0:T(1,128)S(1)} %get-tuple-element.43) | copy-start | bytes 3076
  12.6 8.0 %copy-start.14 = (f32[1,256]{1,0:T(1,128)}, f32[1,256]{1,0:T(1,128)S(1)}, u32[]{:S(2)}) copy-start(f32[1,256]{1,0:T(1,128)S(1)} %get-tuple-element.44) | copy-start | bytes 3076
  12.6 16.8 %copy-start.12 = (f32[1,256]{1,0:T(1,128)}, f32[1,256]{1,0:T(1,128)S(1)}, u32[]{:S(2)}) copy-start(f32[1,256]{1,0:T(1,128)S(1)} %get-tuple-element.45) | copy-start | bytes 3076
  14.8 5.6 %copy-start.20 = (pred[2,256]{1,0:T(4,128)(4,1)}, pred[2,256]{1,0:T(4,128)(4,1)S(1)}, u32[]{:S(2)}) copy-start(pred[2,256]{1,0:T(4,128)(4,1)S(1)} %iota_compare_fusion.5) | copy-start | bytes 1540
  15.5 5.4 %copy-start.26 = (s32[16,1]{0,1:T(1,128)S(1)}, s32[16,1]{0,1:T(1,128)}, u32[]{:S(2)}) copy-start(s32[16,1]{0,1:T(1,128)} %param.18) | copy-start | bytes 196
  17.8 17.2 %copy-start.7 = (bf16[40,256]{1,0:T(8,128)(2,1)}, bf16[40,256]{1,0:T(8,128)(2,1)S(1)}, u32[]{:S(2)}) copy-start(bf16[40,256]{1,0:T(8,128)(2,1)S(1)} %get-tuple-element.23) | copy-start | bytes 61444
  21.2 5.3 %copy-start.19 = (s32[1024]{0:T(1024)}, s32[1024]{0:T(1024)S(1)}, u32[]{:S(2)}) copy-start(s32[1024]{0:T(1024)S(1)} %pad_clamp_fusion.3) | copy-start | bytes 12292
  21.2 5.3 %copy-start.1 = (s32[40]{0:T(128)S(1)}, s32[40]{0:T(128)}, u32[]{:S(2)}) copy-start(s32[40]{0:T(128)} %param.17) | copy-start | bytes 484
  30.8 5.7 %copy-start.2 = (bf16[32,2,128,256]{3,2,1,0:T(8,128)(2,1)S(1)}, bf16[32,2,128,256]{3,2,1,0:T(8,128)(2,1)}, u32[]{:S(2)}) copy-start(bf16[32,2,128,256]{3,2,1,0:T(8,128)(2,1)} %gather_fusion.2) | copy-start | bytes 12582916
  31.8 7.3 %copy-start.23 = (pred[32]{0:T(512)(128)(4,1)}, pred[32]{0:T(512)(128)(4,1)S(1)}, u32[]{:S(2)}) copy-start(pred[32]{0:T(512)(128)(4,1)S(1)} %fusion.87) | copy-start | bytes 100
  41.5 0.7 copy-start.6
  42.9 25.4 %collective-permute-start = (bf16[5,2048]{1,0:T(8,128)(2,1)}, bf16[5,2048]{1,0:T(8,128)(2,1)}, u32[]{:S(2)}, u32[]{:S(2)}) collective-permute-start(bf16[5,2048]{1,0:T(8,128)(2,1)} %get-tuple-element.29), channel_id=1, source_target_pairs={{0,1},{1,2},{2,3},{3,4},{4,5},{5,6},{6,7},{7,0},{8,9},{9,10},{10,1... | collective-permute-start | bytes 61448 | tf_op jit(solution)/shard_map/ppermute | solution.py:78
  44.8 26.1 %collective-permute-start.1 = (bf16[5,2048]{1,0:T(8,128)(2,1)}, bf16[5,2048]{1,0:T(8,128)(2,1)}, u32[]{:S(2)}, u32[]{:S(2)}) collective-permute-start(bf16[5,2048]{1,0:T(8,128)(2,1)} %get-tuple-element.35), channel_id=1, source_target_pairs={{0,2},{1,3},{2,4},{3,5},{4,6},{5,7},{6,0},{7,1},{8,10},{9,11},{10,... | collective-permute-start | bytes 61448 | tf_op jit(solution)/shard_map/ppermute | solution.py:78
  48.1 24.5 %collective-permute-start.2 = (bf16[5,2048]{1,0:T(8,128)(2,1)}, bf16[5,2048]{1,0:T(8,128)(2,1)}, u32[]{:S(2)}, u32[]{:S(2)}) collective-permute-start(bf16[5,2048]{1,0:T(8,128)(2,1)} %get-tuple-element.34), channel_id=1, source_target_pairs={{0,3},{1,4},{2,5},{3,6},{4,7},{5,0},{6,1},{7,2},{8,11},{9,12},{10,... | collective-permute-start | bytes 61448 | tf_op jit(solution)/shard_map/ppermute | solution.py:78
  52.2 20.4 %collective-permute-start.3 = (bf16[5,2048]{1,0:T(8,128)(2,1)}, bf16[5,2048]{1,0:T(8,128)(2,1)}, u32[]{:S(2)}, u32[]{:S(2)}) collective-permute-start(bf16[5,2048]{1,0:T(8,128)(2,1)} %get-tuple-element.33), channel_id=1, source_target_pairs={{0,4},{1,5},{2,6},{3,7},{4,0},{5,1},{6,2},{7,3},{8,12},{9,13},{10,... | collective-permute-start | bytes 61448 | tf_op jit(solution)/shard_map/ppermute | solution.py:78
  52.7 12.8 %copy-start.22 = (s32[1,640]{1,0:T(1,128)S(1)}, s32[1,640]{1,0:T(1,128)}, u32[]{:S(2)}) copy-start(s32[1,640]{1,0:T(1,128)} %param.15) | copy-start | bytes 7684
  52.7 19.9 %collective-permute-start.4 = (bf16[5,2048]{1,0:T(8,128)(2,1)}, bf16[5,2048]{1,0:T(8,128)(2,1)}, u32[]{:S(2)}, u32[]{:S(2)}) collective-permute-start(bf16[5,2048]{1,0:T(8,128)(2,1)} %get-tuple-element.32), channel_id=1, source_target_pairs={{0,5},{1,6},{2,7},{3,0},{4,1},{5,2},{6,3},{7,4},{8,13},{9,14},{10,... | collective-permute-start | bytes 61448 | tf_op jit(solution)/shard_map/ppermute | solution.py:78
  57.7 58.0 %all-to-all-start = ((bf16[32,2,128,256]{3,2,1,0:T(8,128)(2,1)}), bf16[32,2,128,256]{3,2,1,0:T(8,128)(2,1)}, u32[]{:S(2)}, u32[]{:S(2)}) async-start(bf16[32,2,128,256]{3,2,1,0:T(8,128)(2,1)} %select_select_fusion), calls=%async_computation.1 | async-start | bytes 8388608 | tf_op jit(solution)/shard_map/all_to_all | solution.py:126
  65.4 75.2 %reduce-scatter.2.cloned.1.call-start = ((), (), s32[]{:S(2)}) async-start(), calls=%async_computation.4 | async-start | bytes 2949120 | tf_op jit(solution)/shard_map/reduce_scatter | solution.py:163
  68.4 5.4 %collective-permute-start.5 = (bf16[5,2048]{1,0:T(8,128)(2,1)}, bf16[5,2048]{1,0:T(8,128)(2,1)}, u32[]{:S(2)}, u32[]{:S(2)}) collective-permute-start(bf16[5,2048]{1,0:T(8,128)(2,1)} %get-tuple-element.31), channel_id=1, source_target_pairs={{0,6},{1,7},{2,0},{3,1},{4,2},{5,3},{6,4},{7,5},{8,14},{9,15},{10,... | collective-permute-start | bytes 61448 | tf_op jit(solution)/shard_map/ppermute | solution.py:78
  71.0 4.2 %collective-permute-start.6 = (bf16[5,2048]{1,0:T(8,128)(2,1)}, bf16[5,2048]{1,0:T(8,128)(2,1)}, u32[]{:S(2)}, u32[]{:S(2)}) collective-permute-start(bf16[5,2048]{1,0:T(8,128)(2,1)} %get-tuple-element.30), channel_id=1, source_target_pairs={{0,7},{1,0},{2,1},{3,2},{4,3},{5,4},{6,5},{7,6},{8,15},{9,8},{10,9... | collective-permute-start | bytes 61448 | tf_op jit(solution)/shard_map/ppermute | solution.py:78
  76.9 4.0 %copy-start.13 = (f32[1,256]{1,0:T(1,128)S(1)}, f32[1,256]{1,0:T(1,128)}, u32[]{:S(2)}) copy-start(f32[1,256]{1,0:T(1,128)} %copy-done.12) | copy-start | bytes 3076
  76.9 4.0 %copy-start.17 = (f32[1,256]{1,0:T(1,128)S(1)}, f32[1,256]{1,0:T(1,128)}, u32[]{:S(2)}) copy-start(f32[1,256]{1,0:T(1,128)} %copy-done.16) | copy-start | bytes 3076
  76.9 4.1 %copy-start.15 = (f32[1,256]{1,0:T(1,128)S(1)}, f32[1,256]{1,0:T(1,128)}, u32[]{:S(2)}) copy-start(f32[1,256]{1,0:T(1,128)} %copy-done.14) | copy-start | bytes 3076
  76.9 4.9 %copy-start.21 = (pred[2,256]{1,0:T(4,128)(4,1)S(1)}, pred[2,256]{1,0:T(4,128)(4,1)}, u32[]{:S(2)}) copy-start(pred[2,256]{1,0:T(4,128)(4,1)} %copy-done.20) | copy-start | bytes 1540
  81.0 0.7 copy-start.4
  81.0 3.3 %copy-start.5 = (bf16[640,256]{1,0:T(8,128)(2,1)}, bf16[640,256]{1,0:T(8,128)(2,1)S(1)}, u32[]{:S(2)}) copy-start(bf16[640,256]{1,0:T(8,128)(2,1)S(1)} %get-tuple-element.20) | copy-start | bytes 983044
  84.4 1.2 copy-start.3
  85.6 2.4 %copy-start.9 = (bf16[5,2048]{1,0:T(8,128)(2,1)S(1)}, bf16[5,2048]{1,0:T(8,128)(2,1)}, u32[]{:S(2)}) copy-start(bf16[5,2048]{1,0:T(8,128)(2,1)} %fusion.72) | copy-start | bytes 61444
  85.6 13.4 %copy-start.8 = (bf16[40,256]{1,0:T(8,128)(2,1)S(1)}, bf16[40,256]{1,0:T(8,128)(2,1)}, u32[]{:S(2)}) copy-start(bf16[40,256]{1,0:T(8,128)(2,1)} %copy-done.7) | copy-start | bytes 61444
  85.6 13.4 %copy-start.10 = (bf16[40,256]{1,0:T(8,128)(2,1)S(1)}, bf16[40,256]{1,0:T(8,128)(2,1)}, u32[]{:S(2)}) copy-start(bf16[40,256]{1,0:T(8,128)(2,1)} %get-tuple-element.22) | copy-start | bytes 61444
  85.6 14.1 %copy-start.18 = (pred[24,128]{1,0:T(8,128)(4,1)S(1)}, pred[24,128]{1,0:T(8,128)(4,1)}, u32[]{:S(2)}) copy-start(pred[24,128]{1,0:T(8,128)(4,1)} %iota_compare_fusion.3) | copy-start | bytes 9220
  88.0 15.0 %collective-permute-start.7 = (bf16[5,2048]{1,0:T(8,128)(2,1)S(1)}, bf16[5,2048]{1,0:T(8,128)(2,1)S(1)}, u32[]{:S(2)}, u32[]{:S(2)}) collective-permute-start(bf16[5,2048]{1,0:T(8,128)(2,1)S(1)} %copy-done.9), channel_id=1, source_target_pairs={{0,1},{1,2},{2,3},{3,4},{4,5},{5,6},{6,7},{7,0},{8,9},{9,10},{10,1... | collective-permute-start | bytes 61448 | tf_op jit(solution)/shard_map/ppermute | solution.py:89
  88.0 16.7 %collective-permute-start.8 = (bf16[5,2048]{1,0:T(8,128)(2,1)S(1)}, bf16[5,2048]{1,0:T(8,128)(2,1)S(1)}, u32[]{:S(2)}, u32[]{:S(2)}) collective-permute-start(bf16[5,2048]{1,0:T(8,128)(2,1)S(1)} %copy-done.9), channel_id=1, source_target_pairs={{0,2},{1,3},{2,4},{3,5},{4,6},{5,7},{6,0},{7,1},{8,10},{9,11},{10,... | collective-permute-start | bytes 61448 | tf_op jit(solution)/shard_map/ppermute | solution.py:89
  89.7 16.0 %collective-permute-start.9 = (bf16[5,2048]{1,0:T(8,128)(2,1)S(1)}, bf16[5,2048]{1,0:T(8,128)(2,1)S(1)}, u32[]{:S(2)}, u32[]{:S(2)}) collective-permute-start(bf16[5,2048]{1,0:T(8,128)(2,1)S(1)} %copy-done.9), channel_id=1, source_target_pairs={{0,3},{1,4},{2,5},{3,6},{4,7},{5,0},{6,1},{7,2},{8,11},{9,12},{10,... | collective-permute-start | bytes 61448 | tf_op jit(solution)/shard_map/ppermute | solution.py:89
  93.3 13.0 %collective-permute-start.10 = (bf16[5,2048]{1,0:T(8,128)(2,1)S(1)}, bf16[5,2048]{1,0:T(8,128)(2,1)S(1)}, u32[]{:S(2)}, u32[]{:S(2)}) collective-permute-start(bf16[5,2048]{1,0:T(8,128)(2,1)S(1)} %copy-done.9), channel_id=1, source_target_pairs={{0,4},{1,5},{2,6},{3,7},{4,0},{5,1},{6,2},{7,3},{8,12},{9,13},{10,... | collective-permute-start | bytes 61448 | tf_op jit(solution)/shard_map/ppermute | solution.py:89
  94.8 12.1 %collective-permute-start.11 = (bf16[5,2048]{1,0:T(8,128)(2,1)S(1)}, bf16[5,2048]{1,0:T(8,128)(2,1)S(1)}, u32[]{:S(2)}, u32[]{:S(2)}) collective-permute-start(bf16[5,2048]{1,0:T(8,128)(2,1)S(1)} %copy-done.9), channel_id=1, source_target_pairs={{0,5},{1,6},{2,7},{3,0},{4,1},{5,2},{6,3},{7,4},{8,13},{9,14},{10,... | collective-permute-start | bytes 61448 | tf_op jit(solution)/shard_map/ppermute | solution.py:89
  99.7 11.2 %copy-start.25 = (pred[8]{0:T(512)(128)(4,1)S(1)}, pred[8]{0:T(512)(128)(4,1)}, u32[]{:S(2)}) copy-start(pred[8]{0:T(512)(128)(4,1)} %compare_and_fusion) | copy-start | bytes 28
  99.7 13.8 %copy-start.24 = (pred[32]{0:T(512)(128)(4,1)S(1)}, pred[32]{0:T(512)(128)(4,1)}, u32[]{:S(2)}) copy-start(pred[32]{0:T(512)(128)(4,1)} %copy-done.23) | copy-start | bytes 100
  103.1 37.5 %copy-start.11 = (f32[2048]{0:T(1024)S(1)}, f32[2048]{0:T(1024)}, u32[]{:S(2)}) copy-start(f32[2048]{0:T(1024)} %param.25) | copy-start | bytes 24580
  103.1 4.8 %collective-permute-start.12 = (bf16[5,2048]{1,0:T(8,128)(2,1)S(1)}, bf16[5,2048]{1,0:T(8,128)(2,1)S(1)}, u32[]{:S(2)}, u32[]{:S(2)}) collective-permute-start(bf16[5,2048]{1,0:T(8,128)(2,1)S(1)} %copy-done.9), channel_id=1, source_target_pairs={{0,6},{1,7},{2,0},{3,1},{4,2},{5,3},{6,4},{7,5},{8,14},{9,15},{10,... | collective-permute-start | bytes 61448 | tf_op jit(solution)/shard_map/ppermute | solution.py:89
  104.7 3.9 %collective-permute-start.13 = (bf16[5,2048]{1,0:T(8,128)(2,1)S(1)}, bf16[5,2048]{1,0:T(8,128)(2,1)S(1)}, u32[]{:S(2)}, u32[]{:S(2)}) collective-permute-start(bf16[5,2048]{1,0:T(8,128)(2,1)S(1)} %copy-done.9), channel_id=1, source_target_pairs={{0,7},{1,0},{2,1},{3,2},{4,3},{5,4},{6,5},{7,6},{8,15},{9,8},{10,9... | collective-permute-start | bytes 61448 | tf_op jit(solution)/shard_map/ppermute | solution.py:89
  118.5 15.7 %all-to-all-start.1 = ((bf16[32,2,1024]{2,1,0:T(2,128)(2,1)}), bf16[32,2,1024]{2,1,0:T(2,128)(2,1)S(1)}, u32[]{:S(2)}, u32[]{:S(2)}) async-start(bf16[32,2,1024]{2,1,0:T(2,128)(2,1)} %reshape.480), calls=%async_computation.2 | async-start | bytes 262144 | tf_op jit(solution)/shard_map/all_to_all | solution.py:172
Sparse Core Ops, SparseCore 0:
  11.9 49.8 all-gather.1
  99.1 41.3 reduce-scatter.1

commit v8 on v7

--- a/solution.py
+++ b/solution.py
@@ -122,7 +122,6 @@
         updated_rows(past_cache, key_new, value_new, request_ages, picks),
         jnp.zeros((), jnp.bfloat16),
     )
-    send_cache, partial_value = lax.optimization_barrier((send_cache, partial_value))
     moved_cache = lax.all_to_all(send_cache, "rep", split_axis=0, concat_axis=0, tiled=True)
     tp_count = lax.axis_size("tp")
     decode_pieces = partial_value.astype(jnp.bfloat16).reshape(

time: 155 us -> 152 us (0.981)
    select_n x1, other arithmetic: 2.41 us -> 3.99 us  [on_device(): jnp.where(has[:, None, None, None], updated_rows(past_cache, key_new, val...]
  transfers between devices with their start and end apart: 18 -> 18, of which waited for: 7 -> 7; matrix products, arithmetic and copies ran while one was open for 42% -> 41% of each run, Pallas kernels for 0% -> 0%
where the time goes in v8:
time: 152 us; the launch traced here: 151 us
  starting transfers between devices  47.8 us (31%)
  other arithmetic  30.4 us (20%)
  local copies, waits for them, and re-layouts  29.4 us (19%)
  matrix products  14.6 us (10%)
  between operations  14.6 us (10%)
  waiting for transfers between devices  13.7 us (9%)
    ppermute x7, starting transfers between devices, scatter_over_tp(): lax.ppermute(rolled[shift], 'tp', [(i, (i + shift) % n) for i in range(n)])  18.5 us
    ppermute x7, starting transfers between devices, gather_over_tp(): lax.ppermute(own_out, 'tp', [(i, (i + shift) % n) for i in range(n)])  12.4 us
    unnamed x65, local copies, waits for them, and re-layouts  11.8 us
    all_to_all x1, starting transfers between devices, on_device(): lax.all_to_all(send_rows, 'rep', split_axis=0, concat_axis=0, tiled=True)  9.08 us
    all_to_all x1, starting transfers between devices, on_device(): lax.all_to_all(send_cache, 'rep', split_axis=0, concat_axis=0, tiled=True)  7.77 us
    gather x1, local copies, waits for them, and re-layouts, updated_rows(): cache[picks]  5.34 us
    reduce_scatter x1, waiting for transfers between devices, on_device(): lax.psum_scatter(prompt_partial, 'tp', scatter_dimension=0, tiled=True)  5.16 us
    all_to_all x1, waiting for transfers between devices, on_device(): lax.all_to_all(send_rows, 'rep', split_axis=0, concat_axis=0, tiled=True)  4.02 us
  transfers between devices with their start and end apart: 18, of which 7 were waited for; matrix products, arithmetic and copies ran while one was open for 41% of the time, Pallas kernels for 0%

profile of v8, /device:TPU:2, one launch (start us, length us, event | category | flops | bytes accessed | tf_op | source)
XLA Modules:
  0.0 150.5 jit_solution(11178125181152964128)
XLA Ops:
  7.2 1.3 convert_reduce_fusion
  8.5 1.2 fusion.32
  9.8 2.0 %fusion.35 = bf16[80,2048]{1,0:T(8,128)(2,1)} fusion(bf16[80,2048]{1,0:T(8,128)(2,1)} %param.14, f32[2048]{0:T(1024)} %param.21, f32[2048]{0:T(1024)} %param.20, f32[80]{0:T(128)S(1)} %add_rsqrt_fusion.1, f32[80]{0:T(128)S(1)} %broadcast_multiply_fusion.1), kind=kLoop, calls=%fused_computation.45 | loop fusion | flops 983040 | bytes 672384 | tf_op jit(solution)/shard_map/convert_element_type | solution.py:18
  11.8 0.8 fusion.97
  12.6 1.0 convert_reduce_fusion.1
  13.6 1.1 fusion.48
  14.8 0.7 iota_compare_fusion.1
  15.5 1.6 %convolution_bitcast_fusion = f32[3,40,256]{2,1,0:T(8,128)S(1)} fusion(bf16[3,2048,256]{2,1,0:T(8,128)(2,1)S(1)} %copy-done, bf16[40,2048]{1,0:T(8,128)(2,1)} %param.16, f32[2048]{0:T(1024)} %param.21, f32[2048]{0:T(1024)} %param.20, f32[40]{0:T(128)S(1)} %add_rsqrt_fusion, f32[40]{0:T(128)S(1)} %broadcast_multiply_fusion), kind=kOutput, calls=%fused_computation.32 | convolution fusion | flops 126320640 | bytes 3449152 | tf_op jit(solution)/shard_map/rd,cde->cre/dot_general | solution.py:27
  17.8 2.6 %fusion.99 = (f32[40,2]{1,0:T(8,128)S(1)}, f32[40,2,128]{2,1,0:T(2,128)S(1)}) fusion(bf16[40,2,128,256]{3,2,1,0:T(8,128)(2,1)} %param.19, pred[2,256]{1,0:T(4,128)(4,1)S(1)} %iota_compare_fusion.5, bf16[40,256]{1,0:T(8,128)(2,1)S(1)} %get-tuple-element.35, pred[40,128]{1,0:T(8,128)(4,1)S(1)} %iota_compare_fusion.1), kind=kOutput, calls=%fused_computation.187 | convolution fusion | flops 5294000 | bytes 2688832 | tf_op jit(solution)/shard_map/rhc,rlc->rhl/dot_general | solution.py:36
  21.2 0.7 copy.60
  21.9 0.7 gather_fusion
  22.7 2.4 %fusion.21 = f32[40,256]{1,0:T(8,128)S(1)} fusion(bf16[40,2,128,256]{3,2,1,0:T(8,128)(2,1)} %param.19, pred[2,256]{1,0:T(4,128)(4,1)S(1)} %iota_compare_fusion.5, f32[40,2,128]{2,1,0:T(2,128)S(1)} %get-tuple-element.47, f32[40,2]{1,0:T(8,128)} %copy.60, f32[40,2]{1,0:T(8,128)S(1)} %copy.58), kind=kOutput, calls=%fused_computation.34 | convolution fusion | flops 5304320 | bytes 2724672 | tf_op jit(solution)/shard_map/rhl,rlc->rhc/dot_general | solution.py:56
  25.4 0.8 reshape.410
  26.3 1.5 %gather_fusion.5 = bf16[8,5,2048]{2,1,0:T(8,128)(2,1)S(1)} fusion(bf16[8,5,2048]{2,1,0:T(8,128)(2,1)} %reshape.410, s32[1024]{0:T(1024)S(1)} %get-tuple-element.49), kind=kCustom, calls=%fused_computation.clone | custom fusion | bytes 327712 | tf_op jit(solution)/shard_map/jit(_take)/gather | solution.py:75
  28.0 0.7 slice_bitcast_fusion.8
  28.7 1.9 %collective-permute-start = (bf16[5,2048]{1,0:T(8,128)(2,1)}, bf16[5,2048]{1,0:T(8,128)(2,1)}, u32[]{:S(2)}, u32[]{:S(2)}) collective-permute-start(bf16[5,2048]{1,0:T(8,128)(2,1)} %get-tuple-element.25), channel_id=1, source_target_pairs={{0,1},{1,2},{2,3},{3,4},{4,5},{5,6},{6,7},{7,0},{8,9},{9,10},{10,1... | collective-permute-start | bytes 61448 | tf_op jit(solution)/shard_map/ppermute | solution.py:78
  30.6 3.3 %collective-permute-start.1 = (bf16[5,2048]{1,0:T(8,128)(2,1)}, bf16[5,2048]{1,0:T(8,128)(2,1)}, u32[]{:S(2)}, u32[]{:S(2)}) collective-permute-start(bf16[5,2048]{1,0:T(8,128)(2,1)} %get-tuple-element.31), channel_id=1, source_target_pairs={{0,2},{1,3},{2,4},{3,5},{4,6},{5,7},{6,0},{7,1},{8,10},{9,11},{10,... | collective-permute-start | bytes 61448 | tf_op jit(solution)/shard_map/ppermute | solution.py:78
  33.9 4.1 %collective-permute-start.2 = (bf16[5,2048]{1,0:T(8,128)(2,1)}, bf16[5,2048]{1,0:T(8,128)(2,1)}, u32[]{:S(2)}, u32[]{:S(2)}) collective-permute-start(bf16[5,2048]{1,0:T(8,128)(2,1)} %get-tuple-element.30), channel_id=1, source_target_pairs={{0,3},{1,4},{2,5},{3,6},{4,7},{5,0},{6,1},{7,2},{8,11},{9,12},{10,... | collective-permute-start | bytes 61448 | tf_op jit(solution)/shard_map/ppermute | solution.py:78
  38.5 5.0 %collective-permute-start.4 = (bf16[5,2048]{1,0:T(8,128)(2,1)}, bf16[5,2048]{1,0:T(8,128)(2,1)}, u32[]{:S(2)}, u32[]{:S(2)}) collective-permute-start(bf16[5,2048]{1,0:T(8,128)(2,1)} %get-tuple-element.28), channel_id=1, source_target_pairs={{0,5},{1,6},{2,7},{3,0},{4,1},{5,2},{6,3},{7,4},{8,13},{9,14},{10,... | collective-permute-start | bytes 61448 | tf_op jit(solution)/shard_map/ppermute | solution.py:78
  43.5 5.3 %gather_fusion.4 = bf16[32,2,128,256]{3,2,1,0:T(8,128)(2,1)} fusion(bf16[40,2,128,256]{3,2,1,0:T(8,128)(2,1)} %param.19, s32[1024]{0:T(1024)S(1)} %get-tuple-element.48), kind=kCustom, calls=%fused_computation.6 | custom fusion | bytes 8388736 | tf_op jit(solution)/shard_map/gather | solution.py:68
  48.9 0.7 gather_fusion.2
  49.7 0.6 gather_fusion.3
  50.5 4.0 %select_select_fusion = bf16[32,2,128,256]{3,2,1,0:T(8,128)(2,1)} fusion(bf16[32,2,128,256]{3,2,1,0:T(8,128)(2,1)} %gather_fusion.4, pred[32]{0:T(512)(128)(4,1)S(1)} %fusion.86, pred[32,128]{1,0:T(8,128)(4,1)S(1)} %iota_compare_fusion.2, bf16[32,2,256]{2,1,0:T(2,128)(2,1)S(1)} %gather_fusion.3), kind=kLoop, calls=%fused_computation.8 | loop fusion | flops 4194304 | bytes 8425504 | tf_op jit(solution)/shard_map/jit(_where)/select_n | solution.py:120
  54.5 7.8 %all-to-all-start = ((bf16[32,2,128,256]{3,2,1,0:T(8,128)(2,1)}), bf16[32,2,128,256]{3,2,1,0:T(8,128)(2,1)}, u32[]{:S(2)}, u32[]{:S(2)}) async-start(bf16[32,2,128,256]{3,2,1,0:T(8,128)(2,1)} %select_select_fusion), calls=%async_computation.1 | async-start | bytes 8388608 | tf_op jit(solution)/shard_map/all_to_all | solution.py:125
  62.9 0.7 iota_compare_fusion.3
  63.6 1.0 fusion.13
  65.2 2.7 %collective-permute-start.5 = (bf16[5,2048]{1,0:T(8,128)(2,1)}, bf16[5,2048]{1,0:T(8,128)(2,1)}, u32[]{:S(2)}, u32[]{:S(2)}) collective-permute-start(bf16[5,2048]{1,0:T(8,128)(2,1)} %get-tuple-element.27), channel_id=1, source_target_pairs={{0,6},{1,7},{2,0},{3,1},{4,2},{5,3},{6,4},{7,5},{8,14},{9,15},{10,... | collective-permute-start | bytes 61448 | tf_op jit(solution)/shard_map/ppermute | solution.py:78
  67.9 0.9 collective-permute-start.6
  69.5 1.2 collective-permute-done.5
  70.7 1.5 collective-permute-done.6
  72.2 1.7 %fusion.72 = bf16[5,2048]{1,0:T(8,128)(2,1)} fusion(bf16[5,2048]{1,0:T(8,128)(2,1)} %collective-permute-done.6, bf16[5,2048]{1,0:T(8,128)(2,1)} %collective-permute-done.5, bf16[5,2048]{1,0:T(8,128)(2,1)} %collective-permute-done.4, bf16[5,2048]{1,0:T(8,128)(2,1)} %collective-permute-done.3, bf16[5,2048]{1,0:T(8,128)(2,1)} %collective-permute-done.2, ...), kind=kLoop, calls=%fused_computation.93 | loop fusion | flops 194560 | bytes 212996 | tf_op jit(solution)/shard_map/convert_element_type | solution.py:81
  73.9 3.9 %fusion.15 = f32[3,640,256]{2,1,0:T(8,128)S(1)} fusion(bf16[3,2048,256]{2,1,0:T(8,128)(2,1)S(1)} %copy-done, bf16[640,2048]{1,0:T(8,128)(2,1)} %all-gather.2.cloned.1.call-done), kind=kOutput, calls=%fused_computation.30 | convolution fusion | flops 2013265920 | bytes 7733248 | tf_op jit(solution)/shard_map/rd,cde->cre/dot_general | solution.py:132
  78.1 0.7 copy-done.4
  78.7 0.6 fusion.43
  79.4 2.0 %fusion.98 = (f32[2,640]{1,0:T(2,128)S(1)}, f32[2,640,640]{1,2,0:T(8,128)S(1)}) fusion(f32[2,640,640]{1,2,0:T(8,128)S(1)} %fusion.43, pred[640,640]{0,1:T(8,128)(4,1)S(1)} %fusion.13), kind=kOutput, calls=%fused_computation.186 | output fusion | flops 4915839 | bytes 6968320 | tf_op jit(solution)/shard_map/sub | solution.py:147
  81.4 0.8 select_reduce_fusion
  82.6 2.4 %convolution_convert_fusion = bf16[640,2048]{1,0:T(8,128)(2,1)} fusion(bf16[256,2048]{1,0:T(8,128)(2,1)S(1)} %copy-done.3, bf16[640,256]{1,0:T(8,128)(2,1)S(1)} %select_reduce_fusion), kind=kOutput, calls=%fused_computation.12 | convolution fusion | flops 672399360 | bytes 3997696 | tf_op jit(solution)/shard_map/dot_general | solution.py:151
  85.0 1.6 %collective-permute-start.8 = (bf16[5,2048]{1,0:T(8,128)(2,1)S(1)}, bf16[5,2048]{1,0:T(8,128)(2,1)S(1)}, u32[]{:S(2)}, u32[]{:S(2)}) collective-permute-start(bf16[5,2048]{1,0:T(8,128)(2,1)S(1)} %copy-done.9), channel_id=1, source_target_pairs={{0,2},{1,3},{2,4},{3,5},{4,6},{5,7},{6,0},{7,1},{8,10},{9,11},{10,... | collective-permute-start | bytes 61448 | tf_op jit(solution)/shard_map/ppermute | solution.py:89
  86.6 3.6 %collective-permute-start.9 = (bf16[5,2048]{1,0:T(8,128)(2,1)S(1)}, bf16[5,2048]{1,0:T(8,128)(2,1)S(1)}, u32[]{:S(2)}, u32[]{:S(2)}) collective-permute-start(bf16[5,2048]{1,0:T(8,128)(2,1)S(1)} %copy-done.9), channel_id=1, source_target_pairs={{0,3},{1,4},{2,5},{3,6},{4,7},{5,0},{6,1},{7,2},{8,11},{9,12},{10,... | collective-permute-start | bytes 61448 | tf_op jit(solution)/shard_map/ppermute | solution.py:89
  90.2 1.5 collective-permute-start.10
  91.7 4.2 %collective-permute-start.11 = (bf16[5,2048]{1,0:T(8,128)(2,1)S(1)}, bf16[5,2048]{1,0:T(8,128)(2,1)S(1)}, u32[]{:S(2)}, u32[]{:S(2)}) collective-permute-start(bf16[5,2048]{1,0:T(8,128)(2,1)S(1)} %copy-done.9), channel_id=1, source_target_pairs={{0,5},{1,6},{2,7},{3,0},{4,1},{5,2},{6,3},{7,4},{8,13},{9,14},{10,... | collective-permute-start | bytes 61448 | tf_op jit(solution)/shard_map/ppermute | solution.py:89
  96.0 0.6 bitcast_dynamic-update-slice_fusion.7
  96.6 3.4 %slice_select_fusion = bf16[24,2,128,256]{3,2,1,0:T(8,128)(2,1)} fusion(bf16[40,2,128,256]{3,2,1,0:T(8,128)(2,1)} %param.19, pred[24,128]{1,0:T(8,128)(4,1)S(1)} %copy-done.18, bf16[24,2,256]{2,1,0:T(2,128)(2,1)S(1)} %copy.63), kind=kLoop, calls=%fused_computation.13 | loop fusion | flops 1572864 | bytes 6319104 | tf_op jit(solution)/shard_map/jit(_where)/select_n | solution.py:159
  99.9 1.0 collective-permute-start.12
  102.7 0.6 bitcast_dynamic-update-slice_fusion.4
  103.3 0.6 bitcast_dynamic-update-slice_fusion.3
  103.9 0.6 bitcast_dynamic-update-slice_fusion.2
  104.8 0.6 bitcast_dynamic-update-slice_fusion.1
  106.1 1.6 %gather_fusion.6 = bf16[8,5,2048]{2,1,0:T(8,128)(2,1)S(1)} fusion(bf16[8,5,2048]{2,1,0:T(8,128)(2,1)} %bitcast_dynamic-update-slice_fusion, s32[1024]{0:T(1024)} %pad_clamp_fusion.1), kind=kCustom, calls=%fused_computation.1.clone | custom fusion | bytes 327712 | tf_op jit(solution)/shard_map/jit(_take)/gather | solution.py:91
  107.8 0.8 broadcast_select_fusion
  108.6 1.0 reshape.411
  109.6 0.8 gather_fusion.1
  110.4 0.7 broadcast_select_fusion.2
  111.1 1.4 all-to-all-done
  113.0 1.6 %reduce.1 = bf16[32,2048]{1,0:T(8,128)(2,1)S(1)} reduce(bf16[32,1,2048]{2,0,1:T(8,128)(2,1)} %bitcast.146, bf16[]{:T(256)} %broadcast.382), dimensions={1}, to_apply=%copy.65.reduce_sub_computation | reduce | bytes 262146 | tf_op jit(solution)/shard_map/all_to_all | solution.py:171
  114.6 0.7 reshape.480
  115.3 9.1 %all-to-all-start.1 = ((bf16[32,2,1024]{2,1,0:T(2,128)(2,1)}), bf16[32,2,1024]{2,1,0:T(2,128)(2,1)S(1)}, u32[]{:S(2)}, u32[]{:S(2)}) async-start(bf16[32,2,1024]{2,1,0:T(2,128)(2,1)} %reshape.480), calls=%async_computation.2 | async-start | bytes 262144 | tf_op jit(solution)/shard_map/all_to_all | solution.py:171
  124.4 2.0 %pad_maximum_fusion = bf16[2,640,256]{2,1,0:T(8,128)(2,1)} fusion(bf16[1,640,256]{2,1,0:T(8,128)(2,1)} %bitcast.145, bf16[1,640,256]{2,1,0:T(8,128)(2,1)} %bitcast.144), kind=kLoop, calls=%fused_computation.56 | loop fusion | flops 327680 | bytes 1310720 | tf_op jit(solution)/shard_map/stack | solution.py:167
  126.4 0.6 slice.127
  127.0 4.0 %all-to-all-done.1 = bf16[32,2,1024]{2,1,0:T(2,128)(2,1)S(1)} async-done(((bf16[32,2,1024]{2,1,0:T(2,128)(2,1)}), bf16[32,2,1024]{2,1,0:T(2,128)(2,1)S(1)}, u32[]{:S(2)}, u32[]{:S(2)}) %all-to-all-start.1) | async-done | bytes 131104 | tf_op jit(solution)/shard_map/all_to_all | solution.py:171
  131.2 0.7 copy.71
  131.9 5.2 %reduce-scatter.2.cloned.1.call-done = bf16[80,2048]{1,0:T(8,128)(2,1)} async-done(((bf16[640,2048]{1,0:T(8,128)(2,1)}), bf16[80,2048]{1,0:T(8,128)(2,1)}) %reduce-scatter.2.cloned.1.call-update) | async-done | bytes 327696 | tf_op jit(solution)/shard_map/reduce_scatter | solution.py:162
  137.1 1.9 %fusion.37 = bf16[80,2048]{1,0:T(8,128)(2,1)} fusion(bf16[80,2048]{1,0:T(8,128)(2,1)} %param.14, bf16[80,2048]{1,0:T(8,128)(2,1)} %reduce-scatter.2.cloned.1.call-done, f32[2048]{0:T(1024)S(1)} %copy-done.11), kind=kLoop, calls=%fused_computation.47 | loop fusion | flops 819200 | bytes 991232 | tf_op jit(solution)/shard_map/convert_element_type | solution.py:166
  139.0 4.7 %copy.81 = bf16[32,2,128,256]{3,2,1,0:T(8,128)(2,1)} copy(bf16[32,2,128,256]{3,2,1,0:T(8,128)(2,1)} %all-to-all-done) | data formatting | bytes 8388608
  (121 shorter events, 8.7 us)
Async XLA Ops:
  7.2 8.4 %copy-start = (bf16[3,2048,256]{2,1,0:T(8,128)(2,1)S(1)}, bf16[3,2048,256]{2,1,0:T(8,128)(2,1)}, u32[]{:S(2)}) copy-start(bf16[3,2048,256]{2,1,0:T(8,128)(2,1)} %param.22) | copy-start | bytes 9437188
  7.2 66.7 %all-gather.2.cloned.1.call-start = ((), (), s32[]{:S(2)}) async-start(), calls=%async_computation.3 | async-start | bytes 2949120 | tf_op jit(solution)/shard_map/all_gather | solution.py:131
  12.6 8.0 %copy-start.14 = (f32[1,256]{1,0:T(1,128)}, f32[1,256]{1,0:T(1,128)S(1)}, u32[]{:S(2)}) copy-start(f32[1,256]{1,0:T(1,128)S(1)} %get-tuple-element.40) | copy-start | bytes 3076
  12.6 37.0 %copy-start.12 = (f32[1,256]{1,0:T(1,128)}, f32[1,256]{1,0:T(1,128)S(1)}, u32[]{:S(2)}) copy-start(f32[1,256]{1,0:T(1,128)S(1)} %get-tuple-element.41) | copy-start | bytes 3076
  12.6 37.0 %copy-start.16 = (f32[1,256]{1,0:T(1,128)}, f32[1,256]{1,0:T(1,128)S(1)}, u32[]{:S(2)}) copy-start(f32[1,256]{1,0:T(1,128)S(1)} %get-tuple-element.39) | copy-start | bytes 3076
  14.8 7.9 %copy-start.20 = (pred[2,256]{1,0:T(4,128)(4,1)}, pred[2,256]{1,0:T(4,128)(4,1)S(1)}, u32[]{:S(2)}) copy-start(pred[2,256]{1,0:T(4,128)(4,1)S(1)} %iota_compare_fusion.5) | copy-start | bytes 1540
  17.8 7.3 %copy-start.7 = (bf16[40,256]{1,0:T(8,128)(2,1)}, bf16[40,256]{1,0:T(8,128)(2,1)S(1)}, u32[]{:S(2)}) copy-start(bf16[40,256]{1,0:T(8,128)(2,1)S(1)} %get-tuple-element.20) | copy-start | bytes 61444
  20.4 5.8 %copy-start.26 = (s32[16,1]{0,1:T(1,128)S(1)}, s32[16,1]{0,1:T(1,128)}, u32[]{:S(2)}) copy-start(s32[16,1]{0,1:T(1,128)} %param.18) | copy-start | bytes 196
  22.7 2.4 %copy-start.2 = (bf16[256,2048]{1,0:T(8,128)(2,1)S(1)}, bf16[256,2048]{1,0:T(8,128)(2,1)}, u32[]{:S(2)}) copy-start(bf16[256,2048]{1,0:T(8,128)(2,1)} %param.24) | copy-start | bytes 3145732
  26.3 23.3 %copy-start.19 = (s32[1024]{0:T(1024)}, s32[1024]{0:T(1024)S(1)}, u32[]{:S(2)}) copy-start(s32[1024]{0:T(1024)S(1)} %get-tuple-element.48) | copy-start | bytes 12292
  28.0 15.6 %copy-start.6 = (bf16[8,5,2048]{2,1,0:T(8,128)(2,1)}, bf16[8,5,2048]{2,1,0:T(8,128)(2,1)S(1)}, u32[]{:S(2)}) copy-start(bf16[8,5,2048]{2,1,0:T(8,128)(2,1)S(1)} %broadcast_select_fusion.1) | copy-start | bytes 491524
  28.7 36.5 %collective-permute-start = (bf16[5,2048]{1,0:T(8,128)(2,1)}, bf16[5,2048]{1,0:T(8,128)(2,1)}, u32[]{:S(2)}, u32[]{:S(2)}) collective-permute-start(bf16[5,2048]{1,0:T(8,128)(2,1)} %get-tuple-element.25), channel_id=1, source_target_pairs={{0,1},{1,2},{2,3},{3,4},{4,5},{5,6},{6,7},{7,0},{8,9},{9,10},{10,1... | collective-permute-start | bytes 61448 | tf_op jit(solution)/shard_map/ppermute | solution.py:78
  30.6 37.3 %collective-permute-start.1 = (bf16[5,2048]{1,0:T(8,128)(2,1)}, bf16[5,2048]{1,0:T(8,128)(2,1)}, u32[]{:S(2)}, u32[]{:S(2)}) collective-permute-start(bf16[5,2048]{1,0:T(8,128)(2,1)} %get-tuple-element.31), channel_id=1, source_target_pairs={{0,2},{1,3},{2,4},{3,5},{4,6},{5,7},{6,0},{7,1},{8,10},{9,11},{10,... | collective-permute-start | bytes 61448 | tf_op jit(solution)/shard_map/ppermute | solution.py:78
  33.9 35.6 %collective-permute-start.2 = (bf16[5,2048]{1,0:T(8,128)(2,1)}, bf16[5,2048]{1,0:T(8,128)(2,1)}, u32[]{:S(2)}, u32[]{:S(2)}) collective-permute-start(bf16[5,2048]{1,0:T(8,128)(2,1)} %get-tuple-element.30), channel_id=1, source_target_pairs={{0,3},{1,4},{2,5},{3,6},{4,7},{5,0},{6,1},{7,2},{8,11},{9,12},{10,... | collective-permute-start | bytes 61448 | tf_op jit(solution)/shard_map/ppermute | solution.py:78
  38.1 31.4 %collective-permute-start.3 = (bf16[5,2048]{1,0:T(8,128)(2,1)}, bf16[5,2048]{1,0:T(8,128)(2,1)}, u32[]{:S(2)}, u32[]{:S(2)}) collective-permute-start(bf16[5,2048]{1,0:T(8,128)(2,1)} %get-tuple-element.29), channel_id=1, source_target_pairs={{0,4},{1,5},{2,6},{3,7},{4,0},{5,1},{6,2},{7,3},{8,12},{9,13},{10,... | collective-permute-start | bytes 61448 | tf_op jit(solution)/shard_map/ppermute | solution.py:78
  38.5 31.0 %collective-permute-start.4 = (bf16[5,2048]{1,0:T(8,128)(2,1)}, bf16[5,2048]{1,0:T(8,128)(2,1)}, u32[]{:S(2)}, u32[]{:S(2)}) collective-permute-start(bf16[5,2048]{1,0:T(8,128)(2,1)} %get-tuple-element.28), channel_id=1, source_target_pairs={{0,5},{1,6},{2,7},{3,0},{4,1},{5,2},{6,3},{7,4},{8,13},{9,14},{10,... | collective-permute-start | bytes 61448 | tf_op jit(solution)/shard_map/ppermute | solution.py:78
  43.5 5.3 %copy-start.1 = (s32[40]{0:T(128)S(1)}, s32[40]{0:T(128)}, u32[]{:S(2)}) copy-start(s32[40]{0:T(128)} %param.17) | copy-start | bytes 484
  50.4 4.1 %copy-start.23 = (pred[32]{0:T(512)(128)(4,1)}, pred[32]{0:T(512)(128)(4,1)S(1)}, u32[]{:S(2)}) copy-start(pred[32]{0:T(512)(128)(4,1)S(1)} %fusion.86) | copy-start | bytes 100
  54.5 7.8 %copy-start.22 = (s32[1,640]{1,0:T(1,128)S(1)}, s32[1,640]{1,0:T(1,128)}, u32[]{:S(2)}) copy-start(s32[1,640]{1,0:T(1,128)} %param.15) | copy-start | bytes 7684
  54.5 58.0 %all-to-all-start = ((bf16[32,2,128,256]{3,2,1,0:T(8,128)(2,1)}), bf16[32,2,128,256]{3,2,1,0:T(8,128)(2,1)}, u32[]{:S(2)}, u32[]{:S(2)}) async-start(bf16[32,2,128,256]{3,2,1,0:T(8,128)(2,1)} %select_select_fusion), calls=%async_computation.1 | async-start | bytes 8388608 | tf_op jit(solution)/shard_map/all_to_all | solution.py:125
  62.3 74.8 %reduce-scatter.2.cloned.1.call-start = ((), (), s32[]{:S(2)}) async-start(), calls=%async_computation.4 | async-start | bytes 2949120 | tf_op jit(solution)/shard_map/reduce_scatter | solution.py:162
  65.2 5.4 %collective-permute-start.5 = (bf16[5,2048]{1,0:T(8,128)(2,1)}, bf16[5,2048]{1,0:T(8,128)(2,1)}, u32[]{:S(2)}, u32[]{:S(2)}) collective-permute-start(bf16[5,2048]{1,0:T(8,128)(2,1)} %get-tuple-element.27), channel_id=1, source_target_pairs={{0,6},{1,7},{2,0},{3,1},{4,2},{5,3},{6,4},{7,5},{8,14},{9,15},{10,... | collective-permute-start | bytes 61448 | tf_op jit(solution)/shard_map/ppermute | solution.py:78
  67.9 4.2 %collective-permute-start.6 = (bf16[5,2048]{1,0:T(8,128)(2,1)}, bf16[5,2048]{1,0:T(8,128)(2,1)}, u32[]{:S(2)}, u32[]{:S(2)}) collective-permute-start(bf16[5,2048]{1,0:T(8,128)(2,1)} %get-tuple-element.26), channel_id=1, source_target_pairs={{0,7},{1,0},{2,1},{3,2},{4,3},{5,4},{6,5},{7,6},{8,15},{9,8},{10,9... | collective-permute-start | bytes 61448 | tf_op jit(solution)/shard_map/ppermute | solution.py:78
  73.8 4.0 %copy-start.13 = (f32[1,256]{1,0:T(1,128)S(1)}, f32[1,256]{1,0:T(1,128)}, u32[]{:S(2)}) copy-start(f32[1,256]{1,0:T(1,128)} %copy-done.12) | copy-start | bytes 3076
  73.8 4.0 %copy-start.17 = (f32[1,256]{1,0:T(1,128)S(1)}, f32[1,256]{1,0:T(1,128)}, u32[]{:S(2)}) copy-start(f32[1,256]{1,0:T(1,128)} %copy-done.16) | copy-start | bytes 3076
  73.8 4.1 %copy-start.15 = (f32[1,256]{1,0:T(1,128)S(1)}, f32[1,256]{1,0:T(1,128)}, u32[]{:S(2)}) copy-start(f32[1,256]{1,0:T(1,128)} %copy-done.14) | copy-start | bytes 3076
  73.8 4.9 %copy-start.21 = (pred[2,256]{1,0:T(4,128)(4,1)S(1)}, pred[2,256]{1,0:T(4,128)(4,1)}, u32[]{:S(2)}) copy-start(pred[2,256]{1,0:T(4,128)(4,1)} %copy-done.20) | copy-start | bytes 1540
  78.0 0.7 copy-start.4
  78.0 3.4 %copy-start.5 = (bf16[640,256]{1,0:T(8,128)(2,1)}, bf16[640,256]{1,0:T(8,128)(2,1)S(1)}, u32[]{:S(2)}) copy-start(bf16[640,256]{1,0:T(8,128)(2,1)S(1)} %get-tuple-element.17) | copy-start | bytes 983044
  81.4 1.2 copy-start.3
  82.6 2.4 %copy-start.9 = (bf16[5,2048]{1,0:T(8,128)(2,1)S(1)}, bf16[5,2048]{1,0:T(8,128)(2,1)}, u32[]{:S(2)}) copy-start(bf16[5,2048]{1,0:T(8,128)(2,1)} %fusion.72) | copy-start | bytes 61444
  82.6 13.3 %copy-start.8 = (bf16[40,256]{1,0:T(8,128)(2,1)S(1)}, bf16[40,256]{1,0:T(8,128)(2,1)}, u32[]{:S(2)}) copy-start(bf16[40,256]{1,0:T(8,128)(2,1)} %copy-done.7) | copy-start | bytes 61444
  82.6 13.3 %copy-start.10 = (bf16[40,256]{1,0:T(8,128)(2,1)S(1)}, bf16[40,256]{1,0:T(8,128)(2,1)}, u32[]{:S(2)}) copy-start(bf16[40,256]{1,0:T(8,128)(2,1)} %get-tuple-element.19) | copy-start | bytes 61444
  82.6 14.0 %copy-start.18 = (pred[24,128]{1,0:T(8,128)(4,1)S(1)}, pred[24,128]{1,0:T(8,128)(4,1)}, u32[]{:S(2)}) copy-start(pred[24,128]{1,0:T(8,128)(4,1)} %iota_compare_fusion.3) | copy-start | bytes 9220
  85.0 15.0 %collective-permute-start.7 = (bf16[5,2048]{1,0:T(8,128)(2,1)S(1)}, bf16[5,2048]{1,0:T(8,128)(2,1)S(1)}, u32[]{:S(2)}, u32[]{:S(2)}) collective-permute-start(bf16[5,2048]{1,0:T(8,128)(2,1)S(1)} %copy-done.9), channel_id=1, source_target_pairs={{0,1},{1,2},{2,3},{3,4},{4,5},{5,6},{6,7},{7,0},{8,9},{9,10},{10,1... | collective-permute-start | bytes 61448 | tf_op jit(solution)/shard_map/ppermute | solution.py:89
  85.0 16.6 %collective-permute-start.8 = (bf16[5,2048]{1,0:T(8,128)(2,1)S(1)}, bf16[5,2048]{1,0:T(8,128)(2,1)S(1)}, u32[]{:S(2)}, u32[]{:S(2)}) collective-permute-start(bf16[5,2048]{1,0:T(8,128)(2,1)S(1)} %copy-done.9), channel_id=1, source_target_pairs={{0,2},{1,3},{2,4},{3,5},{4,6},{5,7},{6,0},{7,1},{8,10},{9,11},{10,... | collective-permute-start | bytes 61448 | tf_op jit(solution)/shard_map/ppermute | solution.py:89
  86.6 16.1 %collective-permute-start.9 = (bf16[5,2048]{1,0:T(8,128)(2,1)S(1)}, bf16[5,2048]{1,0:T(8,128)(2,1)S(1)}, u32[]{:S(2)}, u32[]{:S(2)}) collective-permute-start(bf16[5,2048]{1,0:T(8,128)(2,1)S(1)} %copy-done.9), channel_id=1, source_target_pairs={{0,3},{1,4},{2,5},{3,6},{4,7},{5,0},{6,1},{7,2},{8,11},{9,12},{10,... | collective-permute-start | bytes 61448 | tf_op jit(solution)/shard_map/ppermute | solution.py:89
  90.2 13.1 %collective-permute-start.10 = (bf16[5,2048]{1,0:T(8,128)(2,1)S(1)}, bf16[5,2048]{1,0:T(8,128)(2,1)S(1)}, u32[]{:S(2)}, u32[]{:S(2)}) collective-permute-start(bf16[5,2048]{1,0:T(8,128)(2,1)S(1)} %copy-done.9), channel_id=1, source_target_pairs={{0,4},{1,5},{2,6},{3,7},{4,0},{5,1},{6,2},{7,3},{8,12},{9,13},{10,... | collective-permute-start | bytes 61448 | tf_op jit(solution)/shard_map/ppermute | solution.py:89
  91.7 12.2 %collective-permute-start.11 = (bf16[5,2048]{1,0:T(8,128)(2,1)S(1)}, bf16[5,2048]{1,0:T(8,128)(2,1)S(1)}, u32[]{:S(2)}, u32[]{:S(2)}) collective-permute-start(bf16[5,2048]{1,0:T(8,128)(2,1)S(1)} %copy-done.9), channel_id=1, source_target_pairs={{0,5},{1,6},{2,7},{3,0},{4,1},{5,2},{6,3},{7,4},{8,13},{9,14},{10,... | collective-permute-start | bytes 61448 | tf_op jit(solution)/shard_map/ppermute | solution.py:89
  96.6 11.2 %copy-start.25 = (pred[8]{0:T(512)(128)(4,1)S(1)}, pred[8]{0:T(512)(128)(4,1)}, u32[]{:S(2)}) copy-start(pred[8]{0:T(512)(128)(4,1)} %compare_and_fusion) | copy-start | bytes 28
  96.6 13.8 %copy-start.24 = (pred[32]{0:T(512)(128)(4,1)S(1)}, pred[32]{0:T(512)(128)(4,1)}, u32[]{:S(2)}) copy-start(pred[32]{0:T(512)(128)(4,1)} %copy-done.23) | copy-start | bytes 100
  99.9 37.1 %copy-start.11 = (f32[2048]{0:T(1024)S(1)}, f32[2048]{0:T(1024)}, u32[]{:S(2)}) copy-start(f32[2048]{0:T(1024)} %param.25) | copy-start | bytes 24580
  99.9 4.8 %collective-permute-start.12 = (bf16[5,2048]{1,0:T(8,128)(2,1)S(1)}, bf16[5,2048]{1,0:T(8,128)(2,1)S(1)}, u32[]{:S(2)}, u32[]{:S(2)}) collective-permute-start(bf16[5,2048]{1,0:T(8,128)(2,1)S(1)} %copy-done.9), channel_id=1, source_target_pairs={{0,6},{1,7},{2,0},{3,1},{4,2},{5,3},{6,4},{7,5},{8,14},{9,15},{10,... | collective-permute-start | bytes 61448 | tf_op jit(solution)/shard_map/ppermute | solution.py:89
  101.6 3.9 %collective-permute-start.13 = (bf16[5,2048]{1,0:T(8,128)(2,1)S(1)}, bf16[5,2048]{1,0:T(8,128)(2,1)S(1)}, u32[]{:S(2)}, u32[]{:S(2)}) collective-permute-start(bf16[5,2048]{1,0:T(8,128)(2,1)S(1)} %copy-done.9), channel_id=1, source_target_pairs={{0,7},{1,0},{2,1},{3,2},{4,3},{5,4},{6,5},{7,6},{8,15},{9,8},{10,9... | collective-permute-start | bytes 61448 | tf_op jit(solution)/shard_map/ppermute | solution.py:89
  115.3 15.7 %all-to-all-start.1 = ((bf16[32,2,1024]{2,1,0:T(2,128)(2,1)}), bf16[32,2,1024]{2,1,0:T(2,128)(2,1)S(1)}, u32[]{:S(2)}, u32[]{:S(2)}) async-start(bf16[32,2,1024]{2,1,0:T(2,128)(2,1)} %reshape.480), calls=%async_computation.2 | async-start | bytes 262144 | tf_op jit(solution)/shard_map/all_to_all | solution.py:171
Sparse Core Ops, SparseCore 0:
  11.9 50.8 all-gather.1
  96.0 41.0 reduce-scatter.1

commit v9 on v6

--- a/solution.py
+++ b/solution.py
@@ -173,6 +173,7 @@
     kept_out = decode_out[:staying]
     send_rows = jnp.where(has[:, None], decode_out[picks], jnp.zeros((), jnp.bfloat16))
     send_rows, moved_cache = lax.optimization_barrier((send_rows, moved_cache))
+    moved_cache = jnp.where(request_ages[0] > 0, moved_cache, jnp.zeros((), jnp.bfloat16))
     moved_out = lax.all_to_all(send_rows, "rep", split_axis=0, concat_axis=0, tiled=True)
     return (prompt_out, prompt_cache, kept_out, kept_cache, moved_out, moved_cache)
 

time: 147 us -> 142 us (0.966)
  local copies, waits for them, and re-layouts: 23.3 us -> 18.6 us
  other arithmetic: 22.4 us -> 27 us
  waiting for transfers between devices: 20.9 us -> 16.4 us
    unnamed x23 -> x22, local copies, waits for them, and re-layouts: 6.32 us -> 1.63 us
    select_n x0 -> x1, other arithmetic: none -> 4.56 us  [on_device(): jnp.where(request_ages[0] > 0, moved_cache, jnp.zeros((), jnp.bfloat16))]
    all_to_all x1, waiting for transfers between devices: 5.1 us -> 1.42 us  [on_device(): lax.all_to_all(send_rows, 'rep', split_axis=0, concat_axis=0, tiled=True)]
  transfers between devices with their start and end apart: 18 -> 18, of which waited for: 5 -> 5; matrix products, arithmetic and copies ran while one was open for 35% -> 40% of each run, Pallas kernels for 0% -> 0%
where the time goes in v9:
time: 142 us
  starting transfers between devices  48.3 us (34%)
  other arithmetic  27 us (19%)
  local copies, waits for them, and re-layouts  18.6 us (13%)
  matrix products  16.8 us (12%)
  waiting for transfers between devices  16.4 us (12%)
  between operations  14.6 us (10%)
    ppermute x7, starting transfers between devices, scatter_over_tp(): lax.ppermute(rolled[shift], 'tp', [(i, (i + shift) % n) for i in range(n)])  18.5 us
    ppermute x7, starting transfers between devices, gather_over_tp(): lax.ppermute(own_out, 'tp', [(i, (i + shift) % n) for i in range(n)])  12.8 us
    all_to_all x1, starting transfers between devices, on_device(): lax.all_to_all(send_rows, 'rep', split_axis=0, concat_axis=0, tiled=True)  9.08 us
    all_to_all x1, waiting for transfers between devices, on_device(): lax.all_to_all(send_cache, 'rep', split_axis=0, concat_axis=0, tiled=True)  8.09 us
    all_to_all x1, starting transfers between devices, on_device(): lax.all_to_all(send_cache, 'rep', split_axis=0, concat_axis=0, tiled=True)  7.8 us
    gather x1, local copies, waits for them, and re-layouts, updated_rows(): cache[picks]  5.35 us
    unnamed x1, matrix products  5.32 us
    reshape x1, local copies, waits for them, and re-layouts, on_device(): split_weight = qkv_weight.reshape(3, model, heads_here, HEAD_DIM)  4.64 us
  transfers between devices with their start and end apart: 18, of which 5 were waited for; matrix products, arithmetic and copies ran while one was open for 40% of the time, Pallas kernels for 0%

profile of v9, /device:TPU:2, one launch (start us, length us, event | category | flops | bytes accessed | tf_op | source)
XLA Modules:
  0.0 141.6 jit_solution(4757921902888815658)
XLA Ops:
  7.2 1.2 convert_reduce_fusion
  8.4 1.2 fusion.28
  9.7 2.0 %fusion.31 = bf16[80,2048]{1,0:T(8,128)(2,1)} fusion(bf16[80,2048]{1,0:T(8,128)(2,1)} %param.14, f32[2048]{0:T(1024)} %param.21, f32[2048]{0:T(1024)} %param.20, f32[80]{0:T(128)S(1)} %add_rsqrt_fusion.1, f32[80]{0:T(128)S(1)} %broadcast_multiply_fusion.1), kind=kLoop, calls=%fused_computation.43 | loop fusion | flops 983040 | bytes 672384 | tf_op jit(solution)/shard_map/convert_element_type | solution.py:18
  11.7 1.0 convert_reduce_fusion.1
  12.7 1.1 fusion.42
  13.9 0.8 fusion.87
  14.7 0.7 iota_compare_fusion.1
  15.4 2.7 %convolution_bitcast_fusion = f32[3,40,256]{2,1,0:T(8,128)S(1)} fusion(bf16[3,2048,256]{2,1,0:T(8,128)(2,1)} %param.22, bf16[40,2048]{1,0:T(8,128)(2,1)} %param.16, f32[2048]{0:T(1024)} %param.21, f32[2048]{0:T(1024)} %param.20, f32[40]{0:T(128)S(1)} %add_rsqrt_fusion, f32[40]{0:T(128)S(1)} %broadcast_multiply_fusion), kind=kOutput, calls=%fused_computation.30 | convolution fusion | flops 126320640 | bytes 3449152 | tf_op jit(solution)/shard_map/rd,cde->cre/dot_general | solution.py:27
  18.2 2.6 %fusion.89 = (f32[40,2]{1,0:T(8,128)S(1)}, f32[40,2,128]{2,1,0:T(2,128)S(1)}) fusion(bf16[40,2,128,256]{3,2,1,0:T(8,128)(2,1)} %param.19, pred[2,256]{1,0:T(4,128)(4,1)S(1)} %iota_compare_fusion.5, bf16[40,256]{1,0:T(8,128)(2,1)S(1)} %get-tuple-element.35, pred[40,128]{1,0:T(8,128)(4,1)S(1)} %iota_compare_fusion.1), kind=kOutput, calls=%fused_computation.178 | convolution fusion | flops 5294000 | bytes 2688832 | tf_op jit(solution)/shard_map/rhc,rlc->rhl/dot_general | solution.py:36
  21.0 0.1 multiply_reduce_fusion
  21.3 0.2 fusion.71
  21.7 0.7 gather_fusion
  22.5 2.3 %fusion.17 = f32[40,256]{1,0:T(8,128)S(1)} fusion(bf16[40,2,128,256]{3,2,1,0:T(8,128)(2,1)} %param.19, pred[2,256]{1,0:T(4,128)(4,1)S(1)} %iota_compare_fusion.5, f32[40,2,128]{2,1,0:T(2,128)S(1)} %get-tuple-element.47, f32[40,2]{1,0:T(8,128)S(1)} %copy.85, f32[40,2]{1,0:T(8,128)S(1)} %copy.83), kind=kOutput, calls=%fused_computation.32 | convolution fusion | flops 5304320 | bytes 2704512 | tf_op jit(solution)/shard_map/rhl,rlc->rhc/dot_general | solution.py:56
  24.8 0.3 convolution_convert_fusion.1
  25.3 0.6 gather_fusion.5
  26.0 2.0 %collective-permute-start = (bf16[5,2048]{1,0:T(8,128)(2,1)S(1)}, bf16[5,2048]{1,0:T(8,128)(2,1)S(1)}, u32[]{:S(2)}, u32[]{:S(2)}) collective-permute-start(bf16[5,2048]{1,0:T(8,128)(2,1)S(1)} %get-tuple-element.25), channel_id=1, source_target_pairs={{0,1},{1,2},{2,3},{3,4},{4,5},{5,6},{6,7},{7,0},{8,9},{9,10},{10,1... | collective-permute-start | bytes 61448 | tf_op jit(solution)/shard_map/ppermute | solution.py:78
  28.0 3.3 %collective-permute-start.1 = (bf16[5,2048]{1,0:T(8,128)(2,1)S(1)}, bf16[5,2048]{1,0:T(8,128)(2,1)S(1)}, u32[]{:S(2)}, u32[]{:S(2)}) collective-permute-start(bf16[5,2048]{1,0:T(8,128)(2,1)S(1)} %get-tuple-element.31), channel_id=1, source_target_pairs={{0,2},{1,3},{2,4},{3,5},{4,6},{5,7},{6,0},{7,1},{8,10},{9,11},{10,... | collective-permute-start | bytes 61448 | tf_op jit(solution)/shard_map/ppermute | solution.py:78
  31.3 4.1 %collective-permute-start.2 = (bf16[5,2048]{1,0:T(8,128)(2,1)S(1)}, bf16[5,2048]{1,0:T(8,128)(2,1)S(1)}, u32[]{:S(2)}, u32[]{:S(2)}) collective-permute-start(bf16[5,2048]{1,0:T(8,128)(2,1)S(1)} %get-tuple-element.30), channel_id=1, source_target_pairs={{0,3},{1,4},{2,5},{3,6},{4,7},{5,0},{6,1},{7,2},{8,11},{9,12},{10,... | collective-permute-start | bytes 61448 | tf_op jit(solution)/shard_map/ppermute | solution.py:78
  35.4 0.5 collective-permute-start.3
  35.9 5.0 %collective-permute-start.4 = (bf16[5,2048]{1,0:T(8,128)(2,1)S(1)}, bf16[5,2048]{1,0:T(8,128)(2,1)S(1)}, u32[]{:S(2)}, u32[]{:S(2)}) collective-permute-start(bf16[5,2048]{1,0:T(8,128)(2,1)S(1)} %get-tuple-element.28), channel_id=1, source_target_pairs={{0,5},{1,6},{2,7},{3,0},{4,1},{5,2},{6,3},{7,4},{8,13},{9,14},{10,... | collective-permute-start | bytes 61448 | tf_op jit(solution)/shard_map/ppermute | solution.py:78
  40.9 5.4 %gather_fusion.4 = bf16[32,2,128,256]{3,2,1,0:T(8,128)(2,1)} fusion(bf16[40,2,128,256]{3,2,1,0:T(8,128)(2,1)} %param.19, s32[1024]{0:T(1024)S(1)} %get-tuple-element.48), kind=kCustom, calls=%fused_computation.6 | custom fusion | bytes 8388736 | tf_op jit(solution)/shard_map/gather | solution.py:68
  46.3 0.7 gather_fusion.2
  47.0 0.6 gather_fusion.3
  47.8 4.0 %select_select_fusion = bf16[32,2,128,256]{3,2,1,0:T(8,128)(2,1)} fusion(bf16[32,2,128,256]{3,2,1,0:T(8,128)(2,1)} %gather_fusion.4, pred[32]{0:T(512)(128)(4,1)S(1)} %fusion.77, pred[32,128]{1,0:T(8,128)(4,1)S(1)} %iota_compare_fusion.2, bf16[32,2,256]{2,1,0:T(2,128)(2,1)S(1)} %gather_fusion.3), kind=kLoop, calls=%fused_computation.8 | loop fusion | flops 4194304 | bytes 8425504 | tf_op jit(solution)/shard_map/jit(_where)/select_n | solution.py:120
  51.9 7.8 %all-to-all-start = ((bf16[32,2,128,256]{3,2,1,0:T(8,128)(2,1)}), bf16[32,2,128,256]{3,2,1,0:T(8,128)(2,1)}, u32[]{:S(2)}, u32[]{:S(2)}) async-start(bf16[32,2,128,256]{3,2,1,0:T(8,128)(2,1)} %select_select_fusion), calls=%async_computation.1 | async-start | bytes 8388608 | tf_op jit(solution)/shard_map/all_to_all | solution.py:125
  59.8 0.3 fusion.11
  60.1 2.6 %collective-permute-start.5 = (bf16[5,2048]{1,0:T(8,128)(2,1)S(1)}, bf16[5,2048]{1,0:T(8,128)(2,1)S(1)}, u32[]{:S(2)}, u32[]{:S(2)}) collective-permute-start(bf16[5,2048]{1,0:T(8,128)(2,1)S(1)} %get-tuple-element.27), channel_id=1, source_target_pairs={{0,6},{1,7},{2,0},{3,1},{4,2},{5,3},{6,4},{7,5},{8,14},{9,15},{10,... | collective-permute-start | bytes 61448 | tf_op jit(solution)/shard_map/ppermute | solution.py:78
  62.8 1.0 collective-permute-start.6
  63.8 4.6 %copy.96 = bf16[3,2048,256]{1,2,0:T(8,128)(2,1)} copy(bf16[3,2048,256]{2,1,0:T(8,128)(2,1)} %param.22) | data formatting | bytes 6291456 | tf_op jit(solution)/shard_map/reshape | solution.py:133
  68.5 0.9 fusion.63
  69.5 5.3 %fusion.90 = f32[640,768]{0,1:S(1)} fusion(bf16[640,2048]{1,0:T(8,128)(2,1)} %all-gather.2.cloned.1.call-done, bf16[2048,768]{0,1:T(8,128)(2,1)} %bitcast.160), kind=kOutput, calls=%fused_computation.179 | convolution fusion | flops 2013265920 | bytes 7733248
  74.8 0.1 fusion.35
  75.0 0.7 fusion.46
  75.6 2.0 %fusion.88 = (f32[2,640]{1,0:T(2,128)S(1)}, f32[2,640,640]{1,2,0:T(8,128)S(1)}) fusion(f32[2,640,640]{1,2,0:T(8,128)S(1)} %fusion.46, pred[640,640]{0,1:T(8,128)(4,1)S(1)} %fusion.11), kind=kOutput, calls=%fused_computation.177 | output fusion | flops 4915839 | bytes 6968320 | tf_op jit(solution)/shard_map/sub | solution.py:150
  77.6 0.5 fusion.13
  78.1 2.4 %convolution_convert_fusion = bf16[640,2048]{1,0:T(8,128)(2,1)} fusion(bf16[640,256]{0,1:T(8,128)(2,1)S(1)} %bitcast.167, bf16[256,2048]{1,0:T(8,128)(2,1)S(1)} %copy-done), kind=kOutput, calls=%fused_computation.13 | convolution fusion | flops 672399360 | bytes 3997696 | tf_op jit(solution)/shard_map/dot_general | solution.py:156
  80.5 1.0 collective-permute-start.7
  81.5 0.4 collective-permute-start.8
  81.9 2.0 %collective-permute-start.9 = (bf16[5,2048]{1,0:T(8,128)(2,1)S(1)}, bf16[5,2048]{1,0:T(8,128)(2,1)S(1)}, u32[]{:S(2)}, u32[]{:S(2)}) collective-permute-start(bf16[5,2048]{1,0:T(8,128)(2,1)S(1)} %fusion.63), channel_id=1, source_target_pairs={{0,3},{1,4},{2,5},{3,6},{4,7},{5,0},{6,1},{7,2},{8,11},{9,12},{10,... | collective-permute-start | bytes 61448 | tf_op jit(solution)/shard_map/ppermute | solution.py:89
  83.9 3.5 %collective-permute-start.10 = (bf16[5,2048]{1,0:T(8,128)(2,1)S(1)}, bf16[5,2048]{1,0:T(8,128)(2,1)S(1)}, u32[]{:S(2)}, u32[]{:S(2)}) collective-permute-start(bf16[5,2048]{1,0:T(8,128)(2,1)S(1)} %fusion.63), channel_id=1, source_target_pairs={{0,4},{1,5},{2,6},{3,7},{4,0},{5,1},{6,2},{7,3},{8,12},{9,13},{10,... | collective-permute-start | bytes 61448 | tf_op jit(solution)/shard_map/ppermute | solution.py:89
  87.5 2.2 %collective-permute-start.11 = (bf16[5,2048]{1,0:T(8,128)(2,1)S(1)}, bf16[5,2048]{1,0:T(8,128)(2,1)S(1)}, u32[]{:S(2)}, u32[]{:S(2)}) collective-permute-start(bf16[5,2048]{1,0:T(8,128)(2,1)S(1)} %fusion.63), channel_id=1, source_target_pairs={{0,5},{1,6},{2,7},{3,0},{4,1},{5,2},{6,3},{7,4},{8,13},{9,14},{10,... | collective-permute-start | bytes 61448 | tf_op jit(solution)/shard_map/ppermute | solution.py:89
  89.7 3.4 %slice_select_fusion = bf16[24,2,128,256]{3,2,1,0:T(8,128)(2,1)} fusion(bf16[40,2,128,256]{3,2,1,0:T(8,128)(2,1)} %param.19, pred[24,128]{1,0:T(8,128)(4,1)S(1)} %iota_compare_fusion.3, bf16[24,2,256]{2,1,0:T(2,128)(2,1)S(1)} %copy.90), kind=kLoop, calls=%fused_computation.14 | loop fusion | flops 1572864 | bytes 6319104 | tf_op jit(solution)/shard_map/jit(_where)/select_n | solution.py:164
  93.1 0.2 copy.88
  93.2 0.2 copy.89
  93.4 0.9 pad_maximum_fusion
  94.3 2.1 %collective-permute-start.12 = (bf16[5,2048]{1,0:T(8,128)(2,1)S(1)}, bf16[5,2048]{1,0:T(8,128)(2,1)S(1)}, u32[]{:S(2)}, u32[]{:S(2)}) collective-permute-start(bf16[5,2048]{1,0:T(8,128)(2,1)S(1)} %fusion.63), channel_id=1, source_target_pairs={{0,6},{1,7},{2,0},{3,1},{4,2},{5,3},{6,4},{7,5},{8,14},{9,15},{10,... | collective-permute-start | bytes 61448 | tf_op jit(solution)/shard_map/ppermute | solution.py:89
  96.4 1.6 %collective-permute-start.13 = (bf16[5,2048]{1,0:T(8,128)(2,1)S(1)}, bf16[5,2048]{1,0:T(8,128)(2,1)S(1)}, u32[]{:S(2)}, u32[]{:S(2)}) collective-permute-start(bf16[5,2048]{1,0:T(8,128)(2,1)S(1)} %fusion.63), channel_id=1, source_target_pairs={{0,7},{1,0},{2,1},{3,2},{4,3},{5,4},{6,5},{7,6},{8,15},{9,8},{10,9... | collective-permute-start | bytes 61448 | tf_op jit(solution)/shard_map/ppermute | solution.py:89
  98.0 1.6 %collective-permute-done.12 = bf16[5,2048]{1,0:T(8,128)(2,1)S(1)} collective-permute-done((bf16[5,2048]{1,0:T(8,128)(2,1)S(1)}, bf16[5,2048]{1,0:T(8,128)(2,1)S(1)}, u32[]{:S(2)}, u32[]{:S(2)}) %collective-permute-start.12) | collective-permute-done | bytes 20512 | tf_op jit(solution)/shard_map/ppermute | solution.py:89
  99.6 0.7 collective-permute-done.13
  100.3 0.6 gather_fusion.6
  100.9 0.1 broadcast_select_fusion.1
  101.1 0.7 gather_fusion.1
  101.8 8.1 %all-to-all-done = bf16[32,2,128,256]{3,2,1,0:T(8,128)(2,1)} async-done(((bf16[32,2,128,256]{3,2,1,0:T(8,128)(2,1)}), bf16[32,2,128,256]{3,2,1,0:T(8,128)(2,1)}, u32[]{:S(2)}, u32[]{:S(2)}) %all-to-all-start) | async-done | bytes 4194336 | tf_op jit(solution)/shard_map/all_to_all | solution.py:125
  109.9 0.5 broadcast.368
  110.4 0.7 reduce.1
  111.1 0.7 reshape.482
  111.8 9.1 %all-to-all-start.1 = ((bf16[32,2,1024]{2,1,0:T(2,128)(2,1)}), bf16[32,2,1024]{2,1,0:T(2,128)(2,1)S(1)}, u32[]{:S(2)}, u32[]{:S(2)}) async-start(bf16[32,2,1024]{2,1,0:T(2,128)(2,1)} %reshape.482), calls=%async_computation.2 | async-start | bytes 262144 | tf_op jit(solution)/shard_map/all_to_all | solution.py:177
  120.9 4.6 %broadcast_select_fusion = bf16[32,2,128,256]{3,2,1,0:T(8,128)(2,1)} fusion(bf16[32,2,128,256]{3,2,1,0:T(8,128)(2,1)} %all-to-all-done, pred[]{:T(512)} %bitcast.57), kind=kLoop, calls=%fused_computation.9 | loop fusion | flops 2097152 | bytes 8388609 | tf_op jit(solution)/shard_map/jit(_where)/select_n | solution.py:176
  125.5 0.6 slice.134
  126.1 1.4 %all-to-all-done.1 = bf16[32,2,1024]{2,1,0:T(2,128)(2,1)S(1)} async-done(((bf16[32,2,1024]{2,1,0:T(2,128)(2,1)}), bf16[32,2,1024]{2,1,0:T(2,128)(2,1)S(1)}, u32[]{:S(2)}, u32[]{:S(2)}) %all-to-all-start.1) | async-done | bytes 131104 | tf_op jit(solution)/shard_map/all_to_all | solution.py:177
  127.6 0.1 reshape.483
  127.7 0.7 copy.101
  128.4 4.6 %reduce-scatter.2.cloned.1.call-done = bf16[80,2048]{1,0:T(8,128)(2,1)} async-done(((bf16[640,2048]{1,0:T(8,128)(2,1)}), bf16[80,2048]{1,0:T(8,128)(2,1)}) %reduce-scatter.2.cloned.1.call-update) | async-done | bytes 327696 | tf_op jit(solution)/shard_map/reduce_scatter | solution.py:167
  133.0 1.8 %fusion.33 = bf16[80,2048]{1,0:T(8,128)(2,1)} fusion(bf16[80,2048]{1,0:T(8,128)(2,1)S(1)} %copy-done.2, bf16[80,2048]{1,0:T(8,128)(2,1)} %reduce-scatter.2.cloned.1.call-done, f32[2048]{0:T(1024)S(1)} %copy-done.3), kind=kLoop, calls=%fused_computation.45 | loop fusion | flops 819200 | bytes 991232 | tf_op jit(solution)/shard_map/convert_element_type | solution.py:171
  (81 shorter events, 1.7 us)
Async XLA Ops:
  7.2 17.6 %copy-start = (bf16[256,2048]{1,0:T(8,128)(2,1)S(1)}, bf16[256,2048]{1,0:T(8,128)(2,1)}, u32[]{:S(2)}) copy-start(bf16[256,2048]{1,0:T(8,128)(2,1)} %param.24) | copy-start | bytes 3145732
  7.2 62.3 %all-gather.2.cloned.1.call-start = ((), (), s32[]{:S(2)}) async-start(), calls=%async_computation.3 | async-start | bytes 2949120 | tf_op jit(solution)/shard_map/all_gather | solution.py:131
  20.8 4.4 %copy-start.5 = (s32[16,1]{0,1:T(1,128)S(1)}, s32[16,1]{0,1:T(1,128)}, u32[]{:S(2)}) copy-start(s32[16,1]{0,1:T(1,128)} %param.18) | copy-start | bytes 196
  26.0 34.1 %collective-permute-start = (bf16[5,2048]{1,0:T(8,128)(2,1)S(1)}, bf16[5,2048]{1,0:T(8,128)(2,1)S(1)}, u32[]{:S(2)}, u32[]{:S(2)}) collective-permute-start(bf16[5,2048]{1,0:T(8,128)(2,1)S(1)} %get-tuple-element.25), channel_id=1, source_target_pairs={{0,1},{1,2},{2,3},{3,4},{4,5},{5,6},{6,7},{7,0},{8,9},{9,10},{10,1... | collective-permute-start | bytes 61448 | tf_op jit(solution)/shard_map/ppermute | solution.py:78
  28.0 34.8 %collective-permute-start.1 = (bf16[5,2048]{1,0:T(8,128)(2,1)S(1)}, bf16[5,2048]{1,0:T(8,128)(2,1)S(1)}, u32[]{:S(2)}, u32[]{:S(2)}) collective-permute-start(bf16[5,2048]{1,0:T(8,128)(2,1)S(1)} %get-tuple-element.31), channel_id=1, source_target_pairs={{0,2},{1,3},{2,4},{3,5},{4,6},{5,7},{6,0},{7,1},{8,10},{9,11},{10,... | collective-permute-start | bytes 61448 | tf_op jit(solution)/shard_map/ppermute | solution.py:78
  31.3 37.2 %collective-permute-start.2 = (bf16[5,2048]{1,0:T(8,128)(2,1)S(1)}, bf16[5,2048]{1,0:T(8,128)(2,1)S(1)}, u32[]{:S(2)}, u32[]{:S(2)}) collective-permute-start(bf16[5,2048]{1,0:T(8,128)(2,1)S(1)} %get-tuple-element.30), channel_id=1, source_target_pairs={{0,3},{1,4},{2,5},{3,6},{4,7},{5,0},{6,1},{7,2},{8,11},{9,12},{10,... | collective-permute-start | bytes 61448 | tf_op jit(solution)/shard_map/ppermute | solution.py:78
  35.4 33.1 %collective-permute-start.3 = (bf16[5,2048]{1,0:T(8,128)(2,1)S(1)}, bf16[5,2048]{1,0:T(8,128)(2,1)S(1)}, u32[]{:S(2)}, u32[]{:S(2)}) collective-permute-start(bf16[5,2048]{1,0:T(8,128)(2,1)S(1)} %get-tuple-element.29), channel_id=1, source_target_pairs={{0,4},{1,5},{2,6},{3,7},{4,0},{5,1},{6,2},{7,3},{8,12},{9,13},{10,... | collective-permute-start | bytes 61448 | tf_op jit(solution)/shard_map/ppermute | solution.py:78
  35.9 32.6 %collective-permute-start.4 = (bf16[5,2048]{1,0:T(8,128)(2,1)S(1)}, bf16[5,2048]{1,0:T(8,128)(2,1)S(1)}, u32[]{:S(2)}, u32[]{:S(2)}) collective-permute-start(bf16[5,2048]{1,0:T(8,128)(2,1)S(1)} %get-tuple-element.28), channel_id=1, source_target_pairs={{0,5},{1,6},{2,7},{3,0},{4,1},{5,2},{6,3},{7,4},{8,13},{9,14},{10,... | collective-permute-start | bytes 61448 | tf_op jit(solution)/shard_map/ppermute | solution.py:78
  40.9 5.4 %copy-start.1 = (s32[40]{0:T(128)S(1)}, s32[40]{0:T(128)}, u32[]{:S(2)}) copy-start(s32[40]{0:T(128)} %param.17) | copy-start | bytes 484
  51.8 7.9 %copy-start.4 = (s32[1,640]{1,0:T(1,128)S(1)}, s32[1,640]{1,0:T(1,128)}, u32[]{:S(2)}) copy-start(s32[1,640]{1,0:T(1,128)} %param.15) | copy-start | bytes 7684
  51.9 58.1 %all-to-all-start = ((bf16[32,2,128,256]{3,2,1,0:T(8,128)(2,1)}), bf16[32,2,128,256]{3,2,1,0:T(8,128)(2,1)}, u32[]{:S(2)}, u32[]{:S(2)}) async-start(bf16[32,2,128,256]{3,2,1,0:T(8,128)(2,1)} %select_select_fusion), calls=%async_computation.1 | async-start | bytes 8388608 | tf_op jit(solution)/shard_map/all_to_all | solution.py:125
  59.7 73.3 %reduce-scatter.2.cloned.1.call-start = ((), (), s32[]{:S(2)}) async-start(), calls=%async_computation.4 | async-start | bytes 2949120 | tf_op jit(solution)/shard_map/reduce_scatter | solution.py:167
  59.8 8.7 %copy-start.3 = (f32[2048]{0:T(1024)S(1)}, f32[2048]{0:T(1024)}, u32[]{:S(2)}) copy-start(f32[2048]{0:T(1024)} %param.25) | copy-start | bytes 24580
  60.1 8.4 %collective-permute-start.5 = (bf16[5,2048]{1,0:T(8,128)(2,1)S(1)}, bf16[5,2048]{1,0:T(8,128)(2,1)S(1)}, u32[]{:S(2)}, u32[]{:S(2)}) collective-permute-start(bf16[5,2048]{1,0:T(8,128)(2,1)S(1)} %get-tuple-element.27), channel_id=1, source_target_pairs={{0,6},{1,7},{2,0},{3,1},{4,2},{5,3},{6,4},{7,5},{8,14},{9,15},{10,... | collective-permute-start | bytes 61448 | tf_op jit(solution)/shard_map/ppermute | solution.py:78
  62.8 5.7 %collective-permute-start.6 = (bf16[5,2048]{1,0:T(8,128)(2,1)S(1)}, bf16[5,2048]{1,0:T(8,128)(2,1)S(1)}, u32[]{:S(2)}, u32[]{:S(2)}) collective-permute-start(bf16[5,2048]{1,0:T(8,128)(2,1)S(1)} %get-tuple-element.26), channel_id=1, source_target_pairs={{0,7},{1,0},{2,1},{3,2},{4,3},{5,4},{6,5},{7,6},{8,15},{9,8},{10,9... | collective-permute-start | bytes 61448 | tf_op jit(solution)/shard_map/ppermute | solution.py:78
  80.5 13.8 %collective-permute-start.7 = (bf16[5,2048]{1,0:T(8,128)(2,1)S(1)}, bf16[5,2048]{1,0:T(8,128)(2,1)S(1)}, u32[]{:S(2)}, u32[]{:S(2)}) collective-permute-start(bf16[5,2048]{1,0:T(8,128)(2,1)S(1)} %fusion.63), channel_id=1, source_target_pairs={{0,1},{1,2},{2,3},{3,4},{4,5},{5,6},{6,7},{7,0},{8,9},{9,10},{10,1... | collective-permute-start | bytes 61448 | tf_op jit(solution)/shard_map/ppermute | solution.py:89
  81.5 14.9 %collective-permute-start.8 = (bf16[5,2048]{1,0:T(8,128)(2,1)S(1)}, bf16[5,2048]{1,0:T(8,128)(2,1)S(1)}, u32[]{:S(2)}, u32[]{:S(2)}) collective-permute-start(bf16[5,2048]{1,0:T(8,128)(2,1)S(1)} %fusion.63), channel_id=1, source_target_pairs={{0,2},{1,3},{2,4},{3,5},{4,6},{5,7},{6,0},{7,1},{8,10},{9,11},{10,... | collective-permute-start | bytes 61448 | tf_op jit(solution)/shard_map/ppermute | solution.py:89
  81.9 16.1 %collective-permute-start.9 = (bf16[5,2048]{1,0:T(8,128)(2,1)S(1)}, bf16[5,2048]{1,0:T(8,128)(2,1)S(1)}, u32[]{:S(2)}, u32[]{:S(2)}) collective-permute-start(bf16[5,2048]{1,0:T(8,128)(2,1)S(1)} %fusion.63), channel_id=1, source_target_pairs={{0,3},{1,4},{2,5},{3,6},{4,7},{5,0},{6,1},{7,2},{8,11},{9,12},{10,... | collective-permute-start | bytes 61448 | tf_op jit(solution)/shard_map/ppermute | solution.py:89
  83.9 14.1 %collective-permute-start.10 = (bf16[5,2048]{1,0:T(8,128)(2,1)S(1)}, bf16[5,2048]{1,0:T(8,128)(2,1)S(1)}, u32[]{:S(2)}, u32[]{:S(2)}) collective-permute-start(bf16[5,2048]{1,0:T(8,128)(2,1)S(1)} %fusion.63), channel_id=1, source_target_pairs={{0,4},{1,5},{2,6},{3,7},{4,0},{5,1},{6,2},{7,3},{8,12},{9,13},{10,... | collective-permute-start | bytes 61448 | tf_op jit(solution)/shard_map/ppermute | solution.py:89
  87.5 10.6 %collective-permute-start.11 = (bf16[5,2048]{1,0:T(8,128)(2,1)S(1)}, bf16[5,2048]{1,0:T(8,128)(2,1)S(1)}, u32[]{:S(2)}, u32[]{:S(2)}) collective-permute-start(bf16[5,2048]{1,0:T(8,128)(2,1)S(1)} %fusion.63), channel_id=1, source_target_pairs={{0,5},{1,6},{2,7},{3,0},{4,1},{5,2},{6,3},{7,4},{8,13},{9,14},{10,... | collective-permute-start | bytes 61448 | tf_op jit(solution)/shard_map/ppermute | solution.py:89
  94.3 5.3 %collective-permute-start.12 = (bf16[5,2048]{1,0:T(8,128)(2,1)S(1)}, bf16[5,2048]{1,0:T(8,128)(2,1)S(1)}, u32[]{:S(2)}, u32[]{:S(2)}) collective-permute-start(bf16[5,2048]{1,0:T(8,128)(2,1)S(1)} %fusion.63), channel_id=1, source_target_pairs={{0,6},{1,7},{2,0},{3,1},{4,2},{5,3},{6,4},{7,5},{8,14},{9,15},{10,... | collective-permute-start | bytes 61448 | tf_op jit(solution)/shard_map/ppermute | solution.py:89
  96.4 3.9 %collective-permute-start.13 = (bf16[5,2048]{1,0:T(8,128)(2,1)S(1)}, bf16[5,2048]{1,0:T(8,128)(2,1)S(1)}, u32[]{:S(2)}, u32[]{:S(2)}) collective-permute-start(bf16[5,2048]{1,0:T(8,128)(2,1)S(1)} %fusion.63), channel_id=1, source_target_pairs={{0,7},{1,0},{2,1},{3,2},{4,3},{5,4},{6,5},{7,6},{8,15},{9,8},{10,9... | collective-permute-start | bytes 61448 | tf_op jit(solution)/shard_map/ppermute | solution.py:89
  111.8 15.7 %all-to-all-start.1 = ((bf16[32,2,1024]{2,1,0:T(2,128)(2,1)}), bf16[32,2,1024]{2,1,0:T(2,128)(2,1)S(1)}, u32[]{:S(2)}, u32[]{:S(2)}) async-start(bf16[32,2,1024]{2,1,0:T(2,128)(2,1)} %reshape.482), calls=%async_computation.2 | async-start | bytes 262144 | tf_op jit(solution)/shard_map/all_to_all | solution.py:177
  120.9 12.1 %copy-start.2 = (bf16[80,2048]{1,0:T(8,128)(2,1)S(1)}, bf16[80,2048]{1,0:T(8,128)(2,1)}, u32[]{:S(2)}) copy-start(bf16[80,2048]{1,0:T(8,128)(2,1)} %param.14) | copy-start | bytes 983044
Sparse Core Ops, SparseCore 0:
  11.8 50.3 all-gather.1
  89.8 43.0 reduce-scatter.1

commit v10 on v9

--- a/solution.py
+++ b/solution.py
@@ -167,6 +167,7 @@
     attended = lax.psum_scatter(prompt_partial, "tp", scatter_dimension=0, tiled=True).astype(
         jnp.float32
     )
+    own_out, kept_cache = lax.optimization_barrier((own_out, kept_cache))
     decode_out = gather_over_tp(own_out)
     prompt_out = (prompt_rows.astype(jnp.float32) + attended + out_bias).astype(jnp.bfloat16)
     prompt_cache = jnp.stack([key_rows, value_rows])

time: 142 us -> 138 us (0.972); the launches traced: 142 us -> 135 us
  waiting for transfers between devices: 16.4 us -> 9.67 us
    reduce_scatter x1, waiting for transfers between devices: 4.57 us -> 0.01 us  [on_device(): lax.psum_scatter(prompt_partial, 'tp', scatter_dimension=0, tiled=True)]
    all_to_all x1, waiting for transfers between devices: 8.09 us -> 4.52 us  [on_device(): lax.all_to_all(send_cache, 'rep', split_axis=0, concat_axis=0, tiled=True)]
    ppermute x7, starting transfers between devices: 12.8 us -> 14.2 us  [gather_over_tp(): lax.ppermute(own_out, 'tp', [(i, (i + shift) % n) for i in range(n)])]
  transfers between devices with their start and end apart: 18 -> 18, of which waited for: 5 -> 5; matrix products, arithmetic and copies ran while one was open for 40% -> 42% of each run, Pallas kernels for 0% -> 0%
where the time goes in v10:
time: 138 us; the launch traced here: 135 us
  starting transfers between devices  48.5 us (35%)
  other arithmetic  27 us (20%)
  local copies, waits for them, and re-layouts  18.5 us (13%)
  matrix products  16.8 us (12%)
  between operations  14.6 us (11%)
  waiting for transfers between devices  9.67 us (7%)
    ppermute x7, starting transfers between devices, scatter_over_tp(): lax.ppermute(rolled[shift], 'tp', [(i, (i + shift) % n) for i in range(n)])  17.3 us
    ppermute x7, starting transfers between devices, gather_over_tp(): lax.ppermute(own_out, 'tp', [(i, (i + shift) % n) for i in range(n)])  14.2 us
    all_to_all x1, starting transfers between devices, on_device(): lax.all_to_all(send_rows, 'rep', split_axis=0, concat_axis=0, tiled=True)  9.08 us
    all_to_all x1, starting transfers between devices, on_device(): lax.all_to_all(send_cache, 'rep', split_axis=0, concat_axis=0, tiled=True)  7.86 us
    gather x1, local copies, waits for them, and re-layouts, updated_rows(): cache[picks]  5.33 us
    unnamed x1, matrix products  5.32 us
    reshape x1, local copies, waits for them, and re-layouts, on_device(): split_weight = qkv_weight.reshape(3, model, heads_here, HEAD_DIM)  4.64 us
    select_n x1, other arithmetic, on_device(): jnp.where(request_ages[0] > 0, moved_cache, jnp.zeros((), jnp.bfloat16))  4.57 us
  transfers between devices with their start and end apart: 18, of which 5 were waited for; matrix products, arithmetic and copies ran while one was open for 42% of the time, Pallas kernels for 0%

profile of v10, /device:TPU:2, one launch (start us, length us, event | category | flops | bytes accessed | tf_op | source)
XLA Modules:
  0.0 135.1 jit_solution(2682573401030760468)
XLA Ops:
  7.2 1.2 convert_reduce_fusion
  8.4 1.2 fusion.28
  9.7 2.0 %fusion.31 = bf16[80,2048]{1,0:T(8,128)(2,1)} fusion(bf16[80,2048]{1,0:T(8,128)(2,1)} %param.14, f32[2048]{0:T(1024)} %param.21, f32[2048]{0:T(1024)} %param.20, f32[80]{0:T(128)S(1)} %add_rsqrt_fusion.1, f32[80]{0:T(128)S(1)} %broadcast_multiply_fusion.1), kind=kLoop, calls=%fused_computation.43 | loop fusion | flops 983040 | bytes 672384 | tf_op jit(solution)/shard_map/convert_element_type | solution.py:18
  11.7 0.8 fusion.87
  12.5 1.0 convert_reduce_fusion.1
  13.6 1.1 fusion.42
  14.7 0.7 iota_compare_fusion.1
  15.4 2.7 %convolution_bitcast_fusion = f32[3,40,256]{2,1,0:T(8,128)S(1)} fusion(bf16[3,2048,256]{2,1,0:T(8,128)(2,1)} %param.22, bf16[40,2048]{1,0:T(8,128)(2,1)} %param.16, f32[2048]{0:T(1024)} %param.21, f32[2048]{0:T(1024)} %param.20, f32[40]{0:T(128)S(1)} %add_rsqrt_fusion, f32[40]{0:T(128)S(1)} %broadcast_multiply_fusion), kind=kOutput, calls=%fused_computation.30 | convolution fusion | flops 126320640 | bytes 3449152 | tf_op jit(solution)/shard_map/rd,cde->cre/dot_general | solution.py:27
  18.2 0.1 multiply_reduce_fusion
  18.5 2.6 %fusion.89 = (f32[40,2]{1,0:T(8,128)S(1)}, f32[40,2,128]{2,1,0:T(2,128)S(1)}) fusion(bf16[40,2,128,256]{3,2,1,0:T(8,128)(2,1)} %param.19, pred[2,256]{1,0:T(4,128)(4,1)S(1)} %iota_compare_fusion.5, bf16[40,256]{1,0:T(8,128)(2,1)S(1)} %get-tuple-element.39, pred[40,128]{1,0:T(8,128)(4,1)S(1)} %iota_compare_fusion.1), kind=kOutput, calls=%fused_computation.178 | convolution fusion | flops 5294000 | bytes 2688832 | tf_op jit(solution)/shard_map/rhc,rlc->rhl/dot_general | solution.py:36
  21.3 0.2 fusion.71
  21.7 0.7 gather_fusion
  22.5 2.3 %fusion.17 = f32[40,256]{1,0:T(8,128)S(1)} fusion(bf16[40,2,128,256]{3,2,1,0:T(8,128)(2,1)} %param.19, pred[2,256]{1,0:T(4,128)(4,1)S(1)} %iota_compare_fusion.5, f32[40,2,128]{2,1,0:T(2,128)S(1)} %get-tuple-element.51, f32[40,2]{1,0:T(8,128)S(1)} %copy.85, f32[40,2]{1,0:T(8,128)S(1)} %copy.83), kind=kOutput, calls=%fused_computation.32 | convolution fusion | flops 5304320 | bytes 2704512 | tf_op jit(solution)/shard_map/rhl,rlc->rhc/dot_general | solution.py:56
  24.8 0.3 convolution_convert_fusion.1
  25.3 0.6 gather_fusion.5
  25.9 0.1 broadcast_select_fusion.2
  26.0 6.0 %collective-permute-start.6 = (bf16[5,2048]{1,0:T(8,128)(2,1)S(1)}, bf16[5,2048]{1,0:T(8,128)(2,1)S(1)}, u32[]{:S(2)}, u32[]{:S(2)}) collective-permute-start(bf16[5,2048]{1,0:T(8,128)(2,1)S(1)} %get-tuple-element.30), channel_id=1, source_target_pairs={{0,7},{1,0},{2,1},{3,2},{4,3},{5,4},{6,5},{7,6},{8,15},{9,8},{10,9... | collective-permute-start | bytes 61448 | tf_op jit(solution)/shard_map/ppermute | solution.py:78
  32.1 1.3 collective-permute-start.5
  33.4 0.4 collective-permute-start.4
  33.8 5.1 %collective-permute-start.3 = (bf16[5,2048]{1,0:T(8,128)(2,1)S(1)}, bf16[5,2048]{1,0:T(8,128)(2,1)S(1)}, u32[]{:S(2)}, u32[]{:S(2)}) collective-permute-start(bf16[5,2048]{1,0:T(8,128)(2,1)S(1)} %get-tuple-element.33), channel_id=1, source_target_pairs={{0,4},{1,5},{2,6},{3,7},{4,0},{5,1},{6,2},{7,3},{8,12},{9,13},{10,... | collective-permute-start | bytes 61448 | tf_op jit(solution)/shard_map/ppermute | solution.py:78
  38.9 5.3 %gather_fusion.4 = bf16[32,2,128,256]{3,2,1,0:T(8,128)(2,1)} fusion(bf16[40,2,128,256]{3,2,1,0:T(8,128)(2,1)} %param.19, s32[1024]{0:T(1024)S(1)} %get-tuple-element.52), kind=kCustom, calls=%fused_computation.6 | custom fusion | bytes 8388736 | tf_op jit(solution)/shard_map/gather | solution.py:68
  44.3 0.7 gather_fusion.2
  45.0 0.6 gather_fusion.3
  45.8 4.0 %select_select_fusion = bf16[32,2,128,256]{3,2,1,0:T(8,128)(2,1)} fusion(bf16[32,2,128,256]{3,2,1,0:T(8,128)(2,1)} %gather_fusion.4, pred[32]{0:T(512)(128)(4,1)S(1)} %fusion.77, pred[32,128]{1,0:T(8,128)(4,1)S(1)} %iota_compare_fusion.2, bf16[32,2,256]{2,1,0:T(2,128)(2,1)S(1)} %gather_fusion.3), kind=kLoop, calls=%fused_computation.8 | loop fusion | flops 4194304 | bytes 8425504 | tf_op jit(solution)/shard_map/jit(_where)/select_n | solution.py:120
  49.8 7.9 %all-to-all-start = ((bf16[32,2,128,256]{3,2,1,0:T(8,128)(2,1)}), bf16[32,2,128,256]{3,2,1,0:T(8,128)(2,1)}, u32[]{:S(2)}, u32[]{:S(2)}) async-start(bf16[32,2,128,256]{3,2,1,0:T(8,128)(2,1)} %select_select_fusion), calls=%async_computation.1 | async-start | bytes 8388608 | tf_op jit(solution)/shard_map/all_to_all | solution.py:125
  57.9 0.3 fusion.11
  58.2 2.4 %collective-permute-start.1 = (bf16[5,2048]{1,0:T(8,128)(2,1)S(1)}, bf16[5,2048]{1,0:T(8,128)(2,1)S(1)}, u32[]{:S(2)}, u32[]{:S(2)}) collective-permute-start(bf16[5,2048]{1,0:T(8,128)(2,1)S(1)} %get-tuple-element.35), channel_id=1, source_target_pairs={{0,2},{1,3},{2,4},{3,5},{4,6},{5,7},{6,0},{7,1},{8,10},{9,11},{10,... | collective-permute-start | bytes 61448 | tf_op jit(solution)/shard_map/ppermute | solution.py:78
  60.6 1.9 %collective-permute-start = (bf16[5,2048]{1,0:T(8,128)(2,1)S(1)}, bf16[5,2048]{1,0:T(8,128)(2,1)S(1)}, u32[]{:S(2)}, u32[]{:S(2)}) collective-permute-start(bf16[5,2048]{1,0:T(8,128)(2,1)S(1)} %get-tuple-element.29), channel_id=1, source_target_pairs={{0,1},{1,2},{2,3},{3,4},{4,5},{5,6},{6,7},{7,0},{8,9},{9,10},{10,1... | collective-permute-start | bytes 61448 | tf_op jit(solution)/shard_map/ppermute | solution.py:78
  62.6 4.6 %copy.96 = bf16[3,2048,256]{1,2,0:T(8,128)(2,1)} copy(bf16[3,2048,256]{2,1,0:T(8,128)(2,1)} %param.22) | data formatting | bytes 6291456 | tf_op jit(solution)/shard_map/reshape | solution.py:133
  67.3 0.9 fusion.63
  68.3 5.3 %fusion.90 = f32[640,768]{0,1:S(1)} fusion(bf16[640,2048]{1,0:T(8,128)(2,1)} %all-gather.2.cloned.1.call-done, bf16[2048,768]{0,1:T(8,128)(2,1)} %bitcast.160), kind=kOutput, calls=%fused_computation.179 | convolution fusion | flops 2013265920 | bytes 7733248
  73.6 0.1 fusion.35
  73.7 0.7 fusion.46
  74.4 2.0 %fusion.88 = (f32[2,640]{1,0:T(2,128)S(1)}, f32[2,640,640]{1,2,0:T(8,128)S(1)}) fusion(f32[2,640,640]{1,2,0:T(8,128)S(1)} %fusion.46, pred[640,640]{0,1:T(8,128)(4,1)S(1)} %fusion.11), kind=kOutput, calls=%fused_computation.177 | output fusion | flops 4915839 | bytes 6968320 | tf_op jit(solution)/shard_map/sub | solution.py:150
  76.4 0.5 fusion.13
  76.9 2.4 %convolution_convert_fusion = bf16[640,2048]{1,0:T(8,128)(2,1)} fusion(bf16[640,256]{0,1:T(8,128)(2,1)S(1)} %bitcast.167, bf16[256,2048]{1,0:T(8,128)(2,1)S(1)} %copy-done), kind=kOutput, calls=%fused_computation.13 | convolution fusion | flops 672399360 | bytes 3997696 | tf_op jit(solution)/shard_map/dot_general | solution.py:156
  79.4 3.4 %slice_select_fusion = bf16[24,2,128,256]{3,2,1,0:T(8,128)(2,1)} fusion(bf16[40,2,128,256]{3,2,1,0:T(8,128)(2,1)} %param.19, pred[24,128]{1,0:T(8,128)(4,1)S(1)} %iota_compare_fusion.3, bf16[24,2,256]{2,1,0:T(2,128)(2,1)S(1)} %copy.90), kind=kLoop, calls=%fused_computation.14 | loop fusion | flops 1572864 | bytes 6319104 | tf_op jit(solution)/shard_map/jit(_where)/select_n | solution.py:164
  82.7 1.0 collective-permute-start.7
  83.7 2.8 %collective-permute-start.8 = (bf16[5,2048]{1,0:T(8,128)(2,1)S(1)}, bf16[5,2048]{1,0:T(8,128)(2,1)S(1)}, u32[]{:S(2)}, u32[]{:S(2)}) collective-permute-start(bf16[5,2048]{1,0:T(8,128)(2,1)S(1)} %fusion.63), channel_id=1, source_target_pairs={{0,2},{1,3},{2,4},{3,5},{4,6},{5,7},{6,0},{7,1},{8,10},{9,11},{10,... | collective-permute-start | bytes 61448 | tf_op jit(solution)/shard_map/ppermute | solution.py:89
  86.5 0.3 collective-permute-start.9
  86.9 5.2 %collective-permute-start.10 = (bf16[5,2048]{1,0:T(8,128)(2,1)S(1)}, bf16[5,2048]{1,0:T(8,128)(2,1)S(1)}, u32[]{:S(2)}, u32[]{:S(2)}) collective-permute-start(bf16[5,2048]{1,0:T(8,128)(2,1)S(1)} %fusion.63), channel_id=1, source_target_pairs={{0,4},{1,5},{2,6},{3,7},{4,0},{5,1},{6,2},{7,3},{8,12},{9,13},{10,... | collective-permute-start | bytes 61448 | tf_op jit(solution)/shard_map/ppermute | solution.py:89
  92.0 0.7 collective-permute-start.11
  92.8 0.2 copy.89
  93.0 0.2 copy.88
  93.2 0.9 pad_maximum_fusion
  94.1 2.9 %collective-permute-start.12 = (bf16[5,2048]{1,0:T(8,128)(2,1)S(1)}, bf16[5,2048]{1,0:T(8,128)(2,1)S(1)}, u32[]{:S(2)}, u32[]{:S(2)}) collective-permute-start(bf16[5,2048]{1,0:T(8,128)(2,1)S(1)} %fusion.63), channel_id=1, source_target_pairs={{0,6},{1,7},{2,0},{3,1},{4,2},{5,3},{6,4},{7,5},{8,14},{9,15},{10,... | collective-permute-start | bytes 61448 | tf_op jit(solution)/shard_map/ppermute | solution.py:89
  96.9 1.3 collective-permute-start.13
  98.3 0.9 collective-permute-done.11
  99.2 1.8 %collective-permute-done.12 = bf16[5,2048]{1,0:T(8,128)(2,1)S(1)} collective-permute-done((bf16[5,2048]{1,0:T(8,128)(2,1)S(1)}, bf16[5,2048]{1,0:T(8,128)(2,1)S(1)}, u32[]{:S(2)}, u32[]{:S(2)}) %collective-permute-start.12) | collective-permute-done | bytes 20512 | tf_op jit(solution)/shard_map/ppermute | solution.py:89
  101.0 0.9 collective-permute-done.13
  101.9 0.6 gather_fusion.6
  102.5 0.1 broadcast_select_fusion.1
  102.7 0.7 gather_fusion.1
  103.4 4.5 %all-to-all-done = bf16[32,2,128,256]{3,2,1,0:T(8,128)(2,1)} async-done(((bf16[32,2,128,256]{3,2,1,0:T(8,128)(2,1)}), bf16[32,2,128,256]{3,2,1,0:T(8,128)(2,1)}, u32[]{:S(2)}, u32[]{:S(2)}) %all-to-all-start) | async-done | bytes 4194336 | tf_op jit(solution)/shard_map/all_to_all | solution.py:125
  108.0 0.5 broadcast.368
  108.5 0.7 reduce.1
  109.1 0.7 reshape.482
  109.9 9.1 %all-to-all-start.1 = ((bf16[32,2,1024]{2,1,0:T(2,128)(2,1)}), bf16[32,2,1024]{2,1,0:T(2,128)(2,1)S(1)}, u32[]{:S(2)}, u32[]{:S(2)}) async-start(bf16[32,2,1024]{2,1,0:T(2,128)(2,1)} %reshape.482), calls=%async_computation.2 | async-start | bytes 262144 | tf_op jit(solution)/shard_map/all_to_all | solution.py:178
  119.0 4.6 %broadcast_select_fusion = bf16[32,2,128,256]{3,2,1,0:T(8,128)(2,1)} fusion(bf16[32,2,128,256]{3,2,1,0:T(8,128)(2,1)} %all-to-all-done, pred[]{:T(512)} %bitcast.57), kind=kLoop, calls=%fused_computation.9 | loop fusion | flops 2097152 | bytes 8388609 | tf_op jit(solution)/shard_map/jit(_where)/select_n | solution.py:177
  123.5 0.6 slice.134
  124.2 1.4 %all-to-all-done.1 = bf16[32,2,1024]{2,1,0:T(2,128)(2,1)S(1)} async-done(((bf16[32,2,1024]{2,1,0:T(2,128)(2,1)}), bf16[32,2,1024]{2,1,0:T(2,128)(2,1)S(1)}, u32[]{:S(2)}, u32[]{:S(2)}) %all-to-all-start.1) | async-done | bytes 131104 | tf_op jit(solution)/shard_map/all_to_all | solution.py:178
  125.6 0.1 reshape.483
  125.7 0.7 copy.101
  126.5 1.8 %fusion.33 = bf16[80,2048]{1,0:T(8,128)(2,1)} fusion(bf16[80,2048]{1,0:T(8,128)(2,1)S(1)} %copy-done.2, bf16[80,2048]{1,0:T(8,128)(2,1)} %reduce-scatter.2.cloned.1.call-done, f32[2048]{0:T(1024)S(1)} %copy-done.3), kind=kLoop, calls=%fused_computation.45 | loop fusion | flops 819200 | bytes 991232 | tf_op jit(solution)/shard_map/convert_element_type | solution.py:172
  (81 shorter events, 1.6 us)
Async XLA Ops:
  7.2 17.6 %copy-start = (bf16[256,2048]{1,0:T(8,128)(2,1)S(1)}, bf16[256,2048]{1,0:T(8,128)(2,1)}, u32[]{:S(2)}) copy-start(bf16[256,2048]{1,0:T(8,128)(2,1)} %param.24) | copy-start | bytes 3145732
  7.2 61.1 %all-gather.2.cloned.1.call-start = ((), (), s32[]{:S(2)}) async-start(), calls=%async_computation.3 | async-start | bytes 2949120 | tf_op jit(solution)/shard_map/all_gather | solution.py:131
  21.1 4.1 %copy-start.5 = (s32[16,1]{0,1:T(1,128)S(1)}, s32[16,1]{0,1:T(1,128)}, u32[]{:S(2)}) copy-start(s32[16,1]{0,1:T(1,128)} %param.18) | copy-start | bytes 196
  26.0 32.2 %collective-permute-start.6 = (bf16[5,2048]{1,0:T(8,128)(2,1)S(1)}, bf16[5,2048]{1,0:T(8,128)(2,1)S(1)}, u32[]{:S(2)}, u32[]{:S(2)}) collective-permute-start(bf16[5,2048]{1,0:T(8,128)(2,1)S(1)} %get-tuple-element.30), channel_id=1, source_target_pairs={{0,7},{1,0},{2,1},{3,2},{4,3},{5,4},{6,5},{7,6},{8,15},{9,8},{10,9... | collective-permute-start | bytes 61448 | tf_op jit(solution)/shard_map/ppermute | solution.py:78
  32.1 28.6 %collective-permute-start.5 = (bf16[5,2048]{1,0:T(8,128)(2,1)S(1)}, bf16[5,2048]{1,0:T(8,128)(2,1)S(1)}, u32[]{:S(2)}, u32[]{:S(2)}) collective-permute-start(bf16[5,2048]{1,0:T(8,128)(2,1)S(1)} %get-tuple-element.31), channel_id=1, source_target_pairs={{0,6},{1,7},{2,0},{3,1},{4,2},{5,3},{6,4},{7,5},{8,14},{9,15},{10,... | collective-permute-start | bytes 61448 | tf_op jit(solution)/shard_map/ppermute | solution.py:78
  33.4 33.9 %collective-permute-start.4 = (bf16[5,2048]{1,0:T(8,128)(2,1)S(1)}, bf16[5,2048]{1,0:T(8,128)(2,1)S(1)}, u32[]{:S(2)}, u32[]{:S(2)}) collective-permute-start(bf16[5,2048]{1,0:T(8,128)(2,1)S(1)} %get-tuple-element.32), channel_id=1, source_target_pairs={{0,5},{1,6},{2,7},{3,0},{4,1},{5,2},{6,3},{7,4},{8,13},{9,14},{10,... | collective-permute-start | bytes 61448 | tf_op jit(solution)/shard_map/ppermute | solution.py:78
  33.8 33.4 %collective-permute-start.3 = (bf16[5,2048]{1,0:T(8,128)(2,1)S(1)}, bf16[5,2048]{1,0:T(8,128)(2,1)S(1)}, u32[]{:S(2)}, u32[]{:S(2)}) collective-permute-start(bf16[5,2048]{1,0:T(8,128)(2,1)S(1)} %get-tuple-element.33), channel_id=1, source_target_pairs={{0,4},{1,5},{2,6},{3,7},{4,0},{5,1},{6,2},{7,3},{8,12},{9,13},{10,... | collective-permute-start | bytes 61448 | tf_op jit(solution)/shard_map/ppermute | solution.py:78
  38.9 28.4 %collective-permute-start.2 = (bf16[5,2048]{1,0:T(8,128)(2,1)S(1)}, bf16[5,2048]{1,0:T(8,128)(2,1)S(1)}, u32[]{:S(2)}, u32[]{:S(2)}) collective-permute-start(bf16[5,2048]{1,0:T(8,128)(2,1)S(1)} %get-tuple-element.34), channel_id=1, source_target_pairs={{0,3},{1,4},{2,5},{3,6},{4,7},{5,0},{6,1},{7,2},{8,11},{9,12},{10,... | collective-permute-start | bytes 61448 | tf_op jit(solution)/shard_map/ppermute | solution.py:78
  38.9 5.3 %copy-start.1 = (s32[40]{0:T(128)S(1)}, s32[40]{0:T(128)}, u32[]{:S(2)}) copy-start(s32[40]{0:T(128)} %param.17) | copy-start | bytes 484
  49.8 7.9 %copy-start.4 = (s32[1,640]{1,0:T(1,128)S(1)}, s32[1,640]{1,0:T(1,128)}, u32[]{:S(2)}) copy-start(s32[1,640]{1,0:T(1,128)} %param.15) | copy-start | bytes 7684
  49.8 58.1 %all-to-all-start = ((bf16[32,2,128,256]{3,2,1,0:T(8,128)(2,1)}), bf16[32,2,128,256]{3,2,1,0:T(8,128)(2,1)}, u32[]{:S(2)}, u32[]{:S(2)}) async-start(bf16[32,2,128,256]{3,2,1,0:T(8,128)(2,1)} %select_select_fusion), calls=%async_computation.1 | async-start | bytes 8388608 | tf_op jit(solution)/shard_map/all_to_all | solution.py:125
  57.7 68.8 %reduce-scatter.2.cloned.1.call-start = ((), (), s32[]{:S(2)}) async-start(), calls=%async_computation.4 | async-start | bytes 2949120 | tf_op jit(solution)/shard_map/reduce_scatter | solution.py:167
  57.9 9.4 %copy-start.3 = (f32[2048]{0:T(1024)S(1)}, f32[2048]{0:T(1024)}, u32[]{:S(2)}) copy-start(f32[2048]{0:T(1024)} %param.25) | copy-start | bytes 24580
  58.2 9.1 %collective-permute-start.1 = (bf16[5,2048]{1,0:T(8,128)(2,1)S(1)}, bf16[5,2048]{1,0:T(8,128)(2,1)S(1)}, u32[]{:S(2)}, u32[]{:S(2)}) collective-permute-start(bf16[5,2048]{1,0:T(8,128)(2,1)S(1)} %get-tuple-element.35), channel_id=1, source_target_pairs={{0,2},{1,3},{2,4},{3,5},{4,6},{5,7},{6,0},{7,1},{8,10},{9,11},{10,... | collective-permute-start | bytes 61448 | tf_op jit(solution)/shard_map/ppermute | solution.py:78
  60.6 6.7 %collective-permute-start = (bf16[5,2048]{1,0:T(8,128)(2,1)S(1)}, bf16[5,2048]{1,0:T(8,128)(2,1)S(1)}, u32[]{:S(2)}, u32[]{:S(2)}) collective-permute-start(bf16[5,2048]{1,0:T(8,128)(2,1)S(1)} %get-tuple-element.29), channel_id=1, source_target_pairs={{0,1},{1,2},{2,3},{3,4},{4,5},{5,6},{6,7},{7,0},{8,9},{9,10},{10,1... | collective-permute-start | bytes 61448 | tf_op jit(solution)/shard_map/ppermute | solution.py:78
  82.7 11.3 %collective-permute-start.7 = (bf16[5,2048]{1,0:T(8,128)(2,1)S(1)}, bf16[5,2048]{1,0:T(8,128)(2,1)S(1)}, u32[]{:S(2)}, u32[]{:S(2)}) collective-permute-start(bf16[5,2048]{1,0:T(8,128)(2,1)S(1)} %fusion.63), channel_id=1, source_target_pairs={{0,1},{1,2},{2,3},{3,4},{4,5},{5,6},{6,7},{7,0},{8,9},{9,10},{10,1... | collective-permute-start | bytes 61448 | tf_op jit(solution)/shard_map/ppermute | solution.py:89
  83.7 13.2 %collective-permute-start.8 = (bf16[5,2048]{1,0:T(8,128)(2,1)S(1)}, bf16[5,2048]{1,0:T(8,128)(2,1)S(1)}, u32[]{:S(2)}, u32[]{:S(2)}) collective-permute-start(bf16[5,2048]{1,0:T(8,128)(2,1)S(1)} %fusion.63), channel_id=1, source_target_pairs={{0,2},{1,3},{2,4},{3,5},{4,6},{5,7},{6,0},{7,1},{8,10},{9,11},{10,... | collective-permute-start | bytes 61448 | tf_op jit(solution)/shard_map/ppermute | solution.py:89
  86.5 11.7 %collective-permute-start.9 = (bf16[5,2048]{1,0:T(8,128)(2,1)S(1)}, bf16[5,2048]{1,0:T(8,128)(2,1)S(1)}, u32[]{:S(2)}, u32[]{:S(2)}) collective-permute-start(bf16[5,2048]{1,0:T(8,128)(2,1)S(1)} %fusion.63), channel_id=1, source_target_pairs={{0,3},{1,4},{2,5},{3,6},{4,7},{5,0},{6,1},{7,2},{8,11},{9,12},{10,... | collective-permute-start | bytes 61448 | tf_op jit(solution)/shard_map/ppermute | solution.py:89
  86.9 11.4 %collective-permute-start.10 = (bf16[5,2048]{1,0:T(8,128)(2,1)S(1)}, bf16[5,2048]{1,0:T(8,128)(2,1)S(1)}, u32[]{:S(2)}, u32[]{:S(2)}) collective-permute-start(bf16[5,2048]{1,0:T(8,128)(2,1)S(1)} %fusion.63), channel_id=1, source_target_pairs={{0,4},{1,5},{2,6},{3,7},{4,0},{5,1},{6,2},{7,3},{8,12},{9,13},{10,... | collective-permute-start | bytes 61448 | tf_op jit(solution)/shard_map/ppermute | solution.py:89
  92.0 7.2 %collective-permute-start.11 = (bf16[5,2048]{1,0:T(8,128)(2,1)S(1)}, bf16[5,2048]{1,0:T(8,128)(2,1)S(1)}, u32[]{:S(2)}, u32[]{:S(2)}) collective-permute-start(bf16[5,2048]{1,0:T(8,128)(2,1)S(1)} %fusion.63), channel_id=1, source_target_pairs={{0,5},{1,6},{2,7},{3,0},{4,1},{5,2},{6,3},{7,4},{8,13},{9,14},{10,... | collective-permute-start | bytes 61448 | tf_op jit(solution)/shard_map/ppermute | solution.py:89
  94.1 7.0 %collective-permute-start.12 = (bf16[5,2048]{1,0:T(8,128)(2,1)S(1)}, bf16[5,2048]{1,0:T(8,128)(2,1)S(1)}, u32[]{:S(2)}, u32[]{:S(2)}) collective-permute-start(bf16[5,2048]{1,0:T(8,128)(2,1)S(1)} %fusion.63), channel_id=1, source_target_pairs={{0,6},{1,7},{2,0},{3,1},{4,2},{5,3},{6,4},{7,5},{8,14},{9,15},{10,... | collective-permute-start | bytes 61448 | tf_op jit(solution)/shard_map/ppermute | solution.py:89
  96.9 5.0 %collective-permute-start.13 = (bf16[5,2048]{1,0:T(8,128)(2,1)S(1)}, bf16[5,2048]{1,0:T(8,128)(2,1)S(1)}, u32[]{:S(2)}, u32[]{:S(2)}) collective-permute-start(bf16[5,2048]{1,0:T(8,128)(2,1)S(1)} %fusion.63), channel_id=1, source_target_pairs={{0,7},{1,0},{2,1},{3,2},{4,3},{5,4},{6,5},{7,6},{8,15},{9,8},{10,9... | collective-permute-start | bytes 61448 | tf_op jit(solution)/shard_map/ppermute | solution.py:89
  109.9 15.7 %all-to-all-start.1 = ((bf16[32,2,1024]{2,1,0:T(2,128)(2,1)}), bf16[32,2,1024]{2,1,0:T(2,128)(2,1)S(1)}, u32[]{:S(2)}, u32[]{:S(2)}) async-start(bf16[32,2,1024]{2,1,0:T(2,128)(2,1)} %reshape.482), calls=%async_computation.2 | async-start | bytes 262144 | tf_op jit(solution)/shard_map/all_to_all | solution.py:178
  119.0 7.5 %copy-start.2 = (bf16[80,2048]{1,0:T(8,128)(2,1)S(1)}, bf16[80,2048]{1,0:T(8,128)(2,1)}, u32[]{:S(2)}) copy-start(bf16[80,2048]{1,0:T(8,128)(2,1)} %param.14) | copy-start | bytes 983044
Sparse Core Ops, SparseCore 0:
  11.8 50.4 all-gather.1
  79.4 46.2 reduce-scatter.1

commit v11 on v10

--- a/solution.py
+++ b/solution.py
@@ -117,11 +117,13 @@
     partial_value, key_new, value_new = decode_partial(
         decode_rows, past_cache, request_ages, norm_gain, norm_bias, qkv_weight, qkv_bias, out_weight
     )
-    send_cache = jnp.where(
-        has[:, None, None, None],
-        updated_rows(past_cache, key_new, value_new, request_ages, picks),
-        jnp.zeros((), jnp.bfloat16),
-    )
+    leave_written = jnp.arange(past_cache.shape[2])[None, :] == request_ages[staying:, None]
+    leave_fresh = jnp.stack([key_new[staying:], value_new[staying:]], axis=1)
+    leave_rows = jnp.where(
+        leave_written[:, None, :, None], leave_fresh[:, :, None, :], past_cache[staying:]
+    )
+    padded = jnp.concatenate([leave_rows, jnp.zeros_like(leave_rows[:1])], axis=0)
+    send_cache = padded[jnp.where(has, picks - staying, leaving)]
     moved_cache = lax.all_to_all(send_cache, "rep", split_axis=0, concat_axis=0, tiled=True)
     tp_count = lax.axis_size("tp")
     decode_pieces = partial_value.astype(jnp.bfloat16).reshape(

time: 138 us -> 138 us (level)
  the two profiles are of different devices: /device:TPU:2 before, /device:TPU:1 now
where the time goes in v11:
time: 138 us; the launch traced here: 137 us
  starting transfers between devices  45.5 us (33%)
  other arithmetic  25.4 us (18%)
  waiting for transfers between devices  19 us (14%)
  matrix products  16.8 us (12%)
  local copies, waits for them, and re-layouts  15.7 us (11%)
  between operations  14.7 us (11%)
    ppermute x7, starting transfers between devices, scatter_over_tp(): lax.ppermute(rolled[shift], 'tp', [(i, (i + shift) % n) for i in range(n)])  17.2 us
    ppermute x7, waiting for transfers between devices, gather_over_tp(): lax.ppermute(own_out, 'tp', [(i, (i + shift) % n) for i in range(n)])  15.4 us
    all_to_all x1, starting transfers between devices, on_device(): lax.all_to_all(send_rows, 'rep', split_axis=0, concat_axis=0, tiled=True)  10.6 us
    all_to_all x1, starting transfers between devices, on_device(): lax.all_to_all(send_cache, 'rep', split_axis=0, concat_axis=0, tiled=True)  9.42 us
    ppermute x7, starting transfers between devices, gather_over_tp(): lax.ppermute(own_out, 'tp', [(i, (i + shift) % n) for i in range(n)])  8.08 us
    unnamed x1, matrix products  5.31 us
    reshape x1, local copies, waits for them, and re-layouts, on_device(): split_weight = qkv_weight.reshape(3, model, heads_here, HEAD_DIM)  4.65 us
    select_n x1, other arithmetic, on_device(): jnp.where(request_ages[0] > 0, moved_cache, jnp.zeros((), jnp.bfloat16))  4.54 us
  transfers between devices with their start and end apart: 18, of which 5 were waited for; matrix products, arithmetic and copies ran while one was open for 38% of the time, Pallas kernels for 0%

profile of v11, /device:TPU:1, one launch (start us, length us, event | category | flops | bytes accessed | tf_op | source)
XLA Modules:
  0.0 137.1 jit_solution(16165183882116044059)
XLA Ops:
  7.2 1.2 convert_reduce_fusion
  8.4 1.2 fusion.28
  9.7 2.0 %fusion.31 = bf16[80,2048]{1,0:T(8,128)(2,1)} fusion(bf16[80,2048]{1,0:T(8,128)(2,1)} %param.14, f32[2048]{0:T(1024)} %param.21, f32[2048]{0:T(1024)} %param.20, f32[80]{0:T(128)S(1)} %add_rsqrt_fusion.1, f32[80]{0:T(128)S(1)} %broadcast_multiply_fusion.1), kind=kLoop, calls=%fused_computation.41 | loop fusion | flops 983040 | bytes 672384 | tf_op jit(solution)/shard_map/convert_element_type | solution.py:18
  11.7 1.0 convert_reduce_fusion.1
  12.8 1.1 fusion.42
  13.9 0.8 fusion.87
  14.7 0.7 iota_compare_fusion.1
  15.4 2.7 %convolution_bitcast_fusion = f32[3,40,256]{2,1,0:T(8,128)S(1)} fusion(bf16[3,2048,256]{2,1,0:T(8,128)(2,1)} %param.22, bf16[40,2048]{1,0:T(8,128)(2,1)} %param.16, f32[2048]{0:T(1024)} %param.21, f32[2048]{0:T(1024)} %param.20, f32[40]{0:T(128)S(1)} %add_rsqrt_fusion, f32[40]{0:T(128)S(1)} %broadcast_multiply_fusion), kind=kOutput, calls=%fused_computation.28 | convolution fusion | flops 126320640 | bytes 3449152 | tf_op jit(solution)/shard_map/rd,cde->cre/dot_general | solution.py:27
  18.3 2.6 %fusion.89 = (f32[40,2]{1,0:T(8,128)S(1)}, f32[40,2,128]{2,1,0:T(2,128)S(1)}) fusion(bf16[40,2,128,256]{3,2,1,0:T(8,128)(2,1)} %param.19, pred[2,256]{1,0:T(4,128)(4,1)S(1)} %iota_compare_fusion.5, bf16[40,256]{1,0:T(8,128)(2,1)S(1)} %get-tuple-element.37, pred[40,128]{1,0:T(8,128)(4,1)S(1)} %iota_compare_fusion.1), kind=kOutput, calls=%fused_computation.178 | convolution fusion | flops 5294000 | bytes 2688832 | tf_op jit(solution)/shard_map/rhc,rlc->rhl/dot_general | solution.py:36
  21.0 0.1 multiply_reduce_fusion
  21.3 0.2 fusion.70
  21.7 0.7 gather_fusion
  22.5 2.3 %fusion.17 = f32[40,256]{1,0:T(8,128)S(1)} fusion(bf16[40,2,128,256]{3,2,1,0:T(8,128)(2,1)} %param.19, pred[2,256]{1,0:T(4,128)(4,1)S(1)} %iota_compare_fusion.5, f32[40,2,128]{2,1,0:T(2,128)S(1)} %get-tuple-element.51, f32[40,2]{1,0:T(8,128)S(1)} %copy.85, f32[40,2]{1,0:T(8,128)S(1)} %copy.83), kind=kOutput, calls=%fused_computation.30 | convolution fusion | flops 5304320 | bytes 2704512 | tf_op jit(solution)/shard_map/rhl,rlc->rhc/dot_general | solution.py:56
  24.8 0.3 convolution_convert_fusion.1
  25.4 0.6 fusion.80
  26.0 0.6 gather_fusion.3
  26.6 0.1 broadcast_select_fusion.2
  26.7 0.7 slice_bitcast_fusion.10
  27.4 2.5 %collective-permute-start = (bf16[5,2048]{1,0:T(8,128)(2,1)}, bf16[5,2048]{1,0:T(8,128)(2,1)}, u32[]{:S(2)}, u32[]{:S(2)}) collective-permute-start(bf16[5,2048]{1,0:T(8,128)(2,1)} %get-tuple-element.29), channel_id=1, source_target_pairs={{0,1},{1,2},{2,3},{3,4},{4,5},{5,6},{6,7},{7,0},{8,9},{9,10},{10,1... | collective-permute-start | bytes 61448 | tf_op jit(solution)/shard_map/ppermute | solution.py:78
  29.8 4.0 %collective-permute-start.6 = (bf16[5,2048]{1,0:T(8,128)(2,1)}, bf16[5,2048]{1,0:T(8,128)(2,1)}, u32[]{:S(2)}, u32[]{:S(2)}) collective-permute-start(bf16[5,2048]{1,0:T(8,128)(2,1)} %get-tuple-element.30), channel_id=1, source_target_pairs={{0,7},{1,0},{2,1},{3,2},{4,3},{5,4},{6,5},{7,6},{8,15},{9,8},{10,9... | collective-permute-start | bytes 61448 | tf_op jit(solution)/shard_map/ppermute | solution.py:78
  33.9 1.8 %collective-permute-start.5 = (bf16[5,2048]{1,0:T(8,128)(2,1)}, bf16[5,2048]{1,0:T(8,128)(2,1)}, u32[]{:S(2)}, u32[]{:S(2)}) collective-permute-start(bf16[5,2048]{1,0:T(8,128)(2,1)} %get-tuple-element.31), channel_id=1, source_target_pairs={{0,6},{1,7},{2,0},{3,1},{4,2},{5,3},{6,4},{7,5},{8,14},{9,15},{10,... | collective-permute-start | bytes 61448 | tf_op jit(solution)/shard_map/ppermute | solution.py:78
  35.7 2.1 %collective-permute-start.4 = (bf16[5,2048]{1,0:T(8,128)(2,1)}, bf16[5,2048]{1,0:T(8,128)(2,1)}, u32[]{:S(2)}, u32[]{:S(2)}) collective-permute-start(bf16[5,2048]{1,0:T(8,128)(2,1)} %get-tuple-element.32), channel_id=1, source_target_pairs={{0,5},{1,6},{2,7},{3,0},{4,1},{5,2},{6,3},{7,4},{8,13},{9,14},{10,... | collective-permute-start | bytes 61448 | tf_op jit(solution)/shard_map/ppermute | solution.py:78
  37.8 2.9 %collective-permute-start.3 = (bf16[5,2048]{1,0:T(8,128)(2,1)}, bf16[5,2048]{1,0:T(8,128)(2,1)}, u32[]{:S(2)}, u32[]{:S(2)}) collective-permute-start(bf16[5,2048]{1,0:T(8,128)(2,1)} %get-tuple-element.33), channel_id=1, source_target_pairs={{0,4},{1,5},{2,6},{3,7},{4,0},{5,1},{6,2},{7,3},{8,12},{9,13},{10,... | collective-permute-start | bytes 61448 | tf_op jit(solution)/shard_map/ppermute | solution.py:78
  40.9 1.8 %slice_select_fusion.1 = bf16[16,2,128,256]{3,2,1,0:T(8,128)(2,1)S(1)} fusion(bf16[40,2,128,256]{3,2,1,0:T(8,128)(2,1)} %param.19, pred[16,128]{1,0:T(8,128)(4,1)S(1)} %iota_compare_fusion.3, bf16[16,2,256]{2,1,0:T(2,128)(2,1)S(1)} %copy.91), kind=kLoop, calls=%fused_computation.20 | loop fusion | flops 1048576 | bytes 4212736 | tf_op jit(solution)/shard_map/jit(_where)/select_n | solution.py:122
  42.6 0.2 concatenate.3
  42.9 2.8 %gather_fusion.2 = bf16[32,2,128,256]{3,2,1,0:T(8,128)(2,1)} fusion(bf16[17,2,128,256]{3,2,1,0:T(8,128)(2,1)S(1)} %concatenate.3, s32[1024]{0:T(1024)S(1)} %get-tuple-element.54), kind=kCustom, calls=%fused_computation.4 | custom fusion | bytes 8388736 | tf_op jit(solution)/shard_map/gather | solution.py:126
  45.7 9.4 %all-to-all-start = ((bf16[32,2,128,256]{3,2,1,0:T(8,128)(2,1)}), bf16[32,2,128,256]{3,2,1,0:T(8,128)(2,1)}, u32[]{:S(2)}, u32[]{:S(2)}) async-start(bf16[32,2,128,256]{3,2,1,0:T(8,128)(2,1)} %gather_fusion.2), calls=%async_computation.1 | async-start | bytes 8388608 | tf_op jit(solution)/shard_map/all_to_all | solution.py:127
  55.4 0.3 fusion.11
  55.7 0.1 collective-permute-start.2
  55.8 3.9 %collective-permute-start.1 = (bf16[5,2048]{1,0:T(8,128)(2,1)S(1)}, bf16[5,2048]{1,0:T(8,128)(2,1)S(1)}, u32[]{:S(2)}, u32[]{:S(2)}) collective-permute-start(bf16[5,2048]{1,0:T(8,128)(2,1)S(1)} %copy-done.6), channel_id=1, source_target_pairs={{0,2},{1,3},{2,4},{3,5},{4,6},{5,7},{6,0},{7,1},{8,10},{9,11},{10,... | collective-permute-start | bytes 61448 | tf_op jit(solution)/shard_map/ppermute | solution.py:78
  59.7 4.6 %copy.96 = bf16[3,2048,256]{1,2,0:T(8,128)(2,1)} copy(bf16[3,2048,256]{2,1,0:T(8,128)(2,1)} %param.22) | data formatting | bytes 6291456 | tf_op jit(solution)/shard_map/reshape | solution.py:135
  64.4 1.0 fusion.63
  65.5 5.3 %fusion.90 = f32[640,768]{0,1:S(1)} fusion(bf16[640,2048]{1,0:T(8,128)(2,1)} %all-gather.2.cloned.1.call-done, bf16[2048,768]{0,1:T(8,128)(2,1)} %bitcast.160), kind=kOutput, calls=%fused_computation.179 | convolution fusion | flops 2013265920 | bytes 7733248
  70.8 0.1 fusion.35
  70.9 0.7 fusion.46
  71.6 2.0 %fusion.88 = (f32[2,640]{1,0:T(2,128)S(1)}, f32[2,640,640]{1,2,0:T(8,128)S(1)}) fusion(f32[2,640,640]{1,2,0:T(8,128)S(1)} %fusion.46, pred[640,640]{0,1:T(8,128)(4,1)S(1)} %fusion.11), kind=kOutput, calls=%fused_computation.177 | output fusion | flops 4915839 | bytes 6968320 | tf_op jit(solution)/shard_map/sub | solution.py:152
  73.6 0.5 fusion.13
  74.1 2.4 %convolution_convert_fusion = bf16[640,2048]{1,0:T(8,128)(2,1)} fusion(bf16[640,256]{0,1:T(8,128)(2,1)S(1)} %bitcast.167, bf16[256,2048]{1,0:T(8,128)(2,1)S(1)} %copy-done), kind=kOutput, calls=%fused_computation.10 | convolution fusion | flops 672399360 | bytes 3997696 | tf_op jit(solution)/shard_map/dot_general | solution.py:158
  76.6 3.4 %slice_select_fusion = bf16[24,2,128,256]{3,2,1,0:T(8,128)(2,1)} fusion(bf16[40,2,128,256]{3,2,1,0:T(8,128)(2,1)} %param.19, pred[24,128]{1,0:T(8,128)(4,1)S(1)} %iota_compare_fusion.2, bf16[24,2,256]{2,1,0:T(2,128)(2,1)S(1)} %copy.90), kind=kLoop, calls=%fused_computation.11 | loop fusion | flops 1572864 | bytes 6319104 | tf_op jit(solution)/shard_map/jit(_where)/select_n | solution.py:166
  80.0 1.1 collective-permute-start.13
  81.1 1.8 %collective-permute-start.12 = (bf16[5,2048]{1,0:T(8,128)(2,1)S(1)}, bf16[5,2048]{1,0:T(8,128)(2,1)S(1)}, u32[]{:S(2)}, u32[]{:S(2)}) collective-permute-start(bf16[5,2048]{1,0:T(8,128)(2,1)S(1)} %fusion.63), channel_id=1, source_target_pairs={{0,6},{1,7},{2,0},{3,1},{4,2},{5,3},{6,4},{7,5},{8,14},{9,15},{10,... | collective-permute-start | bytes 61448 | tf_op jit(solution)/shard_map/ppermute | solution.py:89
  82.9 1.3 collective-permute-start.11
  84.2 2.3 %collective-permute-start.10 = (bf16[5,2048]{1,0:T(8,128)(2,1)S(1)}, bf16[5,2048]{1,0:T(8,128)(2,1)S(1)}, u32[]{:S(2)}, u32[]{:S(2)}) collective-permute-start(bf16[5,2048]{1,0:T(8,128)(2,1)S(1)} %fusion.63), channel_id=1, source_target_pairs={{0,4},{1,5},{2,6},{3,7},{4,0},{5,1},{6,2},{7,3},{8,12},{9,13},{10,... | collective-permute-start | bytes 61448 | tf_op jit(solution)/shard_map/ppermute | solution.py:89
  86.4 1.5 %collective-permute-start.7 = (bf16[5,2048]{1,0:T(8,128)(2,1)S(1)}, bf16[5,2048]{1,0:T(8,128)(2,1)S(1)}, u32[]{:S(2)}, u32[]{:S(2)}) collective-permute-start(bf16[5,2048]{1,0:T(8,128)(2,1)S(1)} %fusion.63), channel_id=1, source_target_pairs={{0,1},{1,2},{2,3},{3,4},{4,5},{5,6},{6,7},{7,0},{8,9},{9,10},{10,1... | collective-permute-start | bytes 61448 | tf_op jit(solution)/shard_map/ppermute | solution.py:89
  87.9 0.2 copy.88
  88.1 0.2 copy.89
  88.3 0.9 pad_maximum_fusion
  89.2 2.4 %collective-permute-done.7 = bf16[5,2048]{1,0:T(8,128)(2,1)S(1)} collective-permute-done((bf16[5,2048]{1,0:T(8,128)(2,1)S(1)}, bf16[5,2048]{1,0:T(8,128)(2,1)S(1)}, u32[]{:S(2)}, u32[]{:S(2)}) %collective-permute-start.7) | collective-permute-done | bytes 20512 | tf_op jit(solution)/shard_map/ppermute | solution.py:89
  91.5 0.2 collective-permute-start.8
  91.7 5.8 %collective-permute-done.8 = bf16[5,2048]{1,0:T(8,128)(2,1)S(1)} collective-permute-done((bf16[5,2048]{1,0:T(8,128)(2,1)S(1)}, bf16[5,2048]{1,0:T(8,128)(2,1)S(1)}, u32[]{:S(2)}, u32[]{:S(2)}) %collective-permute-start.8) | collective-permute-done | bytes 20512 | tf_op jit(solution)/shard_map/ppermute | solution.py:89
  97.5 7.2 %collective-permute-done.9 = bf16[5,2048]{1,0:T(8,128)(2,1)S(1)} collective-permute-done((bf16[5,2048]{1,0:T(8,128)(2,1)S(1)}, bf16[5,2048]{1,0:T(8,128)(2,1)S(1)}, u32[]{:S(2)}, u32[]{:S(2)}) %collective-permute-start.9) | collective-permute-done | bytes 20512 | tf_op jit(solution)/shard_map/ppermute | solution.py:89
  104.8 0.6 gather_fusion.4
  105.5 0.7 gather_fusion.1
  106.3 1.1 all-to-all-done
  107.4 0.5 broadcast.363
  107.9 0.7 reduce.1
  108.6 0.7 reshape.414
  109.3 10.6 %all-to-all-start.1 = ((bf16[32,2,1024]{2,1,0:T(2,128)(2,1)}), bf16[32,2,1024]{2,1,0:T(2,128)(2,1)S(1)}, u32[]{:S(2)}, u32[]{:S(2)}) async-start(bf16[32,2,1024]{2,1,0:T(2,128)(2,1)} %reshape.414), calls=%async_computation.2 | async-start | bytes 262144 | tf_op jit(solution)/shard_map/all_to_all | solution.py:180
  120.0 4.5 %broadcast_select_fusion = bf16[32,2,128,256]{3,2,1,0:T(8,128)(2,1)} fusion(bf16[32,2,128,256]{3,2,1,0:T(8,128)(2,1)} %all-to-all-done, pred[]{:T(512)} %bitcast.59), kind=kLoop, calls=%fused_computation.6 | loop fusion | flops 2097152 | bytes 8388609 | tf_op jit(solution)/shard_map/jit(_where)/select_n | solution.py:179
  124.5 0.6 slice.146
  125.2 2.5 %all-to-all-done.1 = bf16[32,2,1024]{2,1,0:T(2,128)(2,1)S(1)} async-done(((bf16[32,2,1024]{2,1,0:T(2,128)(2,1)}), bf16[32,2,1024]{2,1,0:T(2,128)(2,1)S(1)}, u32[]{:S(2)}, u32[]{:S(2)}) %all-to-all-start.1) | async-done | bytes 131104 | tf_op jit(solution)/shard_map/all_to_all | solution.py:180
  127.7 0.1 reshape.415
  127.8 0.7 copy.101
  128.5 1.8 %fusion.33 = bf16[80,2048]{1,0:T(8,128)(2,1)} fusion(bf16[80,2048]{1,0:T(8,128)(2,1)S(1)} %copy-done.1, bf16[80,2048]{1,0:T(8,128)(2,1)} %reduce-scatter.2.cloned.1.call-done, f32[2048]{0:T(1024)S(1)} %copy-done.8), kind=kLoop, calls=%fused_computation.43 | loop fusion | flops 819200 | bytes 991232 | tf_op jit(solution)/shard_map/convert_element_type | solution.py:174
  (102 shorter events, 1.8 us)
Async XLA Ops:
  7.2 17.6 %copy-start = (bf16[256,2048]{1,0:T(8,128)(2,1)S(1)}, bf16[256,2048]{1,0:T(8,128)(2,1)}, u32[]{:S(2)}) copy-start(bf16[256,2048]{1,0:T(8,128)(2,1)} %param.24) | copy-start | bytes 3145732
  7.2 58.3 %all-gather.2.cloned.1.call-start = ((), (), s32[]{:S(2)}) async-start(), calls=%async_computation.3 | async-start | bytes 2949120 | tf_op jit(solution)/shard_map/all_gather | solution.py:133
  18.2 22.5 %copy-start.2 = (bf16[40,256]{1,0:T(8,128)(2,1)}, bf16[40,256]{1,0:T(8,128)(2,1)S(1)}, u32[]{:S(2)}) copy-start(bf16[40,256]{1,0:T(8,128)(2,1)S(1)} %get-tuple-element.22) | copy-start | bytes 61444
  18.2 22.5 %copy-start.4 = (bf16[40,256]{1,0:T(8,128)(2,1)}, bf16[40,256]{1,0:T(8,128)(2,1)S(1)}, u32[]{:S(2)}) copy-start(bf16[40,256]{1,0:T(8,128)(2,1)S(1)} %get-tuple-element.21) | copy-start | bytes 61444
  20.9 4.3 %copy-start.15 = (s32[16,1]{0,1:T(1,128)S(1)}, s32[16,1]{0,1:T(1,128)}, u32[]{:S(2)}) copy-start(s32[16,1]{0,1:T(1,128)} %param.18) | copy-start | bytes 196
  22.5 18.2 %copy-start.13 = (s32[40]{0:T(128)S(1)}, s32[40]{0:T(128)}, u32[]{:S(2)}) copy-start(s32[40]{0:T(128)} %param.17) | copy-start | bytes 484
  25.3 0.7 copy-start.10
  27.4 28.3 %collective-permute-start = (bf16[5,2048]{1,0:T(8,128)(2,1)}, bf16[5,2048]{1,0:T(8,128)(2,1)}, u32[]{:S(2)}, u32[]{:S(2)}) collective-permute-start(bf16[5,2048]{1,0:T(8,128)(2,1)} %get-tuple-element.29), channel_id=1, source_target_pairs={{0,1},{1,2},{2,3},{3,4},{4,5},{5,6},{6,7},{7,0},{8,9},{9,10},{10,1... | collective-permute-start | bytes 61448 | tf_op jit(solution)/shard_map/ppermute | solution.py:78
  29.8 26.0 %collective-permute-start.6 = (bf16[5,2048]{1,0:T(8,128)(2,1)}, bf16[5,2048]{1,0:T(8,128)(2,1)}, u32[]{:S(2)}, u32[]{:S(2)}) collective-permute-start(bf16[5,2048]{1,0:T(8,128)(2,1)} %get-tuple-element.30), channel_id=1, source_target_pairs={{0,7},{1,0},{2,1},{3,2},{4,3},{5,4},{6,5},{7,6},{8,15},{9,8},{10,9... | collective-permute-start | bytes 61448 | tf_op jit(solution)/shard_map/ppermute | solution.py:78
  33.9 30.5 %collective-permute-start.5 = (bf16[5,2048]{1,0:T(8,128)(2,1)}, bf16[5,2048]{1,0:T(8,128)(2,1)}, u32[]{:S(2)}, u32[]{:S(2)}) collective-permute-start(bf16[5,2048]{1,0:T(8,128)(2,1)} %get-tuple-element.31), channel_id=1, source_target_pairs={{0,6},{1,7},{2,0},{3,1},{4,2},{5,3},{6,4},{7,5},{8,14},{9,15},{10,... | collective-permute-start | bytes 61448 | tf_op jit(solution)/shard_map/ppermute | solution.py:78
  35.7 28.7 %collective-permute-start.4 = (bf16[5,2048]{1,0:T(8,128)(2,1)}, bf16[5,2048]{1,0:T(8,128)(2,1)}, u32[]{:S(2)}, u32[]{:S(2)}) collective-permute-start(bf16[5,2048]{1,0:T(8,128)(2,1)} %get-tuple-element.32), channel_id=1, source_target_pairs={{0,5},{1,6},{2,7},{3,0},{4,1},{5,2},{6,3},{7,4},{8,13},{9,14},{10,... | collective-permute-start | bytes 61448 | tf_op jit(solution)/shard_map/ppermute | solution.py:78
  37.8 26.6 %collective-permute-start.3 = (bf16[5,2048]{1,0:T(8,128)(2,1)}, bf16[5,2048]{1,0:T(8,128)(2,1)}, u32[]{:S(2)}, u32[]{:S(2)}) collective-permute-start(bf16[5,2048]{1,0:T(8,128)(2,1)} %get-tuple-element.33), channel_id=1, source_target_pairs={{0,4},{1,5},{2,6},{3,7},{4,0},{5,1},{6,2},{7,3},{8,12},{9,13},{10,... | collective-permute-start | bytes 61448 | tf_op jit(solution)/shard_map/ppermute | solution.py:78
  45.7 9.5 %copy-start.9 = (s32[1,640]{1,0:T(1,128)S(1)}, s32[1,640]{1,0:T(1,128)}, u32[]{:S(2)}) copy-start(s32[1,640]{1,0:T(1,128)} %param.15) | copy-start | bytes 7684
  45.7 9.6 %copy-start.14 = (s32[40]{0:T(128)S(1)}, s32[40]{0:T(128)}, u32[]{:S(2)}) copy-start(s32[40]{0:T(128)} %param.17) | copy-start | bytes 484
  45.7 9.9 %copy-start.12 = (s32[32]{0:T(128)S(1)}, s32[32]{0:T(128)}, u32[]{:S(2)}) copy-start(s32[32]{0:T(128)} %get-tuple-element.47) | copy-start | bytes 388
  45.7 10.0 %copy-start.7 = (bf16[5,2048]{1,0:T(8,128)(2,1)S(1)}, bf16[5,2048]{1,0:T(8,128)(2,1)}, u32[]{:S(2)}) copy-start(bf16[5,2048]{1,0:T(8,128)(2,1)} %get-tuple-element.34) | copy-start | bytes 61444
  45.7 10.1 %copy-start.6 = (bf16[5,2048]{1,0:T(8,128)(2,1)S(1)}, bf16[5,2048]{1,0:T(8,128)(2,1)}, u32[]{:S(2)}) copy-start(bf16[5,2048]{1,0:T(8,128)(2,1)} %get-tuple-element.35) | copy-start | bytes 61444
  45.7 61.6 %all-to-all-start = ((bf16[32,2,128,256]{3,2,1,0:T(8,128)(2,1)}), bf16[32,2,128,256]{3,2,1,0:T(8,128)(2,1)}, u32[]{:S(2)}, u32[]{:S(2)}) async-start(bf16[32,2,128,256]{3,2,1,0:T(8,128)(2,1)} %gather_fusion.2), calls=%async_computation.1 | async-start | bytes 8388608 | tf_op jit(solution)/shard_map/all_to_all | solution.py:127
  55.2 73.3 %reduce-scatter.2.cloned.1.call-start = ((), (), s32[]{:S(2)}) async-start(), calls=%async_computation.4 | async-start | bytes 2949120 | tf_op jit(solution)/shard_map/reduce_scatter | solution.py:169
  55.7 8.7 %collective-permute-start.2 = (bf16[5,2048]{1,0:T(8,128)(2,1)S(1)}, bf16[5,2048]{1,0:T(8,128)(2,1)S(1)}, u32[]{:S(2)}, u32[]{:S(2)}) collective-permute-start(bf16[5,2048]{1,0:T(8,128)(2,1)S(1)} %copy-done.7), channel_id=1, source_target_pairs={{0,3},{1,4},{2,5},{3,6},{4,7},{5,0},{6,1},{7,2},{8,11},{9,12},{10,... | collective-permute-start | bytes 61448 | tf_op jit(solution)/shard_map/ppermute | solution.py:78
  55.8 8.6 %collective-permute-start.1 = (bf16[5,2048]{1,0:T(8,128)(2,1)S(1)}, bf16[5,2048]{1,0:T(8,128)(2,1)S(1)}, u32[]{:S(2)}, u32[]{:S(2)}) collective-permute-start(bf16[5,2048]{1,0:T(8,128)(2,1)S(1)} %copy-done.6), channel_id=1, source_target_pairs={{0,2},{1,3},{2,4},{3,5},{4,6},{5,7},{6,0},{7,1},{8,10},{9,11},{10,... | collective-permute-start | bytes 61448 | tf_op jit(solution)/shard_map/ppermute | solution.py:78
  59.7 4.8 %copy-start.8 = (f32[2048]{0:T(1024)S(1)}, f32[2048]{0:T(1024)}, u32[]{:S(2)}) copy-start(f32[2048]{0:T(1024)} %param.25) | copy-start | bytes 24580
  74.1 2.5 %copy-start.5 = (bf16[40,256]{1,0:T(8,128)(2,1)S(1)}, bf16[40,256]{1,0:T(8,128)(2,1)}, u32[]{:S(2)}) copy-start(bf16[40,256]{1,0:T(8,128)(2,1)} %copy-done.4) | copy-start | bytes 61444
  74.1 2.5 %copy-start.3 = (bf16[40,256]{1,0:T(8,128)(2,1)S(1)}, bf16[40,256]{1,0:T(8,128)(2,1)}, u32[]{:S(2)}) copy-start(bf16[40,256]{1,0:T(8,128)(2,1)} %copy-done.2) | copy-start | bytes 61444
  80.0 26.2 %copy-start.11 = (pred[32]{0:T(512)(128)(4,1)S(1)}, pred[32]{0:T(512)(128)(4,1)}, u32[]{:S(2)}) copy-start(pred[32]{0:T(512)(128)(4,1)} %copy-done.10) | copy-start | bytes 100
  80.0 24.8 %collective-permute-start.13 = (bf16[5,2048]{1,0:T(8,128)(2,1)S(1)}, bf16[5,2048]{1,0:T(8,128)(2,1)S(1)}, u32[]{:S(2)}, u32[]{:S(2)}) collective-permute-start(bf16[5,2048]{1,0:T(8,128)(2,1)S(1)} %fusion.63), channel_id=1, source_target_pairs={{0,7},{1,0},{2,1},{3,2},{4,3},{5,4},{6,5},{7,6},{8,15},{9,8},{10,9... | collective-permute-start | bytes 61448 | tf_op jit(solution)/shard_map/ppermute | solution.py:89
  81.1 23.7 %collective-permute-start.12 = (bf16[5,2048]{1,0:T(8,128)(2,1)S(1)}, bf16[5,2048]{1,0:T(8,128)(2,1)S(1)}, u32[]{:S(2)}, u32[]{:S(2)}) collective-permute-start(bf16[5,2048]{1,0:T(8,128)(2,1)S(1)} %fusion.63), channel_id=1, source_target_pairs={{0,6},{1,7},{2,0},{3,1},{4,2},{5,3},{6,4},{7,5},{8,14},{9,15},{10,... | collective-permute-start | bytes 61448 | tf_op jit(solution)/shard_map/ppermute | solution.py:89
  82.9 21.8 %collective-permute-start.11 = (bf16[5,2048]{1,0:T(8,128)(2,1)S(1)}, bf16[5,2048]{1,0:T(8,128)(2,1)S(1)}, u32[]{:S(2)}, u32[]{:S(2)}) collective-permute-start(bf16[5,2048]{1,0:T(8,128)(2,1)S(1)} %fusion.63), channel_id=1, source_target_pairs={{0,5},{1,6},{2,7},{3,0},{4,1},{5,2},{6,3},{7,4},{8,13},{9,14},{10,... | collective-permute-start | bytes 61448 | tf_op jit(solution)/shard_map/ppermute | solution.py:89
  84.2 20.5 %collective-permute-start.10 = (bf16[5,2048]{1,0:T(8,128)(2,1)S(1)}, bf16[5,2048]{1,0:T(8,128)(2,1)S(1)}, u32[]{:S(2)}, u32[]{:S(2)}) collective-permute-start(bf16[5,2048]{1,0:T(8,128)(2,1)S(1)} %fusion.63), channel_id=1, source_target_pairs={{0,4},{1,5},{2,6},{3,7},{4,0},{5,1},{6,2},{7,3},{8,12},{9,13},{10,... | collective-permute-start | bytes 61448 | tf_op jit(solution)/shard_map/ppermute | solution.py:89
  86.4 5.1 %collective-permute-start.7 = (bf16[5,2048]{1,0:T(8,128)(2,1)S(1)}, bf16[5,2048]{1,0:T(8,128)(2,1)S(1)}, u32[]{:S(2)}, u32[]{:S(2)}) collective-permute-start(bf16[5,2048]{1,0:T(8,128)(2,1)S(1)} %fusion.63), channel_id=1, source_target_pairs={{0,1},{1,2},{2,3},{3,4},{4,5},{5,6},{6,7},{7,0},{8,9},{9,10},{10,1... | collective-permute-start | bytes 61448 | tf_op jit(solution)/shard_map/ppermute | solution.py:89
  91.5 6.0 %collective-permute-start.8 = (bf16[5,2048]{1,0:T(8,128)(2,1)S(1)}, bf16[5,2048]{1,0:T(8,128)(2,1)S(1)}, u32[]{:S(2)}, u32[]{:S(2)}) collective-permute-start(bf16[5,2048]{1,0:T(8,128)(2,1)S(1)} %fusion.63), channel_id=1, source_target_pairs={{0,2},{1,3},{2,4},{3,5},{4,6},{5,7},{6,0},{7,1},{8,10},{9,11},{10,... | collective-permute-start | bytes 61448 | tf_op jit(solution)/shard_map/ppermute | solution.py:89
  97.5 7.2 %collective-permute-start.9 = (bf16[5,2048]{1,0:T(8,128)(2,1)S(1)}, bf16[5,2048]{1,0:T(8,128)(2,1)S(1)}, u32[]{:S(2)}, u32[]{:S(2)}) collective-permute-start(bf16[5,2048]{1,0:T(8,128)(2,1)S(1)} %fusion.63), channel_id=1, source_target_pairs={{0,3},{1,4},{2,5},{3,6},{4,7},{5,0},{6,1},{7,2},{8,11},{9,12},{10,... | collective-permute-start | bytes 61448 | tf_op jit(solution)/shard_map/ppermute | solution.py:89
  109.3 18.3 %all-to-all-start.1 = ((bf16[32,2,1024]{2,1,0:T(2,128)(2,1)}), bf16[32,2,1024]{2,1,0:T(2,128)(2,1)S(1)}, u32[]{:S(2)}, u32[]{:S(2)}) async-start(bf16[32,2,1024]{2,1,0:T(2,128)(2,1)} %reshape.414), calls=%async_computation.2 | async-start | bytes 262144 | tf_op jit(solution)/shard_map/all_to_all | solution.py:180
  120.0 8.5 %copy-start.1 = (bf16[80,2048]{1,0:T(8,128)(2,1)S(1)}, bf16[80,2048]{1,0:T(8,128)(2,1)}, u32[]{:S(2)}) copy-start(bf16[80,2048]{1,0:T(8,128)(2,1)} %param.14) | copy-start | bytes 983044
Sparse Core Ops, SparseCore 0:
  11.8 50.2 all-gather.1
  76.6 43.7 reduce-scatter.1

commit v12 on v11

--- a/solution.py
+++ b/solution.py
@@ -18,16 +18,17 @@
     return (scaled * norm_gain + norm_bias).astype(jnp.bfloat16)
 
 
-def decode_partial(rows, cache, ages, norm_gain, norm_bias, qkv_weight, qkv_bias, out_weight):
-    count = rows.shape[0]
-    width = qkv_weight.shape[2]
+def decode_project(rows, norm_gain, norm_bias, qkv_weight, qkv_bias):
+    normed = layer_norm(rows, norm_gain, norm_bias)
+    projected = jnp.einsum("rd,cde->cre", normed, qkv_weight, preferred_element_type=jnp.float32)
+    return tuple((projected[i] + qkv_bias[i]).astype(jnp.bfloat16) for i in range(3))
+
+
+def decode_partial(queries, key_new, value_new, cache, ages, out_weight):
+    count = queries.shape[0]
+    width = queries.shape[1]
     heads_here = width // HEAD_DIM
     length = cache.shape[2]
-    normed = layer_norm(rows, norm_gain, norm_bias)
-    projected = jnp.einsum("rd,cde->cre", normed, qkv_weight, preferred_element_type=jnp.float32)
-    queries = (projected[0] + qkv_bias[0]).astype(jnp.bfloat16)
-    key_new = (projected[1] + qkv_bias[1]).astype(jnp.bfloat16)
-    value_new = (projected[2] + qkv_bias[2]).astype(jnp.bfloat16)
     head_of_col = jnp.arange(width) // HEAD_DIM
     diag = jnp.arange(heads_here)[:, None] == head_of_col[None, :]
     q_blocks = jnp.where(diag[None], queries[:, None, :], jnp.zeros((), jnp.bfloat16))
@@ -58,7 +59,7 @@
     context = context + own_prob.astype(jnp.float32)[:, head_of_col] * value_new.astype(jnp.float32)
     context = context.astype(jnp.bfloat16)
     partial_value = jnp.dot(context, out_weight, preferred_element_type=jnp.float32)
-    return partial_value, key_new, value_new
+    return partial_value
 
 
 def updated_rows(cache, key_new, value_new, ages, picks):
@@ -114,8 +115,8 @@
     match = targets[None, :] == jnp.arange(rep_count * CAP)[:, None]
     has = jnp.any(match, axis=1)
     picks = staying + jnp.sum(jnp.where(match, jnp.arange(leaving)[None, :], 0), axis=1)
-    partial_value, key_new, value_new = decode_partial(
-        decode_rows, past_cache, request_ages, norm_gain, norm_bias, qkv_weight, qkv_bias, out_weight
+    queries_new, key_new, value_new = decode_project(
+        decode_rows, norm_gain, norm_bias, qkv_weight, qkv_bias
     )
     leave_written = jnp.arange(past_cache.shape[2])[None, :] == request_ages[staying:, None]
     leave_fresh = jnp.stack([key_new[staying:], value_new[staying:]], axis=1)
@@ -124,7 +125,11 @@
     )
     padded = jnp.concatenate([leave_rows, jnp.zeros_like(leave_rows[:1])], axis=0)
     send_cache = padded[jnp.where(has, picks - staying, leaving)]
+    send_cache, attend_cache = lax.optimization_barrier((send_cache, past_cache))
     moved_cache = lax.all_to_all(send_cache, "rep", split_axis=0, concat_axis=0, tiled=True)
+    partial_value = decode_partial(
+        queries_new, key_new, value_new, attend_cache, request_ages, out_weight
+    )
     tp_count = lax.axis_size("tp")
     decode_pieces = partial_value.astype(jnp.bfloat16).reshape(
         tp_count, decode_rows.shape[0] // tp_count, decode_rows.shape[1]

time: 138 us -> 137 us (level)
  the two profiles are of different devices: /device:TPU:1 before, /device:TPU:2 now
where the time goes in v12:
time: 137 us; the launch traced here: 135 us
  starting transfers between devices  45.7 us (33%)
  other arithmetic  25.4 us (19%)
  matrix products  16.8 us (12%)
  waiting for transfers between devices  16.4 us (12%)
  local copies, waits for them, and re-layouts  15.7 us (11%)
  between operations  14.6 us (11%)
    ppermute x7, starting transfers between devices, scatter_over_tp(): lax.ppermute(rolled[shift], 'tp', [(i, (i + shift) % n) for i in range(n)])  18.5 us
    ppermute x7, waiting for transfers between devices, gather_over_tp(): lax.ppermute(own_out, 'tp', [(i, (i + shift) % n) for i in range(n)])  14.9 us
    ppermute x7, starting transfers between devices, gather_over_tp(): lax.ppermute(own_out, 'tp', [(i, (i + shift) % n) for i in range(n)])  11.8 us
    all_to_all x1, starting transfers between devices, on_device(): lax.all_to_all(send_cache, 'rep', split_axis=0, concat_axis=0, tiled=True)  7.81 us
    all_to_all x1, starting transfers between devices, on_device(): lax.all_to_all(send_rows, 'rep', split_axis=0, concat_axis=0, tiled=True)  7.47 us
    unnamed x1, matrix products  5.32 us
    reshape x1, local copies, waits for them, and re-layouts, on_device(): split_weight = qkv_weight.reshape(3, model, heads_here, HEAD_DIM)  4.64 us
    select_n x1, other arithmetic, on_device(): jnp.where(request_ages[0] > 0, moved_cache, jnp.zeros((), jnp.bfloat16))  4.56 us
  transfers between devices with their start and end apart: 18, of which 4 were waited for; matrix products, arithmetic and copies ran while one was open for 38% of the time, Pallas kernels for 0%

profile of v12, /device:TPU:2, one launch (start us, length us, event | category | flops | bytes accessed | tf_op | source)
XLA Modules:
  0.0 134.7 jit_solution(8503656902205348960)
XLA Ops:
  7.2 1.2 convert_reduce_fusion
  8.4 1.2 fusion.16
  9.7 2.0 %fusion.19 = bf16[80,2048]{1,0:T(8,128)(2,1)} fusion(bf16[80,2048]{1,0:T(8,128)(2,1)} %param.14, f32[2048]{0:T(1024)} %param.21, f32[2048]{0:T(1024)} %param.20, f32[80]{0:T(128)S(1)} %add_rsqrt_fusion.1, f32[80]{0:T(128)S(1)} %broadcast_multiply_fusion.1), kind=kLoop, calls=%fused_computation.39 | loop fusion | flops 983040 | bytes 672384 | tf_op jit(solution)/shard_map/convert_element_type | solution.py:18
  11.7 0.7 fusion.64
  12.4 0.7 select_reduce_fusion
  13.2 1.0 convert_reduce_fusion.1
  14.2 1.1 fusion.30
  15.4 0.7 slice.100
  16.2 0.8 fusion.75
  17.0 2.7 %convolution_bitcast_fusion = f32[3,40,256]{2,1,0:T(8,128)S(1)} fusion(bf16[3,2048,256]{2,1,0:T(8,128)(2,1)} %param.22, bf16[40,2048]{1,0:T(8,128)(2,1)} %param.16, f32[2048]{0:T(1024)} %param.21, f32[2048]{0:T(1024)} %param.20, f32[40]{0:T(128)S(1)} %add_rsqrt_fusion, f32[40]{0:T(128)S(1)} %broadcast_multiply_fusion), kind=kOutput, calls=%fused_computation.26 | convolution fusion | flops 126320640 | bytes 3449152 | tf_op jit(solution)/shard_map/rd,cde->cre/dot_general | solution.py:23
  19.8 1.8 %slice_select_fusion.1 = bf16[16,2,128,256]{3,2,1,0:T(8,128)(2,1)S(1)} fusion(bf16[40,2,128,256]{3,2,1,0:T(8,128)(2,1)} %param.19, pred[16,128]{1,0:T(8,128)(4,1)S(1)} %iota_compare_fusion.4, bf16[16,2,256]{2,1,0:T(2,128)(2,1)S(1)} %copy.80), kind=kLoop, calls=%fused_computation.18 | loop fusion | flops 1048576 | bytes 4212736 | tf_op jit(solution)/shard_map/jit(_where)/select_n | solution.py:123
  21.6 0.2 concatenate.3
  21.8 2.8 %gather_fusion = bf16[32,2,128,256]{3,2,1,0:T(8,128)(2,1)} fusion(bf16[17,2,128,256]{3,2,1,0:T(8,128)(2,1)S(1)} %concatenate.3, s32[1024]{0:T(1024)S(1)} %get-tuple-element.59), kind=kCustom, calls=%fused_computation.2 | custom fusion | bytes 8388736 | tf_op jit(solution)/shard_map/gather | solution.py:127
  24.6 7.8 %all-to-all-start = ((bf16[32,2,128,256]{3,2,1,0:T(8,128)(2,1)}), bf16[32,2,128,256]{3,2,1,0:T(8,128)(2,1)}, u32[]{:S(2)}, u32[]{:S(2)}) async-start(bf16[32,2,128,256]{3,2,1,0:T(8,128)(2,1)} %gather_fusion), calls=%async_computation.1 | async-start | bytes 8388608 | tf_op jit(solution)/shard_map/all_to_all | solution.py:129
  32.6 0.1 multiply_reduce_fusion
  32.9 2.6 %fusion.77 = (f32[40,2]{1,0:T(8,128)S(1)}, f32[40,2,128]{2,1,0:T(2,128)S(1)}) fusion(pred[2,256]{1,0:T(4,128)(4,1)S(1)} %iota_compare_fusion.5, bf16[40,256]{1,0:T(8,128)(2,1)S(1)} %get-tuple-element.42, pred[40,128]{1,0:T(8,128)(4,1)S(1)} %iota_compare_fusion.1, bf16[40,2,128,256]{3,2,1,0:T(8,128)(2,1)} %param.19), kind=kOutput, calls=%fused_computation.176 | convolution fusion | flops 5294000 | bytes 2688832 | tf_op jit(solution)/shard_map/rhc,rlc->rhl/dot_general | solution.py:37
  35.7 0.2 fusion.58
  36.2 0.7 gather_fusion.1
  37.0 2.3 %fusion.11 = f32[40,256]{1,0:T(8,128)S(1)} fusion(pred[2,256]{1,0:T(4,128)(4,1)S(1)} %iota_compare_fusion.5, f32[40,2,128]{2,1,0:T(2,128)S(1)} %get-tuple-element.55, f32[40,2]{1,0:T(8,128)S(1)} %copy.86, f32[40,2]{1,0:T(8,128)S(1)} %copy.84, bf16[40,2,128,256]{3,2,1,0:T(8,128)(2,1)} %param.19), kind=kOutput, calls=%fused_computation.28 | convolution fusion | flops 5304320 | bytes 2704512 | tf_op jit(solution)/shard_map/rhl,rlc->rhc/dot_general | solution.py:57
  39.3 0.3 convolution_convert_fusion.1
  39.7 0.6 gather_fusion.3
  40.3 0.1 broadcast_select_fusion.2
  40.4 1.9 %collective-permute-start = (bf16[5,2048]{1,0:T(8,128)(2,1)S(1)}, bf16[5,2048]{1,0:T(8,128)(2,1)S(1)}, u32[]{:S(2)}, u32[]{:S(2)}) collective-permute-start(bf16[5,2048]{1,0:T(8,128)(2,1)S(1)} %get-tuple-element.33), channel_id=1, source_target_pairs={{0,1},{1,2},{2,3},{3,4},{4,5},{5,6},{6,7},{7,0},{8,9},{9,10},{10,1... | collective-permute-start | bytes 61448 | tf_op jit(solution)/shard_map/ppermute | solution.py:79
  42.3 4.1 %collective-permute-start.6 = (bf16[5,2048]{1,0:T(8,128)(2,1)S(1)}, bf16[5,2048]{1,0:T(8,128)(2,1)S(1)}, u32[]{:S(2)}, u32[]{:S(2)}) collective-permute-start(bf16[5,2048]{1,0:T(8,128)(2,1)S(1)} %get-tuple-element.34), channel_id=1, source_target_pairs={{0,7},{1,0},{2,1},{3,2},{4,3},{5,4},{6,5},{7,6},{8,15},{9,8},{10,9... | collective-permute-start | bytes 61448 | tf_op jit(solution)/shard_map/ppermute | solution.py:79
  46.4 2.4 %collective-permute-start.5 = (bf16[5,2048]{1,0:T(8,128)(2,1)S(1)}, bf16[5,2048]{1,0:T(8,128)(2,1)S(1)}, u32[]{:S(2)}, u32[]{:S(2)}) collective-permute-start(bf16[5,2048]{1,0:T(8,128)(2,1)S(1)} %get-tuple-element.35), channel_id=1, source_target_pairs={{0,6},{1,7},{2,0},{3,1},{4,2},{5,3},{6,4},{7,5},{8,14},{9,15},{10,... | collective-permute-start | bytes 61448 | tf_op jit(solution)/shard_map/ppermute | solution.py:79
  48.8 2.1 %collective-permute-start.4 = (bf16[5,2048]{1,0:T(8,128)(2,1)S(1)}, bf16[5,2048]{1,0:T(8,128)(2,1)S(1)}, u32[]{:S(2)}, u32[]{:S(2)}) collective-permute-start(bf16[5,2048]{1,0:T(8,128)(2,1)S(1)} %get-tuple-element.36), channel_id=1, source_target_pairs={{0,5},{1,6},{2,7},{3,0},{4,1},{5,2},{6,3},{7,4},{8,13},{9,14},{10,... | collective-permute-start | bytes 61448 | tf_op jit(solution)/shard_map/ppermute | solution.py:79
  50.9 3.4 %collective-permute-start.3 = (bf16[5,2048]{1,0:T(8,128)(2,1)S(1)}, bf16[5,2048]{1,0:T(8,128)(2,1)S(1)}, u32[]{:S(2)}, u32[]{:S(2)}) collective-permute-start(bf16[5,2048]{1,0:T(8,128)(2,1)S(1)} %get-tuple-element.37), channel_id=1, source_target_pairs={{0,4},{1,5},{2,6},{3,7},{4,0},{5,1},{6,2},{7,3},{8,12},{9,13},{10,... | collective-permute-start | bytes 61448 | tf_op jit(solution)/shard_map/ppermute | solution.py:79
  54.4 0.3 fusion.7
  54.7 0.5 collective-permute-start.2
  55.2 4.1 %collective-permute-start.1 = (bf16[5,2048]{1,0:T(8,128)(2,1)S(1)}, bf16[5,2048]{1,0:T(8,128)(2,1)S(1)}, u32[]{:S(2)}, u32[]{:S(2)}) collective-permute-start(bf16[5,2048]{1,0:T(8,128)(2,1)S(1)} %get-tuple-element.39), channel_id=1, source_target_pairs={{0,2},{1,3},{2,4},{3,5},{4,6},{5,7},{6,0},{7,1},{8,10},{9,11},{10,... | collective-permute-start | bytes 61448 | tf_op jit(solution)/shard_map/ppermute | solution.py:79
  59.4 4.6 %copy.96 = bf16[3,2048,256]{1,2,0:T(8,128)(2,1)} copy(bf16[3,2048,256]{2,1,0:T(8,128)(2,1)} %param.22) | data formatting | bytes 6291456 | tf_op jit(solution)/shard_map/reshape | solution.py:140
  64.1 0.9 fusion.51
  65.1 5.3 %fusion.78 = f32[640,768]{0,1:S(1)} fusion(bf16[640,2048]{1,0:T(8,128)(2,1)} %all-gather.2.cloned.1.call-done, bf16[2048,768]{0,1:T(8,128)(2,1)} %bitcast.156), kind=kOutput, calls=%fused_computation.177 | convolution fusion | flops 2013265920 | bytes 7733248
  70.4 0.1 fusion.23
  70.5 0.7 fusion.34
  71.2 2.0 %fusion.76 = (f32[2,640]{1,0:T(2,128)S(1)}, f32[2,640,640]{1,2,0:T(8,128)S(1)}) fusion(f32[2,640,640]{1,2,0:T(8,128)S(1)} %fusion.34, pred[640,640]{0,1:T(8,128)(4,1)S(1)} %fusion.7), kind=kOutput, calls=%fused_computation.175 | output fusion | flops 4915839 | bytes 6968320 | tf_op jit(solution)/shard_map/sub | solution.py:157
  73.2 0.5 fusion.9
  73.7 2.4 %convolution_convert_fusion = bf16[640,2048]{1,0:T(8,128)(2,1)} fusion(bf16[640,256]{0,1:T(8,128)(2,1)S(1)} %bitcast.163, bf16[256,2048]{1,0:T(8,128)(2,1)S(1)} %copy-done), kind=kOutput, calls=%fused_computation.10 | convolution fusion | flops 672399360 | bytes 3997696 | tf_op jit(solution)/shard_map/dot_general | solution.py:163
  76.2 3.4 %slice_select_fusion = bf16[24,2,128,256]{3,2,1,0:T(8,128)(2,1)} fusion(bf16[40,2,128,256]{3,2,1,0:T(8,128)(2,1)} %param.19, pred[24,128]{1,0:T(8,128)(4,1)S(1)} %iota_compare_fusion.2, bf16[24,2,256]{2,1,0:T(2,128)(2,1)S(1)} %copy.91), kind=kLoop, calls=%fused_computation.11 | loop fusion | flops 1572864 | bytes 6319104 | tf_op jit(solution)/shard_map/jit(_where)/select_n | solution.py:171
  79.5 1.1 collective-permute-start.13
  80.7 1.3 collective-permute-start.12
  82.0 2.2 %collective-permute-start.11 = (bf16[5,2048]{1,0:T(8,128)(2,1)S(1)}, bf16[5,2048]{1,0:T(8,128)(2,1)S(1)}, u32[]{:S(2)}, u32[]{:S(2)}) collective-permute-start(bf16[5,2048]{1,0:T(8,128)(2,1)S(1)} %fusion.51), channel_id=1, source_target_pairs={{0,5},{1,6},{2,7},{3,0},{4,1},{5,2},{6,3},{7,4},{8,13},{9,14},{10,... | collective-permute-start | bytes 61448 | tf_op jit(solution)/shard_map/ppermute | solution.py:90
  84.1 2.5 %collective-permute-start.10 = (bf16[5,2048]{1,0:T(8,128)(2,1)S(1)}, bf16[5,2048]{1,0:T(8,128)(2,1)S(1)}, u32[]{:S(2)}, u32[]{:S(2)}) collective-permute-start(bf16[5,2048]{1,0:T(8,128)(2,1)S(1)} %fusion.51), channel_id=1, source_target_pairs={{0,4},{1,5},{2,6},{3,7},{4,0},{5,1},{6,2},{7,3},{8,12},{9,13},{10,... | collective-permute-start | bytes 61448 | tf_op jit(solution)/shard_map/ppermute | solution.py:90
  86.6 2.0 %collective-permute-start.7 = (bf16[5,2048]{1,0:T(8,128)(2,1)S(1)}, bf16[5,2048]{1,0:T(8,128)(2,1)S(1)}, u32[]{:S(2)}, u32[]{:S(2)}) collective-permute-start(bf16[5,2048]{1,0:T(8,128)(2,1)S(1)} %fusion.51), channel_id=1, source_target_pairs={{0,1},{1,2},{2,3},{3,4},{4,5},{5,6},{6,7},{7,0},{8,9},{9,10},{10,1... | collective-permute-start | bytes 61448 | tf_op jit(solution)/shard_map/ppermute | solution.py:90
  88.6 0.2 copy.89
  88.8 0.2 copy.90
  89.0 0.9 pad_maximum_fusion
  89.9 2.9 %collective-permute-done.7 = bf16[5,2048]{1,0:T(8,128)(2,1)S(1)} collective-permute-done((bf16[5,2048]{1,0:T(8,128)(2,1)S(1)}, bf16[5,2048]{1,0:T(8,128)(2,1)S(1)}, u32[]{:S(2)}, u32[]{:S(2)}) %collective-permute-start.7) | collective-permute-done | bytes 20512 | tf_op jit(solution)/shard_map/ppermute | solution.py:90
  92.8 1.7 %collective-permute-start.8 = (bf16[5,2048]{1,0:T(8,128)(2,1)S(1)}, bf16[5,2048]{1,0:T(8,128)(2,1)S(1)}, u32[]{:S(2)}, u32[]{:S(2)}) collective-permute-start(bf16[5,2048]{1,0:T(8,128)(2,1)S(1)} %fusion.51), channel_id=1, source_target_pairs={{0,2},{1,3},{2,4},{3,5},{4,6},{5,7},{6,0},{7,1},{8,10},{9,11},{10,... | collective-permute-start | bytes 61448 | tf_op jit(solution)/shard_map/ppermute | solution.py:90
  94.4 5.1 %collective-permute-done.8 = bf16[5,2048]{1,0:T(8,128)(2,1)S(1)} collective-permute-done((bf16[5,2048]{1,0:T(8,128)(2,1)S(1)}, bf16[5,2048]{1,0:T(8,128)(2,1)S(1)}, u32[]{:S(2)}, u32[]{:S(2)}) %collective-permute-start.8) | collective-permute-done | bytes 20512 | tf_op jit(solution)/shard_map/ppermute | solution.py:90
  99.5 1.0 collective-permute-start.9
  100.6 7.0 %collective-permute-done.9 = bf16[5,2048]{1,0:T(8,128)(2,1)S(1)} collective-permute-done((bf16[5,2048]{1,0:T(8,128)(2,1)S(1)}, bf16[5,2048]{1,0:T(8,128)(2,1)S(1)}, u32[]{:S(2)}, u32[]{:S(2)}) %collective-permute-start.9) | collective-permute-done | bytes 20512 | tf_op jit(solution)/shard_map/ppermute | solution.py:90
  107.6 0.6 gather_fusion.4
  108.4 0.7 gather_fusion.2
  109.1 0.5 broadcast.358
  109.6 0.7 reduce.1
  110.3 0.7 reshape.414
  111.0 7.5 %all-to-all-start.1 = ((bf16[32,2,1024]{2,1,0:T(2,128)(2,1)}), bf16[32,2,1024]{2,1,0:T(2,128)(2,1)S(1)}, u32[]{:S(2)}, u32[]{:S(2)}) async-start(bf16[32,2,1024]{2,1,0:T(2,128)(2,1)} %reshape.414), calls=%async_computation.2 | async-start | bytes 262144 | tf_op jit(solution)/shard_map/all_to_all | solution.py:185
  118.5 4.6 %broadcast_select_fusion = bf16[32,2,128,256]{3,2,1,0:T(8,128)(2,1)} fusion(bf16[32,2,128,256]{3,2,1,0:T(8,128)(2,1)} %all-to-all-done, pred[]{:T(512)} %bitcast.59), kind=kLoop, calls=%fused_computation.6 | loop fusion | flops 2097152 | bytes 8388609 | tf_op jit(solution)/shard_map/jit(_where)/select_n | solution.py:184
  123.1 0.6 slice.150
  123.7 1.4 %all-to-all-done.1 = bf16[32,2,1024]{2,1,0:T(2,128)(2,1)S(1)} async-done(((bf16[32,2,1024]{2,1,0:T(2,128)(2,1)}), bf16[32,2,1024]{2,1,0:T(2,128)(2,1)S(1)}, u32[]{:S(2)}, u32[]{:S(2)}) %all-to-all-start.1) | async-done | bytes 131104 | tf_op jit(solution)/shard_map/all_to_all | solution.py:185
  125.2 0.1 reshape.415
  125.3 0.7 copy.105
  126.0 1.8 %fusion.21 = bf16[80,2048]{1,0:T(8,128)(2,1)} fusion(bf16[80,2048]{1,0:T(8,128)(2,1)S(1)} %copy-done.1, bf16[80,2048]{1,0:T(8,128)(2,1)} %reduce-scatter.2.cloned.1.call-done, f32[2048]{0:T(1024)S(1)} %copy-done.2), kind=kLoop, calls=%fused_computation.41 | loop fusion | flops 819200 | bytes 991232 | tf_op jit(solution)/shard_map/convert_element_type | solution.py:179
  (79 shorter events, 1.6 us)
Async XLA Ops:
  7.2 32.1 %copy-start = (bf16[256,2048]{1,0:T(8,128)(2,1)S(1)}, bf16[256,2048]{1,0:T(8,128)(2,1)}, u32[]{:S(2)}) copy-start(bf16[256,2048]{1,0:T(8,128)(2,1)} %param.24) | copy-start | bytes 3145732
  7.2 57.9 %all-gather.2.cloned.1.call-start = ((), (), s32[]{:S(2)}) async-start(), calls=%async_computation.3 | async-start | bytes 2949120 | tf_op jit(solution)/shard_map/all_gather | solution.py:138
  24.6 8.2 %copy-start.4 = (s32[40]{0:T(128)S(1)}, s32[40]{0:T(128)}, u32[]{:S(2)}) copy-start(s32[40]{0:T(128)} %param.17) | copy-start | bytes 484
  24.6 84.5 %all-to-all-start = ((bf16[32,2,128,256]{3,2,1,0:T(8,128)(2,1)}), bf16[32,2,128,256]{3,2,1,0:T(8,128)(2,1)}, u32[]{:S(2)}, u32[]{:S(2)}) async-start(bf16[32,2,128,256]{3,2,1,0:T(8,128)(2,1)} %gather_fusion), calls=%async_computation.1 | async-start | bytes 8388608 | tf_op jit(solution)/shard_map/all_to_all | solution.py:129
  32.5 93.5 %reduce-scatter.2.cloned.1.call-start = ((), (), s32[]{:S(2)}) async-start(), calls=%async_computation.4 | async-start | bytes 2949120 | tf_op jit(solution)/shard_map/reduce_scatter | solution.py:174
  37.0 17.3 %copy-start.3 = (s32[1,640]{1,0:T(1,128)S(1)}, s32[1,640]{1,0:T(1,128)}, u32[]{:S(2)}) copy-start(s32[1,640]{1,0:T(1,128)} %param.15) | copy-start | bytes 7684
  40.4 14.3 %collective-permute-start = (bf16[5,2048]{1,0:T(8,128)(2,1)S(1)}, bf16[5,2048]{1,0:T(8,128)(2,1)S(1)}, u32[]{:S(2)}, u32[]{:S(2)}) collective-permute-start(bf16[5,2048]{1,0:T(8,128)(2,1)S(1)} %get-tuple-element.33), channel_id=1, source_target_pairs={{0,1},{1,2},{2,3},{3,4},{4,5},{5,6},{6,7},{7,0},{8,9},{9,10},{10,1... | collective-permute-start | bytes 61448 | tf_op jit(solution)/shard_map/ppermute | solution.py:79
  42.3 12.9 %collective-permute-start.6 = (bf16[5,2048]{1,0:T(8,128)(2,1)S(1)}, bf16[5,2048]{1,0:T(8,128)(2,1)S(1)}, u32[]{:S(2)}, u32[]{:S(2)}) collective-permute-start(bf16[5,2048]{1,0:T(8,128)(2,1)S(1)} %get-tuple-element.34), channel_id=1, source_target_pairs={{0,7},{1,0},{2,1},{3,2},{4,3},{5,4},{6,5},{7,6},{8,15},{9,8},{10,9... | collective-permute-start | bytes 61448 | tf_op jit(solution)/shard_map/ppermute | solution.py:79
  46.4 17.6 %collective-permute-start.5 = (bf16[5,2048]{1,0:T(8,128)(2,1)S(1)}, bf16[5,2048]{1,0:T(8,128)(2,1)S(1)}, u32[]{:S(2)}, u32[]{:S(2)}) collective-permute-start(bf16[5,2048]{1,0:T(8,128)(2,1)S(1)} %get-tuple-element.35), channel_id=1, source_target_pairs={{0,6},{1,7},{2,0},{3,1},{4,2},{5,3},{6,4},{7,5},{8,14},{9,15},{10,... | collective-permute-start | bytes 61448 | tf_op jit(solution)/shard_map/ppermute | solution.py:79
  48.8 15.3 %collective-permute-start.4 = (bf16[5,2048]{1,0:T(8,128)(2,1)S(1)}, bf16[5,2048]{1,0:T(8,128)(2,1)S(1)}, u32[]{:S(2)}, u32[]{:S(2)}) collective-permute-start(bf16[5,2048]{1,0:T(8,128)(2,1)S(1)} %get-tuple-element.36), channel_id=1, source_target_pairs={{0,5},{1,6},{2,7},{3,0},{4,1},{5,2},{6,3},{7,4},{8,13},{9,14},{10,... | collective-permute-start | bytes 61448 | tf_op jit(solution)/shard_map/ppermute | solution.py:79
  50.9 13.2 %collective-permute-start.3 = (bf16[5,2048]{1,0:T(8,128)(2,1)S(1)}, bf16[5,2048]{1,0:T(8,128)(2,1)S(1)}, u32[]{:S(2)}, u32[]{:S(2)}) collective-permute-start(bf16[5,2048]{1,0:T(8,128)(2,1)S(1)} %get-tuple-element.37), channel_id=1, source_target_pairs={{0,4},{1,5},{2,6},{3,7},{4,0},{5,1},{6,2},{7,3},{8,12},{9,13},{10,... | collective-permute-start | bytes 61448 | tf_op jit(solution)/shard_map/ppermute | solution.py:79
  54.4 9.7 %copy-start.2 = (f32[2048]{0:T(1024)S(1)}, f32[2048]{0:T(1024)}, u32[]{:S(2)}) copy-start(f32[2048]{0:T(1024)} %param.25) | copy-start | bytes 24580
  54.7 9.4 %collective-permute-start.2 = (bf16[5,2048]{1,0:T(8,128)(2,1)S(1)}, bf16[5,2048]{1,0:T(8,128)(2,1)S(1)}, u32[]{:S(2)}, u32[]{:S(2)}) collective-permute-start(bf16[5,2048]{1,0:T(8,128)(2,1)S(1)} %get-tuple-element.38), channel_id=1, source_target_pairs={{0,3},{1,4},{2,5},{3,6},{4,7},{5,0},{6,1},{7,2},{8,11},{9,12},{10,... | collective-permute-start | bytes 61448 | tf_op jit(solution)/shard_map/ppermute | solution.py:79
  55.2 8.9 %collective-permute-start.1 = (bf16[5,2048]{1,0:T(8,128)(2,1)S(1)}, bf16[5,2048]{1,0:T(8,128)(2,1)S(1)}, u32[]{:S(2)}, u32[]{:S(2)}) collective-permute-start(bf16[5,2048]{1,0:T(8,128)(2,1)S(1)} %get-tuple-element.39), channel_id=1, source_target_pairs={{0,2},{1,3},{2,4},{3,5},{4,6},{5,7},{6,0},{7,1},{8,10},{9,11},{10,... | collective-permute-start | bytes 61448 | tf_op jit(solution)/shard_map/ppermute | solution.py:79
  79.5 28.1 %collective-permute-start.13 = (bf16[5,2048]{1,0:T(8,128)(2,1)S(1)}, bf16[5,2048]{1,0:T(8,128)(2,1)S(1)}, u32[]{:S(2)}, u32[]{:S(2)}) collective-permute-start(bf16[5,2048]{1,0:T(8,128)(2,1)S(1)} %fusion.51), channel_id=1, source_target_pairs={{0,7},{1,0},{2,1},{3,2},{4,3},{5,4},{6,5},{7,6},{8,15},{9,8},{10,9... | collective-permute-start | bytes 61448 | tf_op jit(solution)/shard_map/ppermute | solution.py:90
  80.7 26.9 %collective-permute-start.12 = (bf16[5,2048]{1,0:T(8,128)(2,1)S(1)}, bf16[5,2048]{1,0:T(8,128)(2,1)S(1)}, u32[]{:S(2)}, u32[]{:S(2)}) collective-permute-start(bf16[5,2048]{1,0:T(8,128)(2,1)S(1)} %fusion.51), channel_id=1, source_target_pairs={{0,6},{1,7},{2,0},{3,1},{4,2},{5,3},{6,4},{7,5},{8,14},{9,15},{10,... | collective-permute-start | bytes 61448 | tf_op jit(solution)/shard_map/ppermute | solution.py:90
  82.0 25.6 %collective-permute-start.11 = (bf16[5,2048]{1,0:T(8,128)(2,1)S(1)}, bf16[5,2048]{1,0:T(8,128)(2,1)S(1)}, u32[]{:S(2)}, u32[]{:S(2)}) collective-permute-start(bf16[5,2048]{1,0:T(8,128)(2,1)S(1)} %fusion.51), channel_id=1, source_target_pairs={{0,5},{1,6},{2,7},{3,0},{4,1},{5,2},{6,3},{7,4},{8,13},{9,14},{10,... | collective-permute-start | bytes 61448 | tf_op jit(solution)/shard_map/ppermute | solution.py:90
  84.1 23.4 %collective-permute-start.10 = (bf16[5,2048]{1,0:T(8,128)(2,1)S(1)}, bf16[5,2048]{1,0:T(8,128)(2,1)S(1)}, u32[]{:S(2)}, u32[]{:S(2)}) collective-permute-start(bf16[5,2048]{1,0:T(8,128)(2,1)S(1)} %fusion.51), channel_id=1, source_target_pairs={{0,4},{1,5},{2,6},{3,7},{4,0},{5,1},{6,2},{7,3},{8,12},{9,13},{10,... | collective-permute-start | bytes 61448 | tf_op jit(solution)/shard_map/ppermute | solution.py:90
  86.6 6.1 %collective-permute-start.7 = (bf16[5,2048]{1,0:T(8,128)(2,1)S(1)}, bf16[5,2048]{1,0:T(8,128)(2,1)S(1)}, u32[]{:S(2)}, u32[]{:S(2)}) collective-permute-start(bf16[5,2048]{1,0:T(8,128)(2,1)S(1)} %fusion.51), channel_id=1, source_target_pairs={{0,1},{1,2},{2,3},{3,4},{4,5},{5,6},{6,7},{7,0},{8,9},{9,10},{10,1... | collective-permute-start | bytes 61448 | tf_op jit(solution)/shard_map/ppermute | solution.py:90
  92.8 6.7 %collective-permute-start.8 = (bf16[5,2048]{1,0:T(8,128)(2,1)S(1)}, bf16[5,2048]{1,0:T(8,128)(2,1)S(1)}, u32[]{:S(2)}, u32[]{:S(2)}) collective-permute-start(bf16[5,2048]{1,0:T(8,128)(2,1)S(1)} %fusion.51), channel_id=1, source_target_pairs={{0,2},{1,3},{2,4},{3,5},{4,6},{5,7},{6,0},{7,1},{8,10},{9,11},{10,... | collective-permute-start | bytes 61448 | tf_op jit(solution)/shard_map/ppermute | solution.py:90
  99.5 8.0 %collective-permute-start.9 = (bf16[5,2048]{1,0:T(8,128)(2,1)S(1)}, bf16[5,2048]{1,0:T(8,128)(2,1)S(1)}, u32[]{:S(2)}, u32[]{:S(2)}) collective-permute-start(bf16[5,2048]{1,0:T(8,128)(2,1)S(1)} %fusion.51), channel_id=1, source_target_pairs={{0,3},{1,4},{2,5},{3,6},{4,7},{5,0},{6,1},{7,2},{8,11},{9,12},{10,... | collective-permute-start | bytes 61448 | tf_op jit(solution)/shard_map/ppermute | solution.py:90
  111.0 14.1 %all-to-all-start.1 = ((bf16[32,2,1024]{2,1,0:T(2,128)(2,1)}), bf16[32,2,1024]{2,1,0:T(2,128)(2,1)S(1)}, u32[]{:S(2)}, u32[]{:S(2)}) async-start(bf16[32,2,1024]{2,1,0:T(2,128)(2,1)} %reshape.414), calls=%async_computation.2 | async-start | bytes 262144 | tf_op jit(solution)/shard_map/all_to_all | solution.py:185
  118.5 7.5 %copy-start.1 = (bf16[80,2048]{1,0:T(8,128)(2,1)S(1)}, bf16[80,2048]{1,0:T(8,128)(2,1)}, u32[]{:S(2)}) copy-start(bf16[80,2048]{1,0:T(8,128)(2,1)} %param.14) | copy-start | bytes 983044
Sparse Core Ops, SparseCore 0:
  11.8 49.9 all-gather.1
  76.2 44.6 reduce-scatter.1

commit v13 on v12

--- a/solution.py
+++ b/solution.py
@@ -136,18 +136,15 @@
     )
     own_out = scatter_over_tp(decode_pieces, decode_rows, out_bias)
     normed = lax.all_gather(layer_norm(prompt_rows, norm_gain, norm_bias), "tp", axis=0, tiled=True)
-    model = qkv_weight.shape[1]
-    split_weight = qkv_weight.reshape(3, model, heads_here, HEAD_DIM)
-    split_bias = qkv_bias.reshape(3, heads_here, 1, HEAD_DIM)
-    projected = jnp.einsum(
-        "rd,cdhe->chre", normed, split_weight, preferred_element_type=jnp.float32
-    )
-    total_rows = projected.shape[2]
-    head_q = (projected[0] + split_bias[0]).astype(jnp.bfloat16)
-    head_k = (projected[1] + split_bias[1]).astype(jnp.bfloat16)
-    head_v = (projected[2] + split_bias[2]).astype(jnp.bfloat16)
+    projected = jnp.einsum("rd,cde->cre", normed, qkv_weight, preferred_element_type=jnp.float32)
+    total_rows = projected.shape[1]
+    queries = (projected[0] + qkv_bias[0]).astype(jnp.bfloat16)
+    key_rows = (projected[1] + qkv_bias[1]).astype(jnp.bfloat16)
+    value_rows = (projected[2] + qkv_bias[2]).astype(jnp.bfloat16)
+    diag = jnp.arange(heads_here)[:, None] == (jnp.arange(width) // HEAD_DIM)[None, :]
+    q_blocks = jnp.where(diag[:, None, :], queries[None], jnp.zeros((), jnp.bfloat16))
     scores = jnp.einsum(
-        "hqe,hke->hqk", head_q, head_k, preferred_element_type=jnp.float32
+        "hqc,kc->hqk", q_blocks, key_rows, preferred_element_type=jnp.float32
     ) * HEAD_DIM ** (-0.5)
     pieces = prompt_pieces[0]
     position = jnp.arange(total_rows)
@@ -156,10 +153,8 @@
     highest = jnp.max(scores, axis=-1, keepdims=True)
     weights = jnp.exp(scores - highest)
     probs = (weights / jnp.sum(weights, axis=-1, keepdims=True)).astype(jnp.bfloat16)
-    context = jnp.einsum("hqk,hke->qhe", probs, head_v, preferred_element_type=jnp.float32)
-    context = context.reshape(total_rows, width).astype(jnp.bfloat16)
-    key_rows = jnp.transpose(head_k, (1, 0, 2)).reshape(total_rows, width)
-    value_rows = jnp.transpose(head_v, (1, 0, 2)).reshape(total_rows, width)
+    mixed = jnp.einsum("hqk,kc->hqc", probs, value_rows, preferred_element_type=jnp.float32)
+    context = jnp.sum(jnp.where(diag[:, None, :], mixed, 0.0), axis=0).astype(jnp.bfloat16)
     prompt_partial = jnp.dot(context, out_weight, preferred_element_type=jnp.float32).astype(
         jnp.bfloat16
     )

time: 137 us -> 152 us (1.11)
  local copies, waits for them, and re-layouts: 15.7 us -> 23.7 us
  other arithmetic: 25.4 us -> 31.7 us
  waiting for transfers between devices: 16.4 us -> 21.1 us
  matrix products: 16.8 us -> 14.6 us
  starting transfers between devices: 45.7 us -> 43.6 us
    unnamed x20 -> x54, local copies, waits for them, and re-layouts: 1.63 us -> 7.26 us
    unnamed x1 -> x0, matrix products: 5.32 us -> none
    reshape x1 -> x0, local copies, waits for them, and re-layouts: 4.64 us -> none  [on_device(): split_weight = qkv_weight.reshape(3, model, heads_here, HEAD_DIM)]
    dot_general x2 -> x3, matrix products: 1.15 us -> 5.31 us  [the longest x1 3.93 us: on_device(): jnp.einsum('rd,cde->cre', normed, qkv_weight, preferred_element_type=jnp....]
    ppermute x7, starting transfers between devices: 11.8 us -> 9.25 us  [gather_over_tp(): lax.ppermute(own_out, 'tp', [(i, (i + shift) % n) for i in range(n)])]
    ppermute x7, waiting for transfers between devices: 14.9 us -> 17.3 us  [gather_over_tp(): lax.ppermute(own_out, 'tp', [(i, (i + shift) % n) for i in range(n)])]
    ppermute x7, waiting for transfers between devices: 0.02 us -> 2.16 us  [scatter_over_tp(): lax.ppermute(rolled[shift], 'tp', [(i, (i + shift) % n) for i in range(n)])]
    gather x1, local copies, waits for them, and re-layouts: 2.83 us -> 4.45 us  [on_device(): send_cache = padded[jnp.where(has, picks - staying, leaving)]]
  transfers between devices with their start and end apart: 18 -> 18, of which waited for: 4 -> 6; matrix products, arithmetic and copies ran while one was open for 38% -> 42% of each run, Pallas kernels for 0% -> 0%
where the time goes in v13:
time: 152 us; the launch traced here: 149 us
  starting transfers between devices  43.6 us (29%)
  other arithmetic  31.7 us (21%)
  local copies, waits for them, and re-layouts  23.7 us (16%)
  waiting for transfers between devices  21.1 us (14%)
  between operations  14.7 us (10%)
  matrix products  14.6 us (10%)
    ppermute x7, starting transfers between devices, scatter_over_tp(): lax.ppermute(rolled[shift], 'tp', [(i, (i + shift) % n) for i in range(n)])  18.5 us
    ppermute x7, waiting for transfers between devices, gather_over_tp(): lax.ppermute(own_out, 'tp', [(i, (i + shift) % n) for i in range(n)])  17.3 us
    ppermute x7, starting transfers between devices, gather_over_tp(): lax.ppermute(own_out, 'tp', [(i, (i + shift) % n) for i in range(n)])  9.25 us
    all_to_all x1, starting transfers between devices, on_device(): lax.all_to_all(send_rows, 'rep', split_axis=0, concat_axis=0, tiled=True)  8.03 us
    all_to_all x1, starting transfers between devices, on_device(): lax.all_to_all(send_cache, 'rep', split_axis=0, concat_axis=0, tiled=True)  7.81 us
    unnamed x54, local copies, waits for them, and re-layouts  7.26 us
    select_n x1, other arithmetic, on_device(): jnp.where(request_ages[0] > 0, moved_cache, jnp.zeros((), jnp.bfloat16))  4.48 us
    gather x1, local copies, waits for them, and re-layouts, on_device(): send_cache = padded[jnp.where(has, picks - staying, leaving)]  4.45 us
  transfers between devices with their start and end apart: 18, of which 6 were waited for; matrix products, arithmetic and copies ran while one was open for 42% of the time, Pallas kernels for 0%

profile of v13, /device:TPU:2, one launch (start us, length us, event | category | flops | bytes accessed | tf_op | source)
XLA Modules:
  0.0 149.4 jit_solution(10661179958171005372)
XLA Ops:
  7.2 1.3 convert_reduce_fusion
  8.5 1.2 fusion.20
  9.8 2.0 %fusion.23 = bf16[80,2048]{1,0:T(8,128)(2,1)} fusion(bf16[80,2048]{1,0:T(8,128)(2,1)} %param.14, f32[2048]{0:T(1024)} %param.21, f32[2048]{0:T(1024)} %param.20, f32[80]{0:T(128)S(1)} %add_rsqrt_fusion.1, f32[80]{0:T(128)S(1)} %broadcast_multiply_fusion.1), kind=kLoop, calls=%fused_computation.42 | loop fusion | flops 983040 | bytes 672384 | tf_op jit(solution)/shard_map/convert_element_type | solution.py:18
  11.7 0.7 fusion.73
  12.5 0.7 select_reduce_fusion.1
  13.2 1.0 convert_reduce_fusion.1
  14.3 1.1 fusion.36
  15.4 0.7 slice.97
  16.2 0.8 fusion.85
  17.1 1.6 %convolution_bitcast_fusion = f32[3,40,256]{2,1,0:T(8,128)S(1)} fusion(bf16[3,2048,256]{2,1,0:T(8,128)(2,1)S(1)} %copy-done, bf16[40,2048]{1,0:T(8,128)(2,1)} %param.16, f32[2048]{0:T(1024)} %param.21, f32[2048]{0:T(1024)} %param.20, f32[40]{0:T(128)S(1)} %add_rsqrt_fusion, f32[40]{0:T(128)S(1)} %broadcast_multiply_fusion), kind=kOutput, calls=%fused_computation.29 | convolution fusion | flops 126320640 | bytes 3449152 | tf_op jit(solution)/shard_map/rd,cde->cre/dot_general | solution.py:23
  19.4 1.8 %slice_select_fusion.1 = bf16[16,2,128,256]{3,2,1,0:T(8,128)(2,1)S(1)} fusion(bf16[40,2,128,256]{3,2,1,0:T(8,128)(2,1)} %param.19, pred[16,128]{1,0:T(8,128)(4,1)S(1)} %iota_compare_fusion.4, bf16[16,2,256]{2,1,0:T(2,128)(2,1)S(1)} %copy.55), kind=kLoop, calls=%fused_computation.20 | loop fusion | flops 1048576 | bytes 4212736 | tf_op jit(solution)/shard_map/jit(_where)/select_n | solution.py:123
  21.2 1.6 %concatenate.3 = bf16[17,2,128,256]{3,2,1,0:T(8,128)(2,1)} pad(bf16[16,2,128,256]{3,2,1,0:T(8,128)(2,1)S(1)} %slice_select_fusion.1, bf16[]{:T(256)} %constant.86.clone.1), padding=0_1x0_0x0_0x0_0 | pad | bytes 4325378 | tf_op jit(solution)/shard_map/concatenate | solution.py:126
  22.8 4.5 %gather_fusion = bf16[32,2,128,256]{3,2,1,0:T(8,128)(2,1)} fusion(bf16[17,2,128,256]{3,2,1,0:T(8,128)(2,1)} %concatenate.3, s32[1024]{0:T(1024)S(1)} %get-tuple-element.59), kind=kCustom, calls=%fused_computation.2 | custom fusion | bytes 8388736 | tf_op jit(solution)/shard_map/gather | solution.py:127
  27.3 7.8 %all-to-all-start = ((bf16[32,2,128,256]{3,2,1,0:T(8,128)(2,1)}), bf16[32,2,128,256]{3,2,1,0:T(8,128)(2,1)}, u32[]{:S(2)}, u32[]{:S(2)}) async-start(bf16[32,2,128,256]{3,2,1,0:T(8,128)(2,1)} %gather_fusion), calls=%async_computation.1 | async-start | bytes 8388608 | tf_op jit(solution)/shard_map/all_to_all | solution.py:129
  35.5 2.6 %fusion.87 = (f32[40,2]{1,0:T(8,128)S(1)}, f32[40,2,128]{2,1,0:T(2,128)S(1)}) fusion(pred[2,256]{1,0:T(4,128)(4,1)S(1)} %iota_compare_fusion.5, bf16[40,256]{1,0:T(8,128)(2,1)S(1)} %get-tuple-element.42, pred[40,128]{1,0:T(8,128)(4,1)S(1)} %iota_compare_fusion.1, bf16[40,2,128,256]{3,2,1,0:T(8,128)(2,1)} %param.19), kind=kOutput, calls=%fused_computation.186 | convolution fusion | flops 5294000 | bytes 2688832 | tf_op jit(solution)/shard_map/rhc,rlc->rhl/dot_general | solution.py:37
  38.8 0.7 gather_fusion.1
  39.6 2.4 %fusion.15 = f32[40,256]{1,0:T(8,128)S(1)} fusion(pred[2,256]{1,0:T(4,128)(4,1)S(1)} %iota_compare_fusion.5, f32[40,2,128]{2,1,0:T(2,128)S(1)} %get-tuple-element.55, f32[40,2]{1,0:T(8,128)S(1)} %copy.61, f32[40,2]{1,0:T(8,128)S(1)} %copy.59, bf16[40,2,128,256]{3,2,1,0:T(8,128)(2,1)} %param.19), kind=kOutput, calls=%fused_computation.31 | convolution fusion | flops 5304320 | bytes 2704512 | tf_op jit(solution)/shard_map/rhl,rlc->rhc/dot_general | solution.py:57
  42.4 0.8 reshape.360
  43.1 1.5 %gather_fusion.3 = bf16[8,5,2048]{2,1,0:T(8,128)(2,1)S(1)} fusion(bf16[8,5,2048]{2,1,0:T(8,128)(2,1)} %reshape.360, s32[1024]{0:T(1024)S(1)} %get-tuple-element.60), kind=kCustom, calls=%fused_computation.clone | custom fusion | bytes 327712 | tf_op jit(solution)/shard_map/jit(_take)/gather | solution.py:76
  44.8 0.7 copy-done.5
  45.5 2.0 %collective-permute-start = (bf16[5,2048]{1,0:T(8,128)(2,1)S(1)}, bf16[5,2048]{1,0:T(8,128)(2,1)S(1)}, u32[]{:S(2)}, u32[]{:S(2)}) collective-permute-start(bf16[5,2048]{1,0:T(8,128)(2,1)S(1)} %get-tuple-element.33), channel_id=1, source_target_pairs={{0,1},{1,2},{2,3},{3,4},{4,5},{5,6},{6,7},{7,0},{8,9},{9,10},{10,1... | collective-permute-start | bytes 61448 | tf_op jit(solution)/shard_map/ppermute | solution.py:79
  47.5 4.1 %collective-permute-start.6 = (bf16[5,2048]{1,0:T(8,128)(2,1)S(1)}, bf16[5,2048]{1,0:T(8,128)(2,1)S(1)}, u32[]{:S(2)}, u32[]{:S(2)}) collective-permute-start(bf16[5,2048]{1,0:T(8,128)(2,1)S(1)} %get-tuple-element.34), channel_id=1, source_target_pairs={{0,7},{1,0},{2,1},{3,2},{4,3},{5,4},{6,5},{7,6},{8,15},{9,8},{10,9... | collective-permute-start | bytes 61448 | tf_op jit(solution)/shard_map/ppermute | solution.py:79
  51.6 2.4 %collective-permute-start.5 = (bf16[5,2048]{1,0:T(8,128)(2,1)S(1)}, bf16[5,2048]{1,0:T(8,128)(2,1)S(1)}, u32[]{:S(2)}, u32[]{:S(2)}) collective-permute-start(bf16[5,2048]{1,0:T(8,128)(2,1)S(1)} %get-tuple-element.35), channel_id=1, source_target_pairs={{0,6},{1,7},{2,0},{3,1},{4,2},{5,3},{6,4},{7,5},{8,14},{9,15},{10,... | collective-permute-start | bytes 61448 | tf_op jit(solution)/shard_map/ppermute | solution.py:79
  54.0 2.0 %collective-permute-start.4 = (bf16[5,2048]{1,0:T(8,128)(2,1)S(1)}, bf16[5,2048]{1,0:T(8,128)(2,1)}, u32[]{:S(2)}, u32[]{:S(2)}) collective-permute-start(bf16[5,2048]{1,0:T(8,128)(2,1)S(1)} %get-tuple-element.36), channel_id=1, source_target_pairs={{0,5},{1,6},{2,7},{3,0},{4,1},{5,2},{6,3},{7,4},{8,13},{9,14},{10,... | collective-permute-start | bytes 61448 | tf_op jit(solution)/shard_map/ppermute | solution.py:79
  56.0 3.5 %collective-permute-start.3 = (bf16[5,2048]{1,0:T(8,128)(2,1)S(1)}, bf16[5,2048]{1,0:T(8,128)(2,1)}, u32[]{:S(2)}, u32[]{:S(2)}) collective-permute-start(bf16[5,2048]{1,0:T(8,128)(2,1)S(1)} %get-tuple-element.37), channel_id=1, source_target_pairs={{0,4},{1,5},{2,6},{3,7},{4,0},{5,1},{6,2},{7,3},{8,12},{9,13},{10,... | collective-permute-start | bytes 61448 | tf_op jit(solution)/shard_map/ppermute | solution.py:79
  59.5 1.3 iota_compare_fusion.2
  60.8 1.0 fusion.9
  62.8 4.1 %collective-permute-start.1 = (bf16[5,2048]{1,0:T(8,128)(2,1)S(1)}, bf16[5,2048]{1,0:T(8,128)(2,1)S(1)}, u32[]{:S(2)}, u32[]{:S(2)}) collective-permute-start(bf16[5,2048]{1,0:T(8,128)(2,1)S(1)} %get-tuple-element.39), channel_id=1, source_target_pairs={{0,2},{1,3},{2,4},{3,5},{4,6},{5,7},{6,0},{7,1},{8,10},{9,11},{10,... | collective-permute-start | bytes 61448 | tf_op jit(solution)/shard_map/ppermute | solution.py:79
  67.6 1.8 %collective-permute-done.2 = bf16[5,2048]{1,0:T(8,128)(2,1)S(1)} collective-permute-done((bf16[5,2048]{1,0:T(8,128)(2,1)S(1)}, bf16[5,2048]{1,0:T(8,128)(2,1)S(1)}, u32[]{:S(2)}, u32[]{:S(2)}) %collective-permute-start.2) | collective-permute-done | bytes 20512 | tf_op jit(solution)/shard_map/ppermute | solution.py:79
  69.8 1.0 fusion.60
  70.8 3.9 %fusion.11 = f32[3,640,256]{2,1,0:T(8,128)S(1)} fusion(bf16[3,2048,256]{2,1,0:T(8,128)(2,1)S(1)} %copy-done, bf16[640,2048]{1,0:T(8,128)(2,1)} %all-gather.2.cloned.1.call-done), kind=kOutput, calls=%fused_computation.27 | convolution fusion | flops 2013265920 | bytes 7733248 | tf_op jit(solution)/shard_map/rd,cde->cre/dot_general | solution.py:139
  75.0 0.6 fusion.31
  75.8 2.0 %fusion.86 = (f32[2,640]{1,0:T(2,128)S(1)}, f32[2,640,640]{1,2,0:T(8,128)S(1)}) fusion(f32[2,640,640]{1,2,0:T(8,128)S(1)} %fusion.31, pred[640,640]{0,1:T(8,128)(4,1)S(1)} %copy-done.6), kind=kOutput, calls=%fused_computation.185 | output fusion | flops 4915839 | bytes 6968320 | tf_op jit(solution)/shard_map/sub | solution.py:154
  77.7 0.8 select_reduce_fusion
  79.0 2.4 %convolution_convert_fusion = bf16[640,2048]{1,0:T(8,128)(2,1)} fusion(bf16[256,2048]{1,0:T(8,128)(2,1)S(1)} %copy-done.2, bf16[640,256]{1,0:T(8,128)(2,1)S(1)} %select_reduce_fusion), kind=kOutput, calls=%fused_computation.10 | convolution fusion | flops 672399360 | bytes 3997696 | tf_op jit(solution)/shard_map/dot_general | solution.py:158
  81.4 3.4 %slice_select_fusion = bf16[24,2,128,256]{3,2,1,0:T(8,128)(2,1)} fusion(bf16[40,2,128,256]{3,2,1,0:T(8,128)(2,1)} %param.19, pred[24,128]{1,0:T(8,128)(4,1)} %iota_compare_fusion.2, bf16[24,2,256]{2,1,0:T(2,128)(2,1)S(1)} %copy.64), kind=kLoop, calls=%fused_computation.11 | loop fusion | flops 1572864 | bytes 6319104 | tf_op jit(solution)/shard_map/jit(_where)/select_n | solution.py:166
  85.3 4.1 %collective-permute-start.12 = (bf16[5,2048]{1,0:T(8,128)(2,1)S(1)}, bf16[5,2048]{1,0:T(8,128)(2,1)S(1)}, u32[]{:S(2)}, u32[]{:S(2)}) collective-permute-start(bf16[5,2048]{1,0:T(8,128)(2,1)S(1)} %fusion.60), channel_id=1, source_target_pairs={{0,6},{1,7},{2,0},{3,1},{4,2},{5,3},{6,4},{7,5},{8,14},{9,15},{10,... | collective-permute-start | bytes 61448 | tf_op jit(solution)/shard_map/ppermute | solution.py:90
  89.4 1.6 %collective-permute-start.11 = (bf16[5,2048]{1,0:T(8,128)(2,1)S(1)}, bf16[5,2048]{1,0:T(8,128)(2,1)S(1)}, u32[]{:S(2)}, u32[]{:S(2)}) collective-permute-start(bf16[5,2048]{1,0:T(8,128)(2,1)S(1)} %fusion.60), channel_id=1, source_target_pairs={{0,5},{1,6},{2,7},{3,0},{4,1},{5,2},{6,3},{7,4},{8,13},{9,14},{10,... | collective-permute-start | bytes 61448 | tf_op jit(solution)/shard_map/ppermute | solution.py:90
  91.0 2.2 %collective-permute-start.10 = (bf16[5,2048]{1,0:T(8,128)(2,1)S(1)}, bf16[5,2048]{1,0:T(8,128)(2,1)S(1)}, u32[]{:S(2)}, u32[]{:S(2)}) collective-permute-start(bf16[5,2048]{1,0:T(8,128)(2,1)S(1)} %fusion.60), channel_id=1, source_target_pairs={{0,4},{1,5},{2,6},{3,7},{4,0},{5,1},{6,2},{7,3},{8,12},{9,13},{10,... | collective-permute-start | bytes 61448 | tf_op jit(solution)/shard_map/ppermute | solution.py:90
  93.2 0.6 bitcast_dynamic-update-slice_fusion.7
  93.9 0.9 pad_maximum_fusion
  94.8 4.6 %collective-permute-done.7 = bf16[5,2048]{1,0:T(8,128)(2,1)S(1)} collective-permute-done((bf16[5,2048]{1,0:T(8,128)(2,1)S(1)}, bf16[5,2048]{1,0:T(8,128)(2,1)S(1)}, u32[]{:S(2)}, u32[]{:S(2)}) %collective-permute-start.7) | collective-permute-done | bytes 20512 | tf_op jit(solution)/shard_map/ppermute | solution.py:90
  99.9 0.6 bitcast_dynamic-update-slice_fusion.6
  100.6 5.9 %collective-permute-done.8 = bf16[5,2048]{1,0:T(8,128)(2,1)S(1)} collective-permute-done((bf16[5,2048]{1,0:T(8,128)(2,1)S(1)}, bf16[5,2048]{1,0:T(8,128)(2,1)S(1)}, u32[]{:S(2)}, u32[]{:S(2)}) %collective-permute-start.8) | collective-permute-done | bytes 20512 | tf_op jit(solution)/shard_map/ppermute | solution.py:90
  106.7 0.6 bitcast_dynamic-update-slice_fusion.5
  107.4 6.8 %collective-permute-done.9 = bf16[5,2048]{1,0:T(8,128)(2,1)S(1)} collective-permute-done((bf16[5,2048]{1,0:T(8,128)(2,1)S(1)}, bf16[5,2048]{1,0:T(8,128)(2,1)S(1)}, u32[]{:S(2)}, u32[]{:S(2)}) %collective-permute-start.9) | collective-permute-done | bytes 20512 | tf_op jit(solution)/shard_map/ppermute | solution.py:90
  114.2 0.6 bitcast_dynamic-update-slice_fusion.4
  114.8 0.6 bitcast_dynamic-update-slice_fusion.3
  115.4 0.6 bitcast_dynamic-update-slice_fusion.2
  116.0 0.6 bitcast_dynamic-update-slice_fusion.1
  116.7 0.6 bitcast_dynamic-update-slice_fusion
  117.3 1.6 %gather_fusion.4 = bf16[8,5,2048]{2,1,0:T(8,128)(2,1)S(1)} fusion(bf16[8,5,2048]{2,1,0:T(8,128)(2,1)} %bitcast_dynamic-update-slice_fusion, s32[1024]{0:T(1024)} %pad_clamp_fusion.1), kind=kCustom, calls=%fused_computation.1.clone | custom fusion | bytes 327712 | tf_op jit(solution)/shard_map/jit(_take)/gather | solution.py:92
  118.9 0.8 broadcast_select_fusion.1
  119.7 1.0 reshape.361
  120.7 0.8 gather_fusion.2
  121.5 0.7 broadcast_select_fusion.3
  122.8 1.6 %reduce.1 = bf16[32,2048]{1,0:T(8,128)(2,1)S(1)} reduce(bf16[32,1,2048]{2,0,1:T(8,128)(2,1)} %bitcast.145, bf16[]{:T(256)} %broadcast.372), dimensions={1}, to_apply=%copy.65.reduce_sub_computation | reduce | bytes 262146 | tf_op jit(solution)/shard_map/all_to_all | solution.py:180
  124.4 0.7 reshape.414
  125.1 8.0 %all-to-all-start.1 = ((bf16[32,2,1024]{2,1,0:T(2,128)(2,1)}), bf16[32,2,1024]{2,1,0:T(2,128)(2,1)S(1)}, u32[]{:S(2)}, u32[]{:S(2)}) async-start(bf16[32,2,1024]{2,1,0:T(2,128)(2,1)} %reshape.414), calls=%async_computation.2 | async-start | bytes 262144 | tf_op jit(solution)/shard_map/all_to_all | solution.py:180
  133.1 4.5 %broadcast_select_fusion = bf16[32,2,128,256]{3,2,1,0:T(8,128)(2,1)} fusion(bf16[32,2,128,256]{3,2,1,0:T(8,128)(2,1)} %all-to-all-done, pred[]{:T(512)} %bitcast.50), kind=kLoop, calls=%fused_computation.6 | loop fusion | flops 2097152 | bytes 8388609 | tf_op jit(solution)/shard_map/jit(_where)/select_n | solution.py:179
  137.6 0.6 slice.147
  138.3 1.5 %all-to-all-done.1 = bf16[32,2,1024]{2,1,0:T(2,128)(2,1)S(1)} async-done(((bf16[32,2,1024]{2,1,0:T(2,128)(2,1)}), bf16[32,2,1024]{2,1,0:T(2,128)(2,1)S(1)}, u32[]{:S(2)}, u32[]{:S(2)}) %all-to-all-start.1) | async-done | bytes 131104 | tf_op jit(solution)/shard_map/all_to_all | solution.py:180
  139.9 0.7 copy.75
  140.6 1.9 %fusion.25 = bf16[80,2048]{1,0:T(8,128)(2,1)} fusion(bf16[80,2048]{1,0:T(8,128)(2,1)} %param.14, bf16[80,2048]{1,0:T(8,128)(2,1)} %reduce-scatter.2.cloned.1.call-done, f32[2048]{0:T(1024)S(1)} %copy-done.7), kind=kLoop, calls=%fused_computation.44 | loop fusion | flops 819200 | bytes 991232 | tf_op jit(solution)/shard_map/convert_element_type | solution.py:174
  (111 shorter events, 7.1 us)
Async XLA Ops:
  7.2 9.9 %copy-start = (bf16[3,2048,256]{2,1,0:T(8,128)(2,1)S(1)}, bf16[3,2048,256]{2,1,0:T(8,128)(2,1)}, u32[]{:S(2)}) copy-start(bf16[3,2048,256]{2,1,0:T(8,128)(2,1)} %param.22) | copy-start | bytes 9437188
  7.2 63.6 %all-gather.2.cloned.1.call-start = ((), (), s32[]{:S(2)}) async-start(), calls=%async_computation.3 | async-start | bytes 2949120 | tf_op jit(solution)/shard_map/all_gather | solution.py:138
  12.5 8.7 %copy-start.17 = (pred[32]{0:T(512)(128)(4,1)}, pred[32]{0:T(512)(128)(4,1)S(1)}, u32[]{:S(2)}) copy-start(pred[32]{0:T(512)(128)(4,1)S(1)} %fusion.73) | copy-start | bytes 100
  17.1 1.7 %copy-start.12 = (f32[1,256]{1,0:T(1,128)}, f32[1,256]{1,0:T(1,128)S(1)}, u32[]{:S(2)}) copy-start(f32[1,256]{1,0:T(1,128)S(1)} %get-tuple-element.45) | copy-start | bytes 3076
  17.1 18.2 %copy-start.8 = (f32[1,256]{1,0:T(1,128)}, f32[1,256]{1,0:T(1,128)S(1)}, u32[]{:S(2)}) copy-start(f32[1,256]{1,0:T(1,128)S(1)} %get-tuple-element.47) | copy-start | bytes 3076
  17.1 18.2 %copy-start.10 = (f32[1,256]{1,0:T(1,128)}, f32[1,256]{1,0:T(1,128)S(1)}, u32[]{:S(2)}) copy-start(f32[1,256]{1,0:T(1,128)S(1)} %get-tuple-element.46) | copy-start | bytes 3076
  27.3 8.2 %copy-start.19 = (s32[40]{0:T(128)S(1)}, s32[40]{0:T(128)}, u32[]{:S(2)}) copy-start(s32[40]{0:T(128)} %param.17) | copy-start | bytes 484
  27.3 95.0 %all-to-all-start = ((bf16[32,2,128,256]{3,2,1,0:T(8,128)(2,1)}), bf16[32,2,128,256]{3,2,1,0:T(8,128)(2,1)}, u32[]{:S(2)}, u32[]{:S(2)}) async-start(bf16[32,2,128,256]{3,2,1,0:T(8,128)(2,1)} %gather_fusion), calls=%async_computation.1 | async-start | bytes 8388608 | tf_op jit(solution)/shard_map/all_to_all | solution.py:129
  35.1 105.6 %reduce-scatter.2.cloned.1.call-start = ((), (), s32[]{:S(2)}) async-start(), calls=%async_computation.4 | async-start | bytes 2949120 | tf_op jit(solution)/shard_map/reduce_scatter | solution.py:169
  35.5 6.6 %copy-start.14 = (pred[2,256]{1,0:T(4,128)(4,1)}, pred[2,256]{1,0:T(4,128)(4,1)S(1)}, u32[]{:S(2)}) copy-start(pred[2,256]{1,0:T(4,128)(4,1)S(1)} %iota_compare_fusion.5) | copy-start | bytes 1540
  39.6 2.4 %copy-start.1 = (bf16[256,2048]{1,0:T(8,128)(2,1)S(1)}, bf16[256,2048]{1,0:T(8,128)(2,1)}, u32[]{:S(2)}) copy-start(bf16[256,2048]{1,0:T(8,128)(2,1)} %param.24) | copy-start | bytes 3145732
  39.6 19.9 %copy-start.16 = (s32[1,640]{1,0:T(1,128)S(1)}, s32[1,640]{1,0:T(1,128)}, u32[]{:S(2)}) copy-start(s32[1,640]{1,0:T(1,128)} %param.15) | copy-start | bytes 7684
  39.6 30.2 %copy-start.7 = (f32[2048]{0:T(1024)S(1)}, f32[2048]{0:T(1024)}, u32[]{:S(2)}) copy-start(f32[2048]{0:T(1024)} %param.25) | copy-start | bytes 24580
  42.0 25.5 %copy-start.20 = (s32[40]{0:T(128)S(1)}, s32[40]{0:T(128)}, u32[]{:S(2)}) copy-start(s32[40]{0:T(128)} %param.17) | copy-start | bytes 484
  44.8 0.7 copy-start.5
  45.5 17.0 %collective-permute-start = (bf16[5,2048]{1,0:T(8,128)(2,1)S(1)}, bf16[5,2048]{1,0:T(8,128)(2,1)S(1)}, u32[]{:S(2)}, u32[]{:S(2)}) collective-permute-start(bf16[5,2048]{1,0:T(8,128)(2,1)S(1)} %get-tuple-element.33), channel_id=1, source_target_pairs={{0,1},{1,2},{2,3},{3,4},{4,5},{5,6},{6,7},{7,0},{8,9},{9,10},{10,1... | collective-permute-start | bytes 61448 | tf_op jit(solution)/shard_map/ppermute | solution.py:79
  47.5 15.3 %collective-permute-start.6 = (bf16[5,2048]{1,0:T(8,128)(2,1)S(1)}, bf16[5,2048]{1,0:T(8,128)(2,1)S(1)}, u32[]{:S(2)}, u32[]{:S(2)}) collective-permute-start(bf16[5,2048]{1,0:T(8,128)(2,1)S(1)} %get-tuple-element.34), channel_id=1, source_target_pairs={{0,7},{1,0},{2,1},{3,2},{4,3},{5,4},{6,5},{7,6},{8,15},{9,8},{10,9... | collective-permute-start | bytes 61448 | tf_op jit(solution)/shard_map/ppermute | solution.py:79
  51.6 16.0 %collective-permute-start.5 = (bf16[5,2048]{1,0:T(8,128)(2,1)S(1)}, bf16[5,2048]{1,0:T(8,128)(2,1)S(1)}, u32[]{:S(2)}, u32[]{:S(2)}) collective-permute-start(bf16[5,2048]{1,0:T(8,128)(2,1)S(1)} %get-tuple-element.35), channel_id=1, source_target_pairs={{0,6},{1,7},{2,0},{3,1},{4,2},{5,3},{6,4},{7,5},{8,14},{9,15},{10,... | collective-permute-start | bytes 61448 | tf_op jit(solution)/shard_map/ppermute | solution.py:79
  54.0 13.6 %collective-permute-start.4 = (bf16[5,2048]{1,0:T(8,128)(2,1)S(1)}, bf16[5,2048]{1,0:T(8,128)(2,1)}, u32[]{:S(2)}, u32[]{:S(2)}) collective-permute-start(bf16[5,2048]{1,0:T(8,128)(2,1)S(1)} %get-tuple-element.36), channel_id=1, source_target_pairs={{0,5},{1,6},{2,7},{3,0},{4,1},{5,2},{6,3},{7,4},{8,13},{9,14},{10,... | collective-permute-start | bytes 61448 | tf_op jit(solution)/shard_map/ppermute | solution.py:79
  56.0 11.6 %collective-permute-start.3 = (bf16[5,2048]{1,0:T(8,128)(2,1)S(1)}, bf16[5,2048]{1,0:T(8,128)(2,1)}, u32[]{:S(2)}, u32[]{:S(2)}) collective-permute-start(bf16[5,2048]{1,0:T(8,128)(2,1)S(1)} %get-tuple-element.37), channel_id=1, source_target_pairs={{0,4},{1,5},{2,6},{3,7},{4,0},{5,1},{6,2},{7,3},{8,12},{9,13},{10,... | collective-permute-start | bytes 61448 | tf_op jit(solution)/shard_map/ppermute | solution.py:79
  62.5 6.9 %collective-permute-start.2 = (bf16[5,2048]{1,0:T(8,128)(2,1)S(1)}, bf16[5,2048]{1,0:T(8,128)(2,1)S(1)}, u32[]{:S(2)}, u32[]{:S(2)}) collective-permute-start(bf16[5,2048]{1,0:T(8,128)(2,1)S(1)} %get-tuple-element.38), channel_id=1, source_target_pairs={{0,3},{1,4},{2,5},{3,6},{4,7},{5,0},{6,1},{7,2},{8,11},{9,12},{10,... | collective-permute-start | bytes 61448 | tf_op jit(solution)/shard_map/ppermute | solution.py:79
  62.8 6.9 %collective-permute-start.1 = (bf16[5,2048]{1,0:T(8,128)(2,1)S(1)}, bf16[5,2048]{1,0:T(8,128)(2,1)S(1)}, u32[]{:S(2)}, u32[]{:S(2)}) collective-permute-start(bf16[5,2048]{1,0:T(8,128)(2,1)S(1)} %get-tuple-element.39), channel_id=1, source_target_pairs={{0,2},{1,3},{2,4},{3,5},{4,6},{5,7},{6,0},{7,1},{8,10},{9,11},{10,... | collective-permute-start | bytes 61448 | tf_op jit(solution)/shard_map/ppermute | solution.py:79
  70.7 4.0 %copy-start.11 = (f32[1,256]{1,0:T(1,128)S(1)}, f32[1,256]{1,0:T(1,128)}, u32[]{:S(2)}) copy-start(f32[1,256]{1,0:T(1,128)} %copy-done.10) | copy-start | bytes 3076
  70.8 4.1 %copy-start.9 = (f32[1,256]{1,0:T(1,128)S(1)}, f32[1,256]{1,0:T(1,128)}, u32[]{:S(2)}) copy-start(f32[1,256]{1,0:T(1,128)} %copy-done.8) | copy-start | bytes 3076
  70.8 4.1 %copy-start.13 = (f32[1,256]{1,0:T(1,128)S(1)}, f32[1,256]{1,0:T(1,128)}, u32[]{:S(2)}) copy-start(f32[1,256]{1,0:T(1,128)} %copy-done.12) | copy-start | bytes 3076
  70.8 4.2 %copy-start.15 = (pred[2,256]{1,0:T(4,128)(4,1)S(1)}, pred[2,256]{1,0:T(4,128)(4,1)}, u32[]{:S(2)}) copy-start(pred[2,256]{1,0:T(4,128)(4,1)} %copy-done.14) | copy-start | bytes 1540
  74.8 1.0 copy-start.6
  75.0 2.7 %copy-start.3 = (bf16[640,256]{1,0:T(8,128)(2,1)}, bf16[640,256]{1,0:T(8,128)(2,1)S(1)}, u32[]{:S(2)}) copy-start(bf16[640,256]{1,0:T(8,128)(2,1)S(1)} %get-tuple-element.22) | copy-start | bytes 983044
  77.7 1.2 copy-start.2
  81.4 12.5 %copy-start.4 = (bf16[640,256]{1,0:T(8,128)(2,1)S(1)}, bf16[640,256]{1,0:T(8,128)(2,1)}, u32[]{:S(2)}) copy-start(bf16[640,256]{1,0:T(8,128)(2,1)} %copy-done.3) | copy-start | bytes 983044
  81.4 37.5 %copy-start.21 = (pred[8]{0:T(512)(128)(4,1)S(1)}, pred[8]{0:T(512)(128)(4,1)}, u32[]{:S(2)}) copy-start(pred[8]{0:T(512)(128)(4,1)} %compare_and_fusion) | copy-start | bytes 28
  84.8 36.7 %copy-start.18 = (pred[32]{0:T(512)(128)(4,1)S(1)}, pred[32]{0:T(512)(128)(4,1)}, u32[]{:S(2)}) copy-start(pred[32]{0:T(512)(128)(4,1)} %copy-done.17) | copy-start | bytes 100
  84.8 31.8 %collective-permute-start.13 = (bf16[5,2048]{1,0:T(8,128)(2,1)S(1)}, bf16[5,2048]{1,0:T(8,128)(2,1)S(1)}, u32[]{:S(2)}, u32[]{:S(2)}) collective-permute-start(bf16[5,2048]{1,0:T(8,128)(2,1)S(1)} %fusion.60), channel_id=1, source_target_pairs={{0,7},{1,0},{2,1},{3,2},{4,3},{5,4},{6,5},{7,6},{8,15},{9,8},{10,9... | collective-permute-start | bytes 61448 | tf_op jit(solution)/shard_map/ppermute | solution.py:90
  85.3 30.7 %collective-permute-start.12 = (bf16[5,2048]{1,0:T(8,128)(2,1)S(1)}, bf16[5,2048]{1,0:T(8,128)(2,1)S(1)}, u32[]{:S(2)}, u32[]{:S(2)}) collective-permute-start(bf16[5,2048]{1,0:T(8,128)(2,1)S(1)} %fusion.60), channel_id=1, source_target_pairs={{0,6},{1,7},{2,0},{3,1},{4,2},{5,3},{6,4},{7,5},{8,14},{9,15},{10,... | collective-permute-start | bytes 61448 | tf_op jit(solution)/shard_map/ppermute | solution.py:90
  89.4 26.0 %collective-permute-start.11 = (bf16[5,2048]{1,0:T(8,128)(2,1)S(1)}, bf16[5,2048]{1,0:T(8,128)(2,1)S(1)}, u32[]{:S(2)}, u32[]{:S(2)}) collective-permute-start(bf16[5,2048]{1,0:T(8,128)(2,1)S(1)} %fusion.60), channel_id=1, source_target_pairs={{0,5},{1,6},{2,7},{3,0},{4,1},{5,2},{6,3},{7,4},{8,13},{9,14},{10,... | collective-permute-start | bytes 61448 | tf_op jit(solution)/shard_map/ppermute | solution.py:90
  91.0 23.8 %collective-permute-start.10 = (bf16[5,2048]{1,0:T(8,128)(2,1)S(1)}, bf16[5,2048]{1,0:T(8,128)(2,1)S(1)}, u32[]{:S(2)}, u32[]{:S(2)}) collective-permute-start(bf16[5,2048]{1,0:T(8,128)(2,1)S(1)} %fusion.60), channel_id=1, source_target_pairs={{0,4},{1,5},{2,6},{3,7},{4,0},{5,1},{6,2},{7,3},{8,12},{9,13},{10,... | collective-permute-start | bytes 61448 | tf_op jit(solution)/shard_map/ppermute | solution.py:90
  93.2 6.1 %collective-permute-start.7 = (bf16[5,2048]{1,0:T(8,128)(2,1)S(1)}, bf16[5,2048]{1,0:T(8,128)(2,1)S(1)}, u32[]{:S(2)}, u32[]{:S(2)}) collective-permute-start(bf16[5,2048]{1,0:T(8,128)(2,1)S(1)} %fusion.60), channel_id=1, source_target_pairs={{0,1},{1,2},{2,3},{3,4},{4,5},{5,6},{6,7},{7,0},{8,9},{9,10},{10,1... | collective-permute-start | bytes 61448 | tf_op jit(solution)/shard_map/ppermute | solution.py:90
  99.4 7.1 %collective-permute-start.8 = (bf16[5,2048]{1,0:T(8,128)(2,1)S(1)}, bf16[5,2048]{1,0:T(8,128)(2,1)S(1)}, u32[]{:S(2)}, u32[]{:S(2)}) collective-permute-start(bf16[5,2048]{1,0:T(8,128)(2,1)S(1)} %fusion.60), channel_id=1, source_target_pairs={{0,2},{1,3},{2,4},{3,5},{4,6},{5,7},{6,0},{7,1},{8,10},{9,11},{10,... | collective-permute-start | bytes 61448 | tf_op jit(solution)/shard_map/ppermute | solution.py:90
  106.5 7.7 %collective-permute-start.9 = (bf16[5,2048]{1,0:T(8,128)(2,1)S(1)}, bf16[5,2048]{1,0:T(8,128)(2,1)S(1)}, u32[]{:S(2)}, u32[]{:S(2)}) collective-permute-start(bf16[5,2048]{1,0:T(8,128)(2,1)S(1)} %fusion.60), channel_id=1, source_target_pairs={{0,3},{1,4},{2,5},{3,6},{4,7},{5,0},{6,1},{7,2},{8,11},{9,12},{10,... | collective-permute-start | bytes 61448 | tf_op jit(solution)/shard_map/ppermute | solution.py:90
  125.1 14.7 %all-to-all-start.1 = ((bf16[32,2,1024]{2,1,0:T(2,128)(2,1)}), bf16[32,2,1024]{2,1,0:T(2,128)(2,1)S(1)}, u32[]{:S(2)}, u32[]{:S(2)}) async-start(bf16[32,2,1024]{2,1,0:T(2,128)(2,1)} %reshape.414), calls=%async_computation.2 | async-start | bytes 262144 | tf_op jit(solution)/shard_map/all_to_all | solution.py:180
Sparse Core Ops, SparseCore 0:
  11.9 47.1 all-gather.1
  81.5 46.2 reduce-scatter.1
